TPU v7x, 128 devices: a whole 4x4x4 slice. The times are simulated.
128 devices in a mesh: group: 16 (over x, z), mp: 8 (over y, core).
Axes of the slice: x: 4, y: 4, z: 4, core: 2. Of those that a mesh axis runs over, the one named last changes fastest.
Arguments:
- stream: bfloat16 [8192, 3584], P('group', 'mp'), may hold values from -6 to 6
- prenorm_gain: float32 [3584], replicated, may hold values from 0.25 to 12
- query_weight: bfloat16 [3584, 4096], P(None, 'mp'), may hold values from -0.09375 to 0.09375
- key_weight: bfloat16 [3584, 2048], P(None, 'mp'), may hold values from -0.09375 to 0.09375
- value_weight: bfloat16 [3584, 2048], P(None, 'mp'), may hold values from -0.09375 to 0.09375
- output_weight: bfloat16 [4096, 3584], P('mp'), may hold values from -0.09375 to 0.09375
- adapter_down_rows: bfloat16 [64, 16, 3584], P('group', None, 'mp'), may hold values from -0.09375 to 0.09375
- adapter_up_query: bfloat16 [64, 16, 4096], P('group', None, 'mp'), may hold values from -1.5 to 1.5
- request_adapter: int32 [16, 4], replicated, may hold values from 0 to 63
- adapter_row_index: int32 [64], replicated, may hold values from 0 to 63, each once
- request_token_length: int32 [16, 4], replicated, may hold values from 1 to 256, 512 in all within a row
- continues_previous: int32 [16], replicated, may hold values from 0 to 1, as said below
- request_cache_block: int32 [16, 4], replicated, may hold values from 0 to 31, as said below
- cached_length: int32 [16, 4], replicated, may hold values from 1 to 256
- cached_rotated_keys: bfloat16 [32, 256, 2048], P('group', None, 'mp'), may hold values from -6 to 6
- cached_value_rows: bfloat16 [32, 256, 2048], P('group', None, 'mp'), may hold values from -6 to 6
Outputs:
- attn_out: bfloat16 [8192, 3584], P('group', 'mp')
Inputs may be any that keep to these rules, and one draw needn't show every extreme that they name: `continues_previous`: the first group has 0; some group has 1. `request_cache_block`: the owner of block b is group b // 2; blocks may be shared by requests.
All inputs are finite; a program needn't handle non-finite values.
Results may differ from a plain program's by a relative error of at most 0.017.
The roundings to bfloat16 on the way count: a program that leaves them out, or rounds other values in their place, can miss the bound.
Values may be sent and summed in bfloat16 or wider, within the bound.
No kernel may reach another device: no remote copies, remote signals or barrier semaphores. Data moves between devices by JAX's collectives and lax.ppermute only.
A program may use at most 128 MiB of HBM per device.

v0:
```python
import jax
import jax.numpy as jnp
from jax import lax
from jax.sharding import Mesh, PartitionSpec as P

HEAD_WIDTH = 256
REQS = 4


adapter_scale = 2.0


def shifted(value, axis, steps):
    count = lax.axis_size(axis)
    first, last = (max(0, -steps), min(count, count - steps))
    return lax.ppermute(value, axis, [(source, source + steps) for source in range(first, last)])


def rotate(values, position, head_size):
    count = values.shape[0]
    shaped = values.reshape(count, -1, head_size)
    half = head_size // 2
    freq = 10000.0 ** (-jnp.arange(half, dtype=jnp.float32) / half)
    angle = position[:, None, None] * freq[None, None, :]
    cosine = jnp.cos(angle)
    sine = jnp.sin(angle)
    first = shaped[..., :half]
    second = shaped[..., half:]
    turned = jnp.concatenate(
        [first * cosine - second * sine, second * cosine + first * sine], axis=-1
    )
    return turned.reshape(count, -1)


def layout(lengths, cached, split_flag, prev_len, count):
    ends = jnp.cumsum(lengths)
    starts = ends - lengths
    place = jnp.arange(count, dtype=jnp.int32)
    member = ((place[:, None] >= starts[None, :]) & (place[:, None] < ends[None, :])).astype(
        jnp.int32
    )
    request = jnp.sum(member * jnp.arange(lengths.shape[0], dtype=jnp.int32)[None, :], axis=1)
    offset = place - jnp.sum(member * starts[None, :], axis=1)
    extra = jnp.where(request == 0, split_flag * prev_len, 0)
    position = jnp.sum(member * cached[None, :], axis=1) + extra + offset
    return (member, request, position.astype(jnp.float32))


def attend(
    query_vectors,
    keys,
    values,
    prev_keys,
    prev_values,
    cache_keys,
    cache_values,
    request,
    cached,
    split_flag,
    prev_len,
    head_size,
):
    count = query_vectors.shape[0]
    kv_heads = keys.shape[1] // head_size
    ratio = query_vectors.shape[1] // keys.shape[1]
    block = cache_keys.shape[1]
    slots = cache_keys.shape[0] * block
    every_key = jnp.concatenate([cache_keys.reshape(slots, -1), prev_keys, keys], 0).reshape(
        -1, kv_heads, head_size
    )
    every_value = jnp.concatenate(
        [cache_values.reshape(slots, -1), prev_values, values], 0
    ).reshape(-1, kv_heads, head_size)
    slot_req = jnp.arange(slots, dtype=jnp.int32) // block
    slot_col = jnp.arange(slots, dtype=jnp.int32) % block
    cache_ok = (request[:, None] == slot_req[None, :]) & (
        slot_col[None, :] < cached[slot_req][None, :]
    )
    place = jnp.arange(count, dtype=jnp.int32)
    prev_ok = (split_flag == 1) & (request[:, None] == 0) & (place[None, :] >= count - prev_len)
    own_ok = (request[:, None] == request[None, :]) & (place[None, :] <= place[:, None])
    allowed = jnp.concatenate([cache_ok, prev_ok, own_ok], 1)
    grouped = query_vectors.reshape(count, kv_heads, ratio, head_size)
    scores = jnp.einsum(
        "tkrd,skd->krts", grouped, every_key, preferred_element_type=jnp.float32
    ) * head_size ** (-0.5)
    scores = jnp.where(allowed[None, None], scores, jnp.float32(-1e30))
    top = jnp.max(scores, axis=-1, keepdims=True)
    weights = jnp.exp(scores - top)
    total = jnp.sum(weights, axis=-1)
    numer = jnp.einsum(
        "krts,skd->tkrd",
        weights.astype(jnp.bfloat16),
        every_value,
        preferred_element_type=jnp.float32,
    )
    result = numer / jnp.transpose(total, (2, 0, 1))[..., None]
    return result.reshape(count, -1).astype(jnp.bfloat16)


SIDE = 4


def group_of(first, a_coord, b_coord):
    return b_coord * SIDE + a_coord if first == "gz" else a_coord * SIDE + b_coord


def ring_send(value, axis, step):
    return lax.ppermute(value, axis, [(i, (i + step) % SIDE) for i in range(SIDE)])


def route(local, wanted, first, second):
    coords = {"gx": lax.axis_index("gx"), "gz": lax.axis_index("gz")}
    own_a, own_b = coords[first], coords[second]
    per_owner = local.shape[0]
    slots = wanted.shape[1]
    held = jnp.concatenate([local] + [ring_send(local, first, step) for step in range(1, SIDE)])
    me = group_of(first, own_a, own_b)
    askers = group_of(first, own_a, (own_b + jnp.arange(SIDE)) % SIDE)
    owner = wanted // per_owner
    owner_a = (owner // SIDE, owner % SIDE)[first == "gz"]
    owner_b = (owner // SIDE, owner % SIDE)[second == "gz"]
    source = ((own_a - owner_a[askers]) % SIDE) * per_owner + (wanted % per_owner)[askers]
    outgoing = jnp.take(held, source.reshape(-1), axis=0, mode="clip")
    received = jnp.concatenate(
        [outgoing[:slots]]
        + [
            ring_send(outgoing[step * slots:(step + 1) * slots], second, step)
            for step in range(1, SIDE)
        ]
    )
    pick = ((own_b - owner_b[me]) % SIDE) * slots + jnp.arange(slots)
    return jnp.take(received, pick, axis=0, mode="clip")


def on_device(
    stream,
    prenorm_gain,
    query_weight,
    key_weight,
    value_weight,
    output_weight,
    adapter_down_rows,
    adapter_up_query,
    request_adapter,
    adapter_row_index,
    request_token_length,
    continues_previous,
    request_cache_block,
    cached_length,
    cached_rotated_keys,
    cached_value_rows,
):
    count = stream.shape[0]
    group_at = lax.axis_index(("gx", "gz"))
    wanted = adapter_row_index[request_adapter]
    down_width = adapter_down_rows.shape[2]
    adapters = jnp.concatenate([adapter_down_rows, adapter_up_query], axis=2)
    chosen = route(adapters, wanted, "gz", "gx")
    cache_keys = route(cached_rotated_keys, request_cache_block, "gz", "gx")
    cache_values = route(cached_value_rows, request_cache_block, "gx", "gz")
    chosen_down = chosen[:, :, :down_width]
    chosen_up = chosen[:, :, down_width:]
    model_count = lax.axis_size(("my", "mc"))
    spread = lax.all_to_all(
        jnp.broadcast_to(chosen_down, (model_count, *chosen_down.shape)),
        ("my", "mc"),
        0,
        0,
        tiled=True,
    )
    full_down = jnp.moveaxis(spread, 0, 2).reshape(
        *chosen_down.shape[:2], model_count * down_width
    )

    whole = lax.all_gather(stream, ("my", "mc"), axis=1, tiled=True)
    wide = whole.astype(jnp.float32)
    normalized_input = (
        wide * lax.rsqrt(jnp.mean(wide * wide, axis=1, keepdims=True) + 1e-06) * prenorm_gain
    ).astype(jnp.bfloat16)
    before = jnp.maximum(group_at - 1, 0)
    lengths = request_token_length[group_at]
    cached = cached_length[group_at]
    split_flag = continues_previous[group_at]
    prev_len = request_token_length[before, REQS - 1]
    member, request, position = layout(lengths, cached, split_flag, prev_len, count)
    rank_index = adapter_down_rows.shape[1]
    low = jnp.einsum(
        "td,rkd->trk", normalized_input, full_down, preferred_element_type=jnp.float32
    ).reshape(count, REQS * rank_index).astype(jnp.bfloat16)
    own_columns = jnp.repeat(member, rank_index, axis=1).astype(jnp.bfloat16)
    query_update = jnp.dot(
        low * own_columns,
        chosen_up.reshape(REQS * rank_index, -1),
        preferred_element_type=jnp.float32,
    )
    query_vectors = (
        jnp.dot(normalized_input, query_weight, preferred_element_type=jnp.float32)
        + adapter_scale * query_update
    )
    query_vectors = rotate(query_vectors, position, HEAD_WIDTH).astype(jnp.bfloat16)
    keys = rotate(
        jnp.dot(normalized_input, key_weight, preferred_element_type=jnp.float32),
        position,
        HEAD_WIDTH,
    ).astype(jnp.bfloat16)
    values = jnp.dot(normalized_input, value_weight, preferred_element_type=jnp.float32).astype(
        jnp.bfloat16
    )
    prev_both = shifted(jnp.concatenate([keys, values], axis=1), ("gx", "gz"), 1)
    prev_keys, prev_values = prev_both[:, : keys.shape[1]], prev_both[:, keys.shape[1]:]
    attended = attend(
        query_vectors,
        keys,
        values,
        prev_keys,
        prev_values,
        cache_keys,
        cache_values,
        request,
        cached,
        split_flag,
        prev_len,
        HEAD_WIDTH,
    )
    partial_out = jnp.dot(attended, output_weight, preferred_element_type=jnp.float32)
    return lax.psum_scatter(
        partial_out.astype(jnp.bfloat16), ("my", "mc"), scatter_dimension=1, tiled=True
    )


def solution(mesh):
    split = Mesh(mesh.devices.reshape(SIDE, SIDE, 4, 2), ("gx", "gz", "my", "mc"))
    groups = ("gx", "gz")
    model = ("my", "mc")
    placed = (
        P(groups, model),
        P(),
        P(None, model),
        P(None, model),
        P(None, model),
        P(model, None),
        P(groups, None, model),
        P(groups, None, model),
        P(),
        P(),
        P(),
        P(),
        P(),
        P(),
        P(groups, None, model),
        P(groups, None, model),
    )
    return jax.shard_map(
        on_device, mesh=split, in_specs=placed, out_specs=P(groups, model), check_vma=False
    )
```

profile of v0, /device:TPU:0, one launch (start us, length us, event | category | flops | bytes accessed | tf_op | source)
XLA Modules:
  0.0 200.0 jit_solution(5449151460355174102)
XLA Ops:
  6.5 1.1 pad_maximum_fusion.7
  7.7 4.2 %collective-permute-start.15 = (bf16[4,16,960]{2,1,0:T(8,128)(2,1)S(1)}, bf16[4,16,960]{2,1,0:T(8,128)(2,1)S(1)}, u32[]{:S(2)}, u32[]{:S(2)}) collective-permute-start(bf16[4,16,960]{2,1,0:T(8,128)(2,1)S(1)} %pad_maximum_fusion.7), channel_id=1, source_target_pairs={{0,24},{8,0},{16,8},{24,16},{1,25},{9,1},{17,9},{25,17},{2,26},{10... | collective-permute-start | bytes 368648 | tf_op jit(solution)/shard_map/ppermute | solution.py:109
  11.8 1.3 collective-permute-start.13
  13.1 2.3 %collective-permute-start.8 = (bf16[2,256,256]{2,1,0:T(8,128)(2,1)}, bf16[2,256,256]{2,1,0:T(8,128)(2,1)}, u32[]{:S(2)}, u32[]{:S(2)}) collective-permute-start(bf16[2,256,256]{2,1,0:T(8,128)(2,1)} %param.30), channel_id=1, source_target_pairs={{0,16},{8,24},{16,0},{24,8},{1,17},{9,25},{17,1},{25,9},{2,18},{10... | collective-permute-start | bytes 786440 | tf_op jit(solution)/shard_map/ppermute | solution.py:109
  16.0 0.8 copy.56
  17.0 0.8 gather_fusion.8
  28.5 2.5 %compare_select_fusion.2 = s32[1024,1]{0,1:T(1,128)S(1)} fusion(s32[]{:T(128)} %bitcast.14, s32[]{:T(128)} %bitcast.15, s32[]{:T(128)} %bitcast.17, s32[]{:T(128)} %bitcast.16), kind=kLoop, calls=%fused_computation.79 | loop fusion | flops 17408 | bytes 4112 | tf_op jit(solution)/shard_map/gather | solution.py:77
  31.2 0.9 broadcast_and_fusion
  32.1 0.9 fusion.24
  33.0 1.8 multiply_cosine_fusion
  34.8 1.5 compare_and_fusion
  36.9 3.0 %collective-permute-start.1 = (bf16[2,256,256]{2,1,0:T(8,128)(2,1)S(1)}, bf16[2,256,256]{2,1,0:T(8,128)(2,1)S(1)}, u32[]{:S(2)}, u32[]{:S(2)}) collective-permute-start(bf16[2,256,256]{2,1,0:T(8,128)(2,1)S(1)} %copy-done.16), channel_id=1, source_target_pairs={{0,64},{32,96},{64,0},{96,32},{1,65},{33,97},{65,1},{97,33},{2,66}... | collective-permute-start | bytes 786440 | tf_op jit(solution)/shard_map/ppermute | solution.py:109
  41.2 2.6 %collective-permute-start.2 = (bf16[2,256,256]{2,1,0:T(8,128)(2,1)S(1)}, bf16[2,256,256]{2,1,0:T(8,128)(2,1)}, u32[]{:S(2)}, u32[]{:S(2)}) collective-permute-start(bf16[2,256,256]{2,1,0:T(8,128)(2,1)S(1)} %copy-done.16), channel_id=1, source_target_pairs={{0,96},{32,0},{64,32},{96,64},{1,97},{33,1},{65,33},{97,65},{2,98}... | collective-permute-start | bytes 786440 | tf_op jit(solution)/shard_map/ppermute | solution.py:109
  43.9 1.0 pad_maximum_fusion.5
  44.9 0.7 gather_fusion.11
  45.6 0.8 fusion.104
  46.3 1.3 collective-permute-done.1
  47.7 2.7 %collective-permute-start.9 = (bf16[2,256,256]{2,1,0:T(8,128)(2,1)}, bf16[2,256,256]{2,1,0:T(8,128)(2,1)}, u32[]{:S(2)}, u32[]{:S(2)}) collective-permute-start(bf16[2,256,256]{2,1,0:T(8,128)(2,1)} %param.30), channel_id=1, source_target_pairs={{0,24},{8,0},{16,8},{24,16},{1,25},{9,1},{17,9},{25,17},{2,26},{10... | collective-permute-start | bytes 786440 | tf_op jit(solution)/shard_map/ppermute | solution.py:109
  50.4 0.7 collective-permute-done
  51.1 2.3 %collective-permute-start.17 = (bf16[4,16,960]{2,1,0:T(8,128)(2,1)}, bf16[4,16,960]{2,1,0:T(8,128)(2,1)}, u32[]{:S(2)}, u32[]{:S(2)}) collective-permute-start(bf16[4,16,960]{2,1,0:T(8,128)(2,1)} %get-tuple-element.32), channel_id=1, source_target_pairs={{0,64},{32,96},{64,0},{96,32},{1,65},{33,97},{65,1},{97,33},{2,66}... | collective-permute-start | bytes 368648 | tf_op jit(solution)/shard_map/ppermute | solution.py:109
  54.0 1.2 pad_maximum_fusion.2
  55.2 2.3 %gather_fusion.2 = bf16[16,256,256]{2,1,0:T(8,128)(2,1)} fusion(bf16[8,256,256]{2,1,0:T(8,128)(2,1)S(1)} %pad_maximum_fusion.2, s32[1024]{0:T(1024)} %pad_clamp_fusion.7), kind=kCustom, calls=%fused_computation.2 | custom fusion | bytes 4194368 | tf_op jit(solution)/shard_map/jit(_take)/gather | solution.py:124
  57.4 1.6 collective-permute-done.17
  59.0 1.1 collective-permute-start.18
  60.1 2.9 %fusion.100 = (bf16[4,256,256]{2,1,0:T(8,128)(2,1)}, bf16[4,256,256]{2,1,0:T(8,128)(2,1)}, bf16[4,256,256]{2,1,0:T(8,128)(2,1)}, bf16[4,256,256]{2,1,0:T(8,128)(2,1)}) fusion(bf16[16,256,256]{2,1,0:T(8,128)(2,1)} %gather_fusion.2), kind=kLoop, calls=%fused_computation.234 | loop fusion | bytes 4194304 | tf_op jit(solution)/shard_map/slice | solution.py:126
  63.0 3.1 %collective-permute-start.4 = (bf16[4,256,256]{2,1,0:T(8,128)(2,1)}, bf16[4,256,256]{2,1,0:T(8,128)(2,1)}, u32[]{:S(2)}, u32[]{:S(2)}) collective-permute-start(bf16[4,256,256]{2,1,0:T(8,128)(2,1)} %get-tuple-element.16), channel_id=1, source_target_pairs={{0,16},{8,24},{16,0},{24,8},{1,17},{9,25},{17,1},{25,9},{2,18},{10... | collective-permute-start | bytes 1572872 | tf_op jit(solution)/shard_map/ppermute | solution.py:109
  66.1 1.0 pad_maximum_fusion.6
  67.8 0.9 broadcast_in_dim.33
  68.7 4.5 %all-to-all-start = ((bf16[8,4,16,448]{3,2,1,0:T(8,128)(2,1)}), bf16[8,4,16,448]{3,2,1,0:T(8,128)(2,1)S(1)}, u32[]{:S(2)}, u32[]{:S(2)}) async-start(bf16[8,4,16,448]{3,2,1,0:T(8,128)(2,1)} %broadcast_in_dim.33), calls=%async_computation | async-start | bytes 1048576 | tf_op jit(solution)/shard_map/all_to_all | solution.py:165
  73.6 3.0 %collective-permute-start.5 = (bf16[4,256,256]{2,1,0:T(8,128)(2,1)}, bf16[4,256,256]{2,1,0:T(8,128)(2,1)}, u32[]{:S(2)}, u32[]{:S(2)}) collective-permute-start(bf16[4,256,256]{2,1,0:T(8,128)(2,1)} %get-tuple-element.18), channel_id=1, source_target_pairs={{0,24},{8,0},{16,8},{24,16},{1,25},{9,1},{17,9},{25,17},{2,26},{10... | collective-permute-start | bytes 1572872 | tf_op jit(solution)/shard_map/ppermute | solution.py:109
  76.6 1.3 pad_maximum_fusion.3
  77.9 2.0 %gather_fusion.6 = bf16[16,256,256]{2,1,0:T(8,128)(2,1)} fusion(bf16[8,256,256]{2,1,0:T(8,128)(2,1)S(1)} %pad_maximum_fusion.3, s32[1024]{0:T(1024)S(1)} %pad_clamp_fusion.4), kind=kCustom, calls=%fused_computation.6 | custom fusion | bytes 4194368 | tf_op jit(solution)/shard_map/jit(_take)/gather | solution.py:124
  79.9 3.0 %fusion.101 = (bf16[4,256,256]{2,1,0:T(8,128)(2,1)}, bf16[4,256,256]{2,1,0:T(8,128)(2,1)}, bf16[4,256,256]{2,1,0:T(8,128)(2,1)}, bf16[4,256,256]{2,1,0:T(8,128)(2,1)}) fusion(bf16[16,256,256]{2,1,0:T(8,128)(2,1)} %gather_fusion.6), kind=kLoop, calls=%fused_computation.235 | loop fusion | bytes 4194304 | tf_op jit(solution)/shard_map/slice | solution.py:126
  82.9 1.6 collective-permute-start.11
  84.5 0.9 collective-permute-start.10
  85.4 2.3 %collective-permute-start.12 = (bf16[4,256,256]{2,1,0:T(8,128)(2,1)}, bf16[4,256,256]{2,1,0:T(8,128)(2,1)}, u32[]{:S(2)}, u32[]{:S(2)}) collective-permute-start(bf16[4,256,256]{2,1,0:T(8,128)(2,1)} %get-tuple-element.22), channel_id=1, source_target_pairs={{0,96},{32,0},{64,32},{96,64},{1,97},{33,1},{65,33},{97,65},{2,98}... | collective-permute-start | bytes 1572872 | tf_op jit(solution)/shard_map/ppermute | solution.py:109
  88.1 0.7 slice.133
  88.9 1.1 copy.59
  90.0 2.4 %dot_general.31 = bf16[64,3584]{1,0:T(8,128)(2,1)} reshape(bf16[4,16,8,448]{3,2,1,0:T(8,128)(2,1)} %copy.59) | data formatting | bytes 917504 | tf_op jit(solution)/shard_map/td,rkd->trk/dot_general | solution.py:188
  92.4 3.1 %pad_maximum_fusion = bf16[16,256,256]{2,1,0:T(8,128)(2,1)} fusion(bf16[4,256,256]{2,1,0:T(8,128)(2,1)} %collective-permute-done.5, bf16[4,256,256]{2,1,0:T(8,128)(2,1)} %collective-permute-done.4, bf16[4,256,256]{2,1,0:T(8,128)(2,1)} %collective-permute-done.3, bf16[4,256,256]{2,1,0:T(8,128)(2,1)} %get-tuple-element.15), kind=kLoop, calls=%fused_computation.28 | loop fusion | flops 3145728 | bytes 4194304 | tf_op jit(solution)/shard_map/concatenate | solution.py:125
  95.5 2.2 %gather_fusion.3 = bf16[4,256,256]{2,1,0:T(8,128)(2,1)S(1)} fusion(bf16[16,256,256]{2,1,0:T(8,128)(2,1)} %pad_maximum_fusion, s32[1024]{0:T(1024)S(1)} %pad_clamp_fusion.6), kind=kCustom, calls=%fused_computation.3 | custom fusion | bytes 1048592 | tf_op jit(solution)/shard_map/jit(_take)/gather | solution.py:133
  97.7 1.0 copy.65
  98.7 0.9 collective-permute-done.11
  99.6 10.0 %collective-permute-done.10 = bf16[4,256,256]{2,1,0:T(8,128)(2,1)} collective-permute-done((bf16[4,256,256]{2,1,0:T(8,128)(2,1)}, bf16[4,256,256]{2,1,0:T(8,128)(2,1)}, u32[]{:S(2)}, u32[]{:S(2)}) %collective-permute-start.10) | collective-permute-done | bytes 524320 | tf_op jit(solution)/shard_map/ppermute | solution.py:109
  109.6 3.1 %pad_maximum_fusion.1 = bf16[16,256,256]{2,1,0:T(8,128)(2,1)} fusion(bf16[4,256,256]{2,1,0:T(8,128)(2,1)} %collective-permute-done.12, bf16[4,256,256]{2,1,0:T(8,128)(2,1)} %collective-permute-done.11, bf16[4,256,256]{2,1,0:T(8,128)(2,1)} %collective-permute-done.10, bf16[4,256,256]{2,1,0:T(8,128)(2,1)} %get-tuple-element.19), kind=kLoop, calls=%fused_computation.29 | loop fusion | flops 3145728 | bytes 4194304 | tf_op jit(solution)/shard_map/concatenate | solution.py:125
  112.7 3.0 %gather_fusion.7 = bf16[4,256,256]{2,1,0:T(8,128)(2,1)} fusion(bf16[16,256,256]{2,1,0:T(8,128)(2,1)} %pad_maximum_fusion.1, s32[1024]{0:T(1024)S(1)} %pad_clamp_fusion.3), kind=kCustom, calls=%fused_computation.7 | custom fusion | bytes 1048592 | tf_op jit(solution)/shard_map/jit(_take)/gather | solution.py:133
  115.7 3.0 %fusion.2 = f32[512]{0:T(512)S(1)} fusion(bf16[512,3584]{0,1:T(8,128)(2,1)} %all-gather.2.cloned.1.call-done), kind=kLoop, calls=%fused_computation.19 | loop fusion | flops 5504512 | bytes 3672064 | tf_op jit(solution)/shard_map/reduce_sum | solution.py:179
  118.8 1.6 fusion.4
  120.4 1.2 convolution_convert_fusion.1
  122.3 1.0 copy-done.27
  123.2 1.2 convolution_bitcast_fusion
  124.4 1.2 fusion.35
  125.6 0.8 copy.55
  126.5 0.9 pad_maximum_fusion.4
  127.3 2.2 %collective-permute-start.6 = (bf16[512,512]{0,1:T(8,128)(2,1)}, bf16[512,512]{0,1:T(8,128)(2,1)}, u32[]{:S(2)}, u32[]{:S(2)}) collective-permute-start(bf16[512,512]{0,1:T(8,128)(2,1)} %pad_maximum_fusion.4), channel_id=1, source_target_pairs={{0,8},{8,16},{16,24},{24,32},{32,40},{40,48},{48,56},{56,64},{64,7... | collective-permute-start | bytes 1572872 | tf_op jit(solution)/shard_map/ppermute | solution.py:16
  129.6 6.2 %fusion.106 = f32[512,512]{0,1:T(8,128)} fusion(bf16[512,3584]{0,1:T(8,128)(2,1)} %copy-done.3, bf16[3584,512]{1,0:T(8,128)(2,1)} %param.18), kind=kOutput, calls=%fused_computation.240 | convolution fusion | flops 1879048192 | bytes 8388608 | tf_op jit(solution)/shard_map/dot_general | solution.py:198
  135.8 3.3 %fusion.13 = f32[512,512]{0,1:T(8,128)S(1)} fusion(f32[512,512]{0,1:T(8,128)} %fusion.106, bf16[64,512]{1,0:T(8,128)(2,1)S(1)} %bitcast.120, bf16[512,64]{0,1:T(8,128)(2,1)S(1)} %bitcast.121, bf16[64,3584]{1,0:T(8,128)(2,1)S(1)} %copy-done.6, bf16[512,3584]{0,1:T(8,128)(2,1)} %copy-done.3), kind=kOutput, calls=%fused_computation.33 | convolution fusion | flops 269025280 | bytes 6356992 | tf_op jit(solution)/shard_map/dot_general | solution.py:192
  140.1 1.1 subtract_convert_fusion
  141.2 1.1 fusion.103
  142.4 2.9 %fusion.5 = (f32[2,512]{1,0:T(2,128)S(1)}, f32[2048,512,2]{1,0,2:T(8,128)S(1)}) fusion(pred[512,2048]{0,1:T(8,128)(4,1)S(1)} %pad_add_fusion, bf16[512,2,128]{2,0,1:T(8,128)(2,1)S(1)} %get-tuple-element.24, bf16[512,2,128]{2,0,1:T(8,128)(2,1)S(1)} %get-tuple-element.23, bf16[512,256]{1,0:T(8,128)(2,1)} %copy.55, bf16[512,256]{1,0:T(8,128)(2,1)S(1)} %copy.54, ...), kind=kOutput, calls=%fused_computation.22 | convolution fusion | flops 1084226560 | bytes 11014144 | tf_op jit(solution)/shard_map/tkrd,skd->krts/dot_general | solution.py:84
  145.4 2.0 fusion
  147.4 2.8 %divide_convert_fusion = bf16[512,1,2,256]{0,3,2,1:T(8,128)(2,1)S(1)} fusion(f32[2048,512,2]{1,0,2:T(8,128)S(1)} %get-tuple-element.47, f32[2,512]{1,0:T(2,128)S(1)} %get-tuple-element.46, pred[512,2048]{0,1:T(8,128)(4,1)S(1)} %pad_add_fusion, bf16[512,256]{0,1:T(8,128)(2,1)S(1)} %copy-done.15, bf16[512,256]{0,1:T(8,128)(2,1)S(1)} %get-tuple-element.29, ...), kind=kOutput, calls=%fused_computation.51 | convolution fusion | flops 1085800448 | bytes 11018240 | tf_op jit(solution)/shard_map/krts,skd->tkrd/dot_general | solution.py:91
  150.2 3.9 %convolution_convert_fusion = bf16[512,3584]{0,1:T(8,128)(2,1)} fusion(bf16[512,512]{0,1:T(8,128)(2,1)S(1)} %bitcast.127, bf16[512,3584]{1,0:T(8,128)(2,1)S(1)} %copy-done.26), kind=kOutput, calls=%fused_computation.23 | convolution fusion | flops 1880883200 | bytes 7864320 | tf_op jit(solution)/shard_map/dot_general | solution.py:226
  154.2 39.0 %reduce-scatter.2.cloned.1.call-done = bf16[512,448]{0,1:T(8,128)(2,1)} async-done(((bf16[512,3584]{0,1:T(8,128)(2,1)}), bf16[512,448]{0,1:T(8,128)(2,1)}) %reduce-scatter.2.cloned.1.call-update) | async-done | bytes 458768 | tf_op jit(solution)/shard_map/reduce_scatter | solution.py:227
  (146 shorter events, 15.1 us)
Async XLA Ops:
  6.5 113.9 %copy-start = (bf16[3584,256]{1,0:T(8,128)(2,1)S(1)}, bf16[3584,256]{1,0:T(8,128)(2,1)}, u32[]{:S(2)}) copy-start(bf16[3584,256]{1,0:T(8,128)(2,1)} %param.20) | copy-start | bytes 5505028
  6.5 10.3 %copy-start.2 = (s32[64]{0:T(128)S(1)}, s32[64]{0:T(128)}, u32[]{:S(2)}) copy-start(s32[64]{0:T(128)} %param.25) | copy-start | bytes 772
  6.5 109.1 %all-gather.2.cloned.1.call-start = ((), (), s32[]{:S(2)}) async-start(), calls=%async_computation.2 | async-start | bytes 4128768 | tf_op jit(solution)/shard_map/all_gather | solution.py:176
  7.7 29.3 %collective-permute-start.15 = (bf16[4,16,960]{2,1,0:T(8,128)(2,1)S(1)}, bf16[4,16,960]{2,1,0:T(8,128)(2,1)S(1)}, u32[]{:S(2)}, u32[]{:S(2)}) collective-permute-start(bf16[4,16,960]{2,1,0:T(8,128)(2,1)S(1)} %pad_maximum_fusion.7), channel_id=1, source_target_pairs={{0,24},{8,0},{16,8},{24,16},{1,25},{9,1},{17,9},{25,17},{2,26},{10... | collective-permute-start | bytes 368648 | tf_op jit(solution)/shard_map/ppermute | solution.py:109
  11.8 28.1 %collective-permute-start.14 = (bf16[4,16,960]{2,1,0:T(8,128)(2,1)S(1)}, bf16[4,16,960]{2,1,0:T(8,128)(2,1)S(1)}, u32[]{:S(2)}, u32[]{:S(2)}) collective-permute-start(bf16[4,16,960]{2,1,0:T(8,128)(2,1)S(1)} %pad_maximum_fusion.7), channel_id=1, source_target_pairs={{0,16},{8,24},{16,0},{24,8},{1,17},{9,25},{17,1},{25,9},{2,18},{10... | collective-permute-start | bytes 368648 | tf_op jit(solution)/shard_map/ppermute | solution.py:109
  11.8 28.7 %collective-permute-start.13 = (bf16[4,16,960]{2,1,0:T(8,128)(2,1)S(1)}, bf16[4,16,960]{2,1,0:T(8,128)(2,1)S(1)}, u32[]{:S(2)}, u32[]{:S(2)}) collective-permute-start(bf16[4,16,960]{2,1,0:T(8,128)(2,1)S(1)} %pad_maximum_fusion.7), channel_id=1, source_target_pairs={{0,8},{8,16},{16,24},{24,0},{1,9},{9,17},{17,25},{25,1},{2,10},{10... | collective-permute-start | bytes 368648 | tf_op jit(solution)/shard_map/ppermute | solution.py:109
  13.1 60.5 %collective-permute-start.8 = (bf16[2,256,256]{2,1,0:T(8,128)(2,1)}, bf16[2,256,256]{2,1,0:T(8,128)(2,1)}, u32[]{:S(2)}, u32[]{:S(2)}) collective-permute-start(bf16[2,256,256]{2,1,0:T(8,128)(2,1)} %param.30), channel_id=1, source_target_pairs={{0,16},{8,24},{16,0},{24,8},{1,17},{9,25},{17,1},{25,9},{2,18},{10... | collective-permute-start | bytes 786440 | tf_op jit(solution)/shard_map/ppermute | solution.py:109
  15.4 61.2 %collective-permute-start.7 = (bf16[2,256,256]{2,1,0:T(8,128)(2,1)}, bf16[2,256,256]{2,1,0:T(8,128)(2,1)}, u32[]{:S(2)}, u32[]{:S(2)}) collective-permute-start(bf16[2,256,256]{2,1,0:T(8,128)(2,1)} %param.30), channel_id=1, source_target_pairs={{0,8},{8,16},{16,24},{24,0},{1,9},{9,17},{17,25},{25,1},{2,10},{10... | collective-permute-start | bytes 786440 | tf_op jit(solution)/shard_map/ppermute | solution.py:109
  16.9 1.0 copy-start.23
  16.9 2.1 %copy-start.28 = (s32[16]{0:T(128)S(1)}, s32[16]{0:T(128)}, u32[]{:S(2)}) copy-start(s32[16]{0:T(128)} %param.27) | copy-start | bytes 196
  16.9 4.6 %copy-start.22 = (s32[16,4]{0,1:T(4,128)S(1)}, s32[16,4]{0,1:T(4,128)}, u32[]{:S(2)}) copy-start(s32[16,4]{0,1:T(4,128)} %param.29) | copy-start | bytes 772
  16.9 5.7 %copy-start.20 = (s32[16,4]{0,1:T(4,128)S(1)}, s32[16,4]{0,1:T(4,128)}, u32[]{:S(2)}) copy-start(s32[16,4]{0,1:T(4,128)} %param.28) | copy-start | bytes 772
  16.9 20.0 %copy-start.16 = (bf16[2,256,256]{2,1,0:T(8,128)(2,1)S(1)}, bf16[2,256,256]{2,1,0:T(8,128)(2,1)}, u32[]{:S(2)}) copy-start(bf16[2,256,256]{2,1,0:T(8,128)(2,1)} %param.31) | copy-start | bytes 786436
  17.0 26.9 %copy-start.12 = (bf16[4,16,512]{2,1,0:T(8,128)(2,1)S(1)}, bf16[4,16,512]{2,1,0:T(8,128)(2,1)}, u32[]{:S(2)}) copy-start(bf16[4,16,512]{2,1,0:T(8,128)(2,1)} %param.23) | copy-start | bytes 196612
  17.0 26.9 %copy-start.13 = (bf16[4,16,448]{2,1,0:T(8,128)(2,1)S(1)}, bf16[4,16,448]{2,1,0:T(8,128)(2,1)}, u32[]{:S(2)}) copy-start(bf16[4,16,448]{2,1,0:T(8,128)(2,1)} %param.22) | copy-start | bytes 172036
  26.0 14.6 %copy-start.24 = (f32[128]{0:T(128)}, f32[128]{0:T(128)S(1)}, u32[]{:S(2)}) copy-start(f32[128]{0:T(128)S(1)} %multiply_power_fusion) | copy-start | bytes 1540
  36.9 10.8 %collective-permute-start.1 = (bf16[2,256,256]{2,1,0:T(8,128)(2,1)S(1)}, bf16[2,256,256]{2,1,0:T(8,128)(2,1)S(1)}, u32[]{:S(2)}, u32[]{:S(2)}) collective-permute-start(bf16[2,256,256]{2,1,0:T(8,128)(2,1)S(1)} %copy-done.16), channel_id=1, source_target_pairs={{0,64},{32,96},{64,0},{96,32},{1,65},{33,97},{65,1},{97,33},{2,66}... | collective-permute-start | bytes 786440 | tf_op jit(solution)/shard_map/ppermute | solution.py:109
  40.0 11.1 %collective-permute-start = (bf16[2,256,256]{2,1,0:T(8,128)(2,1)S(1)}, bf16[2,256,256]{2,1,0:T(8,128)(2,1)}, u32[]{:S(2)}, u32[]{:S(2)}) collective-permute-start(bf16[2,256,256]{2,1,0:T(8,128)(2,1)S(1)} %copy-done.16), channel_id=1, source_target_pairs={{0,32},{32,64},{64,96},{96,0},{1,33},{33,65},{65,97},{97,1},{2,34}... | collective-permute-start | bytes 786440 | tf_op jit(solution)/shard_map/ppermute | solution.py:109
  40.6 0.7 copy-start.17
  41.2 12.2 %collective-permute-start.2 = (bf16[2,256,256]{2,1,0:T(8,128)(2,1)S(1)}, bf16[2,256,256]{2,1,0:T(8,128)(2,1)}, u32[]{:S(2)}, u32[]{:S(2)}) collective-permute-start(bf16[2,256,256]{2,1,0:T(8,128)(2,1)S(1)} %copy-done.16), channel_id=1, source_target_pairs={{0,96},{32,0},{64,32},{96,64},{1,97},{33,1},{65,33},{97,65},{2,98}... | collective-permute-start | bytes 786440 | tf_op jit(solution)/shard_map/ppermute | solution.py:109
  47.7 28.9 %collective-permute-start.9 = (bf16[2,256,256]{2,1,0:T(8,128)(2,1)}, bf16[2,256,256]{2,1,0:T(8,128)(2,1)}, u32[]{:S(2)}, u32[]{:S(2)}) collective-permute-start(bf16[2,256,256]{2,1,0:T(8,128)(2,1)} %param.30), channel_id=1, source_target_pairs={{0,24},{8,0},{16,8},{24,16},{1,25},{9,1},{17,9},{25,17},{2,26},{10... | collective-permute-start | bytes 786440 | tf_op jit(solution)/shard_map/ppermute | solution.py:109
  51.1 7.9 %collective-permute-start.17 = (bf16[4,16,960]{2,1,0:T(8,128)(2,1)}, bf16[4,16,960]{2,1,0:T(8,128)(2,1)}, u32[]{:S(2)}, u32[]{:S(2)}) collective-permute-start(bf16[4,16,960]{2,1,0:T(8,128)(2,1)} %get-tuple-element.32), channel_id=1, source_target_pairs={{0,64},{32,96},{64,0},{96,32},{1,65},{33,97},{65,1},{97,33},{2,66}... | collective-permute-start | bytes 368648 | tf_op jit(solution)/shard_map/ppermute | solution.py:109
  53.4 9.6 %collective-permute-start.16 = (bf16[4,16,960]{2,1,0:T(8,128)(2,1)}, bf16[4,16,960]{2,1,0:T(8,128)(2,1)}, u32[]{:S(2)}, u32[]{:S(2)}) collective-permute-start(bf16[4,16,960]{2,1,0:T(8,128)(2,1)} %get-tuple-element.33), channel_id=1, source_target_pairs={{0,32},{32,64},{64,96},{96,0},{1,33},{33,65},{65,97},{97,1},{2,34}... | collective-permute-start | bytes 368648 | tf_op jit(solution)/shard_map/ppermute | solution.py:109
  55.1 3.9 %copy-start.18 = (bf16[4,16,960]{2,1,0:T(8,128)(2,1)S(1)}, bf16[4,16,960]{2,1,0:T(8,128)(2,1)}, u32[]{:S(2)}) copy-start(bf16[4,16,960]{2,1,0:T(8,128)(2,1)} %get-tuple-element.34) | copy-start | bytes 368644
  59.0 7.1 %collective-permute-start.18 = (bf16[4,16,960]{2,1,0:T(8,128)(2,1)S(1)}, bf16[4,16,960]{2,1,0:T(8,128)(2,1)S(1)}, u32[]{:S(2)}, u32[]{:S(2)}) collective-permute-start(bf16[4,16,960]{2,1,0:T(8,128)(2,1)S(1)} %copy-done.18), channel_id=1, source_target_pairs={{0,96},{32,0},{64,32},{96,64},{1,97},{33,1},{65,33},{97,65},{2,98}... | collective-permute-start | bytes 368648 | tf_op jit(solution)/shard_map/ppermute | solution.py:109
  63.0 22.5 %collective-permute-start.4 = (bf16[4,256,256]{2,1,0:T(8,128)(2,1)}, bf16[4,256,256]{2,1,0:T(8,128)(2,1)}, u32[]{:S(2)}, u32[]{:S(2)}) collective-permute-start(bf16[4,256,256]{2,1,0:T(8,128)(2,1)} %get-tuple-element.16), channel_id=1, source_target_pairs={{0,16},{8,24},{16,0},{24,8},{1,17},{9,25},{17,1},{25,9},{2,18},{10... | collective-permute-start | bytes 1572872 | tf_op jit(solution)/shard_map/ppermute | solution.py:109
  68.7 20.2 %all-to-all-start = ((bf16[8,4,16,448]{3,2,1,0:T(8,128)(2,1)}), bf16[8,4,16,448]{3,2,1,0:T(8,128)(2,1)S(1)}, u32[]{:S(2)}, u32[]{:S(2)}) async-start(bf16[8,4,16,448]{3,2,1,0:T(8,128)(2,1)} %broadcast_in_dim.33), calls=%async_computation | async-start | bytes 1048576 | tf_op jit(solution)/shard_map/all_to_all | solution.py:165
  73.2 120.0 %reduce-scatter.2.cloned.1.call-start = ((), (), s32[]{:S(2)}) async-start(), calls=%async_computation.3 | async-start | bytes 4128768 | tf_op jit(solution)/shard_map/reduce_scatter | solution.py:227
  73.2 19.2 %collective-permute-start.3 = (bf16[4,256,256]{2,1,0:T(8,128)(2,1)}, bf16[4,256,256]{2,1,0:T(8,128)(2,1)}, u32[]{:S(2)}, u32[]{:S(2)}) collective-permute-start(bf16[4,256,256]{2,1,0:T(8,128)(2,1)} %get-tuple-element.17), channel_id=1, source_target_pairs={{0,8},{8,16},{16,24},{24,0},{1,9},{9,17},{17,25},{25,1},{2,10},{10... | collective-permute-start | bytes 1572872 | tf_op jit(solution)/shard_map/ppermute | solution.py:109
  73.6 18.8 %collective-permute-start.5 = (bf16[4,256,256]{2,1,0:T(8,128)(2,1)}, bf16[4,256,256]{2,1,0:T(8,128)(2,1)}, u32[]{:S(2)}, u32[]{:S(2)}) collective-permute-start(bf16[4,256,256]{2,1,0:T(8,128)(2,1)} %get-tuple-element.18), channel_id=1, source_target_pairs={{0,24},{8,0},{16,8},{24,16},{1,25},{9,1},{17,9},{25,17},{2,26},{10... | collective-permute-start | bytes 1572872 | tf_op jit(solution)/shard_map/ppermute | solution.py:109
  79.9 7.8 %copy-start.21 = (s32[4]{0:T(128)S(1)}, s32[4]{0:T(128)}, u32[]{:S(2)}) copy-start(s32[4]{0:T(128)} %fusion.91) | copy-start | bytes 52
  79.9 7.8 %copy-start.5 = (pred[512,1024]{0,1:T(8,128)(4,1)S(1)}, pred[512,1024]{0,1:T(8,128)(4,1)}, u32[]{:S(2)}) copy-start(pred[512,1024]{0,1:T(8,128)(4,1)} %compare_and_fusion) | copy-start | bytes 1572868
  79.9 7.8 %copy-start.8 = (pred[512,512]{0,1:T(8,128)(4,1)S(1)}, pred[512,512]{0,1:T(8,128)(4,1)}, u32[]{:S(2)}) copy-start(pred[512,512]{0,1:T(8,128)(4,1)} %broadcast_and_fusion) | copy-start | bytes 786436
  79.9 7.8 %copy-start.9 = (pred[512,512]{0,1:T(8,128)(4,1)S(1)}, pred[512,512]{0,1:T(8,128)(4,1)}, u32[]{:S(2)}) copy-start(pred[512,512]{0,1:T(8,128)(4,1)} %fusion.24) | copy-start | bytes 786436
  82.9 16.7 %collective-permute-start.11 = (bf16[4,256,256]{2,1,0:T(8,128)(2,1)}, bf16[4,256,256]{2,1,0:T(8,128)(2,1)}, u32[]{:S(2)}, u32[]{:S(2)}) collective-permute-start(bf16[4,256,256]{2,1,0:T(8,128)(2,1)} %get-tuple-element.20), channel_id=1, source_target_pairs={{0,64},{32,96},{64,0},{96,32},{1,65},{33,97},{65,1},{97,33},{2,66}... | collective-permute-start | bytes 1572872 | tf_op jit(solution)/shard_map/ppermute | solution.py:109
  84.5 25.1 %collective-permute-start.10 = (bf16[4,256,256]{2,1,0:T(8,128)(2,1)}, bf16[4,256,256]{2,1,0:T(8,128)(2,1)}, u32[]{:S(2)}, u32[]{:S(2)}) collective-permute-start(bf16[4,256,256]{2,1,0:T(8,128)(2,1)} %get-tuple-element.21), channel_id=1, source_target_pairs={{0,32},{32,64},{64,96},{96,0},{1,33},{33,65},{65,97},{97,1},{2,34}... | collective-permute-start | bytes 1572872 | tf_op jit(solution)/shard_map/ppermute | solution.py:109
  85.4 24.1 %collective-permute-start.12 = (bf16[4,256,256]{2,1,0:T(8,128)(2,1)}, bf16[4,256,256]{2,1,0:T(8,128)(2,1)}, u32[]{:S(2)}, u32[]{:S(2)}) collective-permute-start(bf16[4,256,256]{2,1,0:T(8,128)(2,1)} %get-tuple-element.22), channel_id=1, source_target_pairs={{0,96},{32,0},{64,32},{96,64},{1,97},{33,1},{65,33},{97,65},{2,98}... | collective-permute-start | bytes 1572872 | tf_op jit(solution)/shard_map/ppermute | solution.py:109
  109.6 9.1 %copy-start.19 = (f32[3584]{0:T(1024)S(1)}, f32[3584]{0:T(1024)}, u32[]{:S(2)}) copy-start(f32[3584]{0:T(1024)} %param.17) | copy-start | bytes 43012
  115.7 3.1 %copy-start.4 = (bf16[512,3584]{0,1:T(8,128)(2,1)S(1)}, bf16[512,3584]{0,1:T(8,128)(2,1)}, u32[]{:S(2)}) copy-start(bf16[512,3584]{0,1:T(8,128)(2,1)} %all-gather.2.cloned.1.call-done) | copy-start | bytes 11010052
  120.4 1.9 copy-start.3
  120.4 2.8 %copy-start.27 = (bf16[3584,256]{1,0:T(8,128)(2,1)S(1)}, bf16[3584,256]{1,0:T(8,128)(2,1)}, u32[]{:S(2)}) copy-start(bf16[3584,256]{1,0:T(8,128)(2,1)} %param.19) | copy-start | bytes 5505028
  123.2 3.2 %copy-start.14 = (bf16[512,256]{0,1:T(8,128)(2,1)}, bf16[512,256]{0,1:T(8,128)(2,1)S(1)}, u32[]{:S(2)}) copy-start(bf16[512,256]{0,1:T(8,128)(2,1)S(1)} %convolution_convert_fusion.1) | copy-start | bytes 786436
  123.2 1.2 copy-start.25
  127.3 8.5 %copy-start.6 = (bf16[64,3584]{1,0:T(8,128)(2,1)S(1)}, bf16[64,3584]{1,0:T(8,128)(2,1)}, u32[]{:S(2)}) copy-start(bf16[64,3584]{1,0:T(8,128)(2,1)} %dot_general.31) | copy-start | bytes 1376260
  127.3 8.5 %copy-start.11 = (bf16[4,16,512]{2,1,0:T(8,128)(2,1)S(1)}, bf16[4,16,512]{2,1,0:T(8,128)(2,1)}, u32[]{:S(2)}) copy-start(bf16[4,16,512]{2,1,0:T(8,128)(2,1)} %slice.133) | copy-start | bytes 196612
  127.3 13.9 %collective-permute-start.6 = (bf16[512,512]{0,1:T(8,128)(2,1)}, bf16[512,512]{0,1:T(8,128)(2,1)}, u32[]{:S(2)}, u32[]{:S(2)}) collective-permute-start(bf16[512,512]{0,1:T(8,128)(2,1)} %pad_maximum_fusion.4), channel_id=1, source_target_pairs={{0,8},{8,16},{16,24},{24,32},{32,40},{40,48},{48,56},{56,64},{64,7... | collective-permute-start | bytes 1572872 | tf_op jit(solution)/shard_map/ppermute | solution.py:16
  139.2 1.0 copy-start.7
  145.4 2.0 %copy-start.10 = (bf16[1024,256]{0,1:T(8,128)(2,1)S(1)}, bf16[1024,256]{0,1:T(8,128)(2,1)}, u32[]{:S(2)}) copy-start(bf16[1024,256]{0,1:T(8,128)(2,1)} %copy.65) | copy-start | bytes 1572868
  145.4 2.0 %copy-start.15 = (bf16[512,256]{0,1:T(8,128)(2,1)S(1)}, bf16[512,256]{0,1:T(8,128)(2,1)}, u32[]{:S(2)}) copy-start(bf16[512,256]{0,1:T(8,128)(2,1)} %copy-done.14) | copy-start | bytes 786436
  147.4 2.8 %copy-start.26 = (bf16[512,3584]{1,0:T(8,128)(2,1)S(1)}, bf16[512,3584]{1,0:T(8,128)(2,1)}, u32[]{:S(2)}) copy-start(bf16[512,3584]{1,0:T(8,128)(2,1)} %param.21) | copy-start | bytes 11010052
  150.2 43.0 %copy-start.1 = (bf16[3584,256]{1,0:T(8,128)(2,1)S(1)}, bf16[3584,256]{1,0:T(8,128)(2,1)}, u32[]{:S(2)}) copy-start(bf16[3584,256]{1,0:T(8,128)(2,1)} %param.20) | copy-start | bytes 5505028
Sparse Core Ops, SparseCore 0:
  16.1 31.8 all-gather.1
  154.3 38.8 reduce-scatter.1
where the time goes:
time: 201 us; the launch traced here: 200 us
  waiting for transfers between devices  53.6 us (27%)
  starting transfers between devices  39.2 us (20%)
  local copies, waits for them, and re-layouts  36.7 us (18%)
  other arithmetic  32.6 us (16%)
  matrix products  21.5 us (11%)
  between operations  16.4 us (8%)
    reduce_scatter x1, waiting for transfers between devices, on_device(): lax.psum_scatter(partial_out.astype(jnp.bfloat16), ('my', 'mc'), scatter_...  39 us
    ppermute x18, starting transfers between devices, ring_send(): lax.ppermute(value, axis, [(i, (i + step) % SIDE) for i in range(SIDE)])  32.5 us
    ppermute x18, waiting for transfers between devices, ring_send(): lax.ppermute(value, axis, [(i, (i + step) % SIDE) for i in range(SIDE)])  14.5 us
    concatenate x3, other arithmetic, route(): jnp.concatenate([outgoing[:slots]] + [ring_send(outgoing[step * slots:(st...  7.28 us
    slice x3, local copies, waits for them, and re-layouts, route(): outgoing[:slots]  6.61 us
    dot_general x1, matrix products, on_device(): jnp.dot(normalized_input, query_weight, preferred_element_type=jnp.float32)  6.23 us
    gather x3, local copies, waits for them, and re-layouts, route(): return jnp.take(received, pick, axis=0, mode='clip')  5.81 us
    gather x3, local copies, waits for them, and re-layouts, route(): outgoing = jnp.take(held, source.reshape(-1), axis=0, mode='clip')  4.99 us
  transfers between devices with their start and end apart: 22, of which 6 were waited for; matrix products, arithmetic and copies ran while one was open for 32% of the time, Pallas kernels for 0%

commit v1 on v0

--- a/solution.py
+++ b/solution.py
@@ -131,6 +131,62 @@
     )
     pick = ((own_b - owner_b[me]) % SIDE) * slots + jnp.arange(slots)
     return jnp.take(received, pick, axis=0, mode="clip")
+
+
+def route_with_adapters(blocks, adapters, block_wanted, adapter_wanted, first, second):
+    coords = {"gx": lax.axis_index("gx"), "gz": lax.axis_index("gz")}
+    own_a, own_b = coords[first], coords[second]
+    rows, lanes = blocks.shape[1], blocks.shape[2]
+    pieces = adapters.shape[0]
+    tile = rows // pieces
+    flat = adapters.reshape(pieces, -1)
+    padded = jnp.pad(flat, ((0, 0), (0, tile * lanes - flat.shape[1])))
+    local = jnp.concatenate([blocks, padded.reshape(1, rows, lanes)])
+    per_block = local.shape[0]
+    held = jnp.concatenate([local] + [ring_send(local, first, step) for step in range(1, SIDE)])
+    held = held.reshape(-1, tile, lanes)
+    me = group_of(first, own_a, own_b)
+    askers = group_of(first, own_a, (own_b + jnp.arange(SIDE)) % SIDE)
+
+    def owners(wanted, per_owner):
+        owner = wanted // per_owner
+        owner_a = (owner // SIDE, owner % SIDE)[first == "gz"]
+        owner_b = (owner // SIDE, owner % SIDE)[second == "gz"]
+        return owner_a, owner_b, wanted % per_owner
+
+    block_a, block_b, block_part = owners(block_wanted, blocks.shape[0])
+    adapter_a, adapter_b, adapter_part = owners(adapter_wanted, pieces)
+    quarter = jnp.arange(pieces)
+    block_items = (
+        (((own_a - block_a[askers]) % SIDE) * per_block + block_part[askers]) * pieces
+    )[..., None] + quarter
+    adapter_items = (
+        ((own_a - adapter_a[askers]) % SIDE) * per_block + per_block - 1
+    ) * pieces + adapter_part[askers]
+    source = jnp.concatenate(
+        [block_items.reshape(SIDE, -1), adapter_items.reshape(SIDE, -1)], axis=1
+    )
+    width = source.shape[1]
+    outgoing = jnp.take(held, source.reshape(-1), axis=0, mode="clip")
+    received = jnp.concatenate(
+        [outgoing[:width]]
+        + [
+            ring_send(outgoing[step * width:(step + 1) * width], second, step)
+            for step in range(1, SIDE)
+        ]
+    )
+    slots = block_wanted.shape[1]
+    slot = jnp.arange(slots)
+    block_pick = (
+        (((own_b - block_b[me]) % SIDE) * width + slot * pieces)[:, None] + quarter
+    ).reshape(-1)
+    adapter_pick = ((own_b - adapter_b[me]) % SIDE) * width + slots * pieces + slot
+    chosen_blocks = jnp.take(received, block_pick, axis=0, mode="clip").reshape(
+        slots, rows, lanes
+    )
+    chosen_adapters = jnp.take(received, adapter_pick, axis=0, mode="clip").reshape(slots, -1)
+    chosen_adapters = chosen_adapters[:, : flat.shape[1]].reshape(slots, *adapters.shape[1:])
+    return chosen_blocks, chosen_adapters
 
 
 def on_device(
@@ -156,8 +212,9 @@
     wanted = adapter_row_index[request_adapter]
     down_width = adapter_down_rows.shape[2]
     adapters = jnp.concatenate([adapter_down_rows, adapter_up_query], axis=2)
-    chosen = route(adapters, wanted, "gz", "gx")
-    cache_keys = route(cached_rotated_keys, request_cache_block, "gz", "gx")
+    cache_keys, chosen = route_with_adapters(
+        cached_rotated_keys, adapters, request_cache_block, wanted, "gz", "gx"
+    )
     cache_values = route(cached_value_rows, request_cache_block, "gx", "gz")
     chosen_down = chosen[:, :, :down_width]
     chosen_up = chosen[:, :, down_width:]

time: 201 us -> 187 us (0.930)
  starting transfers between devices: 39.2 us -> 29 us
  other arithmetic: 32.6 us -> 28.9 us
  local copies, waits for them, and re-layouts: 36.7 us -> 39 us
    ppermute x18 -> x12, starting transfers between devices: 32.5 us -> 19.7 us  [ring_send(): lax.ppermute(value, axis, [(i, (i + step) % SIDE) for i in range(SIDE)])]
    gather x0 -> x7, local copies, waits for them, and re-layouts: none -> 10.1 us  [the longest x1 3.11 us: route_with_adapters(): jnp.take(received, block_pick, axis=0, mode='clip')]
    concatenate x3 -> x1, other arithmetic: 7.28 us -> 3.02 us  [route(): jnp.concatenate([outgoing[:slots]] + [ring_send(outgoing[step * slots:(st...]
    slice x3 -> x1, local copies, waits for them, and re-layouts: 6.61 us -> 2.77 us  [route(): outgoing[:slots]]
    gather x3 -> x1, local copies, waits for them, and re-layouts: 5.81 us -> 2.17 us  [route(): return jnp.take(received, pick, axis=0, mode='clip')]
    slice x0 -> x2, local copies, waits for them, and re-layouts: none -> 3.14 us  [the longest x1 3.1 us: route_with_adapters(): outgoing[:width]]
    concatenate x0 -> x2, other arithmetic: none -> 2.94 us  [the longest x1 2.87 us: route_with_adapters(): jnp.concatenate([outgoing[:width]] + [ring_send(outgoing[step * width:(st...]
    reduce_scatter x1, waiting for transfers between devices: 39 us -> 36.1 us  [on_device(): lax.psum_scatter(partial_out.astype(jnp.bfloat16), ('my', 'mc'), scatter_...]
  transfers between devices with their start and end apart: 22 -> 16, of which waited for: 6 -> 5; matrix products, arithmetic and copies ran while one was open for 32% -> 34% of each run, Pallas kernels for 0% -> 0%
where the time goes in v1:
time: 187 us; the launch traced here: 186 us
  waiting for transfers between devices  52.4 us (28%)
  local copies, waits for them, and re-layouts  39 us (21%)
  starting transfers between devices  29 us (16%)
  other arithmetic  28.9 us (15%)
  matrix products  20.2 us (11%)
  between operations  16.6 us (9%)
    reduce_scatter x1, waiting for transfers between devices, on_device(): lax.psum_scatter(partial_out.astype(jnp.bfloat16), ('my', 'mc'), scatter_...  36.1 us
    ppermute x12, starting transfers between devices, ring_send(): lax.ppermute(value, axis, [(i, (i + step) % SIDE) for i in range(SIDE)])  19.7 us
    ppermute x12, waiting for transfers between devices, ring_send(): lax.ppermute(value, axis, [(i, (i + step) % SIDE) for i in range(SIDE)])  15.4 us
    unnamed x71, local copies, waits for them, and re-layouts  6.87 us
    dot_general x1, matrix products, on_device(): jnp.dot(normalized_input, query_weight, preferred_element_type=jnp.float32)  5.26 us
    ppermute x1, starting transfers between devices, shifted(): lax.ppermute(value, axis, [(source, source + steps) for source in range(f...  4.7 us
    all_to_all x1, starting transfers between devices, on_device(): lax.all_to_all(jnp.broadcast_to(chosen_down, (model_count, *chosen_down.s...  4.42 us
    dot_general x1, matrix products, on_device(): jnp.dot(attended, output_weight, preferred_element_type=jnp.float32)  3.92 us
  transfers between devices with their start and end apart: 16, of which 5 were waited for; matrix products, arithmetic and copies ran while one was open for 34% of the time, Pallas kernels for 0%

profile of v1, /device:TPU:0, one launch (start us, length us, event | category | flops | bytes accessed | tf_op | source)
XLA Modules:
  0.0 186.0 jit_solution(7639174309509673406)
XLA Ops:
  6.5 3.2 %collective-permute-start.1 = (bf16[2,256,256]{2,1,0:T(8,128)(2,1)}, bf16[2,256,256]{2,1,0:T(8,128)(2,1)}, u32[]{:S(2)}, u32[]{:S(2)}) collective-permute-start(bf16[2,256,256]{2,1,0:T(8,128)(2,1)} %param.31), channel_id=1, source_target_pairs={{0,64},{32,96},{64,0},{96,32},{1,65},{33,97},{65,1},{97,33},{2,66}... | collective-permute-start | bytes 786440 | tf_op jit(solution)/shard_map/ppermute | solution.py:109
  9.7 0.6 collective-permute-start
  10.3 1.0 pad_maximum_fusion.4
  11.6 1.7 constant_dynamic-update-slice_fusion.1
  13.3 0.7 constant_dynamic-update-slice_fusion
  14.0 4.0 %collective-permute-start.9 = (bf16[3,256,256]{2,1,0:T(8,128)(2,1)}, bf16[3,256,256]{2,1,0:T(8,128)(2,1)}, u32[]{:S(2)}, u32[]{:S(2)}) collective-permute-start(bf16[3,256,256]{2,1,0:T(8,128)(2,1)} %get-tuple-element.33), channel_id=1, source_target_pairs={{0,24},{8,0},{16,8},{24,16},{1,25},{9,1},{17,9},{25,17},{2,26},{10... | collective-permute-start | bytes 1179656 | tf_op jit(solution)/shard_map/ppermute | solution.py:109
  18.0 1.3 collective-permute-start.7
  19.6 0.8 gather_fusion.6
  21.1 0.6 constant_dynamic-slice_fusion.8
  22.2 0.7 dynamic_slice.24
  26.6 0.6 negate_select_fusion.1
  29.9 0.6 fusion.105
  30.5 2.4 %compare_select_fusion.2 = s32[1024,1]{0,1:T(1,128)S(1)} fusion(s32[]{:T(128)} %bitcast.14, s32[]{:T(128)} %bitcast.15, s32[]{:T(128)} %bitcast.17, s32[]{:T(128)} %bitcast.16), kind=kLoop, calls=%fused_computation.75 | loop fusion | flops 17408 | bytes 4112 | tf_op jit(solution)/shard_map/gather | solution.py:77
  33.0 0.7 iota_add_fusion
  34.1 1.8 multiply_cosine_fusion
  36.0 0.8 compare_and_fusion
  36.8 1.3 pad_add_fusion
  38.1 0.6 pad_clamp_fusion.6
  38.9 2.7 %collective-permute-start.2 = (bf16[2,256,256]{2,1,0:T(8,128)(2,1)}, bf16[2,256,256]{2,1,0:T(8,128)(2,1)}, u32[]{:S(2)}, u32[]{:S(2)}) collective-permute-start(bf16[2,256,256]{2,1,0:T(8,128)(2,1)} %param.31), channel_id=1, source_target_pairs={{0,96},{32,0},{64,32},{96,64},{1,97},{33,1},{65,33},{97,65},{2,98}... | collective-permute-start | bytes 786440 | tf_op jit(solution)/shard_map/ppermute | solution.py:109
  41.6 1.0 constant_dynamic-update-slice_fusion.4
  42.7 1.0 constant_dynamic-update-slice_fusion.3
  43.8 1.1 constant_dynamic-update-slice_fusion.2
  44.8 2.4 %gather_fusion.9 = bf16[80,64,256]{2,1,0:T(8,128)(2,1)} fusion(bf16[48,64,256]{2,1,0:T(8,128)(2,1)S(1)} %bitcast.111, s32[1024]{0:T(1024)S(1)} %pad_clamp_fusion.2), kind=kCustom, calls=%fused_computation.9 | custom fusion | bytes 5243200 | tf_op jit(solution)/shard_map/jit(_take)/gather | solution.py:170
  47.3 3.1 %fusion.101 = (bf16[20,64,256]{2,1,0:T(8,128)(2,1)S(1)}, bf16[20,64,256]{2,1,0:T(8,128)(2,1)}, bf16[20,64,256]{2,1,0:T(8,128)(2,1)}, bf16[20,64,256]{2,1,0:T(8,128)(2,1)}) fusion(bf16[80,64,256]{2,1,0:T(8,128)(2,1)} %gather_fusion.9), kind=kLoop, calls=%fused_computation.238 | loop fusion | bytes 5242880 | tf_op jit(solution)/shard_map/slice | solution.py:172
  50.9 0.9 collective-permute-start.10
  51.8 2.4 %collective-permute-start.12 = (bf16[20,64,256]{2,1,0:T(8,128)(2,1)}, bf16[20,64,256]{2,1,0:T(8,128)(2,1)}, u32[]{:S(2)}, u32[]{:S(2)}) collective-permute-start(bf16[20,64,256]{2,1,0:T(8,128)(2,1)} %get-tuple-element.18), channel_id=1, source_target_pairs={{0,96},{32,0},{64,32},{96,64},{1,97},{33,1},{65,33},{97,65},{2,98}... | collective-permute-start | bytes 1966088 | tf_op jit(solution)/shard_map/ppermute | solution.py:109
  54.1 0.7 fusion.93
  54.9 1.3 pad_maximum_fusion.2
  56.3 2.1 %gather_fusion.2 = bf16[16,256,256]{2,1,0:T(8,128)(2,1)} fusion(bf16[8,256,256]{2,1,0:T(8,128)(2,1)S(1)} %pad_maximum_fusion.2, s32[1024]{0:T(1024)} %pad_clamp_fusion.6), kind=kCustom, calls=%fused_computation.2 | custom fusion | bytes 4194368 | tf_op jit(solution)/shard_map/jit(_take)/gather | solution.py:124
  58.4 2.8 %fusion.102 = (bf16[4,256,256]{2,1,0:T(8,128)(2,1)S(1)}, bf16[4,256,256]{2,1,0:T(8,128)(2,1)}, bf16[4,256,256]{2,1,0:T(8,128)(2,1)}, bf16[4,256,256]{2,1,0:T(8,128)(2,1)}) fusion(bf16[16,256,256]{2,1,0:T(8,128)(2,1)} %gather_fusion.2), kind=kLoop, calls=%fused_computation.239 | loop fusion | bytes 4194304 | tf_op jit(solution)/shard_map/slice | solution.py:126
  61.2 2.2 %collective-permute-start.4 = (bf16[4,256,256]{2,1,0:T(8,128)(2,1)}, bf16[4,256,256]{2,1,0:T(8,128)(2,1)}, u32[]{:S(2)}, u32[]{:S(2)}) collective-permute-start(bf16[4,256,256]{2,1,0:T(8,128)(2,1)} %get-tuple-element.20), channel_id=1, source_target_pairs={{0,16},{8,24},{16,0},{24,8},{1,17},{9,25},{17,1},{25,9},{2,18},{10... | collective-permute-start | bytes 1572872 | tf_op jit(solution)/shard_map/ppermute | solution.py:109
  63.4 0.6 collective-permute-start.3
  63.9 5.9 %collective-permute-done.11 = bf16[20,64,256]{2,1,0:T(8,128)(2,1)} collective-permute-done((bf16[20,64,256]{2,1,0:T(8,128)(2,1)}, bf16[20,64,256]{2,1,0:T(8,128)(2,1)}, u32[]{:S(2)}, u32[]{:S(2)}) %collective-permute-start.11) | collective-permute-done | bytes 655392 | tf_op jit(solution)/shard_map/ppermute | solution.py:109
  69.9 1.9 %collective-permute-start.5 = (bf16[4,256,256]{2,1,0:T(8,128)(2,1)}, bf16[4,256,256]{2,1,0:T(8,128)(2,1)}, u32[]{:S(2)}, u32[]{:S(2)}) collective-permute-start(bf16[4,256,256]{2,1,0:T(8,128)(2,1)} %get-tuple-element.22), channel_id=1, source_target_pairs={{0,24},{8,0},{16,8},{24,16},{1,25},{9,1},{17,9},{25,17},{2,26},{10... | collective-permute-start | bytes 1572872 | tf_op jit(solution)/shard_map/ppermute | solution.py:109
  71.8 9.5 %collective-permute-done.10 = bf16[20,64,256]{2,1,0:T(8,128)(2,1)} collective-permute-done((bf16[20,64,256]{2,1,0:T(8,128)(2,1)}, bf16[20,64,256]{2,1,0:T(8,128)(2,1)}, u32[]{:S(2)}, u32[]{:S(2)}) %collective-permute-start.10) | collective-permute-done | bytes 655392 | tf_op jit(solution)/shard_map/ppermute | solution.py:109
  81.2 2.9 %pad_maximum_fusion = bf16[80,64,256]{2,1,0:T(8,128)(2,1)} fusion(bf16[20,64,256]{2,1,0:T(8,128)(2,1)} %collective-permute-done.12, bf16[20,64,256]{2,1,0:T(8,128)(2,1)} %collective-permute-done.11, bf16[20,64,256]{2,1,0:T(8,128)(2,1)} %collective-permute-done.10, bf16[20,64,256]{2,1,0:T(8,128)(2,1)S(1)} %get-tuple-element.15), kind=kLoop, calls=%fused_computation.27 | loop fusion | flops 3932160 | bytes 5242880 | tf_op jit(solution)/shard_map/concatenate | solution.py:171
  84.1 2.3 %gather_fusion.11 = bf16[4,64,256]{2,1,0:T(8,128)(2,1)S(1)} fusion(bf16[80,64,256]{2,1,0:T(8,128)(2,1)} %pad_maximum_fusion, s32[1024]{0:T(1024)S(1)} %get-tuple-element.51), kind=kCustom, calls=%fused_computation.11 | custom fusion | bytes 262160 | tf_op jit(solution)/shard_map/jit(_take)/gather | solution.py:187
  86.8 0.9 broadcast_in_dim.36
  87.6 4.4 %all-to-all-start = ((bf16[8,4,16,448]{3,2,1,0:T(8,128)(2,1)}), bf16[8,4,16,448]{3,2,1,0:T(8,128)(2,1)S(1)}, u32[]{:S(2)}, u32[]{:S(2)}) async-start(bf16[8,4,16,448]{3,2,1,0:T(8,128)(2,1)} %broadcast_in_dim.36), calls=%async_computation | async-start | bytes 1048576 | tf_op jit(solution)/shard_map/all_to_all | solution.py:222
  92.4 3.0 %pad_maximum_fusion.1 = bf16[16,256,256]{2,1,0:T(8,128)(2,1)} fusion(bf16[4,256,256]{2,1,0:T(8,128)(2,1)} %collective-permute-done.5, bf16[4,256,256]{2,1,0:T(8,128)(2,1)} %collective-permute-done.4, bf16[4,256,256]{2,1,0:T(8,128)(2,1)} %collective-permute-done.3, bf16[4,256,256]{2,1,0:T(8,128)(2,1)S(1)} %get-tuple-element.19), kind=kLoop, calls=%fused_computation.28 | loop fusion | flops 3145728 | bytes 4194304 | tf_op jit(solution)/shard_map/concatenate | solution.py:125
  95.4 2.2 %gather_fusion.3 = bf16[4,256,256]{2,1,0:T(8,128)(2,1)S(1)} fusion(bf16[16,256,256]{2,1,0:T(8,128)(2,1)} %pad_maximum_fusion.1, s32[1024]{0:T(1024)S(1)} %pad_clamp_fusion.5), kind=kCustom, calls=%fused_computation.3 | custom fusion | bytes 1048592 | tf_op jit(solution)/shard_map/jit(_take)/gather | solution.py:133
  97.6 1.0 copy.65
  98.7 3.1 %gather_fusion.10 = bf16[16,64,256]{2,1,0:T(8,128)(2,1)} fusion(bf16[80,64,256]{2,1,0:T(8,128)(2,1)} %pad_maximum_fusion, s32[1024]{0:T(1024)S(1)} %get-tuple-element.52), kind=kCustom, calls=%fused_computation.10 | custom fusion | bytes 1048640 | tf_op jit(solution)/shard_map/jit(_take)/gather | solution.py:184
  101.8 0.6 all-to-all-done
  102.7 0.6 dot_general.31
  103.3 3.0 %fusion.2 = f32[512]{0:T(512)S(1)} fusion(bf16[512,3584]{0,1:T(8,128)(2,1)} %all-gather.2.cloned.1.call-done), kind=kLoop, calls=%fused_computation.18 | loop fusion | flops 5504512 | bytes 3672064 | tf_op jit(solution)/shard_map/reduce_sum | solution.py:236
  106.5 1.6 fusion.4
  108.1 1.2 convolution_convert_fusion.1
  109.2 0.7 copy-done.3
  109.9 1.0 copy-done.29
  110.9 1.2 convolution_bitcast_fusion
  112.1 1.2 fusion.35
  113.3 0.8 copy.58
  114.1 0.9 pad_maximum_fusion.3
  115.0 4.7 %collective-permute-start.6 = (bf16[512,512]{0,1:T(8,128)(2,1)}, bf16[512,512]{0,1:T(8,128)(2,1)}, u32[]{:S(2)}, u32[]{:S(2)}) collective-permute-start(bf16[512,512]{0,1:T(8,128)(2,1)} %pad_maximum_fusion.3), channel_id=1, source_target_pairs={{0,8},{8,16},{16,24},{24,32},{32,40},{40,48},{48,56},{56,64},{64,7... | collective-permute-start | bytes 1572872 | tf_op jit(solution)/shard_map/ppermute | solution.py:16
  119.7 5.3 %fusion.106 = f32[512,512]{0,1:T(8,128)S(1)} fusion(bf16[512,3584]{0,1:T(8,128)(2,1)} %copy-done.3, bf16[3584,512]{1,0:T(8,128)(2,1)} %param.18), kind=kOutput, calls=%fused_computation.243 | convolution fusion | flops 1879048192 | bytes 8388608 | tf_op jit(solution)/shard_map/dot_general | solution.py:255
  125.0 3.0 %fusion.13 = f32[512,512]{0,1:T(8,128)S(1)} fusion(f32[512,512]{0,1:T(8,128)S(1)} %fusion.106, bf16[64,512]{1,0:T(8,128)(2,1)S(1)} %bitcast.118, bf16[512,64]{0,1:T(8,128)(2,1)S(1)} %bitcast.119, bf16[64,3584]{1,0:T(8,128)(2,1)S(1)} %dot_general.31, bf16[512,3584]{0,1:T(8,128)(2,1)} %copy-done.3), kind=kOutput, calls=%fused_computation.32 | convolution fusion | flops 269025280 | bytes 6356992 | tf_op jit(solution)/shard_map/dot_general | solution.py:249
  129.1 0.9 subtract_convert_fusion
  130.2 1.1 fusion.104
  131.4 2.8 %fusion.5 = (f32[2,512]{1,0:T(2,128)S(1)}, f32[2048,512,2]{1,0,2:T(8,128)S(1)}) fusion(pred[512,2048]{0,1:T(8,128)(4,1)S(1)} %copy-done.5, bf16[512,2,128]{2,0,1:T(8,128)(2,1)} %get-tuple-element.24, bf16[512,2,128]{2,0,1:T(8,128)(2,1)} %get-tuple-element.23, bf16[512,256]{1,0:T(8,128)(2,1)S(1)} %copy-done.10, bf16[512,256]{1,0:T(8,128)(2,1)S(1)} %copy.57, ...), kind=kOutput, calls=%fused_computation.21 | convolution fusion | flops 1084226560 | bytes 11014144 | tf_op jit(solution)/shard_map/tkrd,skd->krts/dot_general | solution.py:84
  134.3 2.0 %fusion = f32[2,512]{1,0:T(2,128)S(1)} fusion(f32[2048,512,2]{1,0,2:T(8,128)S(1)} %get-tuple-element.47, f32[2,512]{1,0:T(2,128)S(1)} %get-tuple-element.46, pred[512,2048]{0,1:T(8,128)(4,1)S(1)} %copy-done.5), kind=kLoop, calls=%fused_computation.16 | loop fusion | flops 8387584 | bytes 9445376 | tf_op jit(solution)/shard_map/reduce_sum | solution.py:90
  136.3 2.8 %divide_convert_fusion = bf16[512,1,2,256]{0,3,2,1:T(8,128)(2,1)S(1)} fusion(f32[2048,512,2]{1,0,2:T(8,128)S(1)} %get-tuple-element.47, f32[2,512]{1,0:T(2,128)S(1)} %get-tuple-element.46, pred[512,2048]{0,1:T(8,128)(4,1)S(1)} %copy-done.5, bf16[512,256]{0,1:T(8,128)(2,1)S(1)} %copy-done.12, bf16[512,256]{0,1:T(8,128)(2,1)S(1)} %get-tuple-element.29, ...), kind=kOutput, calls=%fused_computation.49 | convolution fusion | flops 1085800448 | bytes 11018240 | tf_op jit(solution)/shard_map/krts,skd->tkrd/dot_general | solution.py:91
  139.1 3.9 %convolution_convert_fusion = bf16[512,3584]{0,1:T(8,128)(2,1)} fusion(bf16[512,512]{0,1:T(8,128)(2,1)S(1)} %bitcast.125, bf16[512,3584]{1,0:T(8,128)(2,1)S(1)} %copy-done.28), kind=kOutput, calls=%fused_computation.22 | convolution fusion | flops 1880883200 | bytes 7864320 | tf_op jit(solution)/shard_map/dot_general | solution.py:283
  143.1 36.1 %reduce-scatter.2.cloned.1.call-done = bf16[512,448]{0,1:T(8,128)(2,1)} async-done(((bf16[512,3584]{0,1:T(8,128)(2,1)}), bf16[512,448]{0,1:T(8,128)(2,1)}) %reduce-scatter.2.cloned.1.call-update) | async-done | bytes 458768 | tf_op jit(solution)/shard_map/reduce_scatter | solution.py:284
  (145 shorter events, 9.5 us)
Async XLA Ops:
  6.5 101.5 %copy-start = (bf16[3584,256]{1,0:T(8,128)(2,1)S(1)}, bf16[3584,256]{1,0:T(8,128)(2,1)}, u32[]{:S(2)}) copy-start(bf16[3584,256]{1,0:T(8,128)(2,1)} %param.20) | copy-start | bytes 5505028
  6.5 12.8 %copy-start.17 = (s32[16,4]{0,1:T(4,128)S(1)}, s32[16,4]{0,1:T(4,128)}, u32[]{:S(2)}) copy-start(s32[16,4]{0,1:T(4,128)} %param.24) | copy-start | bytes 772
  6.5 13.0 %copy-start.2 = (s32[64]{0:T(128)S(1)}, s32[64]{0:T(128)}, u32[]{:S(2)}) copy-start(s32[64]{0:T(128)} %param.25) | copy-start | bytes 772
  6.5 96.8 %all-gather.2.cloned.1.call-start = ((), (), s32[]{:S(2)}) async-start(), calls=%async_computation.2 | async-start | bytes 4128768 | tf_op jit(solution)/shard_map/all_gather | solution.py:233
  6.5 45.2 %collective-permute-start.1 = (bf16[2,256,256]{2,1,0:T(8,128)(2,1)}, bf16[2,256,256]{2,1,0:T(8,128)(2,1)}, u32[]{:S(2)}, u32[]{:S(2)}) collective-permute-start(bf16[2,256,256]{2,1,0:T(8,128)(2,1)} %param.31), channel_id=1, source_target_pairs={{0,64},{32,96},{64,0},{96,32},{1,65},{33,97},{65,1},{97,33},{2,66}... | collective-permute-start | bytes 786440 | tf_op jit(solution)/shard_map/ppermute | solution.py:109
  9.7 45.2 %collective-permute-start = (bf16[2,256,256]{2,1,0:T(8,128)(2,1)}, bf16[2,256,256]{2,1,0:T(8,128)(2,1)}, u32[]{:S(2)}, u32[]{:S(2)}) collective-permute-start(bf16[2,256,256]{2,1,0:T(8,128)(2,1)} %param.31), channel_id=1, source_target_pairs={{0,32},{32,64},{64,96},{96,0},{1,33},{33,65},{65,97},{97,1},{2,34}... | collective-permute-start | bytes 786440 | tf_op jit(solution)/shard_map/ppermute | solution.py:109
  14.0 29.8 %collective-permute-start.9 = (bf16[3,256,256]{2,1,0:T(8,128)(2,1)}, bf16[3,256,256]{2,1,0:T(8,128)(2,1)}, u32[]{:S(2)}, u32[]{:S(2)}) collective-permute-start(bf16[3,256,256]{2,1,0:T(8,128)(2,1)} %get-tuple-element.33), channel_id=1, source_target_pairs={{0,24},{8,0},{16,8},{24,16},{1,25},{9,1},{17,9},{25,17},{2,26},{10... | collective-permute-start | bytes 1179656 | tf_op jit(solution)/shard_map/ppermute | solution.py:109
  18.0 24.7 %collective-permute-start.8 = (bf16[3,256,256]{2,1,0:T(8,128)(2,1)}, bf16[3,256,256]{2,1,0:T(8,128)(2,1)}, u32[]{:S(2)}, u32[]{:S(2)}) collective-permute-start(bf16[3,256,256]{2,1,0:T(8,128)(2,1)} %get-tuple-element.33), channel_id=1, source_target_pairs={{0,16},{8,24},{16,0},{24,8},{1,17},{9,25},{17,1},{25,9},{2,18},{10... | collective-permute-start | bytes 1179656 | tf_op jit(solution)/shard_map/ppermute | solution.py:109
  18.0 20.9 %collective-permute-start.7 = (bf16[3,256,256]{2,1,0:T(8,128)(2,1)}, bf16[3,256,256]{2,1,0:T(8,128)(2,1)}, u32[]{:S(2)}, u32[]{:S(2)}) collective-permute-start(bf16[3,256,256]{2,1,0:T(8,128)(2,1)} %get-tuple-element.33), channel_id=1, source_target_pairs={{0,8},{8,16},{16,24},{24,0},{1,9},{9,17},{17,25},{25,1},{2,10},{10... | collective-permute-start | bytes 1179656 | tf_op jit(solution)/shard_map/ppermute | solution.py:109
  19.6 1.5 copy-start.21
  19.6 2.6 %copy-start.30 = (s32[16]{0:T(128)S(1)}, s32[16]{0:T(128)}, u32[]{:S(2)}) copy-start(s32[16]{0:T(128)} %param.27) | copy-start | bytes 196
  19.6 5.3 %copy-start.20 = (s32[16,4]{0,1:T(4,128)S(1)}, s32[16,4]{0,1:T(4,128)}, u32[]{:S(2)}) copy-start(s32[16,4]{0,1:T(4,128)} %param.29) | copy-start | bytes 772
  19.6 5.8 %copy-start.18 = (s32[16,4]{0,1:T(4,128)S(1)}, s32[16,4]{0,1:T(4,128)}, u32[]{:S(2)}) copy-start(s32[16,4]{0,1:T(4,128)} %param.28) | copy-start | bytes 772
  25.4 18.3 %copy-start.22 = (s32[4,1]{0,1:T(1,128)}, s32[4,1]{0,1:T(1,128)S(1)}, u32[]{:S(2)}) copy-start(s32[4,1]{0,1:T(1,128)S(1)} %reduce-window.4) | copy-start | bytes 52
  29.8 13.9 %copy-start.26 = (f32[128]{0:T(128)}, f32[128]{0:T(128)S(1)}, u32[]{:S(2)}) copy-start(f32[128]{0:T(128)S(1)} %multiply_power_fusion) | copy-start | bytes 1540
  32.9 0.8 copy-start.24
  33.7 10.0 %copy-start.13 = (f32[512]{0:T(512)}, f32[512]{0:T(512)S(1)}, u32[]{:S(2)}) copy-start(f32[512]{0:T(512)S(1)} %add_convert_fusion.1) | copy-start | bytes 6148
  38.9 16.0 %collective-permute-start.2 = (bf16[2,256,256]{2,1,0:T(8,128)(2,1)}, bf16[2,256,256]{2,1,0:T(8,128)(2,1)}, u32[]{:S(2)}, u32[]{:S(2)}) collective-permute-start(bf16[2,256,256]{2,1,0:T(8,128)(2,1)} %param.31), channel_id=1, source_target_pairs={{0,96},{32,0},{64,32},{96,64},{1,97},{33,1},{65,33},{97,65},{2,98}... | collective-permute-start | bytes 786440 | tf_op jit(solution)/shard_map/ppermute | solution.py:109
  47.3 7.6 %copy-start.16 = (s32[4,4]{1,0:T(4,128)S(1)}, s32[4,4]{1,0:T(4,128)}, u32[]{:S(2)}) copy-start(s32[4,4]{1,0:T(4,128)} %iota_add_fusion) | copy-start | bytes 196
  50.4 19.5 %collective-permute-start.11 = (bf16[20,64,256]{2,1,0:T(8,128)(2,1)}, bf16[20,64,256]{2,1,0:T(8,128)(2,1)}, u32[]{:S(2)}, u32[]{:S(2)}) collective-permute-start(bf16[20,64,256]{2,1,0:T(8,128)(2,1)} %get-tuple-element.16), channel_id=1, source_target_pairs={{0,64},{32,96},{64,0},{96,32},{1,65},{33,97},{65,1},{97,33},{2,66}... | collective-permute-start | bytes 1966088 | tf_op jit(solution)/shard_map/ppermute | solution.py:109
  50.9 30.3 %collective-permute-start.10 = (bf16[20,64,256]{2,1,0:T(8,128)(2,1)}, bf16[20,64,256]{2,1,0:T(8,128)(2,1)}, u32[]{:S(2)}, u32[]{:S(2)}) collective-permute-start(bf16[20,64,256]{2,1,0:T(8,128)(2,1)} %get-tuple-element.17), channel_id=1, source_target_pairs={{0,32},{32,64},{64,96},{96,0},{1,33},{33,65},{65,97},{97,1},{2,34}... | collective-permute-start | bytes 1966088 | tf_op jit(solution)/shard_map/ppermute | solution.py:109
  51.8 29.5 %collective-permute-start.12 = (bf16[20,64,256]{2,1,0:T(8,128)(2,1)}, bf16[20,64,256]{2,1,0:T(8,128)(2,1)}, u32[]{:S(2)}, u32[]{:S(2)}) collective-permute-start(bf16[20,64,256]{2,1,0:T(8,128)(2,1)} %get-tuple-element.18), channel_id=1, source_target_pairs={{0,96},{32,0},{64,32},{96,64},{1,97},{33,1},{65,33},{97,65},{2,98}... | collective-permute-start | bytes 1966088 | tf_op jit(solution)/shard_map/ppermute | solution.py:109
  58.4 13.4 %copy-start.19 = (s32[4]{0:T(128)S(1)}, s32[4]{0:T(128)}, u32[]{:S(2)}) copy-start(s32[4]{0:T(128)} %fusion.94) | copy-start | bytes 52
  61.2 31.2 %collective-permute-start.4 = (bf16[4,256,256]{2,1,0:T(8,128)(2,1)}, bf16[4,256,256]{2,1,0:T(8,128)(2,1)}, u32[]{:S(2)}, u32[]{:S(2)}) collective-permute-start(bf16[4,256,256]{2,1,0:T(8,128)(2,1)} %get-tuple-element.20), channel_id=1, source_target_pairs={{0,16},{8,24},{16,0},{24,8},{1,17},{9,25},{17,1},{25,9},{2,18},{10... | collective-permute-start | bytes 1572872 | tf_op jit(solution)/shard_map/ppermute | solution.py:109
  63.4 29.0 %collective-permute-start.3 = (bf16[4,256,256]{2,1,0:T(8,128)(2,1)}, bf16[4,256,256]{2,1,0:T(8,128)(2,1)}, u32[]{:S(2)}, u32[]{:S(2)}) collective-permute-start(bf16[4,256,256]{2,1,0:T(8,128)(2,1)} %get-tuple-element.21), channel_id=1, source_target_pairs={{0,8},{8,16},{16,24},{24,0},{1,9},{9,17},{17,25},{25,1},{2,10},{10... | collective-permute-start | bytes 1572872 | tf_op jit(solution)/shard_map/ppermute | solution.py:109
  69.9 22.5 %collective-permute-start.5 = (bf16[4,256,256]{2,1,0:T(8,128)(2,1)}, bf16[4,256,256]{2,1,0:T(8,128)(2,1)}, u32[]{:S(2)}, u32[]{:S(2)}) collective-permute-start(bf16[4,256,256]{2,1,0:T(8,128)(2,1)} %get-tuple-element.22), channel_id=1, source_target_pairs={{0,24},{8,0},{16,8},{24,16},{1,25},{9,1},{17,9},{25,17},{2,26},{10... | collective-permute-start | bytes 1572872 | tf_op jit(solution)/shard_map/ppermute | solution.py:109
  84.1 8.2 %copy-start.23 = (s32[4,1]{0,1:T(1,128)S(1)}, s32[4,1]{0,1:T(1,128)}, u32[]{:S(2)}) copy-start(s32[4,1]{0,1:T(1,128)} %copy-done.22) | copy-start | bytes 52
  84.1 8.2 %copy-start.25 = (s32[4]{0:T(128)S(1)}, s32[4]{0:T(128)}, u32[]{:S(2)}) copy-start(s32[4]{0:T(128)} %copy-done.24) | copy-start | bytes 52
  87.6 14.8 %all-to-all-start = ((bf16[8,4,16,448]{3,2,1,0:T(8,128)(2,1)}), bf16[8,4,16,448]{3,2,1,0:T(8,128)(2,1)S(1)}, u32[]{:S(2)}, u32[]{:S(2)}) async-start(bf16[8,4,16,448]{3,2,1,0:T(8,128)(2,1)} %broadcast_in_dim.36), calls=%async_computation | async-start | bytes 1048576 | tf_op jit(solution)/shard_map/all_to_all | solution.py:222
  92.1 87.1 %reduce-scatter.2.cloned.1.call-start = ((), (), s32[]{:S(2)}) async-start(), calls=%async_computation.3 | async-start | bytes 4128768 | tf_op jit(solution)/shard_map/reduce_scatter | solution.py:284
  102.4 3.9 %copy-start.15 = (f32[3584]{0:T(1024)S(1)}, f32[3584]{0:T(1024)}, u32[]{:S(2)}) copy-start(f32[3584]{0:T(1024)} %param.17) | copy-start | bytes 43012
  103.3 3.1 %copy-start.4 = (bf16[512,3584]{0,1:T(8,128)(2,1)S(1)}, bf16[512,3584]{0,1:T(8,128)(2,1)}, u32[]{:S(2)}) copy-start(bf16[512,3584]{0,1:T(8,128)(2,1)} %all-gather.2.cloned.1.call-done) | copy-start | bytes 11010052
  108.0 1.9 %copy-start.3 = (bf16[512,3584]{0,1:T(8,128)(2,1)}, bf16[512,3584]{0,1:T(8,128)(2,1)S(1)}, u32[]{:S(2)}) copy-start(bf16[512,3584]{0,1:T(8,128)(2,1)S(1)} %fusion.4) | copy-start | bytes 11010052
  108.0 2.8 %copy-start.29 = (bf16[3584,256]{1,0:T(8,128)(2,1)S(1)}, bf16[3584,256]{1,0:T(8,128)(2,1)}, u32[]{:S(2)}) copy-start(bf16[3584,256]{1,0:T(8,128)(2,1)} %param.19) | copy-start | bytes 5505028
  110.9 3.2 %copy-start.11 = (bf16[512,256]{0,1:T(8,128)(2,1)}, bf16[512,256]{0,1:T(8,128)(2,1)S(1)}, u32[]{:S(2)}) copy-start(bf16[512,256]{0,1:T(8,128)(2,1)S(1)} %convolution_convert_fusion.1) | copy-start | bytes 786436
  110.9 1.2 copy-start.14
  110.9 1.2 copy-start.27
  115.0 15.2 %collective-permute-start.6 = (bf16[512,512]{0,1:T(8,128)(2,1)}, bf16[512,512]{0,1:T(8,128)(2,1)}, u32[]{:S(2)}, u32[]{:S(2)}) collective-permute-start(bf16[512,512]{0,1:T(8,128)(2,1)} %pad_maximum_fusion.3), channel_id=1, source_target_pairs={{0,8},{8,16},{16,24},{24,32},{32,40},{40,48},{48,56},{56,64},{64,7... | collective-permute-start | bytes 1572872 | tf_op jit(solution)/shard_map/ppermute | solution.py:16
  128.0 1.0 copy-start.6
  128.0 1.0 copy-start.7
  128.3 3.1 %copy-start.5 = (pred[512,2048]{0,1:T(8,128)(4,1)S(1)}, pred[512,2048]{0,1:T(8,128)(4,1)}, u32[]{:S(2)}) copy-start(pred[512,2048]{0,1:T(8,128)(4,1)} %pad_add_fusion) | copy-start | bytes 3145732
  128.3 3.1 %copy-start.10 = (bf16[512,256]{1,0:T(8,128)(2,1)S(1)}, bf16[512,256]{1,0:T(8,128)(2,1)}, u32[]{:S(2)}) copy-start(bf16[512,256]{1,0:T(8,128)(2,1)} %copy.58) | copy-start | bytes 786436
  128.5 2.9 %copy-start.9 = (bf16[16,64,256]{2,1,0:T(8,128)(2,1)S(1)}, bf16[16,64,256]{2,1,0:T(8,128)(2,1)}, u32[]{:S(2)}) copy-start(bf16[16,64,256]{2,1,0:T(8,128)(2,1)} %gather_fusion.10) | copy-start | bytes 1572868
  134.3 2.0 %copy-start.8 = (bf16[1024,256]{0,1:T(8,128)(2,1)S(1)}, bf16[1024,256]{0,1:T(8,128)(2,1)}, u32[]{:S(2)}) copy-start(bf16[1024,256]{0,1:T(8,128)(2,1)} %copy.65) | copy-start | bytes 1572868
  134.3 2.0 %copy-start.12 = (bf16[512,256]{0,1:T(8,128)(2,1)S(1)}, bf16[512,256]{0,1:T(8,128)(2,1)}, u32[]{:S(2)}) copy-start(bf16[512,256]{0,1:T(8,128)(2,1)} %copy-done.11) | copy-start | bytes 786436
  136.3 2.8 %copy-start.28 = (bf16[512,3584]{1,0:T(8,128)(2,1)S(1)}, bf16[512,3584]{1,0:T(8,128)(2,1)}, u32[]{:S(2)}) copy-start(bf16[512,3584]{1,0:T(8,128)(2,1)} %param.21) | copy-start | bytes 11010052
  139.1 40.1 %copy-start.1 = (bf16[3584,256]{1,0:T(8,128)(2,1)S(1)}, bf16[3584,256]{1,0:T(8,128)(2,1)}, u32[]{:S(2)}) copy-start(bf16[3584,256]{1,0:T(8,128)(2,1)} %param.20) | copy-start | bytes 5505028
Sparse Core Ops, SparseCore 0:
  19.4 30.1 all-gather.1
  143.2 35.9 reduce-scatter.1

commit v2 on v1

--- a/solution.py
+++ b/solution.py
@@ -71,11 +71,11 @@
     every_value = jnp.concatenate(
         [cache_values.reshape(slots, -1), prev_values, values], 0
     ).reshape(-1, kv_heads, head_size)
-    slot_req = jnp.arange(slots, dtype=jnp.int32) // block
-    slot_col = jnp.arange(slots, dtype=jnp.int32) % block
-    cache_ok = (request[:, None] == slot_req[None, :]) & (
-        slot_col[None, :] < cached[slot_req][None, :]
-    )
+    owned = jnp.arange(cache_keys.shape[0], dtype=jnp.int32)
+    cache_ok = (
+        (request[:, None, None] == owned[None, :, None])
+        & (jnp.arange(block, dtype=jnp.int32)[None, None, :] < cached[None, :, None])
+    ).reshape(count, slots)
     place = jnp.arange(count, dtype=jnp.int32)
     prev_ok = (split_flag == 1) & (request[:, None] == 0) & (place[None, :] >= count - prev_len)
     own_ok = (request[:, None] == request[None, :]) & (place[None, :] <= place[:, None])
@@ -121,16 +121,18 @@
     owner_a = (owner // SIDE, owner % SIDE)[first == "gz"]
     owner_b = (owner // SIDE, owner % SIDE)[second == "gz"]
     source = ((own_a - owner_a[askers]) % SIDE) * per_owner + (wanted % per_owner)[askers]
-    outgoing = jnp.take(held, source.reshape(-1), axis=0, mode="clip")
-    received = jnp.concatenate(
-        [outgoing[:slots]]
-        + [
-            ring_send(outgoing[step * slots:(step + 1) * slots], second, step)
-            for step in range(1, SIDE)
-        ]
-    )
-    pick = ((own_b - owner_b[me]) % SIDE) * slots + jnp.arange(slots)
-    return jnp.take(received, pick, axis=0, mode="clip")
+    pieces = [jnp.take(held, source[0], axis=0, mode="clip")] + [
+        ring_send(jnp.take(held, source[step], axis=0, mode="clip"), second, step)
+        for step in range(1, SIDE)
+    ]
+    came = (own_b - owner_b[me]) % SIDE
+    return pick_piece(came, pieces)
+
+
+def pick_piece(came, pieces):
+    which = came.reshape(came.shape + (1,) * (pieces[0].ndim - 1))
+    which = jnp.broadcast_to(which, pieces[0].shape)
+    return lax.select_n(which, *pieces)
 
 
 def route_with_adapters(blocks, adapters, block_wanted, adapter_wanted, first, second):
@@ -166,25 +168,17 @@
     source = jnp.concatenate(
         [block_items.reshape(SIDE, -1), adapter_items.reshape(SIDE, -1)], axis=1
     )
-    width = source.shape[1]
-    outgoing = jnp.take(held, source.reshape(-1), axis=0, mode="clip")
-    received = jnp.concatenate(
-        [outgoing[:width]]
-        + [
-            ring_send(outgoing[step * width:(step + 1) * width], second, step)
-            for step in range(1, SIDE)
-        ]
-    )
+    parts = [jnp.take(held, source[0], axis=0, mode="clip")] + [
+        ring_send(jnp.take(held, source[step], axis=0, mode="clip"), second, step)
+        for step in range(1, SIDE)
+    ]
     slots = block_wanted.shape[1]
-    slot = jnp.arange(slots)
-    block_pick = (
-        (((own_b - block_b[me]) % SIDE) * width + slot * pieces)[:, None] + quarter
-    ).reshape(-1)
-    adapter_pick = ((own_b - adapter_b[me]) % SIDE) * width + slots * pieces + slot
-    chosen_blocks = jnp.take(received, block_pick, axis=0, mode="clip").reshape(
-        slots, rows, lanes
-    )
-    chosen_adapters = jnp.take(received, adapter_pick, axis=0, mode="clip").reshape(slots, -1)
+    came = jnp.concatenate(
+        [jnp.repeat((own_b - block_b[me]) % SIDE, pieces), (own_b - adapter_b[me]) % SIDE]
+    )
+    merged = pick_piece(came, parts)
+    chosen_blocks = merged[: slots * adapters.shape[0]].reshape(slots, rows, lanes)
+    chosen_adapters = merged[slots * adapters.shape[0]:].reshape(slots, -1)
     chosen_adapters = chosen_adapters[:, : flat.shape[1]].reshape(slots, *adapters.shape[1:])
     return chosen_blocks, chosen_adapters
 

time: 187 us -> 219 us (1.17)
  waiting for transfers between devices: 52.4 us -> 72.8 us
  local copies, waits for them, and re-layouts: 39 us -> 54.1 us
  starting transfers between devices: 29 us -> 26.2 us
    ppermute x12, waiting for transfers between devices: 15.4 us -> 34.2 us  [ring_send(): lax.ppermute(value, axis, [(i, (i + step) % SIDE) for i in range(SIDE)])]
    unnamed x71 -> x61, local copies, waits for them, and re-layouts: 6.87 us -> 14.4 us
    concatenate x3 -> x0, other arithmetic: 7.21 us -> none  [the longest x1 3.02 us: route(): jnp.concatenate([outgoing[:slots]] + [ring_send(outgoing[step * slots:(st...]
    slice x2, local copies, waits for them, and re-layouts: 5.87 us -> 0.01 us  [route_with_adapters(): merged[:slots * adapters.shape[0]].reshape(slots, rows, lanes)]
    select_n x1 -> x7, other arithmetic: 0.01 us -> 5.86 us  [the longest x6 5.84 us: pick_piece(): return lax.select_n(which, *pieces)]
    gather x6 -> x8, local copies, waits for them, and re-layouts: 12.7 us -> 17.7 us  [the longest x3 8.97 us: route_with_adapters(): jnp.take(held, source[step], axis=0, mode='clip')]
    reduce_scatter x1, waiting for transfers between devices: 36.1 us -> 38.6 us  [on_device(): lax.psum_scatter(partial_out.astype(jnp.bfloat16), ('my', 'mc'), scatter_...]
    gather x5 -> x8, other arithmetic: 3.05 us -> 4.94 us  [the longest x3 2.46 us: route(): jnp.take(held, source[step], axis=0, mode='clip')]
  transfers between devices with their start and end apart: 16 -> 16, of which waited for: 5 -> 4; matrix products, arithmetic and copies ran while one was open for 34% -> 35% of each run, Pallas kernels for 0% -> 0%
where the time goes in v2:
time: 219 us; the launch traced here: 218 us
  waiting for transfers between devices  72.8 us (33%)
  local copies, waits for them, and re-layouts  54.1 us (25%)
  other arithmetic  27.2 us (12%)
  starting transfers between devices  26.2 us (12%)
  matrix products  21.5 us (10%)
  between operations  16.4 us (7%)
    reduce_scatter x1, waiting for transfers between devices, on_device(): lax.psum_scatter(partial_out.astype(jnp.bfloat16), ('my', 'mc'), scatter_...  38.6 us
    ppermute x12, waiting for transfers between devices, ring_send(): lax.ppermute(value, axis, [(i, (i + step) % SIDE) for i in range(SIDE)])  34.2 us
    ppermute x12, starting transfers between devices, ring_send(): lax.ppermute(value, axis, [(i, (i + step) % SIDE) for i in range(SIDE)])  17.9 us
    unnamed x61, local copies, waits for them, and re-layouts  14.4 us
    gather x3, local copies, waits for them, and re-layouts, route_with_adapters(): jnp.take(held, source[step], axis=0, mode='clip')  8.97 us
    dot_general x1, matrix products, on_device(): jnp.dot(normalized_input, query_weight, preferred_element_type=jnp.float32)  6.22 us
    select_n x6, other arithmetic, pick_piece(): return lax.select_n(which, *pieces)  5.84 us
    all_to_all x1, starting transfers between devices, on_device(): lax.all_to_all(jnp.broadcast_to(chosen_down, (model_count, *chosen_down.s...  4.49 us
  transfers between devices with their start and end apart: 16, of which 4 were waited for; matrix products, arithmetic and copies ran while one was open for 35% of the time, Pallas kernels for 0%

profile of v2, /device:TPU:0, one launch (start us, length us, event | category | flops | bytes accessed | tf_op | source)
XLA Modules:
  0.0 218.2 jit_solution(4112259055714260358)
XLA Ops:
  6.5 3.1 %collective-permute-start.1 = (bf16[2,256,256]{2,1,0:T(8,128)(2,1)}, bf16[2,256,256]{2,1,0:T(8,128)(2,1)}, u32[]{:S(2)}, u32[]{:S(2)}) collective-permute-start(bf16[2,256,256]{2,1,0:T(8,128)(2,1)} %param.31), channel_id=1, source_target_pairs={{0,64},{32,96},{64,0},{96,32},{1,65},{33,97},{65,1},{97,33},{2,66}... | collective-permute-start | bytes 786440 | tf_op jit(solution)/shard_map/ppermute | solution.py:109
  10.2 1.0 pad_maximum_fusion.1
  11.5 1.8 constant_dynamic-update-slice_fusion.5
  13.3 0.7 constant_dynamic-update-slice_fusion.4
  14.0 4.0 %collective-permute-start.9 = (bf16[3,256,256]{2,1,0:T(8,128)(2,1)}, bf16[3,256,256]{2,1,0:T(8,128)(2,1)S(1)}, u32[]{:S(2)}, u32[]{:S(2)}) collective-permute-start(bf16[3,256,256]{2,1,0:T(8,128)(2,1)} %get-tuple-element.27), channel_id=1, source_target_pairs={{0,24},{8,0},{16,8},{24,16},{1,25},{9,1},{17,9},{25,17},{2,26},{10... | collective-permute-start | bytes 1179656 | tf_op jit(solution)/shard_map/ppermute | solution.py:109
  18.1 1.3 collective-permute-start.7
  19.4 0.8 copy.54
  20.3 0.8 gather_fusion.6
  33.9 1.8 multiply_cosine_fusion
  35.7 1.4 pad_add_fusion
  38.3 1.8 constant_dynamic-update-slice_fusion.8
  40.1 1.8 constant_dynamic-update-slice_fusion.7
  41.9 0.8 constant_dynamic-update-slice_fusion.6
  42.7 3.0 %gather_fusion.14 = bf16[20,64,256]{2,1,0:T(8,128)(2,1)} fusion(bf16[48,64,256]{2,1,0:T(8,128)(2,1)} %bitcast.20, s32[1024]{0:T(1024)} %pad_clamp_fusion), kind=kCustom, calls=%fused_computation.14 | custom fusion | bytes 1310800 | tf_op jit(solution)/shard_map/jit(_take)/gather | solution.py:172
  45.7 3.1 %gather_fusion.13 = bf16[20,64,256]{2,1,0:T(8,128)(2,1)} fusion(bf16[48,64,256]{2,1,0:T(8,128)(2,1)} %bitcast.20, s32[1024]{0:T(1024)} %pad_clamp_fusion.1), kind=kCustom, calls=%fused_computation.13 | custom fusion | bytes 1310800 | tf_op jit(solution)/shard_map/jit(_take)/gather | solution.py:172
  48.8 2.9 %gather_fusion.12 = bf16[20,64,256]{2,1,0:T(8,128)(2,1)} fusion(bf16[48,64,256]{2,1,0:T(8,128)(2,1)} %bitcast.20, s32[1024]{0:T(1024)S(1)} %pad_clamp_fusion.2), kind=kCustom, calls=%fused_computation.12 | custom fusion | bytes 1310800 | tf_op jit(solution)/shard_map/jit(_take)/gather | solution.py:172
  51.7 4.0 %collective-permute-start.11 = (bf16[20,64,256]{2,1,0:T(8,128)(2,1)}, bf16[20,64,256]{2,1,0:T(8,128)(2,1)}, u32[]{:S(2)}, u32[]{:S(2)}) collective-permute-start(bf16[20,64,256]{2,1,0:T(8,128)(2,1)} %gather_fusion.13), channel_id=1, source_target_pairs={{0,64},{32,96},{64,0},{96,32},{1,65},{33,97},{65,1},{97,33},{2,66}... | collective-permute-start | bytes 1966088 | tf_op jit(solution)/shard_map/ppermute | solution.py:109
  56.3 1.3 pad_clamp_fusion.6
  57.5 1.2 pad_clamp_fusion.7
  59.4 1.0 constant_dynamic-update-slice_fusion.2
  60.4 1.0 constant_dynamic-update-slice_fusion.1
  61.4 28.1 %collective-permute-done.2 = bf16[2,256,256]{2,1,0:T(8,128)(2,1)S(1)} collective-permute-done((bf16[2,256,256]{2,1,0:T(8,128)(2,1)}, bf16[2,256,256]{2,1,0:T(8,128)(2,1)S(1)}, u32[]{:S(2)}, u32[]{:S(2)}) %collective-permute-start.2) | collective-permute-done | bytes 262176 | tf_op jit(solution)/shard_map/ppermute | solution.py:109
  89.5 1.5 gather_fusion.5
  90.9 1.5 gather_fusion.4
  92.5 1.4 gather_fusion.3
  93.9 1.2 collective-permute-start.3
  95.1 1.6 collective-permute-start.4
  96.7 2.9 %gather_fusion.11 = bf16[20,64,256]{2,1,0:T(8,128)(2,1)} fusion(bf16[48,64,256]{2,1,0:T(8,128)(2,1)} %bitcast.20, s32[1024]{0:T(1024)S(1)} %pad_clamp_fusion.3), kind=kCustom, calls=%fused_computation.11 | custom fusion | bytes 1310800 | tf_op jit(solution)/shard_map/jit(_take)/gather | solution.py:171
  99.6 1.5 collective-permute-start.5
  101.0 1.9 select_select_fusion
  103.1 0.8 slice.112
  103.9 1.7 reshape.450
  105.6 0.8 slice.113
  106.4 0.9 broadcast_in_dim.124
  107.3 4.5 %all-to-all-start = ((bf16[8,4,16,448]{3,2,1,0:T(8,128)(2,1)}), bf16[8,4,16,448]{3,2,1,0:T(8,128)(2,1)}, u32[]{:S(2)}, u32[]{:S(2)}) async-start(bf16[8,4,16,448]{3,2,1,0:T(8,128)(2,1)} %broadcast_in_dim.124), calls=%async_computation | async-start | bytes 1048576 | tf_op jit(solution)/shard_map/all_to_all | solution.py:216
  112.0 0.7 pad_clamp_fusion.9
  112.7 1.4 gather_fusion.2
  114.1 5.5 %collective-permute-done.3 = bf16[4,256,256]{2,1,0:T(8,128)(2,1)} collective-permute-done((bf16[4,256,256]{2,1,0:T(8,128)(2,1)}, bf16[4,256,256]{2,1,0:T(8,128)(2,1)}, u32[]{:S(2)}, u32[]{:S(2)}) %collective-permute-start.3) | collective-permute-done | bytes 524320 | tf_op jit(solution)/shard_map/ppermute | solution.py:109
  120.2 1.7 select_select_fusion.1
  121.9 1.0 copy.65
  123.0 1.3 copy.59
  124.9 3.0 %fusion.2 = f32[512]{0:T(512)S(1)} fusion(bf16[512,3584]{0,1:T(8,128)(2,1)} %all-gather.2.cloned.1.call-done), kind=kLoop, calls=%fused_computation.21 | loop fusion | flops 5504512 | bytes 3672064 | tf_op jit(solution)/shard_map/reduce_sum | solution.py:230
  128.1 1.6 fusion.4
  129.7 1.2 convolution_convert_fusion.1
  130.8 0.7 copy-done.2
  131.5 1.0 copy-done.21
  132.5 1.2 convolution_bitcast_fusion
  133.7 1.2 fusion.35
  134.9 0.9 copy.58
  135.7 0.9 pad_maximum_fusion
  136.6 3.6 %collective-permute-start.6 = (bf16[512,512]{0,1:T(8,128)(2,1)}, bf16[512,512]{0,1:T(8,128)(2,1)}, u32[]{:S(2)}, u32[]{:S(2)}) collective-permute-start(bf16[512,512]{0,1:T(8,128)(2,1)} %pad_maximum_fusion), channel_id=1, source_target_pairs={{0,8},{8,16},{16,24},{24,32},{32,40},{40,48},{48,56},{56,64},{64,7... | collective-permute-start | bytes 1572872 | tf_op jit(solution)/shard_map/ppermute | solution.py:16
  140.2 6.2 %fusion.84 = f32[512,512]{0,1:T(8,128)} fusion(bf16[512,3584]{0,1:T(8,128)(2,1)} %copy-done.2, bf16[3584,512]{1,0:T(8,128)(2,1)} %param.18), kind=kOutput, calls=%fused_computation.234 | convolution fusion | flops 1879048192 | bytes 8388608 | tf_op jit(solution)/shard_map/dot_general | solution.py:249
  146.5 3.3 %fusion.13 = f32[512,512]{0,1:T(8,128)S(1)} fusion(f32[512,512]{0,1:T(8,128)} %fusion.84, bf16[64,512]{1,0:T(8,128)(2,1)S(1)} %bitcast.128, bf16[512,64]{0,1:T(8,128)(2,1)S(1)} %bitcast.129, bf16[64,3584]{1,0:T(8,128)(2,1)S(1)} %dot_general.31, bf16[512,3584]{0,1:T(8,128)(2,1)} %copy-done.2), kind=kOutput, calls=%fused_computation.33 | convolution fusion | flops 269025280 | bytes 6356992 | tf_op jit(solution)/shard_map/dot_general | solution.py:243
  149.8 1.1 fusion.82
  150.9 2.1 copy.68
  153.0 2.1 copy.67
  155.1 2.3 %subtract_convert_fusion = (bf16[512,2,128]{2,0,1:T(8,128)(2,1)}, bf16[512,2,128]{2,0,1:T(8,128)(2,1)}) fusion(f32[512,2,128]{2,0,1:T(8,128)} %copy.68, f32[512,2,128]{2,0,1:T(8,128)} %copy.67, f32[512,128]{1,0:T(8,128)} %get-tuple-element.35, f32[512,128]{1,0:T(8,128)} %get-tuple-element.34), kind=kLoop, calls=%fused_computation.58 | loop fusion | flops 1048576 | bytes 2097152 | tf_op jit(solution)/shard_map/convert
  157.4 1.9 fusion.83
  159.2 1.8 copy.57
  161.0 3.0 %fusion.5 = (f32[2,512]{1,0:T(2,128)S(1)}, f32[2048,512,2]{1,0,2:T(8,128)S(1)}) fusion(pred[512,2048]{0,1:T(8,128)(4,1)S(1)} %copy-done.4, bf16[512,2,128]{2,0,1:T(8,128)(2,1)} %get-tuple-element.18, bf16[512,2,128]{2,0,1:T(8,128)(2,1)} %get-tuple-element.17, bf16[512,256]{1,0:T(8,128)(2,1)} %copy.58, bf16[512,256]{1,0:T(8,128)(2,1)} %copy.57, ...), kind=kOutput, calls=%fused_computation.24 | convolution fusion | flops 1084226560 | bytes 11014144 | tf_op jit(solution)/shard_map/tkrd,skd->krts/dot_general | solution.py:84
  164.0 2.0 fusion
  166.1 2.8 %divide_convert_fusion = bf16[512,1,2,256]{0,3,2,1:T(8,128)(2,1)S(1)} fusion(f32[2048,512,2]{1,0,2:T(8,128)S(1)} %get-tuple-element.49, f32[2,512]{1,0:T(2,128)S(1)} %get-tuple-element.48, pred[512,2048]{0,1:T(8,128)(4,1)S(1)} %copy-done.4, bf16[512,256]{0,1:T(8,128)(2,1)S(1)} %copy-done.11, bf16[512,256]{0,1:T(8,128)(2,1)S(1)} %copy-done.12, ...), kind=kOutput, calls=%fused_computation.49 | convolution fusion | flops 1085800448 | bytes 11018240 | tf_op jit(solution)/shard_map/krts,skd->tkrd/dot_general | solution.py:91
  168.9 3.9 %convolution_convert_fusion = bf16[512,3584]{0,1:T(8,128)(2,1)} fusion(bf16[512,512]{0,1:T(8,128)(2,1)S(1)} %bitcast.136, bf16[512,3584]{1,0:T(8,128)(2,1)S(1)} %copy-done.20), kind=kOutput, calls=%fused_computation.25 | convolution fusion | flops 1880883200 | bytes 7864320 | tf_op jit(solution)/shard_map/dot_general | solution.py:277
  172.8 38.6 %reduce-scatter.2.cloned.1.call-done = bf16[512,448]{0,1:T(8,128)(2,1)} async-done(((bf16[512,3584]{0,1:T(8,128)(2,1)}), bf16[512,448]{0,1:T(8,128)(2,1)}) %reduce-scatter.2.cloned.1.call-update) | async-done | bytes 458768 | tf_op jit(solution)/shard_map/reduce_scatter | solution.py:278
  (141 shorter events, 15.6 us)
Async XLA Ops:
  6.5 123.1 %copy-start = (bf16[3584,256]{1,0:T(8,128)(2,1)S(1)}, bf16[3584,256]{1,0:T(8,128)(2,1)}, u32[]{:S(2)}) copy-start(bf16[3584,256]{1,0:T(8,128)(2,1)} %param.20) | copy-start | bytes 5505028
  6.5 13.7 %copy-start.1 = (s32[64]{0:T(128)S(1)}, s32[64]{0:T(128)}, u32[]{:S(2)}) copy-start(s32[64]{0:T(128)} %param.25) | copy-start | bytes 772
  6.5 118.4 %all-gather.2.cloned.1.call-start = ((), (), s32[]{:S(2)}) async-start(), calls=%async_computation.2 | async-start | bytes 4128768 | tf_op jit(solution)/shard_map/all_gather | solution.py:227
  6.5 53.8 %collective-permute-start.1 = (bf16[2,256,256]{2,1,0:T(8,128)(2,1)}, bf16[2,256,256]{2,1,0:T(8,128)(2,1)}, u32[]{:S(2)}, u32[]{:S(2)}) collective-permute-start(bf16[2,256,256]{2,1,0:T(8,128)(2,1)} %param.31), channel_id=1, source_target_pairs={{0,64},{32,96},{64,0},{96,32},{1,65},{33,97},{65,1},{97,33},{2,66}... | collective-permute-start | bytes 786440 | tf_op jit(solution)/shard_map/ppermute | solution.py:109
  9.6 49.1 %collective-permute-start = (bf16[2,256,256]{2,1,0:T(8,128)(2,1)}, bf16[2,256,256]{2,1,0:T(8,128)(2,1)}, u32[]{:S(2)}, u32[]{:S(2)}) collective-permute-start(bf16[2,256,256]{2,1,0:T(8,128)(2,1)} %param.31), channel_id=1, source_target_pairs={{0,32},{32,64},{64,96},{96,0},{1,33},{33,65},{65,97},{97,1},{2,34}... | collective-permute-start | bytes 786440 | tf_op jit(solution)/shard_map/ppermute | solution.py:109
  14.0 27.9 %collective-permute-start.9 = (bf16[3,256,256]{2,1,0:T(8,128)(2,1)}, bf16[3,256,256]{2,1,0:T(8,128)(2,1)S(1)}, u32[]{:S(2)}, u32[]{:S(2)}) collective-permute-start(bf16[3,256,256]{2,1,0:T(8,128)(2,1)} %get-tuple-element.27), channel_id=1, source_target_pairs={{0,24},{8,0},{16,8},{24,16},{1,25},{9,1},{17,9},{25,17},{2,26},{10... | collective-permute-start | bytes 1179656 | tf_op jit(solution)/shard_map/ppermute | solution.py:109
  18.1 22.0 %collective-permute-start.8 = (bf16[3,256,256]{2,1,0:T(8,128)(2,1)}, bf16[3,256,256]{2,1,0:T(8,128)(2,1)}, u32[]{:S(2)}, u32[]{:S(2)}) collective-permute-start(bf16[3,256,256]{2,1,0:T(8,128)(2,1)} %get-tuple-element.27), channel_id=1, source_target_pairs={{0,16},{8,24},{16,0},{24,8},{1,17},{9,25},{17,1},{25,9},{2,18},{10... | collective-permute-start | bytes 1179656 | tf_op jit(solution)/shard_map/ppermute | solution.py:109
  18.1 20.2 %collective-permute-start.7 = (bf16[3,256,256]{2,1,0:T(8,128)(2,1)}, bf16[3,256,256]{2,1,0:T(8,128)(2,1)}, u32[]{:S(2)}, u32[]{:S(2)}) collective-permute-start(bf16[3,256,256]{2,1,0:T(8,128)(2,1)} %get-tuple-element.27), channel_id=1, source_target_pairs={{0,8},{8,16},{16,24},{24,0},{1,9},{9,17},{17,25},{25,1},{2,10},{10... | collective-permute-start | bytes 1179656 | tf_op jit(solution)/shard_map/ppermute | solution.py:109
  20.3 1.0 copy-start.15
  20.3 2.2 %copy-start.22 = (s32[16]{0:T(128)S(1)}, s32[16]{0:T(128)}, u32[]{:S(2)}) copy-start(s32[16]{0:T(128)} %param.27) | copy-start | bytes 196
  20.3 4.7 %copy-start.14 = (s32[16,4]{0,1:T(4,128)S(1)}, s32[16,4]{0,1:T(4,128)}, u32[]{:S(2)}) copy-start(s32[16,4]{0,1:T(4,128)} %param.29) | copy-start | bytes 772
  20.3 5.2 %copy-start.16 = (s32[16,4]{0,1:T(4,128)S(1)}, s32[16,4]{0,1:T(4,128)}, u32[]{:S(2)}) copy-start(s32[16,4]{0,1:T(4,128)} %param.28) | copy-start | bytes 772
  21.1 17.1 %copy-start.9 = (bf16[2,256,256]{2,1,0:T(8,128)(2,1)S(1)}, bf16[2,256,256]{2,1,0:T(8,128)(2,1)}, u32[]{:S(2)}) copy-start(bf16[2,256,256]{2,1,0:T(8,128)(2,1)} %param.31) | copy-start | bytes 786436
  29.8 7.8 %copy-start.17 = (f32[128]{0:T(128)}, f32[128]{0:T(128)S(1)}, u32[]{:S(2)}) copy-start(f32[128]{0:T(128)S(1)} %multiply_power_fusion) | copy-start | bytes 1540
  51.7 47.9 %collective-permute-start.10 = (bf16[20,64,256]{2,1,0:T(8,128)(2,1)}, bf16[20,64,256]{2,1,0:T(8,128)(2,1)S(1)}, u32[]{:S(2)}, u32[]{:S(2)}) collective-permute-start(bf16[20,64,256]{2,1,0:T(8,128)(2,1)} %gather_fusion.12), channel_id=1, source_target_pairs={{0,32},{32,64},{64,96},{96,0},{1,33},{33,65},{65,97},{97,1},{2,34}... | collective-permute-start | bytes 1966088 | tf_op jit(solution)/shard_map/ppermute | solution.py:109
  51.7 49.3 %collective-permute-start.11 = (bf16[20,64,256]{2,1,0:T(8,128)(2,1)}, bf16[20,64,256]{2,1,0:T(8,128)(2,1)}, u32[]{:S(2)}, u32[]{:S(2)}) collective-permute-start(bf16[20,64,256]{2,1,0:T(8,128)(2,1)} %gather_fusion.13), channel_id=1, source_target_pairs={{0,64},{32,96},{64,0},{96,32},{1,65},{33,97},{65,1},{97,33},{2,66}... | collective-permute-start | bytes 1966088 | tf_op jit(solution)/shard_map/ppermute | solution.py:109
  55.8 45.3 %collective-permute-start.12 = (bf16[20,64,256]{2,1,0:T(8,128)(2,1)}, bf16[20,64,256]{2,1,0:T(8,128)(2,1)}, u32[]{:S(2)}, u32[]{:S(2)}) collective-permute-start(bf16[20,64,256]{2,1,0:T(8,128)(2,1)} %gather_fusion.14), channel_id=1, source_target_pairs={{0,96},{32,0},{64,32},{96,64},{1,97},{33,1},{65,33},{97,65},{2,98}... | collective-permute-start | bytes 1966088 | tf_op jit(solution)/shard_map/ppermute | solution.py:109
  58.7 30.7 %collective-permute-start.2 = (bf16[2,256,256]{2,1,0:T(8,128)(2,1)}, bf16[2,256,256]{2,1,0:T(8,128)(2,1)S(1)}, u32[]{:S(2)}, u32[]{:S(2)}) collective-permute-start(bf16[2,256,256]{2,1,0:T(8,128)(2,1)} %param.31), channel_id=1, source_target_pairs={{0,96},{32,0},{64,32},{96,64},{1,97},{33,1},{65,33},{97,65},{2,98}... | collective-permute-start | bytes 786440 | tf_op jit(solution)/shard_map/ppermute | solution.py:109
  93.9 25.7 %collective-permute-start.3 = (bf16[4,256,256]{2,1,0:T(8,128)(2,1)}, bf16[4,256,256]{2,1,0:T(8,128)(2,1)}, u32[]{:S(2)}, u32[]{:S(2)}) collective-permute-start(bf16[4,256,256]{2,1,0:T(8,128)(2,1)} %gather_fusion.3), channel_id=1, source_target_pairs={{0,8},{8,16},{16,24},{24,0},{1,9},{9,17},{17,25},{25,1},{2,10},{10... | collective-permute-start | bytes 1572872 | tf_op jit(solution)/shard_map/ppermute | solution.py:109
  95.1 24.5 %collective-permute-start.4 = (bf16[4,256,256]{2,1,0:T(8,128)(2,1)}, bf16[4,256,256]{2,1,0:T(8,128)(2,1)}, u32[]{:S(2)}, u32[]{:S(2)}) collective-permute-start(bf16[4,256,256]{2,1,0:T(8,128)(2,1)} %gather_fusion.4), channel_id=1, source_target_pairs={{0,16},{8,24},{16,0},{24,8},{1,17},{9,25},{17,1},{25,9},{2,18},{10... | collective-permute-start | bytes 1572872 | tf_op jit(solution)/shard_map/ppermute | solution.py:109
  99.5 20.6 %copy-start.19 = (pred[4]{0:T(512)(128)(4,1)S(1)}, pred[4]{0:T(512)(128)(4,1)}, u32[]{:S(2)}) copy-start(pred[4]{0:T(512)(128)(4,1)} %get-tuple-element.8) | copy-start | bytes 16
  99.5 1.5 copy-start.6
  99.6 20.6 %collective-permute-start.5 = (bf16[4,256,256]{2,1,0:T(8,128)(2,1)}, bf16[4,256,256]{2,1,0:T(8,128)(2,1)}, u32[]{:S(2)}, u32[]{:S(2)}) collective-permute-start(bf16[4,256,256]{2,1,0:T(8,128)(2,1)} %gather_fusion.5), channel_id=1, source_target_pairs={{0,24},{8,0},{16,8},{24,16},{1,25},{9,1},{17,9},{25,17},{2,26},{10... | collective-permute-start | bytes 1572872 | tf_op jit(solution)/shard_map/ppermute | solution.py:109
  102.9 19.9 %copy-start.5 = (bf16[20,64,256]{2,1,0:T(8,128)(2,1)}, bf16[20,64,256]{2,1,0:T(8,128)(2,1)S(1)}, u32[]{:S(2)}) copy-start(bf16[20,64,256]{2,1,0:T(8,128)(2,1)S(1)} %select_select_fusion) | copy-start | bytes 1966084
  107.3 15.7 %all-to-all-start = ((bf16[8,4,16,448]{3,2,1,0:T(8,128)(2,1)}), bf16[8,4,16,448]{3,2,1,0:T(8,128)(2,1)}, u32[]{:S(2)}, u32[]{:S(2)}) async-start(bf16[8,4,16,448]{3,2,1,0:T(8,128)(2,1)} %broadcast_in_dim.124), calls=%async_computation | async-start | bytes 1048576 | tf_op jit(solution)/shard_map/all_to_all | solution.py:216
  111.8 99.6 %reduce-scatter.2.cloned.1.call-start = ((), (), s32[]{:S(2)}) async-start(), calls=%async_computation.3 | async-start | bytes 4128768 | tf_op jit(solution)/shard_map/reduce_scatter | solution.py:278
  114.1 8.8 %copy-start.8 = (bf16[4,16,960]{2,1,0:T(8,128)(2,1)S(1)}, bf16[4,16,960]{2,1,0:T(8,128)(2,1)}, u32[]{:S(2)}) copy-start(bf16[4,16,960]{2,1,0:T(8,128)(2,1)} %reshape.450) | copy-start | bytes 368644
  122.9 5.1 %copy-start.13 = (f32[3584]{0:T(1024)S(1)}, f32[3584]{0:T(1024)}, u32[]{:S(2)}) copy-start(f32[3584]{0:T(1024)} %param.17) | copy-start | bytes 43012
  124.9 3.1 %copy-start.3 = (bf16[512,3584]{0,1:T(8,128)(2,1)S(1)}, bf16[512,3584]{0,1:T(8,128)(2,1)}, u32[]{:S(2)}) copy-start(bf16[512,3584]{0,1:T(8,128)(2,1)} %all-gather.2.cloned.1.call-done) | copy-start | bytes 11010052
  129.7 1.9 copy-start.2
  129.7 2.8 %copy-start.21 = (bf16[3584,256]{1,0:T(8,128)(2,1)S(1)}, bf16[3584,256]{1,0:T(8,128)(2,1)}, u32[]{:S(2)}) copy-start(bf16[3584,256]{1,0:T(8,128)(2,1)} %param.19) | copy-start | bytes 5505028
  132.5 3.2 %copy-start.10 = (bf16[512,256]{0,1:T(8,128)(2,1)}, bf16[512,256]{0,1:T(8,128)(2,1)S(1)}, u32[]{:S(2)}) copy-start(bf16[512,256]{0,1:T(8,128)(2,1)S(1)} %convolution_convert_fusion.1) | copy-start | bytes 786436
  132.5 1.2 copy-start.18
  136.6 20.7 %collective-permute-start.6 = (bf16[512,512]{0,1:T(8,128)(2,1)}, bf16[512,512]{0,1:T(8,128)(2,1)}, u32[]{:S(2)}, u32[]{:S(2)}) collective-permute-start(bf16[512,512]{0,1:T(8,128)(2,1)} %pad_maximum_fusion), channel_id=1, source_target_pairs={{0,8},{8,16},{16,24},{24,32},{32,40},{40,48},{48,56},{56,64},{64,7... | collective-permute-start | bytes 1572872 | tf_op jit(solution)/shard_map/ppermute | solution.py:16
  149.8 11.2 %slice-start = ((bf16[20,64,256]{2,1,0:T(8,128)(2,1)}), bf16[16,64,256]{2,1,0:T(8,128)(2,1)S(1)}, s32[]{:S(2)}) async-start(bf16[20,64,256]{2,1,0:T(8,128)(2,1)} %copy-done.5), calls=%async_computation.4 | async-start | bytes 1048576 | tf_op jit(solution)/shard_map/slice | solution.py:180
  150.9 10.1 %copy-start.4 = (pred[512,2048]{0,1:T(8,128)(4,1)S(1)}, pred[512,2048]{0,1:T(8,128)(4,1)}, u32[]{:S(2)}) copy-start(pred[512,2048]{0,1:T(8,128)(4,1)} %pad_add_fusion) | copy-start | bytes 3145732
  164.0 2.0 copy-start.7
  164.0 2.0 copy-start.11
  164.0 2.0 copy-start.12
  166.1 2.8 %copy-start.20 = (bf16[512,3584]{1,0:T(8,128)(2,1)S(1)}, bf16[512,3584]{1,0:T(8,128)(2,1)}, u32[]{:S(2)}) copy-start(bf16[512,3584]{1,0:T(8,128)(2,1)} %param.21) | copy-start | bytes 11010052
Sparse Core Ops, SparseCore 0:
  19.5 30.2 all-gather.1
  172.9 38.4 reduce-scatter.1

commit v3 on v1

--- a/solution.py
+++ b/solution.py
@@ -109,12 +109,14 @@
     return lax.ppermute(value, axis, [(i, (i + step) % SIDE) for i in range(SIDE)])
 
 
-def route(local, wanted, first, second):
+def ring_collect(local, first):
+    return jnp.concatenate([local] + [ring_send(local, first, step) for step in range(1, SIDE)])
+
+
+def route(held, per_owner, wanted, first, second):
     coords = {"gx": lax.axis_index("gx"), "gz": lax.axis_index("gz")}
     own_a, own_b = coords[first], coords[second]
-    per_owner = local.shape[0]
     slots = wanted.shape[1]
-    held = jnp.concatenate([local] + [ring_send(local, first, step) for step in range(1, SIDE)])
     me = group_of(first, own_a, own_b)
     askers = group_of(first, own_a, (own_b + jnp.arange(SIDE)) % SIDE)
     owner = wanted // per_owner
@@ -133,17 +135,22 @@
     return jnp.take(received, pick, axis=0, mode="clip")
 
 
-def route_with_adapters(blocks, adapters, block_wanted, adapter_wanted, first, second):
+def pack_with_adapters(blocks, adapters):
+    rows, lanes = blocks.shape[1], blocks.shape[2]
+    pieces = adapters.shape[0]
+    flat = adapters.reshape(pieces, -1)
+    padded = jnp.pad(flat, ((0, 0), (0, (rows // pieces) * lanes - flat.shape[1])))
+    return jnp.concatenate([blocks, padded.reshape(1, rows, lanes)])
+
+
+def route_with_adapters(held, blocks, adapters, block_wanted, adapter_wanted, first, second):
     coords = {"gx": lax.axis_index("gx"), "gz": lax.axis_index("gz")}
     own_a, own_b = coords[first], coords[second]
     rows, lanes = blocks.shape[1], blocks.shape[2]
     pieces = adapters.shape[0]
     tile = rows // pieces
     flat = adapters.reshape(pieces, -1)
-    padded = jnp.pad(flat, ((0, 0), (0, tile * lanes - flat.shape[1])))
-    local = jnp.concatenate([blocks, padded.reshape(1, rows, lanes)])
-    per_block = local.shape[0]
-    held = jnp.concatenate([local] + [ring_send(local, first, step) for step in range(1, SIDE)])
+    per_block = blocks.shape[0] + 1
     held = held.reshape(-1, tile, lanes)
     me = group_of(first, own_a, own_b)
     askers = group_of(first, own_a, (own_b + jnp.arange(SIDE)) % SIDE)
@@ -212,10 +219,16 @@
     wanted = adapter_row_index[request_adapter]
     down_width = adapter_down_rows.shape[2]
     adapters = jnp.concatenate([adapter_down_rows, adapter_up_query], axis=2)
+    held_keys = ring_collect(pack_with_adapters(cached_rotated_keys, adapters), "gz")
+    held_values = ring_collect(cached_value_rows, "gx")
+    whole = lax.all_gather(stream, ("my", "mc"), axis=1, tiled=True)
+    held_keys, held_values, whole = lax.optimization_barrier((held_keys, held_values, whole))
     cache_keys, chosen = route_with_adapters(
-        cached_rotated_keys, adapters, request_cache_block, wanted, "gz", "gx"
-    )
-    cache_values = route(cached_value_rows, request_cache_block, "gx", "gz")
+        held_keys, cached_rotated_keys, adapters, request_cache_block, wanted, "gz", "gx"
+    )
+    cache_values = route(
+        held_values, cached_value_rows.shape[0], request_cache_block, "gx", "gz"
+    )
     chosen_down = chosen[:, :, :down_width]
     chosen_up = chosen[:, :, down_width:]
     model_count = lax.axis_size(("my", "mc"))
@@ -230,7 +243,6 @@
         *chosen_down.shape[:2], model_count * down_width
     )
 
-    whole = lax.all_gather(stream, ("my", "mc"), axis=1, tiled=True)
     wide = whole.astype(jnp.float32)
     normalized_input = (
         wide * lax.rsqrt(jnp.mean(wide * wide, axis=1, keepdims=True) + 1e-06) * prenorm_gain

time: 187 us -> 190 us (1.016)
  starting transfers between devices: 29 us -> 34.2 us
  other arithmetic: 28.9 us -> 23.8 us
  local copies, waits for them, and re-layouts: 39 us -> 43.3 us
    ppermute x12, starting transfers between devices: 19.7 us -> 26.2 us  [ring_send(): lax.ppermute(value, axis, [(i, (i + step) % SIDE) for i in range(SIDE)])]
    unnamed x71 -> x53, local copies, waits for them, and re-layouts: 6.87 us -> 8.67 us
  transfers between devices with their start and end apart: 16 -> 16, of which waited for: 5 -> 4; matrix products, arithmetic and copies ran while one was open for 34% -> 28% of each run, Pallas kernels for 0% -> 0%
where the time goes in v3:
time: 190 us; the launch traced here: 189 us
  waiting for transfers between devices  51.3 us (27%)
  local copies, waits for them, and re-layouts  43.3 us (23%)
  starting transfers between devices  34.2 us (18%)
  other arithmetic  23.8 us (13%)
  matrix products  19.8 us (10%)
  between operations  16.5 us (9%)
    reduce_scatter x1, waiting for transfers between devices, on_device(): lax.psum_scatter(partial_out.astype(jnp.bfloat16), ('my', 'mc'), scatter_...  36.9 us
    ppermute x12, starting transfers between devices, ring_send(): lax.ppermute(value, axis, [(i, (i + step) % SIDE) for i in range(SIDE)])  26.2 us
    ppermute x12, waiting for transfers between devices, ring_send(): lax.ppermute(value, axis, [(i, (i + step) % SIDE) for i in range(SIDE)])  13.5 us
    unnamed x53, local copies, waits for them, and re-layouts  8.67 us
    ppermute x1, starting transfers between devices, shifted(): lax.ppermute(value, axis, [(source, source + steps) for source in range(f...  4.43 us
    dot_general x1, matrix products, on_device(): jnp.dot(normalized_input, query_weight, preferred_element_type=jnp.float32)  4.13 us
    dot_general x1, matrix products, on_device(): jnp.dot(attended, output_weight, preferred_element_type=jnp.float32)  3.9 us
    gather x1, local copies, waits for them, and re-layouts, route_with_adapters(): outgoing = jnp.take(held, source.reshape(-1), axis=0, mode='clip')  3.83 us
  transfers between devices with their start and end apart: 16, of which 4 were waited for; matrix products, arithmetic and copies ran while one was open for 28% of the time, Pallas kernels for 0%

profile of v3, /device:TPU:0, one launch (start us, length us, event | category | flops | bytes accessed | tf_op | source)
XLA Modules:
  0.0 189.0 jit_solution(13914129203006710467)
XLA Ops:
  6.6 3.2 %collective-permute-start.4 = (bf16[2,256,256]{2,1,0:T(8,128)(2,1)}, bf16[2,256,256]{2,1,0:T(8,128)(2,1)S(1)}, u32[]{:S(2)}, u32[]{:S(2)}) collective-permute-start(bf16[2,256,256]{2,1,0:T(8,128)(2,1)} %param.31), channel_id=1, source_target_pairs={{0,64},{32,96},{64,0},{96,32},{1,65},{33,97},{65,1},{97,33},{2,66}... | collective-permute-start | bytes 786440 | tf_op jit(solution)/shard_map/ppermute | solution.py:109
  9.8 0.6 collective-permute-start.3
  10.4 2.6 %collective-permute-start.5 = (bf16[2,256,256]{2,1,0:T(8,128)(2,1)}, bf16[2,256,256]{2,1,0:T(8,128)(2,1)}, u32[]{:S(2)}, u32[]{:S(2)}) collective-permute-start(bf16[2,256,256]{2,1,0:T(8,128)(2,1)} %param.31), channel_id=1, source_target_pairs={{0,96},{32,0},{64,32},{96,64},{1,97},{33,1},{65,33},{97,65},{2,98}... | collective-permute-start | bytes 786440 | tf_op jit(solution)/shard_map/ppermute | solution.py:109
  13.0 1.0 pad_maximum_fusion.4
  14.3 1.8 constant_dynamic-update-slice_fusion.1
  16.1 0.7 constant_dynamic-update-slice_fusion
  16.8 3.9 %collective-permute-start.1 = (bf16[3,256,256]{2,1,0:T(8,128)(2,1)}, bf16[3,256,256]{2,1,0:T(8,128)(2,1)}, u32[]{:S(2)}, u32[]{:S(2)}) collective-permute-start(bf16[3,256,256]{2,1,0:T(8,128)(2,1)} %get-tuple-element.39), channel_id=1, source_target_pairs={{0,16},{8,24},{16,0},{24,8},{1,17},{9,25},{17,1},{25,9},{2,18},{10... | collective-permute-start | bytes 1179656 | tf_op jit(solution)/shard_map/ppermute | solution.py:109
  20.7 1.0 collective-permute-start
  21.8 0.7 constant_dynamic-slice_fusion.8
  26.3 0.8 gather_fusion.6
  27.8 0.6 gather_fusion.5
  29.7 0.6 gather_fusion.4
  31.3 0.6 fusion.105
  31.9 2.5 %compare_select_fusion.2 = s32[1024,1]{0,1:T(1,128)S(1)} fusion(s32[]{:T(128)} %bitcast.14, s32[]{:T(128)} %bitcast.15, s32[]{:T(128)} %bitcast.17, s32[]{:T(128)} %bitcast.16), kind=kLoop, calls=%fused_computation.75 | loop fusion | flops 17408 | bytes 4112 | tf_op jit(solution)/shard_map/gather | solution.py:77
  35.1 1.0 multiply_cosine_fusion
  36.1 0.8 compare_and_fusion
  36.9 1.4 pad_add_fusion
  38.5 2.3 %collective-permute-start.2 = (bf16[3,256,256]{2,1,0:T(8,128)(2,1)}, bf16[3,256,256]{2,1,0:T(8,128)(2,1)S(1)}, u32[]{:S(2)}, u32[]{:S(2)}) collective-permute-start(bf16[3,256,256]{2,1,0:T(8,128)(2,1)} %get-tuple-element.39), channel_id=1, source_target_pairs={{0,24},{8,0},{16,8},{24,16},{1,25},{9,1},{17,9},{25,17},{2,26},{10... | collective-permute-start | bytes 1179656 | tf_op jit(solution)/shard_map/ppermute | solution.py:109
  40.8 0.7 copy-done.13
  41.5 1.4 pad_maximum_fusion.2
  42.9 1.8 constant_dynamic-update-slice_fusion.4
  44.7 1.8 constant_dynamic-update-slice_fusion.3
  46.5 1.8 collective-permute-done.2
  48.2 0.8 constant_dynamic-update-slice_fusion.2
  49.0 0.9 all-gather.2.cloned.1.call-done
  49.9 3.0 %fusion.2 = f32[512]{0:T(512)S(1)} fusion(bf16[512,3584]{0,1:T(8,128)(2,1)} %all-gather.2.cloned.1.call-done), kind=kLoop, calls=%fused_computation.18 | loop fusion | flops 5504512 | bytes 3672064 | tf_op jit(solution)/shard_map/reduce_sum | solution.py:248
  53.1 1.6 fusion.4
  54.7 1.9 convolution_convert_fusion.1
  56.6 0.9 copy-done.20
  57.5 1.2 convolution_bitcast_fusion
  58.7 3.8 %gather_fusion.9 = bf16[80,64,256]{2,1,0:T(8,128)(2,1)} fusion(bf16[48,64,256]{2,1,0:T(8,128)(2,1)} %bitcast.19, s32[1024]{0:T(1024)S(1)} %pad_clamp_fusion.2), kind=kCustom, calls=%fused_computation.9 | custom fusion | bytes 5243200 | tf_op jit(solution)/shard_map/jit(_take)/gather | solution.py:177
  62.5 3.1 %fusion.101 = (bf16[20,64,256]{2,1,0:T(8,128)(2,1)S(1)}, bf16[20,64,256]{2,1,0:T(8,128)(2,1)}, bf16[20,64,256]{2,1,0:T(8,128)(2,1)}, bf16[20,64,256]{2,1,0:T(8,128)(2,1)}) fusion(bf16[80,64,256]{2,1,0:T(8,128)(2,1)} %gather_fusion.9), kind=kLoop, calls=%fused_computation.238 | loop fusion | bytes 5242880 | tf_op jit(solution)/shard_map/slice | solution.py:179
  65.6 3.0 %collective-permute-start.11 = (bf16[20,64,256]{2,1,0:T(8,128)(2,1)}, bf16[20,64,256]{2,1,0:T(8,128)(2,1)}, u32[]{:S(2)}, u32[]{:S(2)}) collective-permute-start(bf16[20,64,256]{2,1,0:T(8,128)(2,1)} %get-tuple-element.22), channel_id=1, source_target_pairs={{0,64},{32,96},{64,0},{96,32},{1,65},{33,97},{65,1},{97,33},{2,66}... | collective-permute-start | bytes 1966088 | tf_op jit(solution)/shard_map/ppermute | solution.py:109
  68.6 0.6 collective-permute-start.10
  69.2 1.2 fusion.35
  70.4 0.9 pad_maximum_fusion.3
  71.2 4.4 %collective-permute-start.9 = (bf16[512,512]{0,1:T(8,128)(2,1)}, bf16[512,512]{0,1:T(8,128)(2,1)}, u32[]{:S(2)}, u32[]{:S(2)}) collective-permute-start(bf16[512,512]{0,1:T(8,128)(2,1)} %pad_maximum_fusion.3), channel_id=1, source_target_pairs={{0,8},{8,16},{16,24},{24,32},{32,40},{40,48},{48,56},{56,64},{64,7... | collective-permute-start | bytes 1572872 | tf_op jit(solution)/shard_map/ppermute | solution.py:16
  75.7 1.9 %collective-permute-start.12 = (bf16[20,64,256]{2,1,0:T(8,128)(2,1)}, bf16[20,64,256]{2,1,0:T(8,128)(2,1)}, u32[]{:S(2)}, u32[]{:S(2)}) collective-permute-start(bf16[20,64,256]{2,1,0:T(8,128)(2,1)} %get-tuple-element.24), channel_id=1, source_target_pairs={{0,96},{32,0},{64,32},{96,64},{1,97},{33,1},{65,33},{97,65},{2,98}... | collective-permute-start | bytes 1966088 | tf_op jit(solution)/shard_map/ppermute | solution.py:109
  77.6 2.0 %gather_fusion.2 = bf16[16,256,256]{2,1,0:T(8,128)(2,1)} fusion(bf16[8,256,256]{2,1,0:T(8,128)(2,1)S(1)} %pad_maximum_fusion.2, s32[1024]{0:T(1024)S(1)} %pad_clamp_fusion.6), kind=kCustom, calls=%fused_computation.2 | custom fusion | bytes 4194368 | tf_op jit(solution)/shard_map/jit(_take)/gather | solution.py:126
  79.6 2.9 %fusion.102 = (bf16[4,256,256]{2,1,0:T(8,128)(2,1)S(1)}, bf16[4,256,256]{2,1,0:T(8,128)(2,1)}, bf16[4,256,256]{2,1,0:T(8,128)(2,1)}, bf16[4,256,256]{2,1,0:T(8,128)(2,1)}) fusion(bf16[16,256,256]{2,1,0:T(8,128)(2,1)} %gather_fusion.2), kind=kLoop, calls=%fused_computation.239 | loop fusion | bytes 4194304 | tf_op jit(solution)/shard_map/slice | solution.py:128
  82.5 2.9 %collective-permute-start.7 = (bf16[4,256,256]{2,1,0:T(8,128)(2,1)}, bf16[4,256,256]{2,1,0:T(8,128)(2,1)}, u32[]{:S(2)}, u32[]{:S(2)}) collective-permute-start(bf16[4,256,256]{2,1,0:T(8,128)(2,1)} %get-tuple-element.26), channel_id=1, source_target_pairs={{0,16},{8,24},{16,0},{24,8},{1,17},{9,25},{17,1},{25,9},{2,18},{10... | collective-permute-start | bytes 1572872 | tf_op jit(solution)/shard_map/ppermute | solution.py:109
  85.3 1.3 collective-permute-start.6
  86.6 11.7 %collective-permute-done.10 = bf16[20,64,256]{2,1,0:T(8,128)(2,1)} collective-permute-done((bf16[20,64,256]{2,1,0:T(8,128)(2,1)}, bf16[20,64,256]{2,1,0:T(8,128)(2,1)}, u32[]{:S(2)}, u32[]{:S(2)}) %collective-permute-start.10) | collective-permute-done | bytes 655392 | tf_op jit(solution)/shard_map/ppermute | solution.py:109
  98.4 2.9 %collective-permute-start.8 = (bf16[4,256,256]{2,1,0:T(8,128)(2,1)}, bf16[4,256,256]{2,1,0:T(8,128)(2,1)}, u32[]{:S(2)}, u32[]{:S(2)}) collective-permute-start(bf16[4,256,256]{2,1,0:T(8,128)(2,1)} %get-tuple-element.28), channel_id=1, source_target_pairs={{0,24},{8,0},{16,8},{24,16},{1,25},{9,1},{17,9},{25,17},{2,26},{10... | collective-permute-start | bytes 1572872 | tf_op jit(solution)/shard_map/ppermute | solution.py:109
  101.3 4.1 %fusion.106 = f32[512,512]{0,1:T(8,128)S(1)} fusion(bf16[512,3584]{0,1:T(8,128)(2,1)S(1)} %copy-done.4, bf16[3584,512]{1,0:T(8,128)(2,1)} %param.18), kind=kOutput, calls=%fused_computation.243 | convolution fusion | flops 1879048192 | bytes 8388608 | tf_op jit(solution)/shard_map/dot_general | solution.py:267
  105.5 0.8 copy.58
  106.3 2.8 %pad_maximum_fusion = bf16[80,64,256]{2,1,0:T(8,128)(2,1)} fusion(bf16[20,64,256]{2,1,0:T(8,128)(2,1)} %collective-permute-done.12, bf16[20,64,256]{2,1,0:T(8,128)(2,1)} %collective-permute-done.11, bf16[20,64,256]{2,1,0:T(8,128)(2,1)} %collective-permute-done.10, bf16[20,64,256]{2,1,0:T(8,128)(2,1)S(1)} %get-tuple-element.21), kind=kLoop, calls=%fused_computation.27 | loop fusion | flops 3932160 | bytes 5242880 | tf_op jit(solution)/shard_map/concatenate | solution.py:178
  109.2 2.3 %gather_fusion.11 = bf16[4,64,256]{2,1,0:T(8,128)(2,1)S(1)} fusion(bf16[80,64,256]{2,1,0:T(8,128)(2,1)} %pad_maximum_fusion, s32[1024]{0:T(1024)S(1)} %get-tuple-element.57), kind=kCustom, calls=%fused_computation.11 | custom fusion | bytes 262160 | tf_op jit(solution)/shard_map/jit(_take)/gather | solution.py:194
  111.8 0.8 broadcast_in_dim.36
  112.7 3.5 %all-to-all-start = ((bf16[8,4,16,448]{3,2,1,0:T(8,128)(2,1)}), bf16[8,4,16,448]{3,2,1,0:T(8,128)(2,1)S(1)}, u32[]{:S(2)}, u32[]{:S(2)}) async-start(bf16[8,4,16,448]{3,2,1,0:T(8,128)(2,1)} %broadcast_in_dim.36), calls=%async_computation | async-start | bytes 1048576 | tf_op jit(solution)/shard_map/all_to_all | solution.py:235
  116.2 1.8 fusion.104
  118.0 0.8 copy.57
  118.8 3.0 %pad_maximum_fusion.1 = bf16[16,256,256]{2,1,0:T(8,128)(2,1)} fusion(bf16[4,256,256]{2,1,0:T(8,128)(2,1)} %collective-permute-done.8, bf16[4,256,256]{2,1,0:T(8,128)(2,1)} %collective-permute-done.7, bf16[4,256,256]{2,1,0:T(8,128)(2,1)} %collective-permute-done.6, bf16[4,256,256]{2,1,0:T(8,128)(2,1)S(1)} %get-tuple-element.25), kind=kLoop, calls=%fused_computation.28 | loop fusion | flops 3145728 | bytes 4194304 | tf_op jit(solution)/shard_map/concatenate | solution.py:127
  121.8 2.2 %gather_fusion.3 = bf16[4,256,256]{2,1,0:T(8,128)(2,1)S(1)} fusion(bf16[16,256,256]{2,1,0:T(8,128)(2,1)} %pad_maximum_fusion.1, s32[1024]{0:T(1024)S(1)} %pad_clamp_fusion.5), kind=kCustom, calls=%fused_computation.3 | custom fusion | bytes 1048592 | tf_op jit(solution)/shard_map/jit(_take)/gather | solution.py:135
  124.0 1.0 copy.65
  125.1 3.1 %gather_fusion.10 = bf16[16,64,256]{2,1,0:T(8,128)(2,1)} fusion(bf16[80,64,256]{2,1,0:T(8,128)(2,1)} %pad_maximum_fusion, s32[1024]{0:T(1024)S(1)} %get-tuple-element.58), kind=kCustom, calls=%fused_computation.10 | custom fusion | bytes 1048640 | tf_op jit(solution)/shard_map/jit(_take)/gather | solution.py:191
  128.5 0.6 dot_general.31
  129.1 3.1 %fusion.13 = f32[512,512]{0,1:T(8,128)S(1)} fusion(f32[512,512]{0,1:T(8,128)S(1)} %fusion.106, bf16[64,512]{1,0:T(8,128)(2,1)S(1)} %bitcast.117, bf16[512,64]{0,1:T(8,128)(2,1)S(1)} %bitcast.118, bf16[64,3584]{1,0:T(8,128)(2,1)S(1)} %dot_general.31, bf16[512,3584]{0,1:T(8,128)(2,1)} %copy-done.3), kind=kOutput, calls=%fused_computation.32 | convolution fusion | flops 269025280 | bytes 6356992 | tf_op jit(solution)/shard_map/dot_general | solution.py:261
  132.8 0.7 copy-done.6
  133.5 2.9 %fusion.5 = (f32[2,512]{1,0:T(2,128)S(1)}, f32[2048,512,2]{1,0,2:T(8,128)S(1)}) fusion(pred[512,2048]{0,1:T(8,128)(4,1)S(1)} %copy-done.6, bf16[512,2,128]{2,0,1:T(8,128)(2,1)S(1)} %get-tuple-element.30, bf16[512,2,128]{2,0,1:T(8,128)(2,1)S(1)} %get-tuple-element.29, bf16[512,256]{1,0:T(8,128)(2,1)S(1)} %copy-done.8, bf16[512,256]{1,0:T(8,128)(2,1)} %copy.57, ...), kind=kOutput, calls=%fused_computation.21 | convolution fusion | flops 1084226560 | bytes 11014144 | tf_op jit(solution)/shard_map/tkrd,skd->krts/dot_general | solution.py:84
  136.5 2.0 %fusion = f32[2,512]{1,0:T(2,128)S(1)} fusion(f32[2048,512,2]{1,0,2:T(8,128)S(1)} %get-tuple-element.53, f32[2,512]{1,0:T(2,128)S(1)} %get-tuple-element.52, pred[512,2048]{0,1:T(8,128)(4,1)S(1)} %copy-done.6), kind=kLoop, calls=%fused_computation.16 | loop fusion | flops 8387584 | bytes 9445376 | tf_op jit(solution)/shard_map/reduce_sum | solution.py:90
  138.5 2.8 %divide_convert_fusion = bf16[512,1,2,256]{0,3,2,1:T(8,128)(2,1)S(1)} fusion(f32[2048,512,2]{1,0,2:T(8,128)S(1)} %get-tuple-element.53, f32[2,512]{1,0:T(2,128)S(1)} %get-tuple-element.52, pred[512,2048]{0,1:T(8,128)(4,1)S(1)} %copy-done.6, bf16[512,256]{0,1:T(8,128)(2,1)S(1)} %copy-done.10, bf16[512,256]{0,1:T(8,128)(2,1)S(1)} %copy-done.11, ...), kind=kOutput, calls=%fused_computation.49 | convolution fusion | flops 1085800448 | bytes 11018240 | tf_op jit(solution)/shard_map/krts,skd->tkrd/dot_general | solution.py:91
  141.3 3.9 %convolution_convert_fusion = bf16[512,3584]{0,1:T(8,128)(2,1)} fusion(bf16[512,512]{0,1:T(8,128)(2,1)S(1)} %bitcast.124, bf16[512,3584]{1,0:T(8,128)(2,1)S(1)} %copy-done.19), kind=kOutput, calls=%fused_computation.22 | convolution fusion | flops 1880883200 | bytes 7864320 | tf_op jit(solution)/shard_map/dot_general | solution.py:295
  145.2 36.9 %reduce-scatter.2.cloned.1.call-done = bf16[512,448]{0,1:T(8,128)(2,1)} async-done(((bf16[512,3584]{0,1:T(8,128)(2,1)}), bf16[512,448]{0,1:T(8,128)(2,1)}) %reduce-scatter.2.cloned.1.call-update) | async-done | bytes 458768 | tf_op jit(solution)/shard_map/reduce_scatter | solution.py:296
  (127 shorter events, 7.3 us)
Async XLA Ops:
  6.5 48.1 %copy-start = (bf16[3584,256]{1,0:T(8,128)(2,1)S(1)}, bf16[3584,256]{1,0:T(8,128)(2,1)}, u32[]{:S(2)}) copy-start(bf16[3584,256]{1,0:T(8,128)(2,1)} %param.20) | copy-start | bytes 5505028
  6.5 15.2 %copy-start.18 = (s32[16,4]{0,1:T(4,128)S(1)}, s32[16,4]{0,1:T(4,128)}, u32[]{:S(2)}) copy-start(s32[16,4]{0,1:T(4,128)} %param.26) | copy-start | bytes 772
  6.5 16.6 %copy-start.21 = (s32[16]{0:T(128)S(1)}, s32[16]{0:T(128)}, u32[]{:S(2)}) copy-start(s32[16]{0:T(128)} %param.27) | copy-start | bytes 196
  6.5 19.0 %copy-start.17 = (s32[16,4]{0,1:T(4,128)S(1)}, s32[16,4]{0,1:T(4,128)}, u32[]{:S(2)}) copy-start(s32[16,4]{0,1:T(4,128)} %param.29) | copy-start | bytes 772
  6.5 19.5 %copy-start.15 = (s32[16,4]{0,1:T(4,128)S(1)}, s32[16,4]{0,1:T(4,128)}, u32[]{:S(2)}) copy-start(s32[16,4]{0,1:T(4,128)} %param.24) | copy-start | bytes 772
  6.5 19.7 %copy-start.2 = (s32[64]{0:T(128)S(1)}, s32[64]{0:T(128)}, u32[]{:S(2)}) copy-start(s32[64]{0:T(128)} %param.25) | copy-start | bytes 772
  6.6 43.4 %all-gather.2.cloned.1.call-start = ((), (), s32[]{:S(2)}) async-start(), calls=%async_computation.2 | async-start | bytes 4128768 | tf_op jit(solution)/shard_map/all_gather | solution.py:224
  6.6 31.9 %collective-permute-start.4 = (bf16[2,256,256]{2,1,0:T(8,128)(2,1)}, bf16[2,256,256]{2,1,0:T(8,128)(2,1)S(1)}, u32[]{:S(2)}, u32[]{:S(2)}) collective-permute-start(bf16[2,256,256]{2,1,0:T(8,128)(2,1)} %param.31), channel_id=1, source_target_pairs={{0,64},{32,96},{64,0},{96,32},{1,65},{33,97},{65,1},{97,33},{2,66}... | collective-permute-start | bytes 786440 | tf_op jit(solution)/shard_map/ppermute | solution.py:109
  9.8 31.0 %collective-permute-start.3 = (bf16[2,256,256]{2,1,0:T(8,128)(2,1)}, bf16[2,256,256]{2,1,0:T(8,128)(2,1)S(1)}, u32[]{:S(2)}, u32[]{:S(2)}) collective-permute-start(bf16[2,256,256]{2,1,0:T(8,128)(2,1)} %param.31), channel_id=1, source_target_pairs={{0,32},{32,64},{64,96},{96,0},{1,33},{33,65},{65,97},{97,1},{2,34}... | collective-permute-start | bytes 786440 | tf_op jit(solution)/shard_map/ppermute | solution.py:109
  10.4 31.1 %collective-permute-start.5 = (bf16[2,256,256]{2,1,0:T(8,128)(2,1)}, bf16[2,256,256]{2,1,0:T(8,128)(2,1)}, u32[]{:S(2)}, u32[]{:S(2)}) collective-permute-start(bf16[2,256,256]{2,1,0:T(8,128)(2,1)} %param.31), channel_id=1, source_target_pairs={{0,96},{32,0},{64,32},{96,64},{1,97},{33,1},{65,33},{97,65},{2,98}... | collective-permute-start | bytes 786440 | tf_op jit(solution)/shard_map/ppermute | solution.py:109
  16.8 27.9 %collective-permute-start.1 = (bf16[3,256,256]{2,1,0:T(8,128)(2,1)}, bf16[3,256,256]{2,1,0:T(8,128)(2,1)}, u32[]{:S(2)}, u32[]{:S(2)}) collective-permute-start(bf16[3,256,256]{2,1,0:T(8,128)(2,1)} %get-tuple-element.39), channel_id=1, source_target_pairs={{0,16},{8,24},{16,0},{24,8},{1,17},{9,25},{17,1},{25,9},{2,18},{10... | collective-permute-start | bytes 1179656 | tf_op jit(solution)/shard_map/ppermute | solution.py:109
  20.7 22.2 %collective-permute-start = (bf16[3,256,256]{2,1,0:T(8,128)(2,1)}, bf16[3,256,256]{2,1,0:T(8,128)(2,1)}, u32[]{:S(2)}, u32[]{:S(2)}) collective-permute-start(bf16[3,256,256]{2,1,0:T(8,128)(2,1)} %get-tuple-element.39), channel_id=1, source_target_pairs={{0,8},{8,16},{16,24},{24,0},{1,9},{9,17},{17,25},{25,1},{2,10},{10... | collective-permute-start | bytes 1179656 | tf_op jit(solution)/shard_map/ppermute | solution.py:109
  26.3 0.9 copy-start.16
  38.5 2.3 %copy-start.12 = (bf16[2,256,256]{2,1,0:T(8,128)(2,1)}, bf16[2,256,256]{2,1,0:T(8,128)(2,1)S(1)}, u32[]{:S(2)}) copy-start(bf16[2,256,256]{2,1,0:T(8,128)(2,1)S(1)} %collective-permute-done.4) | copy-start | bytes 786436
  38.5 9.7 %collective-permute-start.2 = (bf16[3,256,256]{2,1,0:T(8,128)(2,1)}, bf16[3,256,256]{2,1,0:T(8,128)(2,1)S(1)}, u32[]{:S(2)}, u32[]{:S(2)}) collective-permute-start(bf16[3,256,256]{2,1,0:T(8,128)(2,1)} %get-tuple-element.39), channel_id=1, source_target_pairs={{0,24},{8,0},{16,8},{24,16},{1,25},{9,1},{17,9},{25,17},{2,26},{10... | collective-permute-start | bytes 1179656 | tf_op jit(solution)/shard_map/ppermute | solution.py:109
  40.8 0.7 copy-start.13
  44.7 8.3 %copy-start.14 = (f32[3584]{0:T(1024)S(1)}, f32[3584]{0:T(1024)}, u32[]{:S(2)}) copy-start(f32[3584]{0:T(1024)} %param.17) | copy-start | bytes 43012
  49.9 3.1 %copy-start.5 = (bf16[512,3584]{0,1:T(8,128)(2,1)S(1)}, bf16[512,3584]{0,1:T(8,128)(2,1)}, u32[]{:S(2)}) copy-start(bf16[512,3584]{0,1:T(8,128)(2,1)} %all-gather.2.cloned.1.call-done) | copy-start | bytes 11010052
  54.7 2.0 %copy-start.3 = (bf16[512,3584]{0,1:T(8,128)(2,1)}, bf16[512,3584]{0,1:T(8,128)(2,1)S(1)}, u32[]{:S(2)}) copy-start(bf16[512,3584]{0,1:T(8,128)(2,1)S(1)} %fusion.4) | copy-start | bytes 11010052
  54.7 2.9 %copy-start.20 = (bf16[3584,256]{1,0:T(8,128)(2,1)S(1)}, bf16[3584,256]{1,0:T(8,128)(2,1)}, u32[]{:S(2)}) copy-start(bf16[3584,256]{1,0:T(8,128)(2,1)} %param.19) | copy-start | bytes 5505028
  62.5 7.8 %copy-start.9 = (bf16[512,256]{0,1:T(8,128)(2,1)S(1)}, bf16[512,256]{0,1:T(8,128)(2,1)}, u32[]{:S(2)}) copy-start(bf16[512,256]{0,1:T(8,128)(2,1)} %convolution_convert_fusion.1) | copy-start | bytes 786436
  65.6 19.7 %collective-permute-start.11 = (bf16[20,64,256]{2,1,0:T(8,128)(2,1)}, bf16[20,64,256]{2,1,0:T(8,128)(2,1)}, u32[]{:S(2)}, u32[]{:S(2)}) collective-permute-start(bf16[20,64,256]{2,1,0:T(8,128)(2,1)} %get-tuple-element.22), channel_id=1, source_target_pairs={{0,64},{32,96},{64,0},{96,32},{1,65},{33,97},{65,1},{97,33},{2,66}... | collective-permute-start | bytes 1966088 | tf_op jit(solution)/shard_map/ppermute | solution.py:109
  68.6 29.8 %collective-permute-start.10 = (bf16[20,64,256]{2,1,0:T(8,128)(2,1)}, bf16[20,64,256]{2,1,0:T(8,128)(2,1)}, u32[]{:S(2)}, u32[]{:S(2)}) collective-permute-start(bf16[20,64,256]{2,1,0:T(8,128)(2,1)} %get-tuple-element.23), channel_id=1, source_target_pairs={{0,32},{32,64},{64,96},{96,0},{1,33},{33,65},{65,97},{97,1},{2,34}... | collective-permute-start | bytes 1966088 | tf_op jit(solution)/shard_map/ppermute | solution.py:109
  71.2 45.0 %collective-permute-start.9 = (bf16[512,512]{0,1:T(8,128)(2,1)}, bf16[512,512]{0,1:T(8,128)(2,1)}, u32[]{:S(2)}, u32[]{:S(2)}) collective-permute-start(bf16[512,512]{0,1:T(8,128)(2,1)} %pad_maximum_fusion.3), channel_id=1, source_target_pairs={{0,8},{8,16},{16,24},{24,32},{32,40},{40,48},{48,56},{56,64},{64,7... | collective-permute-start | bytes 1572872 | tf_op jit(solution)/shard_map/ppermute | solution.py:16
  75.7 30.7 %collective-permute-start.12 = (bf16[20,64,256]{2,1,0:T(8,128)(2,1)}, bf16[20,64,256]{2,1,0:T(8,128)(2,1)}, u32[]{:S(2)}, u32[]{:S(2)}) collective-permute-start(bf16[20,64,256]{2,1,0:T(8,128)(2,1)} %get-tuple-element.24), channel_id=1, source_target_pairs={{0,96},{32,0},{64,32},{96,64},{1,97},{33,1},{65,33},{97,65},{2,98}... | collective-permute-start | bytes 1966088 | tf_op jit(solution)/shard_map/ppermute | solution.py:109
  79.6 21.7 %copy-start.4 = (bf16[512,3584]{0,1:T(8,128)(2,1)S(1)}, bf16[512,3584]{0,1:T(8,128)(2,1)}, u32[]{:S(2)}) copy-start(bf16[512,3584]{0,1:T(8,128)(2,1)} %copy-done.3) | copy-start | bytes 11010052
  82.5 36.4 %collective-permute-start.7 = (bf16[4,256,256]{2,1,0:T(8,128)(2,1)}, bf16[4,256,256]{2,1,0:T(8,128)(2,1)}, u32[]{:S(2)}, u32[]{:S(2)}) collective-permute-start(bf16[4,256,256]{2,1,0:T(8,128)(2,1)} %get-tuple-element.26), channel_id=1, source_target_pairs={{0,16},{8,24},{16,0},{24,8},{1,17},{9,25},{17,1},{25,9},{2,18},{10... | collective-permute-start | bytes 1572872 | tf_op jit(solution)/shard_map/ppermute | solution.py:109
  85.3 33.5 %collective-permute-start.6 = (bf16[4,256,256]{2,1,0:T(8,128)(2,1)}, bf16[4,256,256]{2,1,0:T(8,128)(2,1)}, u32[]{:S(2)}, u32[]{:S(2)}) collective-permute-start(bf16[4,256,256]{2,1,0:T(8,128)(2,1)} %get-tuple-element.27), channel_id=1, source_target_pairs={{0,8},{8,16},{16,24},{24,0},{1,9},{9,17},{17,25},{25,1},{2,10},{10... | collective-permute-start | bytes 1572872 | tf_op jit(solution)/shard_map/ppermute | solution.py:109
  98.4 20.4 %collective-permute-start.8 = (bf16[4,256,256]{2,1,0:T(8,128)(2,1)}, bf16[4,256,256]{2,1,0:T(8,128)(2,1)}, u32[]{:S(2)}, u32[]{:S(2)}) collective-permute-start(bf16[4,256,256]{2,1,0:T(8,128)(2,1)} %get-tuple-element.28), channel_id=1, source_target_pairs={{0,24},{8,0},{16,8},{24,16},{1,25},{9,1},{17,9},{25,17},{2,26},{10... | collective-permute-start | bytes 1572872 | tf_op jit(solution)/shard_map/ppermute | solution.py:109
  112.7 15.6 %all-to-all-start = ((bf16[8,4,16,448]{3,2,1,0:T(8,128)(2,1)}), bf16[8,4,16,448]{3,2,1,0:T(8,128)(2,1)S(1)}, u32[]{:S(2)}, u32[]{:S(2)}) async-start(bf16[8,4,16,448]{3,2,1,0:T(8,128)(2,1)} %broadcast_in_dim.36), calls=%async_computation | async-start | bytes 1048576 | tf_op jit(solution)/shard_map/all_to_all | solution.py:235
  116.2 66.0 %reduce-scatter.2.cloned.1.call-start = ((), (), s32[]{:S(2)}) async-start(), calls=%async_computation.3 | async-start | bytes 4128768 | tf_op jit(solution)/shard_map/reduce_scatter | solution.py:296
  132.3 1.2 copy-start.6
  132.3 1.3 copy-start.8
  136.4 2.0 %copy-start.7 = (bf16[1024,256]{0,1:T(8,128)(2,1)S(1)}, bf16[1024,256]{0,1:T(8,128)(2,1)}, u32[]{:S(2)}) copy-start(bf16[1024,256]{0,1:T(8,128)(2,1)} %copy.65) | copy-start | bytes 1572868
  136.4 2.0 %copy-start.10 = (bf16[512,256]{0,1:T(8,128)(2,1)S(1)}, bf16[512,256]{0,1:T(8,128)(2,1)}, u32[]{:S(2)}) copy-start(bf16[512,256]{0,1:T(8,128)(2,1)} %convolution_convert_fusion.1) | copy-start | bytes 786436
  136.5 2.0 %copy-start.11 = (bf16[512,256]{0,1:T(8,128)(2,1)S(1)}, bf16[512,256]{0,1:T(8,128)(2,1)}, u32[]{:S(2)}) copy-start(bf16[512,256]{0,1:T(8,128)(2,1)} %get-tuple-element.35) | copy-start | bytes 786436
  138.5 2.8 %copy-start.19 = (bf16[512,3584]{1,0:T(8,128)(2,1)S(1)}, bf16[512,3584]{1,0:T(8,128)(2,1)}, u32[]{:S(2)}) copy-start(bf16[512,3584]{1,0:T(8,128)(2,1)} %param.21) | copy-start | bytes 11010052
  141.3 40.8 %copy-start.1 = (bf16[3584,256]{1,0:T(8,128)(2,1)S(1)}, bf16[3584,256]{1,0:T(8,128)(2,1)}, u32[]{:S(2)}) copy-start(bf16[3584,256]{1,0:T(8,128)(2,1)} %param.20) | copy-start | bytes 5505028
Sparse Core Ops, SparseCore 0:
  21.9 28.0 all-gather.1
  145.4 36.7 reduce-scatter.1

commit v4 on v1

--- a/solution.py
+++ b/solution.py
@@ -187,6 +187,22 @@
     chosen_adapters = jnp.take(received, adapter_pick, axis=0, mode="clip").reshape(slots, -1)
     chosen_adapters = chosen_adapters[:, : flat.shape[1]].reshape(slots, *adapters.shape[1:])
     return chosen_blocks, chosen_adapters
+
+
+def scatter_model(partial):
+    count, width = partial.shape
+    piece = width // (2 * SIDE)
+    chip_at, core_at = lax.axis_index("my"), lax.axis_index("mc")
+    blocks = partial.astype(jnp.bfloat16).reshape(count, SIDE, 2, piece)
+    mine = jnp.take(blocks, core_at, axis=2, mode="clip")
+    theirs = jnp.take(blocks, 1 - core_at, axis=2, mode="clip")
+    got = lax.ppermute(theirs, "mc", [(0, 1), (1, 0)])
+    summed = (mine.astype(jnp.float32) + got.astype(jnp.float32)).astype(jnp.bfloat16)
+    total = jnp.take(summed, chip_at, axis=1, mode="clip").astype(jnp.float32)
+    for step in range(1, SIDE):
+        send = jnp.take(summed, (chip_at + step) % SIDE, axis=1, mode="clip")
+        total = total + ring_send(send, "my", step).astype(jnp.float32)
+    return total.astype(jnp.bfloat16)
 
 
 def on_device(
@@ -281,9 +297,7 @@
         HEAD_WIDTH,
     )
     partial_out = jnp.dot(attended, output_weight, preferred_element_type=jnp.float32)
-    return lax.psum_scatter(
-        partial_out.astype(jnp.bfloat16), ("my", "mc"), scatter_dimension=1, tiled=True
-    )
+    return scatter_model(partial_out)
 
 
 def solution(mesh):

time: 187 us -> 191 us (1.021)
  waiting for transfers between devices: 52.4 us -> 39.9 us
  local copies, waits for them, and re-layouts: 39 us -> 46.5 us
  starting transfers between devices: 29 us -> 34.1 us
  other arithmetic: 28.9 us -> 32.6 us
    reduce_scatter x1 -> x0, waiting for transfers between devices: 36.1 us -> none  [on_device(): lax.psum_scatter(partial_out.astype(jnp.bfloat16), ('my', 'mc'), scatter_...]
    ppermute x12 -> x15, waiting for transfers between devices: 15.4 us -> 34.9 us  [ring_send(): lax.ppermute(value, axis, [(i, (i + step) % SIDE) for i in range(SIDE)])]
    convert_element_type x0 -> x1, local copies, waits for them, and re-layouts: none -> 5.94 us  [scatter_model(): blocks = partial.astype(jnp.bfloat16).reshape(count, SIDE, 2, piece)]
    ppermute x12 -> x15, starting transfers between devices: 19.7 us -> 25.1 us  [ring_send(): lax.ppermute(value, axis, [(i, (i + step) % SIDE) for i in range(SIDE)])]
    ppermute x0 -> x1, waiting for transfers between devices: none -> 3.87 us  [scatter_model(): got = lax.ppermute(theirs, 'mc', [(0, 1), (1, 0)])]
    convert_element_type x0 -> x2, other arithmetic: none -> 3.71 us  [the longest x1 2.7 us: scatter_model(): (mine.astype(jnp.float32) + got.astype(jnp.float32)).astype(jnp.bfloat16)]
  transfers between devices with their start and end apart: 16 -> 19, of which waited for: 5 -> 8; matrix products, arithmetic and copies ran while one was open for 34% -> 33% of each run, Pallas kernels for 0% -> 0%
where the time goes in v4:
time: 191 us; the launch traced here: 190 us
  local copies, waits for them, and re-layouts  46.5 us (24%)
  waiting for transfers between devices  39.9 us (21%)
  starting transfers between devices  34.1 us (18%)
  other arithmetic  32.6 us (17%)
  matrix products  20.1 us (11%)
  between operations  16.5 us (9%)
    ppermute x15, waiting for transfers between devices, ring_send(): lax.ppermute(value, axis, [(i, (i + step) % SIDE) for i in range(SIDE)])  34.9 us
    ppermute x15, starting transfers between devices, ring_send(): lax.ppermute(value, axis, [(i, (i + step) % SIDE) for i in range(SIDE)])  25.1 us
    unnamed x71, local copies, waits for them, and re-layouts  6.89 us
    convert_element_type x1, local copies, waits for them, and re-layouts, scatter_model(): blocks = partial.astype(jnp.bfloat16).reshape(count, SIDE, 2, piece)  5.94 us
    dot_general x1, matrix products, on_device(): jnp.dot(normalized_input, query_weight, preferred_element_type=jnp.float32)  5.25 us
    ppermute x1, starting transfers between devices, shifted(): lax.ppermute(value, axis, [(source, source + steps) for source in range(f...  4.49 us
    all_to_all x1, starting transfers between devices, on_device(): lax.all_to_all(jnp.broadcast_to(chosen_down, (model_count, *chosen_down.s...  4.42 us
    dot_general x1, matrix products, on_device(): jnp.dot(attended, output_weight, preferred_element_type=jnp.float32)  3.88 us
  transfers between devices with their start and end apart: 19, of which 8 were waited for; matrix products, arithmetic and copies ran while one was open for 33% of the time, Pallas kernels for 0%

profile of v4, /device:TPU:0, one launch (start us, length us, event | category | flops | bytes accessed | tf_op | source)
XLA Modules:
  0.0 189.7 jit_solution(7332662891223565999)
XLA Ops:
  6.5 3.2 %collective-permute-start.1 = (bf16[2,256,256]{2,1,0:T(8,128)(2,1)}, bf16[2,256,256]{2,1,0:T(8,128)(2,1)}, u32[]{:S(2)}, u32[]{:S(2)}) collective-permute-start(bf16[2,256,256]{2,1,0:T(8,128)(2,1)} %param.31), channel_id=1, source_target_pairs={{0,64},{32,96},{64,0},{96,32},{1,65},{33,97},{65,1},{97,33},{2,66}... | collective-permute-start | bytes 786440 | tf_op jit(solution)/shard_map/ppermute | solution.py:109
  10.3 1.0 pad_maximum_fusion.4
  11.6 1.7 constant_dynamic-update-slice_fusion.1
  14.0 4.0 %collective-permute-start.9 = (bf16[3,256,256]{2,1,0:T(8,128)(2,1)}, bf16[3,256,256]{2,1,0:T(8,128)(2,1)}, u32[]{:S(2)}, u32[]{:S(2)}) collective-permute-start(bf16[3,256,256]{2,1,0:T(8,128)(2,1)} %get-tuple-element.102), channel_id=1, source_target_pairs={{0,24},{8,0},{16,8},{24,16},{1,25},{9,1},{17,9},{25,17},{2,26},{10... | collective-permute-start | bytes 1179656 | tf_op jit(solution)/shard_map/ppermute | solution.py:109
  18.0 1.3 collective-permute-start.7
  19.6 0.8 gather_fusion.6
  30.2 2.4 %compare_select_fusion.2 = s32[1024,1]{0,1:T(1,128)S(1)} fusion(s32[]{:T(128)} %bitcast.14, s32[]{:T(128)} %bitcast.15, s32[]{:T(128)} %bitcast.17, s32[]{:T(128)} %bitcast.16), kind=kLoop, calls=%fused_computation.85 | loop fusion | flops 17408 | bytes 4112 | tf_op jit(solution)/shard_map/gather | solution.py:77
  33.9 1.8 multiply_cosine_fusion
  35.8 0.8 compare_and_fusion
  36.6 1.3 pad_add_fusion
  38.7 2.7 %collective-permute-start.2 = (bf16[2,256,256]{2,1,0:T(8,128)(2,1)}, bf16[2,256,256]{2,1,0:T(8,128)(2,1)}, u32[]{:S(2)}, u32[]{:S(2)}) collective-permute-start(bf16[2,256,256]{2,1,0:T(8,128)(2,1)} %param.31), channel_id=1, source_target_pairs={{0,96},{32,0},{64,32},{96,64},{1,97},{33,1},{65,33},{97,65},{2,98}... | collective-permute-start | bytes 786440 | tf_op jit(solution)/shard_map/ppermute | solution.py:109
  41.4 1.0 constant_dynamic-update-slice_fusion.4
  42.4 1.1 constant_dynamic-update-slice_fusion.3
  43.5 1.0 constant_dynamic-update-slice_fusion.2
  44.6 2.4 %gather_fusion.9 = bf16[80,64,256]{2,1,0:T(8,128)(2,1)} fusion(bf16[48,64,256]{2,1,0:T(8,128)(2,1)S(1)} %bitcast.128, s32[1024]{0:T(1024)S(1)} %pad_clamp_fusion.2), kind=kCustom, calls=%fused_computation.9 | custom fusion | bytes 5243200 | tf_op jit(solution)/shard_map/jit(_take)/gather | solution.py:170
  47.0 3.1 %fusion.105 = (bf16[20,64,256]{2,1,0:T(8,128)(2,1)S(1)}, bf16[20,64,256]{2,1,0:T(8,128)(2,1)}, bf16[20,64,256]{2,1,0:T(8,128)(2,1)}, bf16[20,64,256]{2,1,0:T(8,128)(2,1)}) fusion(bf16[80,64,256]{2,1,0:T(8,128)(2,1)} %gather_fusion.9), kind=kLoop, calls=%fused_computation.248 | loop fusion | bytes 5242880 | tf_op jit(solution)/shard_map/slice | solution.py:172
  50.6 0.8 collective-permute-start.10
  51.4 2.4 %collective-permute-start.12 = (bf16[20,64,256]{2,1,0:T(8,128)(2,1)}, bf16[20,64,256]{2,1,0:T(8,128)(2,1)}, u32[]{:S(2)}, u32[]{:S(2)}) collective-permute-start(bf16[20,64,256]{2,1,0:T(8,128)(2,1)} %get-tuple-element.84), channel_id=1, source_target_pairs={{0,96},{32,0},{64,32},{96,64},{1,97},{33,1},{65,33},{97,65},{2,98}... | collective-permute-start | bytes 1966088 | tf_op jit(solution)/shard_map/ppermute | solution.py:109
  53.8 0.7 fusion.97
  54.7 1.3 pad_maximum_fusion.2
  56.0 2.2 %gather_fusion.2 = bf16[16,256,256]{2,1,0:T(8,128)(2,1)} fusion(bf16[8,256,256]{2,1,0:T(8,128)(2,1)S(1)} %pad_maximum_fusion.2, s32[1024]{0:T(1024)} %pad_clamp_fusion.6), kind=kCustom, calls=%fused_computation.2 | custom fusion | bytes 4194368 | tf_op jit(solution)/shard_map/jit(_take)/gather | solution.py:124
  58.1 2.8 %fusion.106 = (bf16[4,256,256]{2,1,0:T(8,128)(2,1)S(1)}, bf16[4,256,256]{2,1,0:T(8,128)(2,1)}, bf16[4,256,256]{2,1,0:T(8,128)(2,1)}, bf16[4,256,256]{2,1,0:T(8,128)(2,1)}) fusion(bf16[16,256,256]{2,1,0:T(8,128)(2,1)} %gather_fusion.2), kind=kLoop, calls=%fused_computation.249 | loop fusion | bytes 4194304 | tf_op jit(solution)/shard_map/slice | solution.py:126
  60.9 2.3 %collective-permute-start.4 = (bf16[4,256,256]{2,1,0:T(8,128)(2,1)}, bf16[4,256,256]{2,1,0:T(8,128)(2,1)}, u32[]{:S(2)}, u32[]{:S(2)}) collective-permute-start(bf16[4,256,256]{2,1,0:T(8,128)(2,1)} %get-tuple-element.86), channel_id=1, source_target_pairs={{0,16},{8,24},{16,0},{24,8},{1,17},{9,25},{17,1},{25,9},{2,18},{10... | collective-permute-start | bytes 1572872 | tf_op jit(solution)/shard_map/ppermute | solution.py:109
  63.8 5.8 %collective-permute-done.11 = bf16[20,64,256]{2,1,0:T(8,128)(2,1)} collective-permute-done((bf16[20,64,256]{2,1,0:T(8,128)(2,1)}, bf16[20,64,256]{2,1,0:T(8,128)(2,1)}, u32[]{:S(2)}, u32[]{:S(2)}) %collective-permute-start.11) | collective-permute-done | bytes 655392 | tf_op jit(solution)/shard_map/ppermute | solution.py:109
  69.6 2.0 %collective-permute-start.5 = (bf16[4,256,256]{2,1,0:T(8,128)(2,1)}, bf16[4,256,256]{2,1,0:T(8,128)(2,1)}, u32[]{:S(2)}, u32[]{:S(2)}) collective-permute-start(bf16[4,256,256]{2,1,0:T(8,128)(2,1)} %get-tuple-element.88), channel_id=1, source_target_pairs={{0,24},{8,0},{16,8},{24,16},{1,25},{9,1},{17,9},{25,17},{2,26},{10... | collective-permute-start | bytes 1572872 | tf_op jit(solution)/shard_map/ppermute | solution.py:109
  71.6 9.6 %collective-permute-done.10 = bf16[20,64,256]{2,1,0:T(8,128)(2,1)} collective-permute-done((bf16[20,64,256]{2,1,0:T(8,128)(2,1)}, bf16[20,64,256]{2,1,0:T(8,128)(2,1)}, u32[]{:S(2)}, u32[]{:S(2)}) %collective-permute-start.10) | collective-permute-done | bytes 655392 | tf_op jit(solution)/shard_map/ppermute | solution.py:109
  81.2 2.8 %pad_maximum_fusion = bf16[80,64,256]{2,1,0:T(8,128)(2,1)} fusion(bf16[20,64,256]{2,1,0:T(8,128)(2,1)} %collective-permute-done.12, bf16[20,64,256]{2,1,0:T(8,128)(2,1)} %collective-permute-done.11, bf16[20,64,256]{2,1,0:T(8,128)(2,1)} %collective-permute-done.10, bf16[20,64,256]{2,1,0:T(8,128)(2,1)S(1)} %get-tuple-element.81), kind=kLoop, calls=%fused_computation.29 | loop fusion | flops 3932160 | bytes 5242880 | tf_op jit(solution)/shard_map/concatenate | solution.py:171
  84.1 2.3 %gather_fusion.11 = bf16[4,64,256]{2,1,0:T(8,128)(2,1)S(1)} fusion(bf16[80,64,256]{2,1,0:T(8,128)(2,1)} %pad_maximum_fusion, s32[1024]{0:T(1024)S(1)} %get-tuple-element.120), kind=kCustom, calls=%fused_computation.11 | custom fusion | bytes 262160 | tf_op jit(solution)/shard_map/jit(_take)/gather | solution.py:187
  86.7 0.9 broadcast_in_dim.54
  87.6 4.4 %all-to-all-start = ((bf16[8,4,16,448]{3,2,1,0:T(8,128)(2,1)}), bf16[8,4,16,448]{3,2,1,0:T(8,128)(2,1)S(1)}, u32[]{:S(2)}, u32[]{:S(2)}) async-start(bf16[8,4,16,448]{3,2,1,0:T(8,128)(2,1)} %broadcast_in_dim.54), calls=%async_computation | async-start | bytes 1048576 | tf_op jit(solution)/shard_map/all_to_all | solution.py:238
  92.1 3.0 %pad_maximum_fusion.1 = bf16[16,256,256]{2,1,0:T(8,128)(2,1)} fusion(bf16[4,256,256]{2,1,0:T(8,128)(2,1)} %collective-permute-done.5, bf16[4,256,256]{2,1,0:T(8,128)(2,1)} %collective-permute-done.4, bf16[4,256,256]{2,1,0:T(8,128)(2,1)} %collective-permute-done.3, bf16[4,256,256]{2,1,0:T(8,128)(2,1)S(1)} %get-tuple-element.85), kind=kLoop, calls=%fused_computation.30 | loop fusion | flops 3145728 | bytes 4194304 | tf_op jit(solution)/shard_map/concatenate | solution.py:125
  95.1 2.2 %gather_fusion.3 = bf16[4,256,256]{2,1,0:T(8,128)(2,1)S(1)} fusion(bf16[16,256,256]{2,1,0:T(8,128)(2,1)} %pad_maximum_fusion.1, s32[1024]{0:T(1024)S(1)} %pad_clamp_fusion.5), kind=kCustom, calls=%fused_computation.3 | custom fusion | bytes 1048592 | tf_op jit(solution)/shard_map/jit(_take)/gather | solution.py:133
  97.3 1.0 copy.69
  98.4 3.1 %gather_fusion.10 = bf16[16,64,256]{2,1,0:T(8,128)(2,1)} fusion(bf16[80,64,256]{2,1,0:T(8,128)(2,1)} %pad_maximum_fusion, s32[1024]{0:T(1024)S(1)} %get-tuple-element.121), kind=kCustom, calls=%fused_computation.10 | custom fusion | bytes 1048640 | tf_op jit(solution)/shard_map/jit(_take)/gather | solution.py:184
  101.5 0.8 all-to-all-done
  103.3 3.0 %fusion.2 = f32[512]{0:T(512)S(1)} fusion(bf16[512,3584]{0,1:T(8,128)(2,1)} %all-gather.2.cloned.1.call-done), kind=kLoop, calls=%fused_computation.18 | loop fusion | flops 5504512 | bytes 3672064 | tf_op jit(solution)/shard_map/reduce_sum | solution.py:252
  106.4 1.6 fusion.4
  108.0 1.2 convolution_convert_fusion.1
  109.2 0.7 copy-done.3
  109.9 1.0 copy-done.29
  110.8 1.2 convolution_bitcast_fusion
  112.0 1.2 fusion.39
  113.2 0.8 copy.61
  114.1 0.9 pad_maximum_fusion.3
  114.9 4.5 %collective-permute-start.6 = (bf16[512,512]{0,1:T(8,128)(2,1)}, bf16[512,512]{0,1:T(8,128)(2,1)}, u32[]{:S(2)}, u32[]{:S(2)}) collective-permute-start(bf16[512,512]{0,1:T(8,128)(2,1)} %pad_maximum_fusion.3), channel_id=1, source_target_pairs={{0,8},{8,16},{16,24},{24,32},{32,40},{40,48},{48,56},{56,64},{64,7... | collective-permute-start | bytes 1572872 | tf_op jit(solution)/shard_map/ppermute | solution.py:16
  119.4 5.3 %fusion.110 = f32[512,512]{0,1:T(8,128)S(1)} fusion(bf16[512,3584]{0,1:T(8,128)(2,1)} %copy-done.3, bf16[3584,512]{1,0:T(8,128)(2,1)} %param.18), kind=kOutput, calls=%fused_computation.253 | convolution fusion | flops 1879048192 | bytes 8388608 | tf_op jit(solution)/shard_map/dot_general | solution.py:271
  124.7 3.1 %fusion.14 = f32[512,512]{0,1:T(8,128)S(1)} fusion(f32[512,512]{0,1:T(8,128)S(1)} %fusion.110, bf16[64,512]{1,0:T(8,128)(2,1)S(1)} %bitcast.136, bf16[512,64]{0,1:T(8,128)(2,1)S(1)} %bitcast.137, bf16[64,3584]{1,0:T(8,128)(2,1)S(1)} %dot_general.31, bf16[512,3584]{0,1:T(8,128)(2,1)} %copy-done.3), kind=kOutput, calls=%fused_computation.35 | convolution fusion | flops 269025280 | bytes 6356992 | tf_op jit(solution)/shard_map/dot_general | solution.py:265
  128.8 0.9 subtract_convert_fusion
  129.9 1.1 fusion.108
  131.1 2.8 %fusion.5 = (f32[2,512]{1,0:T(2,128)S(1)}, f32[2048,512,2]{1,0,2:T(8,128)S(1)}) fusion(pred[512,2048]{0,1:T(8,128)(4,1)S(1)} %copy-done.5, bf16[512,2,128]{2,0,1:T(8,128)(2,1)} %get-tuple-element.93, bf16[512,2,128]{2,0,1:T(8,128)(2,1)} %get-tuple-element.92, bf16[512,256]{1,0:T(8,128)(2,1)S(1)} %copy-done.11, bf16[512,256]{1,0:T(8,128)(2,1)S(1)} %copy.60, ...), kind=kOutput, calls=%fused_computation.21 | convolution fusion | flops 1084226560 | bytes 11014144 | tf_op jit(solution)/shard_map/tkrd,skd->krts/dot_general | solution.py:84
  134.0 2.0 %fusion = f32[2,512]{1,0:T(2,128)S(1)} fusion(f32[2048,512,2]{1,0,2:T(8,128)S(1)} %get-tuple-element.116, f32[2,512]{1,0:T(2,128)S(1)} %get-tuple-element.115, pred[512,2048]{0,1:T(8,128)(4,1)S(1)} %copy-done.5), kind=kLoop, calls=%fused_computation.16 | loop fusion | flops 8387584 | bytes 9445376 | tf_op jit(solution)/shard_map/reduce_sum | solution.py:90
  136.0 2.8 %divide_convert_fusion = bf16[512,1,2,256]{0,3,2,1:T(8,128)(2,1)S(1)} fusion(f32[2048,512,2]{1,0,2:T(8,128)S(1)} %get-tuple-element.116, f32[2,512]{1,0:T(2,128)S(1)} %get-tuple-element.115, pred[512,2048]{0,1:T(8,128)(4,1)S(1)} %copy-done.5, bf16[512,256]{0,1:T(8,128)(2,1)S(1)} %copy-done.13, bf16[512,256]{0,1:T(8,128)(2,1)S(1)} %get-tuple-element.98, ...), kind=kOutput, calls=%fused_computation.52 | convolution fusion | flops 1085800448 | bytes 11018240 | tf_op jit(solution)/shard_map/krts,skd->tkrd/dot_general | solution.py:91
  138.8 3.9 %convolution_convert_fusion = bf16[512,3584]{1,0:T(8,128)(2,1)} fusion(bf16[512,512]{0,1:T(8,128)(2,1)S(1)} %bitcast.134, bf16[512,3584]{1,0:T(8,128)(2,1)S(1)} %copy-done.6), kind=kOutput, calls=%fused_computation.22 | convolution fusion | flops 1880883200 | bytes 7864320 | tf_op jit(solution)/shard_map/dot_general | solution.py:299
  142.7 5.9 %copy.66 = bf16[512,3584]{0,1:T(8,128)(2,1)} copy(bf16[512,3584]{1,0:T(8,128)(2,1)} %convolution_convert_fusion) | data formatting | bytes 7340032 | tf_op jit(solution)/shard_map/convert_element_type | solution.py:196
  148.6 1.6 dynamic-slice_bitcast_fusion
  150.4 3.9 %collective-permute-done.13 = bf16[512,4,448]{0,2,1:T(8,128)(2,1)} collective-permute-done((bf16[512,4,448]{0,2,1:T(8,128)(2,1)S(1)}, bf16[512,4,448]{0,2,1:T(8,128)(2,1)}, u32[]{:S(2)}, u32[]{:S(2)}) %collective-permute-start.13) | collective-permute-done | bytes 1835040 | tf_op jit(solution)/shard_map/ppermute | solution.py:199
  154.2 2.7 %fusion.10 = bf16[512,4,448]{0,2,1:T(8,128)(2,1)S(1)} fusion(bf16[512,4,448]{0,2,1:T(8,128)(2,1)} %collective-permute-done.13, bf16[512,4,2,448]{0,3,2,1:T(8,128)(2,1)} %bitcast.127, s32[]{:T(128)S(6)} %axis_index.64), kind=kLoop, calls=%fused_computation.28 | loop fusion | flops 3670016 | bytes 5505028 | tf_op jit(solution)/shard_map/convert_element_type | solution.py:200
  157.1 1.7 collective-permute-start.14
  158.8 1.6 collective-permute-start.16
  160.4 2.0 %collective-permute-start.15 = (bf16[512,448]{0,1:T(8,128)(2,1)S(1)}, bf16[512,448]{0,1:T(8,128)(2,1)S(1)}, u32[]{:S(2)}, u32[]{:S(2)}) collective-permute-start(bf16[512,448]{0,1:T(8,128)(2,1)S(1)} %get-tuple-element.91), channel_id=1, source_target_pairs={{0,4},{2,6},{4,0},{6,2},{1,5},{3,7},{5,1},{7,3},{8,12},{10,14},{12... | collective-permute-start | bytes 1376264 | tf_op jit(solution)/shard_map/ppermute | solution.py:109
  162.3 8.6 %collective-permute-done.14 = bf16[512,448]{0,1:T(8,128)(2,1)S(1)} collective-permute-done((bf16[512,448]{0,1:T(8,128)(2,1)S(1)}, bf16[512,448]{0,1:T(8,128)(2,1)S(1)}, u32[]{:S(2)}, u32[]{:S(2)}) %collective-permute-start.14) | collective-permute-done | bytes 458784 | tf_op jit(solution)/shard_map/ppermute | solution.py:109
  170.9 1.3 collective-permute-done.16
  172.2 9.6 %collective-permute-done.15 = bf16[512,448]{0,1:T(8,128)(2,1)S(1)} collective-permute-done((bf16[512,448]{0,1:T(8,128)(2,1)S(1)}, bf16[512,448]{0,1:T(8,128)(2,1)S(1)}, u32[]{:S(2)}, u32[]{:S(2)}) %collective-permute-start.15) | collective-permute-done | bytes 458784 | tf_op jit(solution)/shard_map/ppermute | solution.py:109
  181.8 1.0 fusion.30
  (155 shorter events, 15.5 us)
Async XLA Ops:
  6.5 101.4 %copy-start = (bf16[3584,256]{1,0:T(8,128)(2,1)S(1)}, bf16[3584,256]{1,0:T(8,128)(2,1)}, u32[]{:S(2)}) copy-start(bf16[3584,256]{1,0:T(8,128)(2,1)} %param.20) | copy-start | bytes 5505028
  6.5 12.8 %copy-start.18 = (s32[16,4]{0,1:T(4,128)S(1)}, s32[16,4]{0,1:T(4,128)}, u32[]{:S(2)}) copy-start(s32[16,4]{0,1:T(4,128)} %param.24) | copy-start | bytes 772
  6.5 13.0 %copy-start.2 = (s32[64]{0:T(128)S(1)}, s32[64]{0:T(128)}, u32[]{:S(2)}) copy-start(s32[64]{0:T(128)} %param.25) | copy-start | bytes 772
  6.5 96.7 %all-gather.2.cloned.1.call-start = ((), (), s32[]{:S(2)}) async-start(), calls=%async_computation.1 | async-start | bytes 4128768 | tf_op jit(solution)/shard_map/all_gather | solution.py:249
  6.5 44.9 %collective-permute-start.1 = (bf16[2,256,256]{2,1,0:T(8,128)(2,1)}, bf16[2,256,256]{2,1,0:T(8,128)(2,1)}, u32[]{:S(2)}, u32[]{:S(2)}) collective-permute-start(bf16[2,256,256]{2,1,0:T(8,128)(2,1)} %param.31), channel_id=1, source_target_pairs={{0,64},{32,96},{64,0},{96,32},{1,65},{33,97},{65,1},{97,33},{2,66}... | collective-permute-start | bytes 786440 | tf_op jit(solution)/shard_map/ppermute | solution.py:109
  9.7 44.9 %collective-permute-start = (bf16[2,256,256]{2,1,0:T(8,128)(2,1)}, bf16[2,256,256]{2,1,0:T(8,128)(2,1)}, u32[]{:S(2)}, u32[]{:S(2)}) collective-permute-start(bf16[2,256,256]{2,1,0:T(8,128)(2,1)} %param.31), channel_id=1, source_target_pairs={{0,32},{32,64},{64,96},{96,0},{1,33},{33,65},{65,97},{97,1},{2,34}... | collective-permute-start | bytes 786440 | tf_op jit(solution)/shard_map/ppermute | solution.py:109
  14.0 29.6 %collective-permute-start.9 = (bf16[3,256,256]{2,1,0:T(8,128)(2,1)}, bf16[3,256,256]{2,1,0:T(8,128)(2,1)}, u32[]{:S(2)}, u32[]{:S(2)}) collective-permute-start(bf16[3,256,256]{2,1,0:T(8,128)(2,1)} %get-tuple-element.102), channel_id=1, source_target_pairs={{0,24},{8,0},{16,8},{24,16},{1,25},{9,1},{17,9},{25,17},{2,26},{10... | collective-permute-start | bytes 1179656 | tf_op jit(solution)/shard_map/ppermute | solution.py:109
  18.0 24.4 %collective-permute-start.8 = (bf16[3,256,256]{2,1,0:T(8,128)(2,1)}, bf16[3,256,256]{2,1,0:T(8,128)(2,1)}, u32[]{:S(2)}, u32[]{:S(2)}) collective-permute-start(bf16[3,256,256]{2,1,0:T(8,128)(2,1)} %get-tuple-element.102), channel_id=1, source_target_pairs={{0,16},{8,24},{16,0},{24,8},{1,17},{9,25},{17,1},{25,9},{2,18},{10... | collective-permute-start | bytes 1179656 | tf_op jit(solution)/shard_map/ppermute | solution.py:109
  18.0 20.7 %collective-permute-start.7 = (bf16[3,256,256]{2,1,0:T(8,128)(2,1)}, bf16[3,256,256]{2,1,0:T(8,128)(2,1)}, u32[]{:S(2)}, u32[]{:S(2)}) collective-permute-start(bf16[3,256,256]{2,1,0:T(8,128)(2,1)} %get-tuple-element.102), channel_id=1, source_target_pairs={{0,8},{8,16},{16,24},{24,0},{1,9},{9,17},{17,25},{25,1},{2,10},{10... | collective-permute-start | bytes 1179656 | tf_op jit(solution)/shard_map/ppermute | solution.py:109
  19.6 1.5 copy-start.22
  19.6 2.6 %copy-start.30 = (s32[16]{0:T(128)S(1)}, s32[16]{0:T(128)}, u32[]{:S(2)}) copy-start(s32[16]{0:T(128)} %param.27) | copy-start | bytes 196
  19.6 5.1 %copy-start.21 = (s32[16,4]{0,1:T(4,128)S(1)}, s32[16,4]{0,1:T(4,128)}, u32[]{:S(2)}) copy-start(s32[16,4]{0,1:T(4,128)} %param.29) | copy-start | bytes 772
  19.6 5.6 %copy-start.19 = (s32[16,4]{0,1:T(4,128)S(1)}, s32[16,4]{0,1:T(4,128)}, u32[]{:S(2)}) copy-start(s32[16,4]{0,1:T(4,128)} %param.28) | copy-start | bytes 772
  25.2 18.3 %copy-start.23 = (s32[4,1]{0,1:T(1,128)}, s32[4,1]{0,1:T(1,128)S(1)}, u32[]{:S(2)}) copy-start(s32[4,1]{0,1:T(1,128)S(1)} %reduce-window.4) | copy-start | bytes 52
  29.6 13.9 %copy-start.27 = (f32[128]{0:T(128)}, f32[128]{0:T(128)S(1)}, u32[]{:S(2)}) copy-start(f32[128]{0:T(128)S(1)} %multiply_power_fusion) | copy-start | bytes 1540
  32.7 0.8 copy-start.25
  33.5 10.0 %copy-start.14 = (f32[512]{0:T(512)}, f32[512]{0:T(512)S(1)}, u32[]{:S(2)}) copy-start(f32[512]{0:T(512)S(1)} %add_convert_fusion.1) | copy-start | bytes 6148
  38.7 16.0 %collective-permute-start.2 = (bf16[2,256,256]{2,1,0:T(8,128)(2,1)}, bf16[2,256,256]{2,1,0:T(8,128)(2,1)}, u32[]{:S(2)}, u32[]{:S(2)}) collective-permute-start(bf16[2,256,256]{2,1,0:T(8,128)(2,1)} %param.31), channel_id=1, source_target_pairs={{0,96},{32,0},{64,32},{96,64},{1,97},{33,1},{65,33},{97,65},{2,98}... | collective-permute-start | bytes 786440 | tf_op jit(solution)/shard_map/ppermute | solution.py:109
  47.0 7.6 %copy-start.17 = (s32[4,4]{1,0:T(4,128)S(1)}, s32[4,4]{1,0:T(4,128)}, u32[]{:S(2)}) copy-start(s32[4,4]{1,0:T(4,128)} %iota_add_fusion) | copy-start | bytes 196
  50.1 19.5 %collective-permute-start.11 = (bf16[20,64,256]{2,1,0:T(8,128)(2,1)}, bf16[20,64,256]{2,1,0:T(8,128)(2,1)}, u32[]{:S(2)}, u32[]{:S(2)}) collective-permute-start(bf16[20,64,256]{2,1,0:T(8,128)(2,1)} %get-tuple-element.82), channel_id=1, source_target_pairs={{0,64},{32,96},{64,0},{96,32},{1,65},{33,97},{65,1},{97,33},{2,66}... | collective-permute-start | bytes 1966088 | tf_op jit(solution)/shard_map/ppermute | solution.py:109
  50.6 30.6 %collective-permute-start.10 = (bf16[20,64,256]{2,1,0:T(8,128)(2,1)}, bf16[20,64,256]{2,1,0:T(8,128)(2,1)}, u32[]{:S(2)}, u32[]{:S(2)}) collective-permute-start(bf16[20,64,256]{2,1,0:T(8,128)(2,1)} %get-tuple-element.83), channel_id=1, source_target_pairs={{0,32},{32,64},{64,96},{96,0},{1,33},{33,65},{65,97},{97,1},{2,34}... | collective-permute-start | bytes 1966088 | tf_op jit(solution)/shard_map/ppermute | solution.py:109
  51.4 29.8 %collective-permute-start.12 = (bf16[20,64,256]{2,1,0:T(8,128)(2,1)}, bf16[20,64,256]{2,1,0:T(8,128)(2,1)}, u32[]{:S(2)}, u32[]{:S(2)}) collective-permute-start(bf16[20,64,256]{2,1,0:T(8,128)(2,1)} %get-tuple-element.84), channel_id=1, source_target_pairs={{0,96},{32,0},{64,32},{96,64},{1,97},{33,1},{65,33},{97,65},{2,98}... | collective-permute-start | bytes 1966088 | tf_op jit(solution)/shard_map/ppermute | solution.py:109
  58.1 13.4 %copy-start.20 = (s32[4]{0:T(128)S(1)}, s32[4]{0:T(128)}, u32[]{:S(2)}) copy-start(s32[4]{0:T(128)} %fusion.98) | copy-start | bytes 52
  60.9 31.2 %collective-permute-start.4 = (bf16[4,256,256]{2,1,0:T(8,128)(2,1)}, bf16[4,256,256]{2,1,0:T(8,128)(2,1)}, u32[]{:S(2)}, u32[]{:S(2)}) collective-permute-start(bf16[4,256,256]{2,1,0:T(8,128)(2,1)} %get-tuple-element.86), channel_id=1, source_target_pairs={{0,16},{8,24},{16,0},{24,8},{1,17},{9,25},{17,1},{25,9},{2,18},{10... | collective-permute-start | bytes 1572872 | tf_op jit(solution)/shard_map/ppermute | solution.py:109
  63.2 28.9 %collective-permute-start.3 = (bf16[4,256,256]{2,1,0:T(8,128)(2,1)}, bf16[4,256,256]{2,1,0:T(8,128)(2,1)}, u32[]{:S(2)}, u32[]{:S(2)}) collective-permute-start(bf16[4,256,256]{2,1,0:T(8,128)(2,1)} %get-tuple-element.87), channel_id=1, source_target_pairs={{0,8},{8,16},{16,24},{24,0},{1,9},{9,17},{17,25},{25,1},{2,10},{10... | collective-permute-start | bytes 1572872 | tf_op jit(solution)/shard_map/ppermute | solution.py:109
  69.6 22.6 %collective-permute-start.5 = (bf16[4,256,256]{2,1,0:T(8,128)(2,1)}, bf16[4,256,256]{2,1,0:T(8,128)(2,1)}, u32[]{:S(2)}, u32[]{:S(2)}) collective-permute-start(bf16[4,256,256]{2,1,0:T(8,128)(2,1)} %get-tuple-element.88), channel_id=1, source_target_pairs={{0,24},{8,0},{16,8},{24,16},{1,25},{9,1},{17,9},{25,17},{2,26},{10... | collective-permute-start | bytes 1572872 | tf_op jit(solution)/shard_map/ppermute | solution.py:109
  84.1 8.0 %copy-start.24 = (s32[4,1]{0,1:T(1,128)S(1)}, s32[4,1]{0,1:T(1,128)}, u32[]{:S(2)}) copy-start(s32[4,1]{0,1:T(1,128)} %copy-done.23) | copy-start | bytes 52
  84.1 8.0 %copy-start.26 = (s32[4]{0:T(128)S(1)}, s32[4]{0:T(128)}, u32[]{:S(2)}) copy-start(s32[4]{0:T(128)} %copy-done.25) | copy-start | bytes 52
  87.6 14.8 %all-to-all-start = ((bf16[8,4,16,448]{3,2,1,0:T(8,128)(2,1)}), bf16[8,4,16,448]{3,2,1,0:T(8,128)(2,1)S(1)}, u32[]{:S(2)}, u32[]{:S(2)}) async-start(bf16[8,4,16,448]{3,2,1,0:T(8,128)(2,1)} %broadcast_in_dim.54), calls=%async_computation | async-start | bytes 1048576 | tf_op jit(solution)/shard_map/all_to_all | solution.py:238
  102.4 3.9 %copy-start.16 = (f32[3584]{0:T(1024)S(1)}, f32[3584]{0:T(1024)}, u32[]{:S(2)}) copy-start(f32[3584]{0:T(1024)} %param.17) | copy-start | bytes 43012
  103.3 3.1 %copy-start.4 = (bf16[512,3584]{0,1:T(8,128)(2,1)S(1)}, bf16[512,3584]{0,1:T(8,128)(2,1)}, u32[]{:S(2)}) copy-start(bf16[512,3584]{0,1:T(8,128)(2,1)} %all-gather.2.cloned.1.call-done) | copy-start | bytes 11010052
  108.0 1.9 copy-start.3
  108.0 2.8 %copy-start.29 = (bf16[3584,256]{1,0:T(8,128)(2,1)S(1)}, bf16[3584,256]{1,0:T(8,128)(2,1)}, u32[]{:S(2)}) copy-start(bf16[3584,256]{1,0:T(8,128)(2,1)} %param.19) | copy-start | bytes 5505028
  110.8 3.2 %copy-start.12 = (bf16[512,256]{0,1:T(8,128)(2,1)}, bf16[512,256]{0,1:T(8,128)(2,1)S(1)}, u32[]{:S(2)}) copy-start(bf16[512,256]{0,1:T(8,128)(2,1)S(1)} %convolution_convert_fusion.1) | copy-start | bytes 786436
  110.8 1.2 copy-start.15
  110.8 1.2 copy-start.28
  114.9 14.9 %collective-permute-start.6 = (bf16[512,512]{0,1:T(8,128)(2,1)}, bf16[512,512]{0,1:T(8,128)(2,1)}, u32[]{:S(2)}, u32[]{:S(2)}) collective-permute-start(bf16[512,512]{0,1:T(8,128)(2,1)} %pad_maximum_fusion.3), channel_id=1, source_target_pairs={{0,8},{8,16},{16,24},{24,32},{32,40},{40,48},{48,56},{56,64},{64,7... | collective-permute-start | bytes 1572872 | tf_op jit(solution)/shard_map/ppermute | solution.py:16
  127.8 1.0 copy-start.7
  127.8 1.0 copy-start.8
  128.1 3.0 %copy-start.5 = (pred[512,2048]{0,1:T(8,128)(4,1)S(1)}, pred[512,2048]{0,1:T(8,128)(4,1)}, u32[]{:S(2)}) copy-start(pred[512,2048]{0,1:T(8,128)(4,1)} %pad_add_fusion) | copy-start | bytes 3145732
  128.1 3.0 %copy-start.11 = (bf16[512,256]{1,0:T(8,128)(2,1)S(1)}, bf16[512,256]{1,0:T(8,128)(2,1)}, u32[]{:S(2)}) copy-start(bf16[512,256]{1,0:T(8,128)(2,1)} %copy.61) | copy-start | bytes 786436
  128.3 2.8 %copy-start.10 = (bf16[16,64,256]{2,1,0:T(8,128)(2,1)S(1)}, bf16[16,64,256]{2,1,0:T(8,128)(2,1)}, u32[]{:S(2)}) copy-start(bf16[16,64,256]{2,1,0:T(8,128)(2,1)} %gather_fusion.10) | copy-start | bytes 1572868
  134.0 2.0 %copy-start.9 = (bf16[1024,256]{0,1:T(8,128)(2,1)S(1)}, bf16[1024,256]{0,1:T(8,128)(2,1)}, u32[]{:S(2)}) copy-start(bf16[1024,256]{0,1:T(8,128)(2,1)} %copy.69) | copy-start | bytes 1572868
  134.0 2.0 %copy-start.13 = (bf16[512,256]{0,1:T(8,128)(2,1)S(1)}, bf16[512,256]{0,1:T(8,128)(2,1)}, u32[]{:S(2)}) copy-start(bf16[512,256]{0,1:T(8,128)(2,1)} %copy-done.12) | copy-start | bytes 786436
  136.0 2.8 %copy-start.6 = (bf16[512,3584]{1,0:T(8,128)(2,1)S(1)}, bf16[512,3584]{1,0:T(8,128)(2,1)}, u32[]{:S(2)}) copy-start(bf16[512,3584]{1,0:T(8,128)(2,1)} %param.21) | copy-start | bytes 11010052
  150.3 4.0 %collective-permute-start.13 = (bf16[512,4,448]{0,2,1:T(8,128)(2,1)S(1)}, bf16[512,4,448]{0,2,1:T(8,128)(2,1)}, u32[]{:S(2)}, u32[]{:S(2)}) collective-permute-start(bf16[512,4,448]{0,2,1:T(8,128)(2,1)S(1)} %dynamic-slice_bitcast_fusion), channel_id=1, source_target_pairs={{0,1},{1,0},{2,3},{3,2},{4,5},{5,4},{6,7},{7,6},{8,9},{9,8},{10,11... | collective-permute-start | bytes 5505032 | tf_op jit(solution)/shard_map/ppermute | solution.py:199
  154.2 28.6 %copy-start.1 = (bf16[3584,256]{1,0:T(8,128)(2,1)S(1)}, bf16[3584,256]{1,0:T(8,128)(2,1)}, u32[]{:S(2)}) copy-start(bf16[3584,256]{1,0:T(8,128)(2,1)} %param.20) | copy-start | bytes 5505028
  157.1 13.8 %collective-permute-start.14 = (bf16[512,448]{0,1:T(8,128)(2,1)S(1)}, bf16[512,448]{0,1:T(8,128)(2,1)S(1)}, u32[]{:S(2)}, u32[]{:S(2)}) collective-permute-start(bf16[512,448]{0,1:T(8,128)(2,1)S(1)} %get-tuple-element.89), channel_id=1, source_target_pairs={{0,2},{2,4},{4,6},{6,0},{1,3},{3,5},{5,7},{7,1},{8,10},{10,12},{12... | collective-permute-start | bytes 1376264 | tf_op jit(solution)/shard_map/ppermute | solution.py:109
  158.8 13.4 %collective-permute-start.16 = (bf16[512,448]{0,1:T(8,128)(2,1)S(1)}, bf16[512,448]{0,1:T(8,128)(2,1)S(1)}, u32[]{:S(2)}, u32[]{:S(2)}) collective-permute-start(bf16[512,448]{0,1:T(8,128)(2,1)S(1)} %get-tuple-element.90), channel_id=1, source_target_pairs={{0,6},{2,0},{4,2},{6,4},{1,7},{3,1},{5,3},{7,5},{8,14},{10,8},{12,... | collective-permute-start | bytes 1376264 | tf_op jit(solution)/shard_map/ppermute | solution.py:109
  160.4 21.5 %collective-permute-start.15 = (bf16[512,448]{0,1:T(8,128)(2,1)S(1)}, bf16[512,448]{0,1:T(8,128)(2,1)S(1)}, u32[]{:S(2)}, u32[]{:S(2)}) collective-permute-start(bf16[512,448]{0,1:T(8,128)(2,1)S(1)} %get-tuple-element.91), channel_id=1, source_target_pairs={{0,4},{2,6},{4,0},{6,2},{1,5},{3,7},{5,1},{7,3},{8,12},{10,14},{12... | collective-permute-start | bytes 1376264 | tf_op jit(solution)/shard_map/ppermute | solution.py:109
Sparse Core Ops, SparseCore 0:
  19.4 30.1 all-gather.1

commit v5 on v1

--- a/solution.py
+++ b/solution.py
@@ -114,13 +114,13 @@
     own_a, own_b = coords[first], coords[second]
     per_owner = local.shape[0]
     slots = wanted.shape[1]
-    held = jnp.concatenate([local] + [ring_send(local, first, step) for step in range(1, SIDE)])
+    held = lax.all_gather(local, first, axis=0, tiled=True)
     me = group_of(first, own_a, own_b)
     askers = group_of(first, own_a, (own_b + jnp.arange(SIDE)) % SIDE)
     owner = wanted // per_owner
     owner_a = (owner // SIDE, owner % SIDE)[first == "gz"]
     owner_b = (owner // SIDE, owner % SIDE)[second == "gz"]
-    source = ((own_a - owner_a[askers]) % SIDE) * per_owner + (wanted % per_owner)[askers]
+    source = owner_a[askers] * per_owner + (wanted % per_owner)[askers]
     outgoing = jnp.take(held, source.reshape(-1), axis=0, mode="clip")
     received = jnp.concatenate(
         [outgoing[:slots]]

time: 187 us -> 191 us (1.021)
  waiting for transfers between devices: 52.4 us -> 60.1 us
  starting transfers between devices: 29 us -> 21.3 us
  local copies, waits for them, and re-layouts: 39 us -> 43.4 us
    ppermute x12 -> x9, starting transfers between devices: 19.7 us -> 14.3 us  [ring_send(): lax.ppermute(value, axis, [(i, (i + step) % SIDE) for i in range(SIDE)])]
    all_to_all x1, waiting for transfers between devices: 0.61 us -> 4.55 us  [on_device(): lax.all_to_all(jnp.broadcast_to(chosen_down, (model_count, *chosen_down.s...]
    ppermute x1, starting transfers between devices: 4.7 us -> 2.23 us  [shifted(): lax.ppermute(value, axis, [(source, source + steps) for source in range(f...]
    ppermute x12 -> x9, waiting for transfers between devices: 15.4 us -> 17.7 us  [ring_send(): lax.ppermute(value, axis, [(i, (i + step) % SIDE) for i in range(SIDE)])]
    unnamed x71 -> x55, local copies, waits for them, and re-layouts: 6.87 us -> 6.75 us
  transfers between devices with their start and end apart: 16 -> 14, of which waited for: 5 -> 6; matrix products, arithmetic and copies ran while one was open for 34% -> 36% of each run, Pallas kernels for 0% -> 0%
where the time goes in v5:
time: 191 us; the launch traced here: 190 us
  waiting for transfers between devices  60.1 us (31%)
  local copies, waits for them, and re-layouts  43.4 us (23%)
  other arithmetic  27.9 us (15%)
  matrix products  21.4 us (11%)
  starting transfers between devices  21.3 us (11%)
  between operations  16.2 us (8%)
    reduce_scatter x1, waiting for transfers between devices, on_device(): lax.psum_scatter(partial_out.astype(jnp.bfloat16), ('my', 'mc'), scatter_...  37.1 us
    ppermute x9, waiting for transfers between devices, ring_send(): lax.ppermute(value, axis, [(i, (i + step) % SIDE) for i in range(SIDE)])  17.7 us
    ppermute x9, starting transfers between devices, ring_send(): lax.ppermute(value, axis, [(i, (i + step) % SIDE) for i in range(SIDE)])  14.3 us
    unnamed x55, local copies, waits for them, and re-layouts  6.75 us
    dot_general x1, matrix products, on_device(): jnp.dot(normalized_input, query_weight, preferred_element_type=jnp.float32)  6.24 us
    all_to_all x1, waiting for transfers between devices, on_device(): lax.all_to_all(jnp.broadcast_to(chosen_down, (model_count, *chosen_down.s...  4.55 us
    all_to_all x1, starting transfers between devices, on_device(): lax.all_to_all(jnp.broadcast_to(chosen_down, (model_count, *chosen_down.s...  4.47 us
    dot_general x1, matrix products, on_device(): jnp.dot(attended, output_weight, preferred_element_type=jnp.float32)  3.9 us
  transfers between devices with their start and end apart: 14, of which 6 were waited for; matrix products, arithmetic and copies ran while one was open for 36% of the time, Pallas kernels for 0%

profile of v5, /device:TPU:0, one launch (start us, length us, event | category | flops | bytes accessed | tf_op | source)
XLA Modules:
  0.0 190.4 jit_solution(2823890584582236844)
XLA Ops:
  6.5 0.7 all-gather.3.cloned.1.call-update
  7.3 1.0 pad_maximum_fusion.3
  8.6 1.7 constant_dynamic-update-slice_fusion.1
  10.3 0.7 constant_dynamic-update-slice_fusion
  11.0 4.1 %collective-permute-start.6 = (bf16[3,256,256]{2,1,0:T(8,128)(2,1)}, bf16[3,256,256]{2,1,0:T(8,128)(2,1)}, u32[]{:S(2)}, u32[]{:S(2)}) collective-permute-start(bf16[3,256,256]{2,1,0:T(8,128)(2,1)} %get-tuple-element.33), channel_id=1, source_target_pairs={{0,24},{8,0},{16,8},{24,16},{1,25},{9,1},{17,9},{25,17},{2,26},{10... | collective-permute-start | bytes 1179656 | tf_op jit(solution)/shard_map/ppermute | solution.py:109
  15.1 1.3 collective-permute-start.4
  16.7 0.8 gather_fusion.6
  18.8 0.6 constant_dynamic-slice_fusion.8
  19.7 0.6 dynamic_slice.24
  23.2 0.6 gather_fusion.5
  26.3 2.4 %compare_select_fusion.2 = s32[1024,1]{0,1:T(1,128)S(1)} fusion(s32[]{:T(128)} %bitcast.13, s32[]{:T(128)} %bitcast.14, s32[]{:T(128)} %bitcast.16, s32[]{:T(128)} %bitcast.15), kind=kLoop, calls=%fused_computation.74 | loop fusion | flops 17408 | bytes 4112 | tf_op jit(solution)/shard_map/gather | solution.py:77
  29.1 0.9 broadcast_and_fusion
  30.0 0.9 fusion.24
  30.9 1.8 multiply_cosine_fusion
  32.9 2.7 %collective-permute-done.4 = bf16[3,256,256]{2,1,0:T(8,128)(2,1)} collective-permute-done((bf16[3,256,256]{2,1,0:T(8,128)(2,1)}, bf16[3,256,256]{2,1,0:T(8,128)(2,1)}, u32[]{:S(2)}, u32[]{:S(2)}) %collective-permute-start.4) | collective-permute-done | bytes 393248 | tf_op jit(solution)/shard_map/ppermute | solution.py:109
  35.6 1.0 constant_dynamic-update-slice_fusion.4
  36.6 1.0 constant_dynamic-update-slice_fusion.3
  37.7 1.0 constant_dynamic-update-slice_fusion.2
  38.7 2.4 %gather_fusion.9 = bf16[80,64,256]{2,1,0:T(8,128)(2,1)} fusion(bf16[48,64,256]{2,1,0:T(8,128)(2,1)S(1)} %bitcast.109, s32[1024]{0:T(1024)S(1)} %pad_clamp_fusion.2), kind=kCustom, calls=%fused_computation.9 | custom fusion | bytes 5243200 | tf_op jit(solution)/shard_map/jit(_take)/gather | solution.py:170
  41.2 3.0 %fusion.97 = (bf16[20,64,256]{2,1,0:T(8,128)(2,1)S(1)}, bf16[20,64,256]{2,1,0:T(8,128)(2,1)}, bf16[20,64,256]{2,1,0:T(8,128)(2,1)}, bf16[20,64,256]{2,1,0:T(8,128)(2,1)S(1)}) fusion(bf16[80,64,256]{2,1,0:T(8,128)(2,1)} %gather_fusion.9), kind=kLoop, calls=%fused_computation.230 | loop fusion | bytes 5242880 | tf_op jit(solution)/shard_map/slice | solution.py:172
  44.2 3.0 %collective-permute-start.8 = (bf16[20,64,256]{2,1,0:T(8,128)(2,1)}, bf16[20,64,256]{2,1,0:T(8,128)(2,1)}, u32[]{:S(2)}, u32[]{:S(2)}) collective-permute-start(bf16[20,64,256]{2,1,0:T(8,128)(2,1)} %get-tuple-element.16), channel_id=1, source_target_pairs={{0,64},{32,96},{64,0},{96,32},{1,65},{33,97},{65,1},{97,33},{2,66}... | collective-permute-start | bytes 1966088 | tf_op jit(solution)/shard_map/ppermute | solution.py:109
  47.2 0.6 collective-permute-start.7
  47.8 2.6 %collective-permute-start.9 = (bf16[20,64,256]{2,1,0:T(8,128)(2,1)S(1)}, bf16[20,64,256]{2,1,0:T(8,128)(2,1)}, u32[]{:S(2)}, u32[]{:S(2)}) collective-permute-start(bf16[20,64,256]{2,1,0:T(8,128)(2,1)S(1)} %get-tuple-element.18), channel_id=1, source_target_pairs={{0,96},{32,0},{64,32},{96,64},{1,97},{33,1},{65,33},{97,65},{2,98}... | collective-permute-start | bytes 1966088 | tf_op jit(solution)/shard_map/ppermute | solution.py:109
  50.6 0.6 pad_clamp_fusion
  51.2 1.5 compare_and_fusion
  52.7 3.3 %gather_fusion.2 = bf16[16,256,256]{2,1,0:T(8,128)(2,1)} fusion(bf16[8,256,256]{2,1,0:T(8,128)(2,1)} %all-gather.3.cloned.1.call-done, s32[1024]{0:T(1024)S(1)} %pad_clamp_fusion.6), kind=kCustom, calls=%fused_computation.2 | custom fusion | bytes 4194368 | tf_op jit(solution)/shard_map/jit(_take)/gather | solution.py:124
  55.9 2.9 %fusion.98 = (bf16[4,256,256]{2,1,0:T(8,128)(2,1)}, bf16[4,256,256]{2,1,0:T(8,128)(2,1)}, bf16[4,256,256]{2,1,0:T(8,128)(2,1)}, bf16[4,256,256]{2,1,0:T(8,128)(2,1)}) fusion(bf16[16,256,256]{2,1,0:T(8,128)(2,1)} %gather_fusion.2), kind=kLoop, calls=%fused_computation.231 | loop fusion | bytes 4194304 | tf_op jit(solution)/shard_map/slice | solution.py:126
  58.8 0.6 collective-permute-start.1
  59.4 1.2 collective-permute-start
  60.6 3.1 %collective-permute-done.8 = bf16[20,64,256]{2,1,0:T(8,128)(2,1)} collective-permute-done((bf16[20,64,256]{2,1,0:T(8,128)(2,1)}, bf16[20,64,256]{2,1,0:T(8,128)(2,1)}, u32[]{:S(2)}, u32[]{:S(2)}) %collective-permute-start.8) | collective-permute-done | bytes 655392 | tf_op jit(solution)/shard_map/ppermute | solution.py:109
  63.7 0.9 collective-permute-start.2
  64.6 11.7 %collective-permute-done.7 = bf16[20,64,256]{2,1,0:T(8,128)(2,1)} collective-permute-done((bf16[20,64,256]{2,1,0:T(8,128)(2,1)}, bf16[20,64,256]{2,1,0:T(8,128)(2,1)}, u32[]{:S(2)}, u32[]{:S(2)}) %collective-permute-start.7) | collective-permute-done | bytes 655392 | tf_op jit(solution)/shard_map/ppermute | solution.py:109
  76.5 2.9 %pad_maximum_fusion = bf16[80,64,256]{2,1,0:T(8,128)(2,1)} fusion(bf16[20,64,256]{2,1,0:T(8,128)(2,1)} %collective-permute-done.9, bf16[20,64,256]{2,1,0:T(8,128)(2,1)} %collective-permute-done.8, bf16[20,64,256]{2,1,0:T(8,128)(2,1)} %collective-permute-done.7, bf16[20,64,256]{2,1,0:T(8,128)(2,1)S(1)} %get-tuple-element.15), kind=kLoop, calls=%fused_computation.27 | loop fusion | flops 3932160 | bytes 5242880 | tf_op jit(solution)/shard_map/concatenate | solution.py:171
  79.4 2.3 %gather_fusion.11 = bf16[4,64,256]{2,1,0:T(8,128)(2,1)S(1)} fusion(bf16[80,64,256]{2,1,0:T(8,128)(2,1)} %pad_maximum_fusion, s32[1024]{0:T(1024)S(1)} %get-tuple-element.51), kind=kCustom, calls=%fused_computation.11 | custom fusion | bytes 262160 | tf_op jit(solution)/shard_map/jit(_take)/gather | solution.py:187
  82.0 0.9 broadcast_in_dim.36
  82.9 4.5 %all-to-all-start = ((bf16[8,4,16,448]{3,2,1,0:T(8,128)(2,1)}), bf16[8,4,16,448]{3,2,1,0:T(8,128)(2,1)S(1)}, u32[]{:S(2)}, u32[]{:S(2)}) async-start(bf16[8,4,16,448]{3,2,1,0:T(8,128)(2,1)} %broadcast_in_dim.36), calls=%async_computation | async-start | bytes 1048576 | tf_op jit(solution)/shard_map/all_to_all | solution.py:222
  87.6 1.6 pad_add_fusion
  89.2 0.7 slice.116
  89.9 3.2 %gather_fusion.10 = bf16[16,64,256]{2,1,0:T(8,128)(2,1)} fusion(bf16[80,64,256]{2,1,0:T(8,128)(2,1)} %pad_maximum_fusion, s32[1024]{0:T(1024)} %get-tuple-element.52), kind=kCustom, calls=%fused_computation.10 | custom fusion | bytes 1048640 | tf_op jit(solution)/shard_map/jit(_take)/gather | solution.py:184
  93.2 4.5 %all-to-all-done = bf16[8,4,16,448]{3,2,1,0:T(8,128)(2,1)S(1)} async-done(((bf16[8,4,16,448]{3,2,1,0:T(8,128)(2,1)}), bf16[8,4,16,448]{3,2,1,0:T(8,128)(2,1)S(1)}, u32[]{:S(2)}, u32[]{:S(2)}) %all-to-all-start) | async-done | bytes 458784 | tf_op jit(solution)/shard_map/all_to_all | solution.py:222
  97.7 1.1 copy.59
  98.8 2.4 %dot_general.31 = bf16[64,3584]{1,0:T(8,128)(2,1)} reshape(bf16[4,16,8,448]{3,2,1,0:T(8,128)(2,1)} %copy.59) | data formatting | bytes 917504 | tf_op jit(solution)/shard_map/td,rkd->trk/dot_general | solution.py:245
  101.3 3.1 %pad_maximum_fusion.1 = bf16[16,256,256]{2,1,0:T(8,128)(2,1)} fusion(bf16[4,256,256]{2,1,0:T(8,128)(2,1)} %collective-permute-done.2, bf16[4,256,256]{2,1,0:T(8,128)(2,1)} %collective-permute-done.1, bf16[4,256,256]{2,1,0:T(8,128)(2,1)} %collective-permute-done, bf16[4,256,256]{2,1,0:T(8,128)(2,1)} %get-tuple-element.19), kind=kLoop, calls=%fused_computation.28 | loop fusion | flops 3145728 | bytes 4194304 | tf_op jit(solution)/shard_map/concatenate | solution.py:125
  104.4 2.2 %gather_fusion.3 = bf16[4,256,256]{2,1,0:T(8,128)(2,1)S(1)} fusion(bf16[16,256,256]{2,1,0:T(8,128)(2,1)} %pad_maximum_fusion.1, s32[1024]{0:T(1024)S(1)} %pad_clamp_fusion.5), kind=kCustom, calls=%fused_computation.3 | custom fusion | bytes 1048592 | tf_op jit(solution)/shard_map/jit(_take)/gather | solution.py:133
  106.6 1.0 copy.65
  107.6 3.0 %fusion.2 = f32[512]{0:T(512)S(1)} fusion(bf16[512,3584]{0,1:T(8,128)(2,1)} %all-gather.5.cloned.1.call-done), kind=kLoop, calls=%fused_computation.18 | loop fusion | flops 5504512 | bytes 3672064 | tf_op jit(solution)/shard_map/reduce_sum | solution.py:236
  110.7 1.6 fusion.4
  112.3 1.2 convolution_convert_fusion.1
  113.5 0.7 copy-done.3
  114.2 1.0 copy-done.21
  115.2 1.2 convolution_bitcast_fusion
  116.3 1.2 fusion.35
  117.5 0.8 copy.58
  118.4 0.8 pad_maximum_fusion.2
  119.2 2.2 %collective-permute-start.3 = (bf16[512,512]{0,1:T(8,128)(2,1)}, bf16[512,512]{0,1:T(8,128)(2,1)}, u32[]{:S(2)}, u32[]{:S(2)}) collective-permute-start(bf16[512,512]{0,1:T(8,128)(2,1)} %pad_maximum_fusion.2), channel_id=1, source_target_pairs={{0,8},{8,16},{16,24},{24,32},{32,40},{40,48},{48,56},{56,64},{64,7... | collective-permute-start | bytes 1572872 | tf_op jit(solution)/shard_map/ppermute | solution.py:16
  121.4 6.2 %fusion.102 = f32[512,512]{0,1:T(8,128)} fusion(bf16[512,3584]{0,1:T(8,128)(2,1)} %copy-done.3, bf16[3584,512]{1,0:T(8,128)(2,1)} %param.18), kind=kOutput, calls=%fused_computation.235 | convolution fusion | flops 1879048192 | bytes 8388608 | tf_op jit(solution)/shard_map/dot_general | solution.py:255
  127.7 3.3 %fusion.13 = f32[512,512]{0,1:T(8,128)S(1)} fusion(f32[512,512]{0,1:T(8,128)} %fusion.102, bf16[64,512]{1,0:T(8,128)(2,1)S(1)} %bitcast.116, bf16[512,64]{0,1:T(8,128)(2,1)S(1)} %bitcast.117, bf16[64,3584]{1,0:T(8,128)(2,1)S(1)} %copy-done.5, bf16[512,3584]{0,1:T(8,128)(2,1)} %copy-done.3), kind=kOutput, calls=%fused_computation.32 | convolution fusion | flops 269025280 | bytes 6356992 | tf_op jit(solution)/shard_map/dot_general | solution.py:249
  132.0 1.9 subtract_convert_fusion
  133.9 1.1 fusion.100
  135.1 2.8 %fusion.5 = (f32[2,512]{1,0:T(2,128)S(1)}, f32[2048,512,2]{1,0,2:T(8,128)S(1)}) fusion(pred[512,2048]{0,1:T(8,128)(4,1)S(1)} %pad_add_fusion, bf16[512,2,128]{2,0,1:T(8,128)(2,1)} %get-tuple-element.24, bf16[512,2,128]{2,0,1:T(8,128)(2,1)} %get-tuple-element.23, bf16[512,256]{1,0:T(8,128)(2,1)S(1)} %copy-done.10, bf16[512,256]{1,0:T(8,128)(2,1)S(1)} %copy.57, ...), kind=kOutput, calls=%fused_computation.21 | convolution fusion | flops 1084226560 | bytes 11014144 | tf_op jit(solution)/shard_map/tkrd,skd->krts/dot_general | solution.py:84
  138.0 2.0 %fusion = f32[2,512]{1,0:T(2,128)S(1)} fusion(f32[2048,512,2]{1,0,2:T(8,128)S(1)} %get-tuple-element.47, f32[2,512]{1,0:T(2,128)S(1)} %get-tuple-element.46, pred[512,2048]{0,1:T(8,128)(4,1)S(1)} %pad_add_fusion), kind=kLoop, calls=%fused_computation.16 | loop fusion | flops 8387584 | bytes 9445376 | tf_op jit(solution)/shard_map/reduce_sum | solution.py:90
  140.0 2.8 %divide_convert_fusion = bf16[512,1,2,256]{0,3,2,1:T(8,128)(2,1)S(1)} fusion(f32[2048,512,2]{1,0,2:T(8,128)S(1)} %get-tuple-element.47, f32[2,512]{1,0:T(2,128)S(1)} %get-tuple-element.46, pred[512,2048]{0,1:T(8,128)(4,1)S(1)} %pad_add_fusion, bf16[512,256]{0,1:T(8,128)(2,1)S(1)} %copy-done.12, bf16[512,256]{0,1:T(8,128)(2,1)S(1)} %get-tuple-element.29, ...), kind=kOutput, calls=%fused_computation.48 | convolution fusion | flops 1085800448 | bytes 11018240 | tf_op jit(solution)/shard_map/krts,skd->tkrd/dot_general | solution.py:91
  142.8 3.9 %convolution_convert_fusion = bf16[512,3584]{0,1:T(8,128)(2,1)} fusion(bf16[512,512]{0,1:T(8,128)(2,1)S(1)} %bitcast.123, bf16[512,3584]{1,0:T(8,128)(2,1)S(1)} %copy-done.20), kind=kOutput, calls=%fused_computation.22 | convolution fusion | flops 1880883200 | bytes 7864320 | tf_op jit(solution)/shard_map/dot_general | solution.py:283
  146.7 37.1 %reduce-scatter.2.cloned.1.call-done = bf16[512,448]{0,1:T(8,128)(2,1)} async-done(((bf16[512,3584]{0,1:T(8,128)(2,1)}), bf16[512,448]{0,1:T(8,128)(2,1)}) %reduce-scatter.2.cloned.1.call-update) | async-done | bytes 458768 | tf_op jit(solution)/shard_map/reduce_scatter | solution.py:284
  (123 shorter events, 7.6 us)
Async XLA Ops:
  6.5 105.8 %copy-start = (bf16[3584,256]{1,0:T(8,128)(2,1)S(1)}, bf16[3584,256]{1,0:T(8,128)(2,1)}, u32[]{:S(2)}) copy-start(bf16[3584,256]{1,0:T(8,128)(2,1)} %param.20) | copy-start | bytes 5505028
  6.5 9.9 %copy-start.14 = (s32[16,4]{0,1:T(4,128)S(1)}, s32[16,4]{0,1:T(4,128)}, u32[]{:S(2)}) copy-start(s32[16,4]{0,1:T(4,128)} %param.24) | copy-start | bytes 772
  6.5 10.1 %copy-start.2 = (s32[64]{0:T(128)S(1)}, s32[64]{0:T(128)}, u32[]{:S(2)}) copy-start(s32[64]{0:T(128)} %param.25) | copy-start | bytes 772
  6.5 46.1 %all-gather.3.cloned.1.call-start = ((), (), s32[]{:S(2)}) async-start(), calls=%async_computation.2 | async-start | bytes 1310720 | tf_op jit(solution)/shard_map/all_gather | solution.py:117
  7.3 100.3 %all-gather.5.cloned.1.call-start = ((), (), s32[]{:S(2)}) async-start(), calls=%async_computation.3 | async-start | bytes 4128768 | tf_op jit(solution)/shard_map/all_gather | solution.py:233
  11.0 26.7 %collective-permute-start.6 = (bf16[3,256,256]{2,1,0:T(8,128)(2,1)}, bf16[3,256,256]{2,1,0:T(8,128)(2,1)}, u32[]{:S(2)}, u32[]{:S(2)}) collective-permute-start(bf16[3,256,256]{2,1,0:T(8,128)(2,1)} %get-tuple-element.33), channel_id=1, source_target_pairs={{0,24},{8,0},{16,8},{24,16},{1,25},{9,1},{17,9},{25,17},{2,26},{10... | collective-permute-start | bytes 1179656 | tf_op jit(solution)/shard_map/ppermute | solution.py:109
  15.1 21.6 %collective-permute-start.5 = (bf16[3,256,256]{2,1,0:T(8,128)(2,1)}, bf16[3,256,256]{2,1,0:T(8,128)(2,1)}, u32[]{:S(2)}, u32[]{:S(2)}) collective-permute-start(bf16[3,256,256]{2,1,0:T(8,128)(2,1)} %get-tuple-element.33), channel_id=1, source_target_pairs={{0,16},{8,24},{16,0},{24,8},{1,17},{9,25},{17,1},{25,9},{2,18},{10... | collective-permute-start | bytes 1179656 | tf_op jit(solution)/shard_map/ppermute | solution.py:109
  15.1 20.5 %collective-permute-start.4 = (bf16[3,256,256]{2,1,0:T(8,128)(2,1)}, bf16[3,256,256]{2,1,0:T(8,128)(2,1)}, u32[]{:S(2)}, u32[]{:S(2)}) collective-permute-start(bf16[3,256,256]{2,1,0:T(8,128)(2,1)} %get-tuple-element.33), channel_id=1, source_target_pairs={{0,8},{8,16},{16,24},{24,0},{1,9},{9,17},{17,25},{25,1},{2,10},{10... | collective-permute-start | bytes 1179656 | tf_op jit(solution)/shard_map/ppermute | solution.py:109
  16.7 0.9 copy-start.15
  16.7 2.2 %copy-start.17 = (s32[16,4]{0,1:T(4,128)S(1)}, s32[16,4]{0,1:T(4,128)}, u32[]{:S(2)}) copy-start(s32[16,4]{0,1:T(4,128)} %param.26) | copy-start | bytes 772
  16.7 2.8 %copy-start.16 = (s32[16,4]{0,1:T(4,128)S(1)}, s32[16,4]{0,1:T(4,128)}, u32[]{:S(2)}) copy-start(s32[16,4]{0,1:T(4,128)} %param.29) | copy-start | bytes 772
  16.7 2.9 %copy-start.22 = (s32[16]{0:T(128)S(1)}, s32[16]{0:T(128)}, u32[]{:S(2)}) copy-start(s32[16]{0:T(128)} %param.27) | copy-start | bytes 196
  25.7 15.4 %copy-start.18 = (f32[128]{0:T(128)}, f32[128]{0:T(128)S(1)}, u32[]{:S(2)}) copy-start(f32[128]{0:T(128)S(1)} %multiply_power_fusion) | copy-start | bytes 1540
  44.2 19.5 %collective-permute-start.8 = (bf16[20,64,256]{2,1,0:T(8,128)(2,1)}, bf16[20,64,256]{2,1,0:T(8,128)(2,1)}, u32[]{:S(2)}, u32[]{:S(2)}) collective-permute-start(bf16[20,64,256]{2,1,0:T(8,128)(2,1)} %get-tuple-element.16), channel_id=1, source_target_pairs={{0,64},{32,96},{64,0},{96,32},{1,65},{33,97},{65,1},{97,33},{2,66}... | collective-permute-start | bytes 1966088 | tf_op jit(solution)/shard_map/ppermute | solution.py:109
  47.2 29.1 %collective-permute-start.7 = (bf16[20,64,256]{2,1,0:T(8,128)(2,1)}, bf16[20,64,256]{2,1,0:T(8,128)(2,1)}, u32[]{:S(2)}, u32[]{:S(2)}) collective-permute-start(bf16[20,64,256]{2,1,0:T(8,128)(2,1)} %get-tuple-element.17), channel_id=1, source_target_pairs={{0,32},{32,64},{64,96},{96,0},{1,33},{33,65},{65,97},{97,1},{2,34}... | collective-permute-start | bytes 1966088 | tf_op jit(solution)/shard_map/ppermute | solution.py:109
  47.8 28.7 %collective-permute-start.9 = (bf16[20,64,256]{2,1,0:T(8,128)(2,1)S(1)}, bf16[20,64,256]{2,1,0:T(8,128)(2,1)}, u32[]{:S(2)}, u32[]{:S(2)}) collective-permute-start(bf16[20,64,256]{2,1,0:T(8,128)(2,1)S(1)} %get-tuple-element.18), channel_id=1, source_target_pairs={{0,96},{32,0},{64,32},{96,64},{1,97},{33,1},{65,33},{97,65},{2,98}... | collective-permute-start | bytes 1966088 | tf_op jit(solution)/shard_map/ppermute | solution.py:109
  58.8 42.4 %collective-permute-start.1 = (bf16[4,256,256]{2,1,0:T(8,128)(2,1)}, bf16[4,256,256]{2,1,0:T(8,128)(2,1)}, u32[]{:S(2)}, u32[]{:S(2)}) collective-permute-start(bf16[4,256,256]{2,1,0:T(8,128)(2,1)} %get-tuple-element.20), channel_id=1, source_target_pairs={{0,16},{8,24},{16,0},{24,8},{1,17},{9,25},{17,1},{25,9},{2,18},{10... | collective-permute-start | bytes 1572872 | tf_op jit(solution)/shard_map/ppermute | solution.py:109
  59.4 41.9 %collective-permute-start = (bf16[4,256,256]{2,1,0:T(8,128)(2,1)}, bf16[4,256,256]{2,1,0:T(8,128)(2,1)}, u32[]{:S(2)}, u32[]{:S(2)}) collective-permute-start(bf16[4,256,256]{2,1,0:T(8,128)(2,1)} %get-tuple-element.21), channel_id=1, source_target_pairs={{0,8},{8,16},{16,24},{24,0},{1,9},{9,17},{17,25},{25,1},{2,10},{10... | collective-permute-start | bytes 1572872 | tf_op jit(solution)/shard_map/ppermute | solution.py:109
  63.7 37.6 %collective-permute-start.2 = (bf16[4,256,256]{2,1,0:T(8,128)(2,1)}, bf16[4,256,256]{2,1,0:T(8,128)(2,1)}, u32[]{:S(2)}, u32[]{:S(2)}) collective-permute-start(bf16[4,256,256]{2,1,0:T(8,128)(2,1)} %get-tuple-element.22), channel_id=1, source_target_pairs={{0,24},{8,0},{16,8},{24,16},{1,25},{9,1},{17,9},{25,17},{2,26},{10... | collective-permute-start | bytes 1572872 | tf_op jit(solution)/shard_map/ppermute | solution.py:109
  82.9 14.8 %all-to-all-start = ((bf16[8,4,16,448]{3,2,1,0:T(8,128)(2,1)}), bf16[8,4,16,448]{3,2,1,0:T(8,128)(2,1)S(1)}, u32[]{:S(2)}, u32[]{:S(2)}) async-start(bf16[8,4,16,448]{3,2,1,0:T(8,128)(2,1)} %broadcast_in_dim.36), calls=%async_computation | async-start | bytes 1048576 | tf_op jit(solution)/shard_map/all_to_all | solution.py:222
  87.4 96.5 %reduce-scatter.2.cloned.1.call-start = ((), (), s32[]{:S(2)}) async-start(), calls=%async_computation.4 | async-start | bytes 4128768 | tf_op jit(solution)/shard_map/reduce_scatter | solution.py:284
  106.6 4.1 %copy-start.13 = (f32[3584]{0:T(1024)S(1)}, f32[3584]{0:T(1024)}, u32[]{:S(2)}) copy-start(f32[3584]{0:T(1024)} %param.17) | copy-start | bytes 43012
  107.6 3.1 %copy-start.4 = (bf16[512,3584]{0,1:T(8,128)(2,1)S(1)}, bf16[512,3584]{0,1:T(8,128)(2,1)}, u32[]{:S(2)}) copy-start(bf16[512,3584]{0,1:T(8,128)(2,1)} %all-gather.5.cloned.1.call-done) | copy-start | bytes 11010052
  112.3 1.9 copy-start.3
  112.3 2.8 %copy-start.21 = (bf16[3584,256]{1,0:T(8,128)(2,1)S(1)}, bf16[3584,256]{1,0:T(8,128)(2,1)}, u32[]{:S(2)}) copy-start(bf16[3584,256]{1,0:T(8,128)(2,1)} %param.19) | copy-start | bytes 5505028
  115.2 3.2 %copy-start.11 = (bf16[512,256]{0,1:T(8,128)(2,1)}, bf16[512,256]{0,1:T(8,128)(2,1)S(1)}, u32[]{:S(2)}) copy-start(bf16[512,256]{0,1:T(8,128)(2,1)S(1)} %convolution_convert_fusion.1) | copy-start | bytes 786436
  115.2 1.2 copy-start.19
  119.2 8.5 %copy-start.5 = (bf16[64,3584]{1,0:T(8,128)(2,1)S(1)}, bf16[64,3584]{1,0:T(8,128)(2,1)}, u32[]{:S(2)}) copy-start(bf16[64,3584]{1,0:T(8,128)(2,1)} %dot_general.31) | copy-start | bytes 1376260
  119.2 8.5 %copy-start.9 = (bf16[4,16,512]{2,1,0:T(8,128)(2,1)S(1)}, bf16[4,16,512]{2,1,0:T(8,128)(2,1)}, u32[]{:S(2)}) copy-start(bf16[4,16,512]{2,1,0:T(8,128)(2,1)} %slice.116) | copy-start | bytes 196612
  119.2 14.7 %collective-permute-start.3 = (bf16[512,512]{0,1:T(8,128)(2,1)}, bf16[512,512]{0,1:T(8,128)(2,1)}, u32[]{:S(2)}, u32[]{:S(2)}) collective-permute-start(bf16[512,512]{0,1:T(8,128)(2,1)} %pad_maximum_fusion.2), channel_id=1, source_target_pairs={{0,8},{8,16},{16,24},{24,32},{32,40},{40,48},{48,56},{56,64},{64,7... | collective-permute-start | bytes 1572872 | tf_op jit(solution)/shard_map/ppermute | solution.py:16
  131.1 1.0 copy-start.6
  131.4 3.7 %copy-start.8 = (bf16[16,64,256]{2,1,0:T(8,128)(2,1)S(1)}, bf16[16,64,256]{2,1,0:T(8,128)(2,1)}, u32[]{:S(2)}) copy-start(bf16[16,64,256]{2,1,0:T(8,128)(2,1)} %gather_fusion.10) | copy-start | bytes 1572868
  131.6 3.5 %copy-start.10 = (bf16[512,256]{1,0:T(8,128)(2,1)S(1)}, bf16[512,256]{1,0:T(8,128)(2,1)}, u32[]{:S(2)}) copy-start(bf16[512,256]{1,0:T(8,128)(2,1)} %copy.58) | copy-start | bytes 786436
  137.9 2.0 %copy-start.7 = (bf16[1024,256]{0,1:T(8,128)(2,1)S(1)}, bf16[1024,256]{0,1:T(8,128)(2,1)}, u32[]{:S(2)}) copy-start(bf16[1024,256]{0,1:T(8,128)(2,1)} %copy.65) | copy-start | bytes 1572868
  138.0 2.0 %copy-start.12 = (bf16[512,256]{0,1:T(8,128)(2,1)S(1)}, bf16[512,256]{0,1:T(8,128)(2,1)}, u32[]{:S(2)}) copy-start(bf16[512,256]{0,1:T(8,128)(2,1)} %copy-done.11) | copy-start | bytes 786436
  140.0 2.8 %copy-start.20 = (bf16[512,3584]{1,0:T(8,128)(2,1)S(1)}, bf16[512,3584]{1,0:T(8,128)(2,1)}, u32[]{:S(2)}) copy-start(bf16[512,3584]{1,0:T(8,128)(2,1)} %param.21) | copy-start | bytes 11010052
  142.8 41.0 %copy-start.1 = (bf16[3584,256]{1,0:T(8,128)(2,1)S(1)}, bf16[3584,256]{1,0:T(8,128)(2,1)}, u32[]{:S(2)}) copy-start(bf16[3584,256]{1,0:T(8,128)(2,1)} %param.20) | copy-start | bytes 5505028
Sparse Core Ops, SparseCore 0:
  9.0 26.4 all-gather.2
  37.2 30.2 all-gather.4
  146.9 36.9 reduce-scatter.1

commit v6 on v1

--- a/solution.py
+++ b/solution.py
@@ -5,6 +5,7 @@
 
 HEAD_WIDTH = 256
 REQS = 4
+MOSTLEN = 256
 
 
 adapter_scale = 2.0
@@ -71,13 +72,18 @@
     every_value = jnp.concatenate(
         [cache_values.reshape(slots, -1), prev_values, values], 0
     ).reshape(-1, kv_heads, head_size)
-    slot_req = jnp.arange(slots, dtype=jnp.int32) // block
-    slot_col = jnp.arange(slots, dtype=jnp.int32) % block
-    cache_ok = (request[:, None] == slot_req[None, :]) & (
-        slot_col[None, :] < cached[slot_req][None, :]
-    )
+    owned = jnp.arange(cache_keys.shape[0], dtype=jnp.int32)
+    cache_ok = (
+        (request[:, None, None] == owned[None, :, None])
+        & (jnp.arange(block, dtype=jnp.int32)[None, None, :] < cached[None, :, None])
+    ).reshape(count, slots)
     place = jnp.arange(count, dtype=jnp.int32)
-    prev_ok = (split_flag == 1) & (request[:, None] == 0) & (place[None, :] >= count - prev_len)
+    kept = jnp.arange(prev_keys.shape[0], dtype=jnp.int32)
+    prev_ok = (
+        (split_flag == 1)
+        & (request[:, None] == 0)
+        & (kept[None, :] >= prev_keys.shape[0] - prev_len)
+    )
     own_ok = (request[:, None] == request[None, :]) & (place[None, :] <= place[:, None])
     allowed = jnp.concatenate([cache_ok, prev_ok, own_ok], 1)
     grouped = query_vectors.reshape(count, kv_heads, ratio, head_size)
@@ -264,7 +270,8 @@
     values = jnp.dot(normalized_input, value_weight, preferred_element_type=jnp.float32).astype(
         jnp.bfloat16
     )
-    prev_both = shifted(jnp.concatenate([keys, values], axis=1), ("gx", "gz"), 1)
+    tail = count - MOSTLEN
+    prev_both = shifted(jnp.concatenate([keys[tail:], values[tail:]], axis=1), ("gx", "gz"), 1)
     prev_keys, prev_values = prev_both[:, : keys.shape[1]], prev_both[:, keys.shape[1]:]
     attended = attend(
         query_vectors,

time: 187 us -> 182 us (0.973)
  waiting for transfers between devices: 52.4 us -> 57.6 us
  starting transfers between devices: 29 us -> 24.2 us
  other arithmetic: 28.9 us -> 24.6 us
    ppermute x12, waiting for transfers between devices: 15.4 us -> 20.2 us  [ring_send(): lax.ppermute(value, axis, [(i, (i + step) % SIDE) for i in range(SIDE)])]
    ppermute x1, starting transfers between devices: 4.7 us -> 2.03 us  [shifted(): lax.ppermute(value, axis, [(source, source + steps) for source in range(f...]
    gather x1 -> x0, other arithmetic: 2.42 us -> none  [attend(): cached[slot_req][None, :]]
    ppermute x12, starting transfers between devices: 19.7 us -> 17.5 us  [ring_send(): lax.ppermute(value, axis, [(i, (i + step) % SIDE) for i in range(SIDE)])]
    unnamed x71 -> x69, local copies, waits for them, and re-layouts: 6.87 us -> 6.01 us
  transfers between devices with their start and end apart: 16 -> 16, of which waited for: 5 -> 5; matrix products, arithmetic and copies ran while one was open for 34% -> 33% of each run, Pallas kernels for 0% -> 0%
where the time goes in v6:
time: 182 us; the launch traced here: 181 us
  waiting for transfers between devices  57.6 us (32%)
  local copies, waits for them, and re-layouts  38.1 us (21%)
  other arithmetic  24.6 us (14%)
  starting transfers between devices  24.2 us (13%)
  matrix products  19.6 us (11%)
  between operations  16.6 us (9%)
    reduce_scatter x1, waiting for transfers between devices, on_device(): lax.psum_scatter(partial_out.astype(jnp.bfloat16), ('my', 'mc'), scatter_...  36.8 us
    ppermute x12, waiting for transfers between devices, ring_send(): lax.ppermute(value, axis, [(i, (i + step) % SIDE) for i in range(SIDE)])  20.2 us
    ppermute x12, starting transfers between devices, ring_send(): lax.ppermute(value, axis, [(i, (i + step) % SIDE) for i in range(SIDE)])  17.5 us
    unnamed x69, local copies, waits for them, and re-layouts  6.01 us
    dot_general x1, matrix products, on_device(): jnp.dot(normalized_input, query_weight, preferred_element_type=jnp.float32)  5.25 us
    all_to_all x1, starting transfers between devices, on_device(): lax.all_to_all(jnp.broadcast_to(chosen_down, (model_count, *chosen_down.s...  4.42 us
    dot_general x1, matrix products, on_device(): jnp.dot(attended, output_weight, preferred_element_type=jnp.float32)  3.91 us
  transfers between devices with their start and end apart: 16, of which 5 were waited for; matrix products, arithmetic and copies ran while one was open for 33% of the time, Pallas kernels for 0%

profile of v6, /device:TPU:0, one launch (start us, length us, event | category | flops | bytes accessed | tf_op | source)
XLA Modules:
  0.0 180.7 jit_solution(14869334275584080598)
XLA Ops:
  6.6 3.2 %collective-permute-start.1 = (bf16[2,256,256]{2,1,0:T(8,128)(2,1)}, bf16[2,256,256]{2,1,0:T(8,128)(2,1)}, u32[]{:S(2)}, u32[]{:S(2)}) collective-permute-start(bf16[2,256,256]{2,1,0:T(8,128)(2,1)} %param.31), channel_id=1, source_target_pairs={{0,64},{32,96},{64,0},{96,32},{1,65},{33,97},{65,1},{97,33},{2,66}... | collective-permute-start | bytes 786440 | tf_op jit(solution)/shard_map/ppermute | solution.py:115
  9.8 0.6 collective-permute-start
  10.4 1.0 pad_maximum_fusion.5
  11.7 1.7 constant_dynamic-update-slice_fusion.1
  13.4 0.7 constant_dynamic-update-slice_fusion
  14.0 4.0 %collective-permute-start.9 = (bf16[3,256,256]{2,1,0:T(8,128)(2,1)}, bf16[3,256,256]{2,1,0:T(8,128)(2,1)}, u32[]{:S(2)}, u32[]{:S(2)}) collective-permute-start(bf16[3,256,256]{2,1,0:T(8,128)(2,1)} %get-tuple-element.31), channel_id=1, source_target_pairs={{0,24},{8,0},{16,8},{24,16},{1,25},{9,1},{17,9},{25,17},{2,26},{10... | collective-permute-start | bytes 1179656 | tf_op jit(solution)/shard_map/ppermute | solution.py:115
  18.1 1.3 collective-permute-start.7
  19.4 0.6 constant_dynamic-slice_fusion.7
  20.7 1.3 dynamic_slice.24
  24.6 0.8 gather_fusion.6
  25.6 0.6 gather_fusion.8
  26.2 0.6 gather_fusion.5
  26.7 0.6 gather_fusion.1
  28.0 0.6 gather_fusion.4
  28.6 0.6 fusion.45
  29.2 0.6 negate_select_fusion.1
  31.5 0.6 iota_add_fusion
  32.5 1.8 %multiply_cosine_fusion = (f32[512,128]{1,0:T(8,128)}, f32[512,128]{1,0:T(8,128)}) fusion(f32[128]{0:T(128)S(1)} %multiply_power_fusion, f32[512]{0:T(512)S(1)} %add_convert_fusion.1), kind=kLoop, calls=%fused_computation.58 | loop fusion | flops 65536 | bytes 526848 | tf_op jit(solution)/shard_map/cos | solution.py:26
  34.3 1.3 pad_add_fusion
  35.6 0.6 pad_clamp_fusion.6
  36.4 1.7 collective-permute-done.7
  38.0 2.6 %collective-permute-start.2 = (bf16[2,256,256]{2,1,0:T(8,128)(2,1)}, bf16[2,256,256]{2,1,0:T(8,128)(2,1)}, u32[]{:S(2)}, u32[]{:S(2)}) collective-permute-start(bf16[2,256,256]{2,1,0:T(8,128)(2,1)} %param.31), channel_id=1, source_target_pairs={{0,96},{32,0},{64,32},{96,64},{1,97},{33,1},{65,33},{97,65},{2,98}... | collective-permute-start | bytes 786440 | tf_op jit(solution)/shard_map/ppermute | solution.py:115
  40.7 1.0 constant_dynamic-update-slice_fusion.4
  41.7 1.0 constant_dynamic-update-slice_fusion.3
  42.8 1.0 constant_dynamic-update-slice_fusion.2
  43.8 2.4 %gather_fusion.9 = bf16[80,64,256]{2,1,0:T(8,128)(2,1)} fusion(bf16[48,64,256]{2,1,0:T(8,128)(2,1)S(1)} %bitcast.112, s32[1024]{0:T(1024)S(1)} %pad_clamp_fusion.2), kind=kCustom, calls=%fused_computation.9 | custom fusion | bytes 5243200 | tf_op jit(solution)/shard_map/jit(_take)/gather | solution.py:176
  46.2 3.0 %fusion.95 = (bf16[20,64,256]{2,1,0:T(8,128)(2,1)S(1)}, bf16[20,64,256]{2,1,0:T(8,128)(2,1)}, bf16[20,64,256]{2,1,0:T(8,128)(2,1)}, bf16[20,64,256]{2,1,0:T(8,128)(2,1)}) fusion(bf16[80,64,256]{2,1,0:T(8,128)(2,1)} %gather_fusion.9), kind=kLoop, calls=%fused_computation.224 | loop fusion | bytes 5242880 | tf_op jit(solution)/shard_map/slice | solution.py:178
  49.8 0.9 collective-permute-start.10
  50.8 2.3 %collective-permute-start.12 = (bf16[20,64,256]{2,1,0:T(8,128)(2,1)}, bf16[20,64,256]{2,1,0:T(8,128)(2,1)}, u32[]{:S(2)}, u32[]{:S(2)}) collective-permute-start(bf16[20,64,256]{2,1,0:T(8,128)(2,1)} %get-tuple-element.16), channel_id=1, source_target_pairs={{0,96},{32,0},{64,32},{96,64},{1,97},{33,1},{65,33},{97,65},{2,98}... | collective-permute-start | bytes 1966088 | tf_op jit(solution)/shard_map/ppermute | solution.py:115
  53.1 0.7 fusion.88
  53.9 1.3 pad_maximum_fusion.2
  55.2 2.1 %gather_fusion.2 = bf16[16,256,256]{2,1,0:T(8,128)(2,1)} fusion(bf16[8,256,256]{2,1,0:T(8,128)(2,1)S(1)} %pad_maximum_fusion.2, s32[1024]{0:T(1024)} %pad_clamp_fusion.6), kind=kCustom, calls=%fused_computation.2 | custom fusion | bytes 4194368 | tf_op jit(solution)/shard_map/jit(_take)/gather | solution.py:130
  57.3 2.8 %fusion.96 = (bf16[4,256,256]{2,1,0:T(8,128)(2,1)S(1)}, bf16[4,256,256]{2,1,0:T(8,128)(2,1)}, bf16[4,256,256]{2,1,0:T(8,128)(2,1)}, bf16[4,256,256]{2,1,0:T(8,128)(2,1)}) fusion(bf16[16,256,256]{2,1,0:T(8,128)(2,1)} %gather_fusion.2), kind=kLoop, calls=%fused_computation.225 | loop fusion | bytes 4194304 | tf_op jit(solution)/shard_map/slice | solution.py:132
  60.1 0.7 collective-permute-start.4
  60.9 1.0 collective-permute-start.3
  61.9 7.0 %collective-permute-done.11 = bf16[20,64,256]{2,1,0:T(8,128)(2,1)} collective-permute-done((bf16[20,64,256]{2,1,0:T(8,128)(2,1)}, bf16[20,64,256]{2,1,0:T(8,128)(2,1)}, u32[]{:S(2)}, u32[]{:S(2)}) %collective-permute-start.11) | collective-permute-done | bytes 655392 | tf_op jit(solution)/shard_map/ppermute | solution.py:115
  68.8 0.8 collective-permute-start.5
  69.7 11.6 %collective-permute-done.10 = bf16[20,64,256]{2,1,0:T(8,128)(2,1)} collective-permute-done((bf16[20,64,256]{2,1,0:T(8,128)(2,1)}, bf16[20,64,256]{2,1,0:T(8,128)(2,1)}, u32[]{:S(2)}, u32[]{:S(2)}) %collective-permute-start.10) | collective-permute-done | bytes 655392 | tf_op jit(solution)/shard_map/ppermute | solution.py:115
  81.2 2.8 %pad_maximum_fusion = bf16[80,64,256]{2,1,0:T(8,128)(2,1)} fusion(bf16[20,64,256]{2,1,0:T(8,128)(2,1)} %collective-permute-done.12, bf16[20,64,256]{2,1,0:T(8,128)(2,1)} %collective-permute-done.11, bf16[20,64,256]{2,1,0:T(8,128)(2,1)} %collective-permute-done.10, bf16[20,64,256]{2,1,0:T(8,128)(2,1)S(1)} %get-tuple-element.13), kind=kLoop, calls=%fused_computation.27 | loop fusion | flops 3932160 | bytes 5242880 | tf_op jit(solution)/shard_map/concatenate | solution.py:177
  84.1 2.3 %gather_fusion.11 = bf16[4,64,256]{2,1,0:T(8,128)(2,1)S(1)} fusion(bf16[80,64,256]{2,1,0:T(8,128)(2,1)} %pad_maximum_fusion, s32[1024]{0:T(1024)S(1)} %get-tuple-element.46), kind=kCustom, calls=%fused_computation.11 | custom fusion | bytes 262160 | tf_op jit(solution)/shard_map/jit(_take)/gather | solution.py:193
  86.7 0.8 broadcast_in_dim.36
  87.6 4.4 %all-to-all-start = ((bf16[8,4,16,448]{3,2,1,0:T(8,128)(2,1)}), bf16[8,4,16,448]{3,2,1,0:T(8,128)(2,1)S(1)}, u32[]{:S(2)}, u32[]{:S(2)}) async-start(bf16[8,4,16,448]{3,2,1,0:T(8,128)(2,1)} %broadcast_in_dim.36), calls=%async_computation | async-start | bytes 1048576 | tf_op jit(solution)/shard_map/all_to_all | solution.py:228
  92.3 3.0 %pad_maximum_fusion.1 = bf16[16,256,256]{2,1,0:T(8,128)(2,1)} fusion(bf16[4,256,256]{2,1,0:T(8,128)(2,1)} %collective-permute-done.5, bf16[4,256,256]{2,1,0:T(8,128)(2,1)} %collective-permute-done.4, bf16[4,256,256]{2,1,0:T(8,128)(2,1)} %collective-permute-done.3, bf16[4,256,256]{2,1,0:T(8,128)(2,1)S(1)} %get-tuple-element.17), kind=kLoop, calls=%fused_computation.28 | loop fusion | flops 3145728 | bytes 4194304 | tf_op jit(solution)/shard_map/concatenate | solution.py:131
  95.4 2.2 %gather_fusion.3 = bf16[4,256,256]{2,1,0:T(8,128)(2,1)S(1)} fusion(bf16[16,256,256]{2,1,0:T(8,128)(2,1)} %pad_maximum_fusion.1, s32[1024]{0:T(1024)S(1)} %pad_clamp_fusion.5), kind=kCustom, calls=%fused_computation.3 | custom fusion | bytes 1048592 | tf_op jit(solution)/shard_map/jit(_take)/gather | solution.py:139
  97.6 1.0 copy.65
  98.7 3.1 %gather_fusion.10 = bf16[16,64,256]{2,1,0:T(8,128)(2,1)} fusion(bf16[80,64,256]{2,1,0:T(8,128)(2,1)} %pad_maximum_fusion, s32[1024]{0:T(1024)S(1)} %get-tuple-element.47), kind=kCustom, calls=%fused_computation.10 | custom fusion | bytes 1048640 | tf_op jit(solution)/shard_map/jit(_take)/gather | solution.py:190
  101.8 0.6 all-to-all-done
  102.7 0.6 dot_general.31
  103.3 3.0 %fusion = f32[512]{0:T(512)S(1)} fusion(bf16[512,3584]{0,1:T(8,128)(2,1)} %all-gather.2.cloned.1.call-done), kind=kLoop, calls=%fused_computation.14 | loop fusion | flops 5504512 | bytes 3672064 | tf_op jit(solution)/shard_map/reduce_sum | solution.py:242
  106.4 1.6 fusion.2
  108.0 1.2 convolution_bitcast_fusion
  109.2 1.2 fusion.36
  110.8 1.2 convolution_convert_fusion.1
  112.0 0.8 copy.58
  112.9 0.8 pad_maximum_fusion.4
  113.6 2.0 %collective-permute-start.6 = (bf16[256,512]{0,1:T(8,128)(2,1)}, bf16[256,512]{0,1:T(8,128)(2,1)}, u32[]{:S(2)}, u32[]{:S(2)}) collective-permute-start(bf16[256,512]{0,1:T(8,128)(2,1)} %pad_maximum_fusion.4), channel_id=1, source_target_pairs={{0,8},{8,16},{16,24},{24,32},{32,40},{40,48},{48,56},{56,64},{64,7... | collective-permute-start | bytes 786440 | tf_op jit(solution)/shard_map/ppermute | solution.py:17
  115.6 5.3 %fusion.99 = f32[512,512]{0,1:T(8,128)S(1)} fusion(bf16[512,3584]{0,1:T(8,128)(2,1)} %copy-done.3, bf16[3584,512]{1,0:T(8,128)(2,1)} %param.18), kind=kOutput, calls=%fused_computation.228 | convolution fusion | flops 1879048192 | bytes 8388608 | tf_op jit(solution)/shard_map/dot_general | solution.py:261
  120.9 3.1 %fusion.13 = f32[512,512]{0,1:T(8,128)S(1)} fusion(f32[512,512]{0,1:T(8,128)S(1)} %fusion.99, bf16[64,512]{1,0:T(8,128)(2,1)S(1)} %bitcast.119, bf16[512,64]{0,1:T(8,128)(2,1)S(1)} %bitcast.120, bf16[64,3584]{1,0:T(8,128)(2,1)S(1)} %dot_general.31, bf16[512,3584]{0,1:T(8,128)(2,1)} %copy-done.3), kind=kOutput, calls=%fused_computation.32 | convolution fusion | flops 269025280 | bytes 6356992 | tf_op jit(solution)/shard_map/dot_general | solution.py:255
  125.2 1.0 fusion.98
  126.3 2.6 %fusion.5 = (f32[2,512]{1,0:T(2,128)S(1)}, f32[1792,512,2]{1,0,2:T(8,128)S(1)}) fusion(pred[512,1792]{0,1:T(8,128)(4,1)S(1)} %copy-done.5, bf16[512,2,128]{2,0,1:T(8,128)(2,1)S(1)} %get-tuple-element.22, bf16[512,2,128]{2,0,1:T(8,128)(2,1)S(1)} %get-tuple-element.21, bf16[512,256]{1,0:T(8,128)(2,1)S(1)} %copy-done.9, bf16[256,256]{1,0:T(8,128)(2,1)S(1)} %copy.57, ...), kind=kOutput, calls=%fused_computation.22 | convolution fusion | flops 948829184 | bytes 9703424 | tf_op jit(solution)/shard_map/tkrd,skd->krts/dot_general | solution.py:90
  128.9 1.7 fusion.3
  130.7 2.4 %divide_convert_fusion = bf16[512,1,2,256]{0,3,2,1:T(8,128)(2,1)S(1)} fusion(f32[1792,512,2]{1,0,2:T(8,128)S(1)} %get-tuple-element.41, f32[2,512]{1,0:T(2,128)S(1)} %get-tuple-element.40, pred[512,1792]{0,1:T(8,128)(4,1)S(1)} %copy-done.5, bf16[512,256]{0,1:T(8,128)(2,1)S(1)} %copy-done.11, bf16[256,256]{0,1:T(8,128)(2,1)S(1)} %get-tuple-element.27, ...), kind=kOutput, calls=%fused_computation.38 | convolution fusion | flops 950140928 | bytes 9707520 | tf_op jit(solution)/shard_map/krts,skd->tkrd/dot_general | solution.py:97
  133.1 3.9 %convolution_convert_fusion = bf16[512,3584]{0,1:T(8,128)(2,1)} fusion(bf16[512,512]{0,1:T(8,128)(2,1)S(1)} %bitcast.127, bf16[512,3584]{1,0:T(8,128)(2,1)S(1)} %copy-done.27), kind=kOutput, calls=%fused_computation.21 | convolution fusion | flops 1880883200 | bytes 7864320 | tf_op jit(solution)/shard_map/dot_general | solution.py:290
  137.1 36.8 %reduce-scatter.2.cloned.1.call-done = bf16[512,448]{0,1:T(8,128)(2,1)} async-done(((bf16[512,3584]{0,1:T(8,128)(2,1)}), bf16[512,448]{0,1:T(8,128)(2,1)}) %reduce-scatter.2.cloned.1.call-update) | async-done | bytes 458768 | tf_op jit(solution)/shard_map/reduce_scatter | solution.py:291
  (144 shorter events, 7.8 us)
Async XLA Ops:
  6.5 101.4 %copy-start = (bf16[3584,256]{1,0:T(8,128)(2,1)S(1)}, bf16[3584,256]{1,0:T(8,128)(2,1)}, u32[]{:S(2)}) copy-start(bf16[3584,256]{1,0:T(8,128)(2,1)} %param.19) | copy-start | bytes 5505028
  6.5 12.9 %copy-start.17 = (s32[16,4]{0,1:T(4,128)S(1)}, s32[16,4]{0,1:T(4,128)}, u32[]{:S(2)}) copy-start(s32[16,4]{0,1:T(4,128)} %param.26) | copy-start | bytes 772
  6.5 17.4 %copy-start.16 = (s32[16,4]{0,1:T(4,128)S(1)}, s32[16,4]{0,1:T(4,128)}, u32[]{:S(2)}) copy-start(s32[16,4]{0,1:T(4,128)} %param.29) | copy-start | bytes 772
  6.5 17.9 %copy-start.18 = (s32[16,4]{0,1:T(4,128)S(1)}, s32[16,4]{0,1:T(4,128)}, u32[]{:S(2)}) copy-start(s32[16,4]{0,1:T(4,128)} %param.24) | copy-start | bytes 772
  6.5 18.1 %copy-start.2 = (s32[64]{0:T(128)S(1)}, s32[64]{0:T(128)}, u32[]{:S(2)}) copy-start(s32[64]{0:T(128)} %param.25) | copy-start | bytes 772
  6.5 96.7 %all-gather.2.cloned.1.call-start = ((), (), s32[]{:S(2)}) async-start(), calls=%async_computation.2 | async-start | bytes 4128768 | tf_op jit(solution)/shard_map/all_gather | solution.py:239
  6.6 44.2 %collective-permute-start.1 = (bf16[2,256,256]{2,1,0:T(8,128)(2,1)}, bf16[2,256,256]{2,1,0:T(8,128)(2,1)}, u32[]{:S(2)}, u32[]{:S(2)}) collective-permute-start(bf16[2,256,256]{2,1,0:T(8,128)(2,1)} %param.31), channel_id=1, source_target_pairs={{0,64},{32,96},{64,0},{96,32},{1,65},{33,97},{65,1},{97,33},{2,66}... | collective-permute-start | bytes 786440 | tf_op jit(solution)/shard_map/ppermute | solution.py:115
  9.8 44.1 %collective-permute-start = (bf16[2,256,256]{2,1,0:T(8,128)(2,1)}, bf16[2,256,256]{2,1,0:T(8,128)(2,1)}, u32[]{:S(2)}, u32[]{:S(2)}) collective-permute-start(bf16[2,256,256]{2,1,0:T(8,128)(2,1)} %param.31), channel_id=1, source_target_pairs={{0,32},{32,64},{64,96},{96,0},{1,33},{33,65},{65,97},{97,1},{2,34}... | collective-permute-start | bytes 786440 | tf_op jit(solution)/shard_map/ppermute | solution.py:115
  14.0 28.7 %collective-permute-start.9 = (bf16[3,256,256]{2,1,0:T(8,128)(2,1)}, bf16[3,256,256]{2,1,0:T(8,128)(2,1)}, u32[]{:S(2)}, u32[]{:S(2)}) collective-permute-start(bf16[3,256,256]{2,1,0:T(8,128)(2,1)} %get-tuple-element.31), channel_id=1, source_target_pairs={{0,24},{8,0},{16,8},{24,16},{1,25},{9,1},{17,9},{25,17},{2,26},{10... | collective-permute-start | bytes 1179656 | tf_op jit(solution)/shard_map/ppermute | solution.py:115
  18.1 23.6 %collective-permute-start.8 = (bf16[3,256,256]{2,1,0:T(8,128)(2,1)}, bf16[3,256,256]{2,1,0:T(8,128)(2,1)}, u32[]{:S(2)}, u32[]{:S(2)}) collective-permute-start(bf16[3,256,256]{2,1,0:T(8,128)(2,1)} %get-tuple-element.31), channel_id=1, source_target_pairs={{0,16},{8,24},{16,0},{24,8},{1,17},{9,25},{17,1},{25,9},{2,18},{10... | collective-permute-start | bytes 1179656 | tf_op jit(solution)/shard_map/ppermute | solution.py:115
  18.1 20.0 %collective-permute-start.7 = (bf16[3,256,256]{2,1,0:T(8,128)(2,1)}, bf16[3,256,256]{2,1,0:T(8,128)(2,1)}, u32[]{:S(2)}, u32[]{:S(2)}) collective-permute-start(bf16[3,256,256]{2,1,0:T(8,128)(2,1)} %get-tuple-element.31), channel_id=1, source_target_pairs={{0,8},{8,16},{16,24},{24,0},{1,9},{9,17},{17,25},{25,1},{2,10},{10... | collective-permute-start | bytes 1179656 | tf_op jit(solution)/shard_map/ppermute | solution.py:115
  24.4 6.3 %copy-start.21 = (s32[4,1]{0,1:T(1,128)}, s32[4,1]{0,1:T(1,128)S(1)}, u32[]{:S(2)}) copy-start(s32[4,1]{0,1:T(1,128)S(1)} %reduce-window.4) | copy-start | bytes 52
  24.6 0.9 copy-start.19
  30.6 0.5 copy-start.23
  31.5 12.3 %copy-start.25 = (f32[128]{0:T(128)}, f32[128]{0:T(128)S(1)}, u32[]{:S(2)}) copy-start(f32[128]{0:T(128)S(1)} %multiply_power_fusion) | copy-start | bytes 1540
  32.2 11.7 %copy-start.12 = (f32[512]{0:T(512)}, f32[512]{0:T(512)S(1)}, u32[]{:S(2)}) copy-start(f32[512]{0:T(512)S(1)} %add_convert_fusion.1) | copy-start | bytes 6148
  38.0 15.8 %collective-permute-start.2 = (bf16[2,256,256]{2,1,0:T(8,128)(2,1)}, bf16[2,256,256]{2,1,0:T(8,128)(2,1)}, u32[]{:S(2)}, u32[]{:S(2)}) collective-permute-start(bf16[2,256,256]{2,1,0:T(8,128)(2,1)} %param.31), channel_id=1, source_target_pairs={{0,96},{32,0},{64,32},{96,64},{1,97},{33,1},{65,33},{97,65},{2,98}... | collective-permute-start | bytes 786440 | tf_op jit(solution)/shard_map/ppermute | solution.py:115
  46.2 7.5 %copy-start.15 = (s32[4,4]{1,0:T(4,128)S(1)}, s32[4,4]{1,0:T(4,128)}, u32[]{:S(2)}) copy-start(s32[4,4]{1,0:T(4,128)} %iota_add_fusion) | copy-start | bytes 196
  49.3 19.5 %collective-permute-start.11 = (bf16[20,64,256]{2,1,0:T(8,128)(2,1)}, bf16[20,64,256]{2,1,0:T(8,128)(2,1)}, u32[]{:S(2)}, u32[]{:S(2)}) collective-permute-start(bf16[20,64,256]{2,1,0:T(8,128)(2,1)} %get-tuple-element.14), channel_id=1, source_target_pairs={{0,64},{32,96},{64,0},{96,32},{1,65},{33,97},{65,1},{97,33},{2,66}... | collective-permute-start | bytes 1966088 | tf_op jit(solution)/shard_map/ppermute | solution.py:115
  49.8 31.4 %collective-permute-start.10 = (bf16[20,64,256]{2,1,0:T(8,128)(2,1)}, bf16[20,64,256]{2,1,0:T(8,128)(2,1)}, u32[]{:S(2)}, u32[]{:S(2)}) collective-permute-start(bf16[20,64,256]{2,1,0:T(8,128)(2,1)} %get-tuple-element.15), channel_id=1, source_target_pairs={{0,32},{32,64},{64,96},{96,0},{1,33},{33,65},{65,97},{97,1},{2,34}... | collective-permute-start | bytes 1966088 | tf_op jit(solution)/shard_map/ppermute | solution.py:115
  50.8 30.5 %collective-permute-start.12 = (bf16[20,64,256]{2,1,0:T(8,128)(2,1)}, bf16[20,64,256]{2,1,0:T(8,128)(2,1)}, u32[]{:S(2)}, u32[]{:S(2)}) collective-permute-start(bf16[20,64,256]{2,1,0:T(8,128)(2,1)} %get-tuple-element.16), channel_id=1, source_target_pairs={{0,96},{32,0},{64,32},{96,64},{1,97},{33,1},{65,33},{97,65},{2,98}... | collective-permute-start | bytes 1966088 | tf_op jit(solution)/shard_map/ppermute | solution.py:115
  57.3 12.3 %copy-start.20 = (s32[4]{0:T(128)S(1)}, s32[4]{0:T(128)}, u32[]{:S(2)}) copy-start(s32[4]{0:T(128)} %fusion.89) | copy-start | bytes 52
  60.1 32.2 %collective-permute-start.4 = (bf16[4,256,256]{2,1,0:T(8,128)(2,1)}, bf16[4,256,256]{2,1,0:T(8,128)(2,1)}, u32[]{:S(2)}, u32[]{:S(2)}) collective-permute-start(bf16[4,256,256]{2,1,0:T(8,128)(2,1)} %get-tuple-element.18), channel_id=1, source_target_pairs={{0,16},{8,24},{16,0},{24,8},{1,17},{9,25},{17,1},{25,9},{2,18},{10... | collective-permute-start | bytes 1572872 | tf_op jit(solution)/shard_map/ppermute | solution.py:115
  60.9 31.5 %collective-permute-start.3 = (bf16[4,256,256]{2,1,0:T(8,128)(2,1)}, bf16[4,256,256]{2,1,0:T(8,128)(2,1)}, u32[]{:S(2)}, u32[]{:S(2)}) collective-permute-start(bf16[4,256,256]{2,1,0:T(8,128)(2,1)} %get-tuple-element.19), channel_id=1, source_target_pairs={{0,8},{8,16},{16,24},{24,0},{1,9},{9,17},{17,25},{25,1},{2,10},{10... | collective-permute-start | bytes 1572872 | tf_op jit(solution)/shard_map/ppermute | solution.py:115
  68.8 23.5 %collective-permute-start.5 = (bf16[4,256,256]{2,1,0:T(8,128)(2,1)}, bf16[4,256,256]{2,1,0:T(8,128)(2,1)}, u32[]{:S(2)}, u32[]{:S(2)}) collective-permute-start(bf16[4,256,256]{2,1,0:T(8,128)(2,1)} %get-tuple-element.20), channel_id=1, source_target_pairs={{0,24},{8,0},{16,8},{24,16},{1,25},{9,1},{17,9},{25,17},{2,26},{10... | collective-permute-start | bytes 1572872 | tf_op jit(solution)/shard_map/ppermute | solution.py:115
  84.1 8.2 %copy-start.22 = (s32[4,1]{0,1:T(1,128)S(1)}, s32[4,1]{0,1:T(1,128)}, u32[]{:S(2)}) copy-start(s32[4,1]{0,1:T(1,128)} %copy-done.21) | copy-start | bytes 52
  84.1 8.2 %copy-start.24 = (s32[4]{0:T(128)S(1)}, s32[4]{0:T(128)}, u32[]{:S(2)}) copy-start(s32[4]{0:T(128)} %copy-done.23) | copy-start | bytes 52
  87.6 14.8 %all-to-all-start = ((bf16[8,4,16,448]{3,2,1,0:T(8,128)(2,1)}), bf16[8,4,16,448]{3,2,1,0:T(8,128)(2,1)S(1)}, u32[]{:S(2)}, u32[]{:S(2)}) async-start(bf16[8,4,16,448]{3,2,1,0:T(8,128)(2,1)} %broadcast_in_dim.36), calls=%async_computation | async-start | bytes 1048576 | tf_op jit(solution)/shard_map/all_to_all | solution.py:228
  92.0 81.8 %reduce-scatter.2.cloned.1.call-start = ((), (), s32[]{:S(2)}) async-start(), calls=%async_computation.3 | async-start | bytes 4128768 | tf_op jit(solution)/shard_map/reduce_scatter | solution.py:291
  102.4 3.9 %copy-start.14 = (f32[3584]{0:T(1024)S(1)}, f32[3584]{0:T(1024)}, u32[]{:S(2)}) copy-start(f32[3584]{0:T(1024)} %param.17) | copy-start | bytes 43012
  103.2 3.1 %copy-start.4 = (bf16[512,3584]{0,1:T(8,128)(2,1)S(1)}, bf16[512,3584]{0,1:T(8,128)(2,1)}, u32[]{:S(2)}) copy-start(bf16[512,3584]{0,1:T(8,128)(2,1)} %all-gather.2.cloned.1.call-done) | copy-start | bytes 11010052
  108.0 2.5 %copy-start.3 = (bf16[512,3584]{0,1:T(8,128)(2,1)}, bf16[512,3584]{0,1:T(8,128)(2,1)S(1)}, u32[]{:S(2)}) copy-start(bf16[512,3584]{0,1:T(8,128)(2,1)S(1)} %fusion.2) | copy-start | bytes 11010052
  108.0 1.2 copy-start.13
  108.0 1.2 copy-start.26
  108.0 2.8 %copy-start.28 = (bf16[3584,256]{1,0:T(8,128)(2,1)S(1)}, bf16[3584,256]{1,0:T(8,128)(2,1)}, u32[]{:S(2)}) copy-start(bf16[3584,256]{1,0:T(8,128)(2,1)} %param.20) | copy-start | bytes 5505028
  112.0 1.6 copy-start.10
  113.6 11.5 %collective-permute-start.6 = (bf16[256,512]{0,1:T(8,128)(2,1)}, bf16[256,512]{0,1:T(8,128)(2,1)}, u32[]{:S(2)}, u32[]{:S(2)}) collective-permute-start(bf16[256,512]{0,1:T(8,128)(2,1)} %pad_maximum_fusion.4), channel_id=1, source_target_pairs={{0,8},{8,16},{16,24},{24,32},{32,40},{40,48},{48,56},{56,64},{64,7... | collective-permute-start | bytes 786440 | tf_op jit(solution)/shard_map/ppermute | solution.py:17
  124.0 1.0 copy-start.6
  124.0 1.0 copy-start.7
  124.1 2.2 %copy-start.5 = (pred[512,1792]{0,1:T(8,128)(4,1)S(1)}, pred[512,1792]{0,1:T(8,128)(4,1)}, u32[]{:S(2)}) copy-start(pred[512,1792]{0,1:T(8,128)(4,1)} %pad_add_fusion) | copy-start | bytes 2752516
  124.1 2.2 %copy-start.9 = (bf16[512,256]{1,0:T(8,128)(2,1)S(1)}, bf16[512,256]{1,0:T(8,128)(2,1)}, u32[]{:S(2)}) copy-start(bf16[512,256]{1,0:T(8,128)(2,1)} %copy.58) | copy-start | bytes 786436
  128.9 1.7 copy-start.8
  128.9 1.7 copy-start.11
  130.7 2.5 %copy-start.27 = (bf16[512,3584]{1,0:T(8,128)(2,1)S(1)}, bf16[512,3584]{1,0:T(8,128)(2,1)}, u32[]{:S(2)}) copy-start(bf16[512,3584]{1,0:T(8,128)(2,1)} %param.21) | copy-start | bytes 11010052
  133.1 40.7 %copy-start.1 = (bf16[3584,256]{1,0:T(8,128)(2,1)S(1)}, bf16[3584,256]{1,0:T(8,128)(2,1)}, u32[]{:S(2)}) copy-start(bf16[3584,256]{1,0:T(8,128)(2,1)} %param.19) | copy-start | bytes 5505028
Sparse Core Ops, SparseCore 0:
  19.5 30.1 all-gather.1
  137.2 36.5 reduce-scatter.1

commit v7 on v2

--- a/solution.py
+++ b/solution.py
@@ -5,6 +5,7 @@
 
 HEAD_WIDTH = 256
 REQS = 4
+MOSTLEN = 256
 
 
 adapter_scale = 2.0
@@ -77,7 +78,12 @@
         & (jnp.arange(block, dtype=jnp.int32)[None, None, :] < cached[None, :, None])
     ).reshape(count, slots)
     place = jnp.arange(count, dtype=jnp.int32)
-    prev_ok = (split_flag == 1) & (request[:, None] == 0) & (place[None, :] >= count - prev_len)
+    kept = jnp.arange(prev_keys.shape[0], dtype=jnp.int32)
+    prev_ok = (
+        (split_flag == 1)
+        & (request[:, None] == 0)
+        & (kept[None, :] >= prev_keys.shape[0] - prev_len)
+    )
     own_ok = (request[:, None] == request[None, :]) & (place[None, :] <= place[:, None])
     allowed = jnp.concatenate([cache_ok, prev_ok, own_ok], 1)
     grouped = query_vectors.reshape(count, kv_heads, ratio, head_size)
@@ -121,18 +127,17 @@
     owner_a = (owner // SIDE, owner % SIDE)[first == "gz"]
     owner_b = (owner // SIDE, owner % SIDE)[second == "gz"]
     source = ((own_a - owner_a[askers]) % SIDE) * per_owner + (wanted % per_owner)[askers]
-    pieces = [jnp.take(held, source[0], axis=0, mode="clip")] + [
-        ring_send(jnp.take(held, source[step], axis=0, mode="clip"), second, step)
+    outgoing = jnp.take(held, source.reshape(-1), axis=0, mode="clip")
+    pieces = [outgoing[:slots]] + [
+        ring_send(outgoing[step * slots:(step + 1) * slots], second, step)
         for step in range(1, SIDE)
     ]
-    came = (own_b - owner_b[me]) % SIDE
-    return pick_piece(came, pieces)
+    return pick_piece((own_b - owner_b[me]) % SIDE, pieces)
 
 
 def pick_piece(came, pieces):
     which = came.reshape(came.shape + (1,) * (pieces[0].ndim - 1))
-    which = jnp.broadcast_to(which, pieces[0].shape)
-    return lax.select_n(which, *pieces)
+    return lax.select_n(jnp.broadcast_to(which, pieces[0].shape), *pieces)
 
 
 def route_with_adapters(blocks, adapters, block_wanted, adapter_wanted, first, second):
@@ -168,8 +173,10 @@
     source = jnp.concatenate(
         [block_items.reshape(SIDE, -1), adapter_items.reshape(SIDE, -1)], axis=1
     )
-    parts = [jnp.take(held, source[0], axis=0, mode="clip")] + [
-        ring_send(jnp.take(held, source[step], axis=0, mode="clip"), second, step)
+    width = source.shape[1]
+    outgoing = jnp.take(held, source.reshape(-1), axis=0, mode="clip")
+    parts = [outgoing[:width]] + [
+        ring_send(outgoing[step * width:(step + 1) * width], second, step)
         for step in range(1, SIDE)
     ]
     slots = block_wanted.shape[1]
@@ -177,8 +184,8 @@
         [jnp.repeat((own_b - block_b[me]) % SIDE, pieces), (own_b - adapter_b[me]) % SIDE]
     )
     merged = pick_piece(came, parts)
-    chosen_blocks = merged[: slots * adapters.shape[0]].reshape(slots, rows, lanes)
-    chosen_adapters = merged[slots * adapters.shape[0]:].reshape(slots, -1)
+    chosen_blocks = merged[: slots * pieces].reshape(slots, rows, lanes)
+    chosen_adapters = merged[slots * pieces:].reshape(slots, -1)
     chosen_adapters = chosen_adapters[:, : flat.shape[1]].reshape(slots, *adapters.shape[1:])
     return chosen_blocks, chosen_adapters
 
@@ -258,7 +265,8 @@
     values = jnp.dot(normalized_input, value_weight, preferred_element_type=jnp.float32).astype(
         jnp.bfloat16
     )
-    prev_both = shifted(jnp.concatenate([keys, values], axis=1), ("gx", "gz"), 1)
+    tail = count - MOSTLEN
+    prev_both = shifted(jnp.concatenate([keys[tail:], values[tail:]], axis=1), ("gx", "gz"), 1)
     prev_keys, prev_values = prev_both[:, : keys.shape[1]], prev_both[:, keys.shape[1]:]
     attended = attend(
         query_vectors,

time: 219 us -> 185 us (0.84)
  local copies, waits for them, and re-layouts: 54.1 us -> 37 us
  waiting for transfers between devices: 72.8 us -> 66 us
  other arithmetic: 27.2 us -> 22.5 us
  starting transfers between devices: 26.2 us -> 21.7 us
    gather x8 -> x2, local copies, waits for them, and re-layouts: 17.7 us -> 4.53 us  [the longest x1 2.44 us: route_with_adapters(): outgoing = jnp.take(held, source.reshape(-1), axis=0, mode='clip')]
    ppermute x12, waiting for transfers between devices: 34.2 us -> 25.7 us  [ring_send(): lax.ppermute(value, axis, [(i, (i + step) % SIDE) for i in range(SIDE)])]
    slice x2 -> x5, local copies, waits for them, and re-layouts: 0.01 us -> 5.48 us  [the longest x1 2.96 us: route_with_adapters(): outgoing[step * width:(step + 1) * width]]
    gather x8 -> x2, other arithmetic: 4.94 us -> 0.01 us  [the longest x1 0.01 us: route_with_adapters(): outgoing = jnp.take(held, source.reshape(-1), axis=0, mode='clip')]
    all_to_all x1, waiting for transfers between devices: 0.01 us -> 4.37 us  [on_device(): lax.all_to_all(jnp.broadcast_to(chosen_down, (model_count, *chosen_down.s...]
    unnamed x61 -> x62, local copies, waits for them, and re-layouts: 14.4 us -> 10.3 us
    ppermute x12, starting transfers between devices: 17.9 us -> 14.9 us  [ring_send(): lax.ppermute(value, axis, [(i, (i + step) % SIDE) for i in range(SIDE)])]
    reduce_scatter x1, waiting for transfers between devices: 38.6 us -> 35.8 us  [on_device(): lax.psum_scatter(partial_out.astype(jnp.bfloat16), ('my', 'mc'), scatter_...]
  transfers between devices with their start and end apart: 16 -> 16, of which waited for: 4 -> 6; matrix products, arithmetic and copies ran while one was open for 35% -> 31% of each run, Pallas kernels for 0% -> 0%
where the time goes in v7:
time: 185 us
  waiting for transfers between devices  66 us (36%)
  local copies, waits for them, and re-layouts  37 us (20%)
  other arithmetic  22.5 us (12%)
  starting transfers between devices  21.7 us (12%)
  matrix products  20.9 us (11%)
  between operations  16.6 us (9%)
    reduce_scatter x1, waiting for transfers between devices, on_device(): lax.psum_scatter(partial_out.astype(jnp.bfloat16), ('my', 'mc'), scatter_...  35.8 us
    ppermute x12, waiting for transfers between devices, ring_send(): lax.ppermute(value, axis, [(i, (i + step) % SIDE) for i in range(SIDE)])  25.7 us
    ppermute x12, starting transfers between devices, ring_send(): lax.ppermute(value, axis, [(i, (i + step) % SIDE) for i in range(SIDE)])  14.9 us
    unnamed x62, local copies, waits for them, and re-layouts  10.3 us
    dot_general x1, matrix products, on_device(): jnp.dot(normalized_input, query_weight, preferred_element_type=jnp.float32)  6.23 us
    select_n x6, other arithmetic, pick_piece(): return lax.select_n(jnp.broadcast_to(which, pieces[0].shape), *pieces)  5.43 us
    all_to_all x1, starting transfers between devices, on_device(): lax.all_to_all(jnp.broadcast_to(chosen_down, (model_count, *chosen_down.s...  4.41 us
    all_to_all x1, waiting for transfers between devices, on_device(): lax.all_to_all(jnp.broadcast_to(chosen_down, (model_count, *chosen_down.s...  4.37 us
  transfers between devices with their start and end apart: 16, of which 6 were waited for; matrix products, arithmetic and copies ran while one was open for 31% of the time, Pallas kernels for 0%

profile of v7, /device:TPU:0, one launch (start us, length us, event | category | flops | bytes accessed | tf_op | source)
XLA Modules:
  0.0 184.6 jit_solution(12886294805341199631)
XLA Ops:
  6.5 3.1 %collective-permute-start.1 = (bf16[2,256,256]{2,1,0:T(8,128)(2,1)}, bf16[2,256,256]{2,1,0:T(8,128)(2,1)}, u32[]{:S(2)}, u32[]{:S(2)}) collective-permute-start(bf16[2,256,256]{2,1,0:T(8,128)(2,1)} %param.31), channel_id=1, source_target_pairs={{0,64},{32,96},{64,0},{96,32},{1,65},{33,97},{65,1},{97,33},{2,66}... | collective-permute-start | bytes 786440 | tf_op jit(solution)/shard_map/ppermute | solution.py:115
  9.6 0.6 collective-permute-start
  10.2 1.0 pad_maximum_fusion.3
  11.5 1.7 constant_dynamic-update-slice_fusion.1
  13.2 0.7 constant_dynamic-update-slice_fusion
  13.9 4.0 %collective-permute-start.9 = (bf16[3,256,256]{2,1,0:T(8,128)(2,1)}, bf16[3,256,256]{2,1,0:T(8,128)(2,1)}, u32[]{:S(2)}, u32[]{:S(2)}) collective-permute-start(bf16[3,256,256]{2,1,0:T(8,128)(2,1)} %get-tuple-element.33), channel_id=1, source_target_pairs={{0,24},{8,0},{16,8},{24,16},{1,25},{9,1},{17,9},{25,17},{2,26},{10... | collective-permute-start | bytes 1179656 | tf_op jit(solution)/shard_map/ppermute | solution.py:115
  17.9 1.3 collective-permute-start.7
  19.3 0.8 copy.54
  20.2 0.8 gather_fusion.3
  21.1 0.6 constant_dynamic-slice_fusion.7
  22.3 0.7 dynamic_slice.24
  25.6 0.6 gather_fusion
  26.1 0.6 gather_fusion.1
  26.7 0.6 gather_fusion.5
  28.6 0.6 gather_fusion.6
  31.1 1.3 pad_add_fusion
  32.5 0.6 broadcast_compare_fusion.6
  33.1 4.8 %collective-permute-done.7 = bf16[3,256,256]{2,1,0:T(8,128)(2,1)} collective-permute-done((bf16[3,256,256]{2,1,0:T(8,128)(2,1)}, bf16[3,256,256]{2,1,0:T(8,128)(2,1)}, u32[]{:S(2)}, u32[]{:S(2)}) %collective-permute-start.7) | collective-permute-done | bytes 393248 | tf_op jit(solution)/shard_map/ppermute | solution.py:115
  37.9 2.6 %collective-permute-start.2 = (bf16[2,256,256]{2,1,0:T(8,128)(2,1)}, bf16[2,256,256]{2,1,0:T(8,128)(2,1)}, u32[]{:S(2)}, u32[]{:S(2)}) collective-permute-start(bf16[2,256,256]{2,1,0:T(8,128)(2,1)} %param.31), channel_id=1, source_target_pairs={{0,96},{32,0},{64,32},{96,64},{1,97},{33,1},{65,33},{97,65},{2,98}... | collective-permute-start | bytes 786440 | tf_op jit(solution)/shard_map/ppermute | solution.py:115
  40.5 1.0 constant_dynamic-update-slice_fusion.4
  41.6 1.0 constant_dynamic-update-slice_fusion.3
  42.6 1.0 constant_dynamic-update-slice_fusion.2
  43.7 2.4 %gather_fusion.8 = bf16[80,64,256]{2,1,0:T(8,128)(2,1)} fusion(bf16[48,64,256]{2,1,0:T(8,128)(2,1)S(1)} %bitcast.110, s32[1024]{0:T(1024)S(1)} %pad_clamp_fusion), kind=kCustom, calls=%fused_computation.8 | custom fusion | bytes 5243200 | tf_op jit(solution)/shard_map/jit(_take)/gather | solution.py:177
  46.1 3.0 %fusion.88 = (bf16[20,64,256]{2,1,0:T(8,128)(2,1)}, bf16[20,64,256]{2,1,0:T(8,128)(2,1)}, bf16[20,64,256]{2,1,0:T(8,128)(2,1)}) fusion(bf16[80,64,256]{2,1,0:T(8,128)(2,1)} %gather_fusion.8), kind=kLoop, calls=%fused_computation.218 | loop fusion | bytes 3932160 | tf_op jit(solution)/shard_map/slice | solution.py:179
  49.1 1.3 collective-permute-start.11
  50.5 0.6 collective-permute-start.10
  51.1 1.8 multiply_cosine_fusion
  52.9 1.2 pad_maximum_fusion
  54.2 2.1 %gather_fusion.2 = bf16[16,256,256]{2,1,0:T(8,128)(2,1)} fusion(bf16[8,256,256]{2,1,0:T(8,128)(2,1)S(1)} %pad_maximum_fusion, s32[1024]{0:T(1024)S(1)} %pad_clamp_fusion.3), kind=kCustom, calls=%fused_computation.2 | custom fusion | bytes 4194368 | tf_op jit(solution)/shard_map/jit(_take)/gather | solution.py:130
  56.3 2.5 %fusion.89 = (bf16[4,256,256]{2,1,0:T(8,128)(2,1)}, bf16[4,256,256]{2,1,0:T(8,128)(2,1)}, bf16[4,256,256]{2,1,0:T(8,128)(2,1)}) fusion(bf16[16,256,256]{2,1,0:T(8,128)(2,1)} %gather_fusion.2), kind=kLoop, calls=%fused_computation.219 | loop fusion | bytes 3145728 | tf_op jit(solution)/shard_map/slice | solution.py:132
  58.8 0.9 collective-permute-start.5
  60.0 6.9 %collective-permute-done.12 = bf16[20,64,256]{2,1,0:T(8,128)(2,1)S(1)} collective-permute-done((bf16[20,64,256]{2,1,0:T(8,128)(2,1)}, bf16[20,64,256]{2,1,0:T(8,128)(2,1)S(1)}, u32[]{:S(2)}, u32[]{:S(2)}) %collective-permute-start.12) | collective-permute-done | bytes 655392 | tf_op jit(solution)/shard_map/ppermute | solution.py:115
  67.0 1.7 collective-permute-done.11
  68.7 12.3 %collective-permute-done.10 = bf16[20,64,256]{2,1,0:T(8,128)(2,1)} collective-permute-done((bf16[20,64,256]{2,1,0:T(8,128)(2,1)}, bf16[20,64,256]{2,1,0:T(8,128)(2,1)}, u32[]{:S(2)}, u32[]{:S(2)}) %collective-permute-start.10) | collective-permute-done | bytes 655392 | tf_op jit(solution)/shard_map/ppermute | solution.py:115
  81.0 1.9 %fusion.27 = bf16[20,64,256]{2,1,0:T(8,128)(2,1)S(1)} fusion(bf16[20,64,256]{2,1,0:T(8,128)(2,1)} %collective-permute-done.10, bf16[80,64,256]{2,1,0:T(8,128)(2,1)} %gather_fusion.8, bf16[20,64,256]{2,1,0:T(8,128)(2,1)} %collective-permute-done.11, bf16[20,64,256]{2,1,0:T(8,128)(2,1)} %copy-done.6, pred[20]{0:T(512)(128)(4,1)} %get-tuple-element.45, ...), kind=kLoop, calls=%fused_computation.48 | loop fusion | flops 983040 | bytes 3276860 | tf_op jit(solution)/shard_map/select_n | solution.py:140
  83.3 0.9 broadcast_in_dim.51
  84.2 4.4 %all-to-all-start = ((bf16[8,4,16,448]{3,2,1,0:T(8,128)(2,1)}), bf16[8,4,16,448]{3,2,1,0:T(8,128)(2,1)S(1)}, u32[]{:S(2)}, u32[]{:S(2)}) async-start(bf16[8,4,16,448]{3,2,1,0:T(8,128)(2,1)} %broadcast_in_dim.51), calls=%async_computation | async-start | bytes 1048576 | tf_op jit(solution)/shard_map/all_to_all | solution.py:223
  88.8 0.6 broadcast_compare_fusion.5
  89.4 0.8 copy-done.9
  90.2 1.7 fusion.28
  91.9 1.0 copy.65
  93.0 1.6 slice.125
  94.6 4.4 %all-to-all-done = bf16[8,4,16,448]{3,2,1,0:T(8,128)(2,1)S(1)} async-done(((bf16[8,4,16,448]{3,2,1,0:T(8,128)(2,1)}), bf16[8,4,16,448]{3,2,1,0:T(8,128)(2,1)S(1)}, u32[]{:S(2)}, u32[]{:S(2)}) %all-to-all-start) | async-done | bytes 458784 | tf_op jit(solution)/shard_map/all_to_all | solution.py:223
  99.2 0.6 dot_general.31
  99.8 3.0 %fusion = f32[512]{0:T(512)S(1)} fusion(bf16[512,3584]{0,1:T(8,128)(2,1)} %all-gather.2.cloned.1.call-done), kind=kLoop, calls=%fused_computation.11 | loop fusion | flops 5504512 | bytes 3672064 | tf_op jit(solution)/shard_map/reduce_sum | solution.py:237
  103.0 1.6 fusion.2
  104.6 1.2 convolution_bitcast_fusion
  105.7 1.2 fusion.38
  107.4 1.2 convolution_convert_fusion.1
  108.6 0.9 copy.58
  109.4 0.7 pad_maximum_fusion.2
  110.2 2.1 %collective-permute-start.6 = (bf16[256,512]{0,1:T(8,128)(2,1)}, bf16[256,512]{0,1:T(8,128)(2,1)}, u32[]{:S(2)}, u32[]{:S(2)}) collective-permute-start(bf16[256,512]{0,1:T(8,128)(2,1)} %pad_maximum_fusion.2), channel_id=1, source_target_pairs={{0,8},{8,16},{16,24},{24,32},{32,40},{40,48},{48,56},{56,64},{64,7... | collective-permute-start | bytes 786440 | tf_op jit(solution)/shard_map/ppermute | solution.py:17
  112.3 6.2 %fusion.92 = f32[512,512]{0,1:T(8,128)} fusion(bf16[512,3584]{0,1:T(8,128)(2,1)} %copy-done.2, bf16[3584,512]{1,0:T(8,128)(2,1)} %param.18), kind=kOutput, calls=%fused_computation.222 | convolution fusion | flops 1879048192 | bytes 8388608 | tf_op jit(solution)/shard_map/dot_general | solution.py:256
  118.5 3.3 %fusion.13 = f32[512,512]{0,1:T(8,128)S(1)} fusion(f32[512,512]{0,1:T(8,128)} %fusion.92, bf16[64,512]{1,0:T(8,128)(2,1)S(1)} %bitcast.116, bf16[512,64]{0,1:T(8,128)(2,1)S(1)} %bitcast.117, bf16[64,3584]{1,0:T(8,128)(2,1)S(1)} %dot_general.31, bf16[512,3584]{0,1:T(8,128)(2,1)} %copy-done.2), kind=kOutput, calls=%fused_computation.27 | convolution fusion | flops 269025280 | bytes 6356992 | tf_op jit(solution)/shard_map/dot_general | solution.py:250
  121.9 1.1 fusion.90
  123.0 2.1 %copy.68 = f32[512,2,128]{2,0,1:T(8,128)} copy(f32[512,2,128]{0,2,1:T(8,128)} %get-tuple-element.25) | data formatting | bytes 1048576
  125.1 2.0 %copy.67 = f32[512,2,128]{2,0,1:T(8,128)} copy(f32[512,2,128]{0,2,1:T(8,128)} %get-tuple-element.26) | data formatting | bytes 1048576
  127.1 2.3 %subtract_convert_fusion = (bf16[512,2,128]{2,0,1:T(8,128)(2,1)}, bf16[512,2,128]{2,0,1:T(8,128)(2,1)}) fusion(f32[512,2,128]{2,0,1:T(8,128)} %copy.68, f32[512,2,128]{2,0,1:T(8,128)} %copy.67, f32[512,128]{1,0:T(8,128)} %get-tuple-element.41, f32[512,128]{1,0:T(8,128)} %get-tuple-element.40), kind=kLoop, calls=%fused_computation.55 | loop fusion | flops 1048576 | bytes 2097152 | tf_op jit(solution)/shard_map/convert
  129.4 1.6 fusion.91
  131.2 2.7 %fusion.5 = (f32[2,512]{1,0:T(2,128)S(1)}, f32[1792,512,2]{1,0,2:T(8,128)S(1)}) fusion(pred[512,1792]{0,1:T(8,128)(4,1)S(1)} %copy-done.4, bf16[512,2,128]{2,0,1:T(8,128)(2,1)} %get-tuple-element.24, bf16[512,2,128]{2,0,1:T(8,128)(2,1)} %get-tuple-element.23, bf16[512,256]{1,0:T(8,128)(2,1)} %copy.58, bf16[256,256]{1,0:T(8,128)(2,1)S(1)} %copy.57, ...), kind=kOutput, calls=%fused_computation.19 | convolution fusion | flops 948829184 | bytes 9703424 | tf_op jit(solution)/shard_map/tkrd,skd->krts/dot_general | solution.py:90
  133.9 1.7 fusion.3
  135.6 2.4 %divide_convert_fusion = bf16[512,1,2,256]{0,3,2,1:T(8,128)(2,1)S(1)} fusion(f32[1792,512,2]{1,0,2:T(8,128)S(1)} %get-tuple-element.47, f32[2,512]{1,0:T(2,128)S(1)} %get-tuple-element.46, pred[512,1792]{0,1:T(8,128)(4,1)S(1)} %copy-done.4, bf16[512,256]{0,1:T(8,128)(2,1)S(1)} %copy-done.14, bf16[256,256]{0,1:T(8,128)(2,1)S(1)} %copy-done.12, ...), kind=kOutput, calls=%fused_computation.33 | convolution fusion | flops 950140928 | bytes 9707520 | tf_op jit(solution)/shard_map/krts,skd->tkrd/dot_general | solution.py:97
  138.1 3.9 %convolution_convert_fusion = bf16[512,3584]{0,1:T(8,128)(2,1)} fusion(bf16[512,512]{0,1:T(8,128)(2,1)S(1)} %bitcast.124, bf16[512,3584]{1,0:T(8,128)(2,1)S(1)} %copy-done.22), kind=kOutput, calls=%fused_computation.18 | convolution fusion | flops 1880883200 | bytes 7864320 | tf_op jit(solution)/shard_map/dot_general | solution.py:285
  142.0 35.8 %reduce-scatter.2.cloned.1.call-done = bf16[512,448]{0,1:T(8,128)(2,1)} async-done(((bf16[512,3584]{0,1:T(8,128)(2,1)}), bf16[512,448]{0,1:T(8,128)(2,1)}) %reduce-scatter.2.cloned.1.call-update) | async-done | bytes 458768 | tf_op jit(solution)/shard_map/reduce_scatter | solution.py:286
  (136 shorter events, 6.7 us)
Async XLA Ops:
  6.5 98.0 %copy-start = (bf16[3584,256]{1,0:T(8,128)(2,1)S(1)}, bf16[3584,256]{1,0:T(8,128)(2,1)}, u32[]{:S(2)}) copy-start(bf16[3584,256]{1,0:T(8,128)(2,1)} %param.19) | copy-start | bytes 5505028
  6.5 13.6 %copy-start.1 = (s32[64]{0:T(128)S(1)}, s32[64]{0:T(128)}, u32[]{:S(2)}) copy-start(s32[64]{0:T(128)} %param.25) | copy-start | bytes 772
  6.5 93.3 %all-gather.2.cloned.1.call-start = ((), (), s32[]{:S(2)}) async-start(), calls=%async_computation.2 | async-start | bytes 4128768 | tf_op jit(solution)/shard_map/all_gather | solution.py:234
  6.5 43.9 %collective-permute-start.1 = (bf16[2,256,256]{2,1,0:T(8,128)(2,1)}, bf16[2,256,256]{2,1,0:T(8,128)(2,1)}, u32[]{:S(2)}, u32[]{:S(2)}) collective-permute-start(bf16[2,256,256]{2,1,0:T(8,128)(2,1)} %param.31), channel_id=1, source_target_pairs={{0,64},{32,96},{64,0},{96,32},{1,65},{33,97},{65,1},{97,33},{2,66}... | collective-permute-start | bytes 786440 | tf_op jit(solution)/shard_map/ppermute | solution.py:115
  9.6 43.3 %collective-permute-start = (bf16[2,256,256]{2,1,0:T(8,128)(2,1)}, bf16[2,256,256]{2,1,0:T(8,128)(2,1)}, u32[]{:S(2)}, u32[]{:S(2)}) collective-permute-start(bf16[2,256,256]{2,1,0:T(8,128)(2,1)} %param.31), channel_id=1, source_target_pairs={{0,32},{32,64},{64,96},{96,0},{1,33},{33,65},{65,97},{97,1},{2,34}... | collective-permute-start | bytes 786440 | tf_op jit(solution)/shard_map/ppermute | solution.py:115
  13.9 28.7 %collective-permute-start.9 = (bf16[3,256,256]{2,1,0:T(8,128)(2,1)}, bf16[3,256,256]{2,1,0:T(8,128)(2,1)}, u32[]{:S(2)}, u32[]{:S(2)}) collective-permute-start(bf16[3,256,256]{2,1,0:T(8,128)(2,1)} %get-tuple-element.33), channel_id=1, source_target_pairs={{0,24},{8,0},{16,8},{24,16},{1,25},{9,1},{17,9},{25,17},{2,26},{10... | collective-permute-start | bytes 1179656 | tf_op jit(solution)/shard_map/ppermute | solution.py:115
  17.9 23.6 %collective-permute-start.8 = (bf16[3,256,256]{2,1,0:T(8,128)(2,1)}, bf16[3,256,256]{2,1,0:T(8,128)(2,1)}, u32[]{:S(2)}, u32[]{:S(2)}) collective-permute-start(bf16[3,256,256]{2,1,0:T(8,128)(2,1)} %get-tuple-element.33), channel_id=1, source_target_pairs={{0,16},{8,24},{16,0},{24,8},{1,17},{9,25},{17,1},{25,9},{2,18},{10... | collective-permute-start | bytes 1179656 | tf_op jit(solution)/shard_map/ppermute | solution.py:115
  17.9 20.0 %collective-permute-start.7 = (bf16[3,256,256]{2,1,0:T(8,128)(2,1)}, bf16[3,256,256]{2,1,0:T(8,128)(2,1)}, u32[]{:S(2)}, u32[]{:S(2)}) collective-permute-start(bf16[3,256,256]{2,1,0:T(8,128)(2,1)} %get-tuple-element.33), channel_id=1, source_target_pairs={{0,8},{8,16},{16,24},{24,0},{1,9},{9,17},{17,25},{25,1},{2,10},{10... | collective-permute-start | bytes 1179656 | tf_op jit(solution)/shard_map/ppermute | solution.py:115
  20.2 1.0 copy-start.17
  20.2 2.1 %copy-start.24 = (s32[16]{0:T(128)S(1)}, s32[16]{0:T(128)}, u32[]{:S(2)}) copy-start(s32[16]{0:T(128)} %param.27) | copy-start | bytes 196
  20.2 4.8 %copy-start.16 = (s32[16,4]{0,1:T(4,128)S(1)}, s32[16,4]{0,1:T(4,128)}, u32[]{:S(2)}) copy-start(s32[16,4]{0,1:T(4,128)} %param.29) | copy-start | bytes 772
  20.2 5.3 %copy-start.18 = (s32[16,4]{0,1:T(4,128)S(1)}, s32[16,4]{0,1:T(4,128)}, u32[]{:S(2)}) copy-start(s32[16,4]{0,1:T(4,128)} %param.28) | copy-start | bytes 772
  37.9 15.0 %collective-permute-start.2 = (bf16[2,256,256]{2,1,0:T(8,128)(2,1)}, bf16[2,256,256]{2,1,0:T(8,128)(2,1)}, u32[]{:S(2)}, u32[]{:S(2)}) collective-permute-start(bf16[2,256,256]{2,1,0:T(8,128)(2,1)} %param.31), channel_id=1, source_target_pairs={{0,96},{32,0},{64,32},{96,64},{1,97},{33,1},{65,33},{97,65},{2,98}... | collective-permute-start | bytes 786440 | tf_op jit(solution)/shard_map/ppermute | solution.py:115
  46.1 6.8 %copy-start.11 = (bf16[2,256,256]{2,1,0:T(8,128)(2,1)S(1)}, bf16[2,256,256]{2,1,0:T(8,128)(2,1)}, u32[]{:S(2)}) copy-start(bf16[2,256,256]{2,1,0:T(8,128)(2,1)} %param.31) | copy-start | bytes 786436
  49.1 17.9 %collective-permute-start.12 = (bf16[20,64,256]{2,1,0:T(8,128)(2,1)}, bf16[20,64,256]{2,1,0:T(8,128)(2,1)S(1)}, u32[]{:S(2)}, u32[]{:S(2)}) collective-permute-start(bf16[20,64,256]{2,1,0:T(8,128)(2,1)} %get-tuple-element.17), channel_id=1, source_target_pairs={{0,96},{32,0},{64,32},{96,64},{1,97},{33,1},{65,33},{97,65},{2,98}... | collective-permute-start | bytes 1966088 | tf_op jit(solution)/shard_map/ppermute | solution.py:115
  49.1 19.5 %collective-permute-start.11 = (bf16[20,64,256]{2,1,0:T(8,128)(2,1)}, bf16[20,64,256]{2,1,0:T(8,128)(2,1)}, u32[]{:S(2)}, u32[]{:S(2)}) collective-permute-start(bf16[20,64,256]{2,1,0:T(8,128)(2,1)} %get-tuple-element.18), channel_id=1, source_target_pairs={{0,64},{32,96},{64,0},{96,32},{1,65},{33,97},{65,1},{97,33},{2,66}... | collective-permute-start | bytes 1966088 | tf_op jit(solution)/shard_map/ppermute | solution.py:115
  50.5 30.5 %collective-permute-start.10 = (bf16[20,64,256]{2,1,0:T(8,128)(2,1)}, bf16[20,64,256]{2,1,0:T(8,128)(2,1)}, u32[]{:S(2)}, u32[]{:S(2)}) collective-permute-start(bf16[20,64,256]{2,1,0:T(8,128)(2,1)} %get-tuple-element.19), channel_id=1, source_target_pairs={{0,32},{32,64},{64,96},{96,0},{1,33},{33,65},{65,97},{97,1},{2,34}... | collective-permute-start | bytes 1966088 | tf_op jit(solution)/shard_map/ppermute | solution.py:115
  51.1 1.8 copy-start.19
  58.8 31.4 %copy-start.21 = (pred[4]{0:T(512)(128)(4,1)S(1)}, pred[4]{0:T(512)(128)(4,1)}, u32[]{:S(2)}) copy-start(pred[4]{0:T(512)(128)(4,1)} %get-tuple-element.8) | copy-start | bytes 16
  58.8 30.6 %collective-permute-start.5 = (bf16[4,256,256]{2,1,0:T(8,128)(2,1)}, bf16[4,256,256]{2,1,0:T(8,128)(2,1)S(1)}, u32[]{:S(2)}, u32[]{:S(2)}) collective-permute-start(bf16[4,256,256]{2,1,0:T(8,128)(2,1)} %get-tuple-element.20), channel_id=1, source_target_pairs={{0,24},{8,0},{16,8},{24,16},{1,25},{9,1},{17,9},{25,17},{2,26},{10... | collective-permute-start | bytes 1572872 | tf_op jit(solution)/shard_map/ppermute | solution.py:115
  59.7 29.8 %collective-permute-start.4 = (bf16[4,256,256]{2,1,0:T(8,128)(2,1)}, bf16[4,256,256]{2,1,0:T(8,128)(2,1)}, u32[]{:S(2)}, u32[]{:S(2)}) collective-permute-start(bf16[4,256,256]{2,1,0:T(8,128)(2,1)} %get-tuple-element.21), channel_id=1, source_target_pairs={{0,16},{8,24},{16,0},{24,8},{1,17},{9,25},{17,1},{25,9},{2,18},{10... | collective-permute-start | bytes 1572872 | tf_op jit(solution)/shard_map/ppermute | solution.py:115
  66.9 14.1 %copy-start.6 = (bf16[20,64,256]{2,1,0:T(8,128)(2,1)}, bf16[20,64,256]{2,1,0:T(8,128)(2,1)S(1)}, u32[]{:S(2)}) copy-start(bf16[20,64,256]{2,1,0:T(8,128)(2,1)S(1)} %collective-permute-done.12) | copy-start | bytes 1966084
  67.0 22.5 %collective-permute-start.3 = (bf16[4,256,256]{2,1,0:T(8,128)(2,1)}, bf16[4,256,256]{2,1,0:T(8,128)(2,1)}, u32[]{:S(2)}, u32[]{:S(2)}) collective-permute-start(bf16[4,256,256]{2,1,0:T(8,128)(2,1)} %get-tuple-element.22), channel_id=1, source_target_pairs={{0,8},{8,16},{16,24},{24,0},{1,9},{9,17},{17,25},{25,1},{2,10},{10... | collective-permute-start | bytes 1572872 | tf_op jit(solution)/shard_map/ppermute | solution.py:115
  82.9 10.1 %copy-start.5 = (bf16[20,64,256]{2,1,0:T(8,128)(2,1)}, bf16[20,64,256]{2,1,0:T(8,128)(2,1)S(1)}, u32[]{:S(2)}) copy-start(bf16[20,64,256]{2,1,0:T(8,128)(2,1)S(1)} %fusion.27) | copy-start | bytes 1966084
  83.3 0.9 copy-start.8
  84.2 14.8 %all-to-all-start = ((bf16[8,4,16,448]{3,2,1,0:T(8,128)(2,1)}), bf16[8,4,16,448]{3,2,1,0:T(8,128)(2,1)S(1)}, u32[]{:S(2)}, u32[]{:S(2)}) async-start(bf16[8,4,16,448]{3,2,1,0:T(8,128)(2,1)} %broadcast_in_dim.51), calls=%async_computation | async-start | bytes 1048576 | tf_op jit(solution)/shard_map/all_to_all | solution.py:223
  88.6 89.2 %reduce-scatter.2.cloned.1.call-start = ((), (), s32[]{:S(2)}) async-start(), calls=%async_computation.3 | async-start | bytes 4128768 | tf_op jit(solution)/shard_map/reduce_scatter | solution.py:286
  89.4 0.8 copy-start.9
  94.5 8.3 %copy-start.15 = (f32[3584]{0:T(1024)S(1)}, f32[3584]{0:T(1024)}, u32[]{:S(2)}) copy-start(f32[3584]{0:T(1024)} %param.17) | copy-start | bytes 43012
  99.8 3.1 %copy-start.3 = (bf16[512,3584]{0,1:T(8,128)(2,1)S(1)}, bf16[512,3584]{0,1:T(8,128)(2,1)}, u32[]{:S(2)}) copy-start(bf16[512,3584]{0,1:T(8,128)(2,1)} %all-gather.2.cloned.1.call-done) | copy-start | bytes 11010052
  104.5 2.4 %copy-start.2 = (bf16[512,3584]{0,1:T(8,128)(2,1)}, bf16[512,3584]{0,1:T(8,128)(2,1)S(1)}, u32[]{:S(2)}) copy-start(bf16[512,3584]{0,1:T(8,128)(2,1)S(1)} %fusion.2) | copy-start | bytes 11010052
  104.5 1.2 copy-start.20
  104.6 2.8 %copy-start.23 = (bf16[3584,256]{1,0:T(8,128)(2,1)S(1)}, bf16[3584,256]{1,0:T(8,128)(2,1)}, u32[]{:S(2)}) copy-start(bf16[3584,256]{1,0:T(8,128)(2,1)} %param.20) | copy-start | bytes 5505028
  108.5 10.0 %copy-start.13 = (bf16[512,256]{0,1:T(8,128)(2,1)}, bf16[512,256]{0,1:T(8,128)(2,1)S(1)}, u32[]{:S(2)}) copy-start(bf16[512,256]{0,1:T(8,128)(2,1)S(1)} %convolution_convert_fusion.1) | copy-start | bytes 786436
  110.2 8.4 %copy-start.10 = (bf16[4,16,512]{2,1,0:T(8,128)(2,1)S(1)}, bf16[4,16,512]{2,1,0:T(8,128)(2,1)}, u32[]{:S(2)}) copy-start(bf16[4,16,512]{2,1,0:T(8,128)(2,1)} %slice.125) | copy-start | bytes 196612
  110.2 19.2 %collective-permute-start.6 = (bf16[256,512]{0,1:T(8,128)(2,1)}, bf16[256,512]{0,1:T(8,128)(2,1)}, u32[]{:S(2)}, u32[]{:S(2)}) collective-permute-start(bf16[256,512]{0,1:T(8,128)(2,1)} %pad_maximum_fusion.2), channel_id=1, source_target_pairs={{0,8},{8,16},{16,24},{24,32},{32,40},{40,48},{48,56},{56,64},{64,7... | collective-permute-start | bytes 786440 | tf_op jit(solution)/shard_map/ppermute | solution.py:17
  121.9 9.3 %slice-start = ((bf16[20,64,256]{2,1,0:T(8,128)(2,1)}), bf16[16,64,256]{2,1,0:T(8,128)(2,1)S(1)}, s32[]{:S(2)}) async-start(bf16[20,64,256]{2,1,0:T(8,128)(2,1)} %copy-done.5), calls=%async_computation.4 | async-start | bytes 1048576 | tf_op jit(solution)/shard_map/slice | solution.py:187
  122.9 8.2 %copy-start.4 = (pred[512,1792]{0,1:T(8,128)(4,1)S(1)}, pred[512,1792]{0,1:T(8,128)(4,1)}, u32[]{:S(2)}) copy-start(pred[512,1792]{0,1:T(8,128)(4,1)} %pad_add_fusion) | copy-start | bytes 2752516
  133.8 1.7 copy-start.7
  133.9 1.7 copy-start.12
  133.9 1.7 copy-start.14
  135.6 2.4 %copy-start.22 = (bf16[512,3584]{1,0:T(8,128)(2,1)S(1)}, bf16[512,3584]{1,0:T(8,128)(2,1)}, u32[]{:S(2)}) copy-start(bf16[512,3584]{1,0:T(8,128)(2,1)} %param.21) | copy-start | bytes 11010052
Sparse Core Ops, SparseCore 0:
  19.3 30.2 all-gather.1
  142.1 35.6 reduce-scatter.1

commit v8 on v6

--- a/solution.py
+++ b/solution.py
@@ -225,16 +225,11 @@
     chosen_down = chosen[:, :, :down_width]
     chosen_up = chosen[:, :, down_width:]
     model_count = lax.axis_size(("my", "mc"))
-    spread = lax.all_to_all(
-        jnp.broadcast_to(chosen_down, (model_count, *chosen_down.shape)),
-        ("my", "mc"),
-        0,
-        0,
-        tiled=True,
-    )
-    full_down = jnp.moveaxis(spread, 0, 2).reshape(
-        *chosen_down.shape[:2], model_count * down_width
-    )
+    lanes = 1024
+    widened = jnp.pad(chosen_down, ((0, 0), (0, 0), (0, lanes - down_width)))
+    gathered = lax.all_gather(widened, ("my", "mc"), axis=2, tiled=True)
+    full_down = gathered.reshape(*chosen_down.shape[:2], model_count, lanes)[..., :down_width]
+    full_down = full_down.reshape(*chosen_down.shape[:2], model_count * down_width)
 
     whole = lax.all_gather(stream, ("my", "mc"), axis=1, tiled=True)
     wide = whole.astype(jnp.float32)

time: 182 us -> 226 us (1.24)
  waiting for transfers between devices: 57.6 us -> 102 us
  other arithmetic: 24.6 us -> 21.1 us
  local copies, waits for them, and re-layouts: 38.1 us -> 41.1 us
    ppermute x12, waiting for transfers between devices: 20.2 us -> 62.4 us  [ring_send(): lax.ppermute(value, axis, [(i, (i + step) % SIDE) for i in range(SIDE)])]
    all_to_all x1 -> x0, starting transfers between devices: 4.42 us -> none  [on_device(): lax.all_to_all(jnp.broadcast_to(chosen_down, (model_count, *chosen_down.s...]
    ppermute x12, starting transfers between devices: 17.5 us -> 21.2 us  [ring_send(): lax.ppermute(value, axis, [(i, (i + step) % SIDE) for i in range(SIDE)])]
    unnamed x69 -> x66, local copies, waits for them, and re-layouts: 6.01 us -> 8.77 us
  transfers between devices with their start and end apart: 16 -> 16, of which waited for: 5 -> 8; matrix products, arithmetic and copies ran while one was open for 33% -> 19% of each run, Pallas kernels for 0% -> 0%
where the time goes in v8:
time: 226 us; the launch traced here: 225 us
  waiting for transfers between devices  102 us (45%)
  local copies, waits for them, and re-layouts  41.1 us (18%)
  starting transfers between devices  23.6 us (10%)
  other arithmetic  21.1 us (9%)
  matrix products  20.9 us (9%)
  between operations  16.3 us (7%)
    ppermute x12, waiting for transfers between devices, ring_send(): lax.ppermute(value, axis, [(i, (i + step) % SIDE) for i in range(SIDE)])  62.4 us
    reduce_scatter x1, waiting for transfers between devices, on_device(): lax.psum_scatter(partial_out.astype(jnp.bfloat16), ('my', 'mc'), scatter_...  38.6 us
    ppermute x12, starting transfers between devices, ring_send(): lax.ppermute(value, axis, [(i, (i + step) % SIDE) for i in range(SIDE)])  21.2 us
    unnamed x66, local copies, waits for them, and re-layouts  8.77 us
    dot_general x1, matrix products, on_device(): jnp.dot(normalized_input, query_weight, preferred_element_type=jnp.float32)  6.22 us
  transfers between devices with their start and end apart: 16, of which 8 were waited for; matrix products, arithmetic and copies ran while one was open for 19% of the time, Pallas kernels for 0%

profile of v8, /device:TPU:0, one launch (start us, length us, event | category | flops | bytes accessed | tf_op | source)
XLA Modules:
  0.0 224.7 jit_solution(14464462163250459667)
XLA Ops:
  6.5 1.1 pad_maximum_fusion.5
  8.0 1.7 constant_dynamic-update-slice_fusion.1
  9.7 0.7 constant_dynamic-update-slice_fusion
  10.3 4.1 %collective-permute-start.9 = (bf16[3,256,256]{2,1,0:T(8,128)(2,1)}, bf16[3,256,256]{2,1,0:T(8,128)(2,1)}, u32[]{:S(2)}, u32[]{:S(2)}) collective-permute-start(bf16[3,256,256]{2,1,0:T(8,128)(2,1)} %get-tuple-element.31), channel_id=1, source_target_pairs={{0,24},{8,0},{16,8},{24,16},{1,25},{9,1},{17,9},{25,17},{2,26},{10... | collective-permute-start | bytes 1179656 | tf_op jit(solution)/shard_map/ppermute | solution.py:115
  14.5 1.3 collective-permute-start.7
  15.7 0.8 copy.39
  16.6 0.8 gather_fusion.6
  17.8 0.6 gather_fusion.8
  20.4 14.6 %collective-permute-done.7 = bf16[3,256,256]{2,1,0:T(8,128)(2,1)} collective-permute-done((bf16[3,256,256]{2,1,0:T(8,128)(2,1)}, bf16[3,256,256]{2,1,0:T(8,128)(2,1)}, u32[]{:S(2)}, u32[]{:S(2)}) %collective-permute-start.7) | collective-permute-done | bytes 393248 | tf_op jit(solution)/shard_map/ppermute | solution.py:115
  35.0 1.0 constant_dynamic-update-slice_fusion.4
  36.0 1.0 constant_dynamic-update-slice_fusion.3
  37.1 1.0 constant_dynamic-update-slice_fusion.2
  38.1 2.4 %gather_fusion.9 = bf16[80,64,256]{2,1,0:T(8,128)(2,1)} fusion(bf16[48,64,256]{2,1,0:T(8,128)(2,1)S(1)} %bitcast.115, s32[1024]{0:T(1024)S(1)} %pad_clamp_fusion.2), kind=kCustom, calls=%fused_computation.9 | custom fusion | bytes 5243200 | tf_op jit(solution)/shard_map/jit(_take)/gather | solution.py:176
  40.5 3.0 %fusion.95 = (bf16[20,64,256]{2,1,0:T(8,128)(2,1)S(1)}, bf16[20,64,256]{2,1,0:T(8,128)(2,1)}, bf16[20,64,256]{2,1,0:T(8,128)(2,1)}, bf16[20,64,256]{2,1,0:T(8,128)(2,1)S(1)}) fusion(bf16[80,64,256]{2,1,0:T(8,128)(2,1)} %gather_fusion.9), kind=kLoop, calls=%fused_computation.224 | loop fusion | bytes 5242880 | tf_op jit(solution)/shard_map/slice | solution.py:178
  43.5 3.0 %collective-permute-start.11 = (bf16[20,64,256]{2,1,0:T(8,128)(2,1)}, bf16[20,64,256]{2,1,0:T(8,128)(2,1)}, u32[]{:S(2)}, u32[]{:S(2)}) collective-permute-start(bf16[20,64,256]{2,1,0:T(8,128)(2,1)} %get-tuple-element.14), channel_id=1, source_target_pairs={{0,64},{32,96},{64,0},{96,32},{1,65},{33,97},{65,1},{97,33},{2,66}... | collective-permute-start | bytes 1966088 | tf_op jit(solution)/shard_map/ppermute | solution.py:115
  46.5 0.6 collective-permute-start.10
  47.1 2.6 %collective-permute-start.12 = (bf16[20,64,256]{2,1,0:T(8,128)(2,1)S(1)}, bf16[20,64,256]{2,1,0:T(8,128)(2,1)}, u32[]{:S(2)}, u32[]{:S(2)}) collective-permute-start(bf16[20,64,256]{2,1,0:T(8,128)(2,1)S(1)} %get-tuple-element.16), channel_id=1, source_target_pairs={{0,96},{32,0},{64,32},{96,64},{1,97},{33,1},{65,33},{97,65},{2,98}... | collective-permute-start | bytes 1966088 | tf_op jit(solution)/shard_map/ppermute | solution.py:115
  49.9 0.6 pad_clamp_fusion
  50.5 12.4 %collective-permute-done.11 = bf16[20,64,256]{2,1,0:T(8,128)(2,1)} collective-permute-done((bf16[20,64,256]{2,1,0:T(8,128)(2,1)}, bf16[20,64,256]{2,1,0:T(8,128)(2,1)}, u32[]{:S(2)}, u32[]{:S(2)}) %collective-permute-start.11) | collective-permute-done | bytes 655392 | tf_op jit(solution)/shard_map/ppermute | solution.py:115
  63.0 12.7 %collective-permute-done.10 = bf16[20,64,256]{2,1,0:T(8,128)(2,1)} collective-permute-done((bf16[20,64,256]{2,1,0:T(8,128)(2,1)}, bf16[20,64,256]{2,1,0:T(8,128)(2,1)}, u32[]{:S(2)}, u32[]{:S(2)}) %collective-permute-start.10) | collective-permute-done | bytes 655392 | tf_op jit(solution)/shard_map/ppermute | solution.py:115
  75.8 2.9 %pad_maximum_fusion = bf16[80,64,256]{2,1,0:T(8,128)(2,1)} fusion(bf16[20,64,256]{2,1,0:T(8,128)(2,1)} %collective-permute-done.12, bf16[20,64,256]{2,1,0:T(8,128)(2,1)} %collective-permute-done.11, bf16[20,64,256]{2,1,0:T(8,128)(2,1)} %collective-permute-done.10, bf16[20,64,256]{2,1,0:T(8,128)(2,1)S(1)} %get-tuple-element.13), kind=kLoop, calls=%fused_computation.27 | loop fusion | flops 3932160 | bytes 5242880 | tf_op jit(solution)/shard_map/concatenate | solution.py:177
  78.7 2.3 %gather_fusion.11 = bf16[4,64,256]{2,1,0:T(8,128)(2,1)S(1)} fusion(bf16[80,64,256]{2,1,0:T(8,128)(2,1)} %pad_maximum_fusion, s32[1024]{0:T(1024)S(1)} %get-tuple-element.46), kind=kCustom, calls=%fused_computation.11 | custom fusion | bytes 262160 | tf_op jit(solution)/shard_map/jit(_take)/gather | solution.py:193
  81.4 0.7 pad.9
  82.2 0.7 all-gather.3.cloned.1.call-update
  82.9 2.1 collective-permute-start.1
  85.0 1.4 collective-permute-start
  86.5 1.8 collective-permute-start.2
  89.4 0.6 dynamic_slice.24
  90.0 0.6 constant_dynamic-slice_fusion.7
  93.8 0.6 pad_clamp_fusion.5
  94.8 0.6 pad_clamp_fusion.6
  95.6 2.6 %collective-permute-done = bf16[2,256,256]{2,1,0:T(8,128)(2,1)S(1)} collective-permute-done((bf16[2,256,256]{2,1,0:T(8,128)(2,1)S(1)}, bf16[2,256,256]{2,1,0:T(8,128)(2,1)S(1)}, u32[]{:S(2)}, u32[]{:S(2)}) %collective-permute-start) | collective-permute-done | bytes 262176 | tf_op jit(solution)/shard_map/ppermute | solution.py:115
  98.2 0.7 copy-done.12
  99.0 1.3 pad_maximum_fusion.2
  100.2 2.2 gather_fusion.2
  102.4 1.7 fusion.96
  104.1 1.0 collective-permute-start.4
  105.1 3.2 %collective-permute-start.5 = (bf16[4,256,256]{2,1,0:T(8,128)(2,1)S(1)}, bf16[4,256,256]{2,1,0:T(8,128)(2,1)S(1)}, u32[]{:S(2)}, u32[]{:S(2)}) collective-permute-start(bf16[4,256,256]{2,1,0:T(8,128)(2,1)S(1)} %get-tuple-element.20), channel_id=1, source_target_pairs={{0,24},{8,0},{16,8},{24,16},{1,25},{9,1},{17,9},{25,17},{2,26},{10... | collective-permute-start | bytes 1572872 | tf_op jit(solution)/shard_map/ppermute | solution.py:115
  108.8 1.8 multiply_cosine_fusion
  110.9 9.7 %collective-permute-done.4 = bf16[4,256,256]{2,1,0:T(8,128)(2,1)S(1)} collective-permute-done((bf16[4,256,256]{2,1,0:T(8,128)(2,1)S(1)}, bf16[4,256,256]{2,1,0:T(8,128)(2,1)S(1)}, u32[]{:S(2)}, u32[]{:S(2)}) %collective-permute-start.4) | collective-permute-done | bytes 524320 | tf_op jit(solution)/shard_map/ppermute | solution.py:115
  120.5 10.3 %collective-permute-done.3 = bf16[4,256,256]{2,1,0:T(8,128)(2,1)S(1)} collective-permute-done((bf16[4,256,256]{2,1,0:T(8,128)(2,1)S(1)}, bf16[4,256,256]{2,1,0:T(8,128)(2,1)S(1)}, u32[]{:S(2)}, u32[]{:S(2)}) %collective-permute-start.3) | collective-permute-done | bytes 524320 | tf_op jit(solution)/shard_map/ppermute | solution.py:115
  130.8 1.7 pad_maximum_fusion.1
  132.5 2.3 %gather_fusion.3 = bf16[4,256,256]{2,1,0:T(8,128)(2,1)S(1)} fusion(bf16[16,256,256]{2,1,0:T(8,128)(2,1)} %pad_maximum_fusion.1, s32[1024]{0:T(1024)} %pad_clamp_fusion.5), kind=kCustom, calls=%fused_computation.3 | custom fusion | bytes 1048592 | tf_op jit(solution)/shard_map/jit(_take)/gather | solution.py:139
  134.8 1.0 copy.49
  135.8 1.6 slice.126
  137.4 3.2 %gather_fusion.10 = bf16[16,64,256]{2,1,0:T(8,128)(2,1)} fusion(bf16[80,64,256]{2,1,0:T(8,128)(2,1)} %pad_maximum_fusion, s32[1024]{0:T(1024)} %get-tuple-element.47), kind=kCustom, calls=%fused_computation.10 | custom fusion | bytes 1048640 | tf_op jit(solution)/shard_map/jit(_take)/gather | solution.py:190
  140.7 1.8 copy.55
  142.5 1.3 dot_general.31
  143.9 3.0 %fusion = f32[512]{0:T(512)S(1)} fusion(bf16[512,3584]{0,1:T(8,128)(2,1)} %all-gather.3.cloned.1.call-done), kind=kLoop, calls=%fused_computation.14 | loop fusion | flops 5504512 | bytes 3672064 | tf_op jit(solution)/shard_map/reduce_sum | solution.py:237
  147.0 2.1 fusion.2
  149.1 1.2 convolution_bitcast_fusion
  150.3 1.2 fusion.36
  151.9 1.2 convolution_convert_fusion.1
  153.1 0.8 copy.43
  154.0 0.7 pad_maximum_fusion.4
  154.7 2.3 %collective-permute-start.6 = (bf16[256,512]{0,1:T(8,128)(2,1)}, bf16[256,512]{0,1:T(8,128)(2,1)}, u32[]{:S(2)}, u32[]{:S(2)}) collective-permute-start(bf16[256,512]{0,1:T(8,128)(2,1)} %pad_maximum_fusion.4), channel_id=1, source_target_pairs={{0,8},{8,16},{16,24},{24,32},{32,40},{40,48},{48,56},{56,64},{64,7... | collective-permute-start | bytes 786440 | tf_op jit(solution)/shard_map/ppermute | solution.py:17
  157.0 6.2 %fusion.99 = f32[512,512]{0,1:T(8,128)} fusion(bf16[512,3584]{0,1:T(8,128)(2,1)} %copy-done.3, bf16[3584,512]{1,0:T(8,128)(2,1)} %param.18), kind=kOutput, calls=%fused_computation.228 | convolution fusion | flops 1879048192 | bytes 8388608 | tf_op jit(solution)/shard_map/dot_general | solution.py:256
  163.2 3.3 %fusion.13 = f32[512,512]{0,1:T(8,128)S(1)} fusion(f32[512,512]{0,1:T(8,128)} %fusion.99, bf16[64,512]{1,0:T(8,128)(2,1)S(1)} %bitcast.123, bf16[512,64]{0,1:T(8,128)(2,1)S(1)} %bitcast.124, bf16[64,3584]{1,0:T(8,128)(2,1)S(1)} %copy-done.5, bf16[512,3584]{0,1:T(8,128)(2,1)} %copy-done.3), kind=kOutput, calls=%fused_computation.32 | convolution fusion | flops 269025280 | bytes 6356992 | tf_op jit(solution)/shard_map/dot_general | solution.py:250
  167.7 1.0 fusion.98
  168.8 2.7 %fusion.5 = (f32[2,512]{1,0:T(2,128)S(1)}, f32[1792,512,2]{1,0,2:T(8,128)S(1)}) fusion(pred[512,1792]{0,1:T(8,128)(4,1)S(1)} %pad_add_fusion, bf16[512,2,128]{2,0,1:T(8,128)(2,1)S(1)} %get-tuple-element.22, bf16[512,2,128]{2,0,1:T(8,128)(2,1)S(1)} %get-tuple-element.21, bf16[512,256]{1,0:T(8,128)(2,1)} %copy.43, bf16[256,256]{1,0:T(8,128)(2,1)S(1)} %copy.42, ...), kind=kOutput, calls=%fused_computation.22 | convolution fusion | flops 948829184 | bytes 9703424 | tf_op jit(solution)/shard_map/tkrd,skd->krts/dot_general | solution.py:90
  171.5 1.7 fusion.3
  173.2 2.4 %divide_convert_fusion = bf16[512,1,2,256]{0,3,2,1:T(8,128)(2,1)S(1)} fusion(f32[1792,512,2]{1,0,2:T(8,128)S(1)} %get-tuple-element.41, f32[2,512]{1,0:T(2,128)S(1)} %get-tuple-element.40, pred[512,1792]{0,1:T(8,128)(4,1)S(1)} %pad_add_fusion, bf16[512,256]{0,1:T(8,128)(2,1)S(1)} %copy-done.16, bf16[256,256]{0,1:T(8,128)(2,1)S(1)} %get-tuple-element.27, ...), kind=kOutput, calls=%fused_computation.38 | convolution fusion | flops 950140928 | bytes 9707520 | tf_op jit(solution)/shard_map/krts,skd->tkrd/dot_general | solution.py:97
  175.7 3.9 %convolution_convert_fusion = bf16[512,3584]{0,1:T(8,128)(2,1)} fusion(bf16[512,512]{0,1:T(8,128)(2,1)S(1)} %bitcast.131, bf16[512,3584]{1,0:T(8,128)(2,1)S(1)} %copy-done.24), kind=kOutput, calls=%fused_computation.21 | convolution fusion | flops 1880883200 | bytes 7864320 | tf_op jit(solution)/shard_map/dot_general | solution.py:285
  179.6 38.6 %reduce-scatter.2.cloned.1.call-done = bf16[512,448]{0,1:T(8,128)(2,1)} async-done(((bf16[512,3584]{0,1:T(8,128)(2,1)}), bf16[512,448]{0,1:T(8,128)(2,1)}) %reduce-scatter.2.cloned.1.call-update) | async-done | bytes 458768 | tf_op jit(solution)/shard_map/reduce_scatter | solution.py:286
  (142 shorter events, 8.5 us)
Async XLA Ops:
  6.5 142.6 %copy-start = (bf16[3584,256]{1,0:T(8,128)(2,1)S(1)}, bf16[3584,256]{1,0:T(8,128)(2,1)}, u32[]{:S(2)}) copy-start(bf16[3584,256]{1,0:T(8,128)(2,1)} %param.19) | copy-start | bytes 5505028
  6.5 10.1 %copy-start.2 = (s32[64]{0:T(128)S(1)}, s32[64]{0:T(128)}, u32[]{:S(2)}) copy-start(s32[64]{0:T(128)} %param.25) | copy-start | bytes 772
  6.5 134.1 %all-gather.5.cloned.1.call-start = ((), (), s32[]{:S(2)}) async-start(), calls=%async_computation.2 | async-start | bytes 1179648 | tf_op jit(solution)/shard_map/all_gather | solution.py:230
  10.3 26.7 %collective-permute-start.9 = (bf16[3,256,256]{2,1,0:T(8,128)(2,1)}, bf16[3,256,256]{2,1,0:T(8,128)(2,1)}, u32[]{:S(2)}, u32[]{:S(2)}) collective-permute-start(bf16[3,256,256]{2,1,0:T(8,128)(2,1)} %get-tuple-element.31), channel_id=1, source_target_pairs={{0,24},{8,0},{16,8},{24,16},{1,25},{9,1},{17,9},{25,17},{2,26},{10... | collective-permute-start | bytes 1179656 | tf_op jit(solution)/shard_map/ppermute | solution.py:115
  14.5 21.6 %collective-permute-start.8 = (bf16[3,256,256]{2,1,0:T(8,128)(2,1)}, bf16[3,256,256]{2,1,0:T(8,128)(2,1)}, u32[]{:S(2)}, u32[]{:S(2)}) collective-permute-start(bf16[3,256,256]{2,1,0:T(8,128)(2,1)} %get-tuple-element.31), channel_id=1, source_target_pairs={{0,16},{8,24},{16,0},{24,8},{1,17},{9,25},{17,1},{25,9},{2,18},{10... | collective-permute-start | bytes 1179656 | tf_op jit(solution)/shard_map/ppermute | solution.py:115
  14.5 20.5 %collective-permute-start.7 = (bf16[3,256,256]{2,1,0:T(8,128)(2,1)}, bf16[3,256,256]{2,1,0:T(8,128)(2,1)}, u32[]{:S(2)}, u32[]{:S(2)}) collective-permute-start(bf16[3,256,256]{2,1,0:T(8,128)(2,1)} %get-tuple-element.31), channel_id=1, source_target_pairs={{0,8},{8,16},{16,24},{24,0},{1,9},{9,17},{17,25},{25,1},{2,10},{10... | collective-permute-start | bytes 1179656 | tf_op jit(solution)/shard_map/ppermute | solution.py:115
  16.6 1.0 copy-start.19
  17.8 32.0 %copy-start.13 = (s32[16,4]{1,0:T(8,128)}, s32[16,4]{1,0:T(8,128)S(1)}, u32[]{:S(2)}) copy-start(s32[16,4]{1,0:T(8,128)S(1)} %get-tuple-element.35) | copy-start | bytes 772
  43.5 19.5 %collective-permute-start.11 = (bf16[20,64,256]{2,1,0:T(8,128)(2,1)}, bf16[20,64,256]{2,1,0:T(8,128)(2,1)}, u32[]{:S(2)}, u32[]{:S(2)}) collective-permute-start(bf16[20,64,256]{2,1,0:T(8,128)(2,1)} %get-tuple-element.14), channel_id=1, source_target_pairs={{0,64},{32,96},{64,0},{96,32},{1,65},{33,97},{65,1},{97,33},{2,66}... | collective-permute-start | bytes 1966088 | tf_op jit(solution)/shard_map/ppermute | solution.py:115
  46.5 29.1 %collective-permute-start.10 = (bf16[20,64,256]{2,1,0:T(8,128)(2,1)}, bf16[20,64,256]{2,1,0:T(8,128)(2,1)}, u32[]{:S(2)}, u32[]{:S(2)}) collective-permute-start(bf16[20,64,256]{2,1,0:T(8,128)(2,1)} %get-tuple-element.15), channel_id=1, source_target_pairs={{0,32},{32,64},{64,96},{96,0},{1,33},{33,65},{65,97},{97,1},{2,34}... | collective-permute-start | bytes 1966088 | tf_op jit(solution)/shard_map/ppermute | solution.py:115
  47.1 28.7 %collective-permute-start.12 = (bf16[20,64,256]{2,1,0:T(8,128)(2,1)S(1)}, bf16[20,64,256]{2,1,0:T(8,128)(2,1)}, u32[]{:S(2)}, u32[]{:S(2)}) collective-permute-start(bf16[20,64,256]{2,1,0:T(8,128)(2,1)S(1)} %get-tuple-element.16), channel_id=1, source_target_pairs={{0,96},{32,0},{64,32},{96,64},{1,97},{33,1},{65,33},{97,65},{2,98}... | collective-permute-start | bytes 1966088 | tf_op jit(solution)/shard_map/ppermute | solution.py:115
  75.8 7.1 %copy-start.10 = (bf16[2,256,256]{2,1,0:T(8,128)(2,1)S(1)}, bf16[2,256,256]{2,1,0:T(8,128)(2,1)}, u32[]{:S(2)}) copy-start(bf16[2,256,256]{2,1,0:T(8,128)(2,1)} %param.31) | copy-start | bytes 786436
  75.8 12.5 %copy-start.14 = (s32[16,4]{1,0:T(8,128)S(1)}, s32[16,4]{1,0:T(8,128)}, u32[]{:S(2)}) copy-start(s32[16,4]{1,0:T(8,128)} %copy-done.13) | copy-start | bytes 772
  75.8 13.7 %copy-start.26 = (s32[16]{0:T(128)S(1)}, s32[16]{0:T(128)}, u32[]{:S(2)}) copy-start(s32[16]{0:T(128)} %param.27) | copy-start | bytes 196
  75.8 14.3 %copy-start.21 = (s32[16,4]{0,1:T(4,128)S(1)}, s32[16,4]{0,1:T(4,128)}, u32[]{:S(2)}) copy-start(s32[16,4]{0,1:T(4,128)} %param.26) | copy-start | bytes 772
  75.8 17.4 %copy-start.20 = (s32[16,4]{0,1:T(4,128)S(1)}, s32[16,4]{0,1:T(4,128)}, u32[]{:S(2)}) copy-start(s32[16,4]{0,1:T(4,128)} %param.29) | copy-start | bytes 772
  81.4 16.9 %copy-start.8 = (bf16[4,16,960]{2,1,0:T(8,128)(2,1)}, bf16[4,16,960]{2,1,0:T(8,128)(2,1)S(1)}, u32[]{:S(2)}) copy-start(bf16[4,16,960]{2,1,0:T(8,128)(2,1)S(1)} %reshape.640) | copy-start | bytes 368644
  82.1 61.7 %all-gather.3.cloned.1.call-start = ((), (), s32[]{:S(2)}) async-start(), calls=%async_computation.1 | async-start | bytes 4128768 | tf_op jit(solution)/shard_map/all_gather | solution.py:234
  82.9 135.3 %reduce-scatter.2.cloned.1.call-start = ((), (), s32[]{:S(2)}) async-start(), calls=%async_computation.3 | async-start | bytes 4128768 | tf_op jit(solution)/shard_map/reduce_scatter | solution.py:286
  82.9 12.7 %collective-permute-start.1 = (bf16[2,256,256]{2,1,0:T(8,128)(2,1)S(1)}, bf16[2,256,256]{2,1,0:T(8,128)(2,1)S(1)}, u32[]{:S(2)}, u32[]{:S(2)}) collective-permute-start(bf16[2,256,256]{2,1,0:T(8,128)(2,1)S(1)} %copy-done.10), channel_id=1, source_target_pairs={{0,64},{32,96},{64,0},{96,32},{1,65},{33,97},{65,1},{97,33},{2,66}... | collective-permute-start | bytes 786440 | tf_op jit(solution)/shard_map/ppermute | solution.py:115
  85.0 13.2 %collective-permute-start = (bf16[2,256,256]{2,1,0:T(8,128)(2,1)S(1)}, bf16[2,256,256]{2,1,0:T(8,128)(2,1)S(1)}, u32[]{:S(2)}, u32[]{:S(2)}) collective-permute-start(bf16[2,256,256]{2,1,0:T(8,128)(2,1)S(1)} %copy-done.10), channel_id=1, source_target_pairs={{0,32},{32,64},{64,96},{96,0},{1,33},{33,65},{65,97},{97,1},{2,34}... | collective-permute-start | bytes 786440 | tf_op jit(solution)/shard_map/ppermute | solution.py:115
  86.5 12.5 %collective-permute-start.2 = (bf16[2,256,256]{2,1,0:T(8,128)(2,1)S(1)}, bf16[2,256,256]{2,1,0:T(8,128)(2,1)}, u32[]{:S(2)}, u32[]{:S(2)}) collective-permute-start(bf16[2,256,256]{2,1,0:T(8,128)(2,1)S(1)} %copy-done.10), channel_id=1, source_target_pairs={{0,96},{32,0},{64,32},{96,64},{1,97},{33,1},{65,33},{97,65},{2,98}... | collective-permute-start | bytes 786440 | tf_op jit(solution)/shard_map/ppermute | solution.py:115
  93.4 1.2 copy-start.17
  95.6 2.6 %copy-start.11 = (bf16[2,256,256]{2,1,0:T(8,128)(2,1)}, bf16[2,256,256]{2,1,0:T(8,128)(2,1)S(1)}, u32[]{:S(2)}) copy-start(bf16[2,256,256]{2,1,0:T(8,128)(2,1)S(1)} %collective-permute-done.1) | copy-start | bytes 786436
  98.2 0.7 copy-start.12
  102.4 5.9 %copy-start.18 = (s32[4]{0:T(128)S(1)}, s32[4]{0:T(128)}, u32[]{:S(2)}) copy-start(s32[4]{0:T(128)} %copy-done.17) | copy-start | bytes 52
  104.1 16.4 %collective-permute-start.4 = (bf16[4,256,256]{2,1,0:T(8,128)(2,1)S(1)}, bf16[4,256,256]{2,1,0:T(8,128)(2,1)S(1)}, u32[]{:S(2)}, u32[]{:S(2)}) collective-permute-start(bf16[4,256,256]{2,1,0:T(8,128)(2,1)S(1)} %get-tuple-element.18), channel_id=1, source_target_pairs={{0,16},{8,24},{16,0},{24,8},{1,17},{9,25},{17,1},{25,9},{2,18},{10... | collective-permute-start | bytes 1572872 | tf_op jit(solution)/shard_map/ppermute | solution.py:115
  105.1 25.7 %collective-permute-start.3 = (bf16[4,256,256]{2,1,0:T(8,128)(2,1)S(1)}, bf16[4,256,256]{2,1,0:T(8,128)(2,1)S(1)}, u32[]{:S(2)}, u32[]{:S(2)}) collective-permute-start(bf16[4,256,256]{2,1,0:T(8,128)(2,1)S(1)} %get-tuple-element.19), channel_id=1, source_target_pairs={{0,8},{8,16},{16,24},{24,0},{1,9},{9,17},{17,25},{25,1},{2,10},{10... | collective-permute-start | bytes 1572872 | tf_op jit(solution)/shard_map/ppermute | solution.py:115
  105.1 25.7 %collective-permute-start.5 = (bf16[4,256,256]{2,1,0:T(8,128)(2,1)S(1)}, bf16[4,256,256]{2,1,0:T(8,128)(2,1)S(1)}, u32[]{:S(2)}, u32[]{:S(2)}) collective-permute-start(bf16[4,256,256]{2,1,0:T(8,128)(2,1)S(1)} %get-tuple-element.20), channel_id=1, source_target_pairs={{0,24},{8,0},{16,8},{24,16},{1,25},{9,1},{17,9},{25,17},{2,26},{10... | collective-permute-start | bytes 1572872 | tf_op jit(solution)/shard_map/ppermute | solution.py:115
  108.4 22.5 %copy-start.22 = (f32[128]{0:T(128)}, f32[128]{0:T(128)S(1)}, u32[]{:S(2)}) copy-start(f32[128]{0:T(128)S(1)} %multiply_power_fusion) | copy-start | bytes 1540
  143.9 3.1 %copy-start.4 = (bf16[512,3584]{0,1:T(8,128)(2,1)S(1)}, bf16[512,3584]{0,1:T(8,128)(2,1)}, u32[]{:S(2)}) copy-start(bf16[512,3584]{0,1:T(8,128)(2,1)} %all-gather.3.cloned.1.call-done) | copy-start | bytes 11010052
  149.1 2.4 %copy-start.3 = (bf16[512,3584]{0,1:T(8,128)(2,1)}, bf16[512,3584]{0,1:T(8,128)(2,1)S(1)}, u32[]{:S(2)}) copy-start(bf16[512,3584]{0,1:T(8,128)(2,1)S(1)} %fusion.2) | copy-start | bytes 11010052
  149.1 1.2 copy-start.23
  149.1 2.8 %copy-start.25 = (bf16[3584,256]{1,0:T(8,128)(2,1)S(1)}, bf16[3584,256]{1,0:T(8,128)(2,1)}, u32[]{:S(2)}) copy-start(bf16[3584,256]{1,0:T(8,128)(2,1)} %param.20) | copy-start | bytes 5505028
  153.1 10.1 %copy-start.15 = (bf16[512,256]{0,1:T(8,128)(2,1)}, bf16[512,256]{0,1:T(8,128)(2,1)S(1)}, u32[]{:S(2)}) copy-start(bf16[512,256]{0,1:T(8,128)(2,1)S(1)} %convolution_convert_fusion.1) | copy-start | bytes 786436
  154.7 8.5 %copy-start.5 = (bf16[64,3584]{1,0:T(8,128)(2,1)S(1)}, bf16[64,3584]{1,0:T(8,128)(2,1)}, u32[]{:S(2)}) copy-start(bf16[64,3584]{1,0:T(8,128)(2,1)} %dot_general.31) | copy-start | bytes 1376260
  154.7 8.5 %copy-start.9 = (bf16[4,16,512]{2,1,0:T(8,128)(2,1)S(1)}, bf16[4,16,512]{2,1,0:T(8,128)(2,1)}, u32[]{:S(2)}) copy-start(bf16[4,16,512]{2,1,0:T(8,128)(2,1)} %slice.126) | copy-start | bytes 196612
  154.7 13.0 %collective-permute-start.6 = (bf16[256,512]{0,1:T(8,128)(2,1)}, bf16[256,512]{0,1:T(8,128)(2,1)}, u32[]{:S(2)}, u32[]{:S(2)}) collective-permute-start(bf16[256,512]{0,1:T(8,128)(2,1)} %pad_maximum_fusion.4), channel_id=1, source_target_pairs={{0,8},{8,16},{16,24},{24,32},{32,40},{40,48},{48,56},{56,64},{64,7... | collective-permute-start | bytes 786440 | tf_op jit(solution)/shard_map/ppermute | solution.py:17
  166.6 1.0 copy-start.6
  171.5 1.7 copy-start.7
  171.5 1.7 copy-start.16
  173.2 2.4 %copy-start.24 = (bf16[512,3584]{1,0:T(8,128)(2,1)S(1)}, bf16[512,3584]{1,0:T(8,128)(2,1)}, u32[]{:S(2)}) copy-start(bf16[512,3584]{1,0:T(8,128)(2,1)} %param.21) | copy-start | bytes 11010052
  175.7 42.5 %copy-start.1 = (bf16[3584,256]{1,0:T(8,128)(2,1)S(1)}, bf16[3584,256]{1,0:T(8,128)(2,1)}, u32[]{:S(2)}) copy-start(bf16[3584,256]{1,0:T(8,128)(2,1)} %param.19) | copy-start | bytes 5505028
Sparse Core Ops, SparseCore 0:
  82.2 22.2 all-gather.4
  106.2 29.7 all-gather.2
  179.7 38.3 reduce-scatter.1

commit v9 on v6

--- a/solution.py
+++ b/solution.py
@@ -126,7 +126,8 @@
     owner = wanted // per_owner
     owner_a = (owner // SIDE, owner % SIDE)[first == "gz"]
     owner_b = (owner // SIDE, owner % SIDE)[second == "gz"]
-    source = ((own_a - owner_a[askers]) % SIDE) * per_owner + (wanted % per_owner)[askers]
+    table = ((own_a - owner_a) % SIDE) * per_owner + wanted % per_owner
+    source = jnp.take(table, askers, axis=0, mode="clip")
     outgoing = jnp.take(held, source.reshape(-1), axis=0, mode="clip")
     received = jnp.concatenate(
         [outgoing[:slots]]
@@ -163,15 +164,14 @@
     block_a, block_b, block_part = owners(block_wanted, blocks.shape[0])
     adapter_a, adapter_b, adapter_part = owners(adapter_wanted, pieces)
     quarter = jnp.arange(pieces)
-    block_items = (
-        (((own_a - block_a[askers]) % SIDE) * per_block + block_part[askers]) * pieces
+    block_table = (
+        (((own_a - block_a) % SIDE) * per_block + block_part) * pieces
     )[..., None] + quarter
-    adapter_items = (
-        ((own_a - adapter_a[askers]) % SIDE) * per_block + per_block - 1
-    ) * pieces + adapter_part[askers]
-    source = jnp.concatenate(
-        [block_items.reshape(SIDE, -1), adapter_items.reshape(SIDE, -1)], axis=1
-    )
+    adapter_table = (((own_a - adapter_a) % SIDE) * per_block + per_block - 1) * pieces + adapter_part
+    table = jnp.concatenate(
+        [block_table.reshape(block_table.shape[0], -1), adapter_table], axis=1
+    )
+    source = jnp.take(table, askers, axis=0, mode="clip")
     width = source.shape[1]
     outgoing = jnp.take(held, source.reshape(-1), axis=0, mode="clip")
     received = jnp.concatenate(

time: 182 us -> 182 us (level)
  waiting for transfers between devices: 57.6 us -> 60.4 us
  local copies, waits for them, and re-layouts: 38.1 us -> 35.6 us
    ppermute x12, waiting for transfers between devices: 20.2 us -> 23 us  [ring_send(): lax.ppermute(value, axis, [(i, (i + step) % SIDE) for i in range(SIDE)])]
    gather x7 -> x2, local copies, waits for them, and re-layouts: 3.43 us -> 1.24 us  [the longest x1 0.68 us: route(): source = jnp.take(table, askers, axis=0, mode='clip')]
    unnamed x69 -> x65, local copies, waits for them, and re-layouts: 6.01 us -> 5.7 us
  transfers between devices with their start and end apart: 16 -> 16, of which waited for: 5 -> 5; matrix products, arithmetic and copies ran while one was open for 33% -> 32% of each run, Pallas kernels for 0% -> 0%
where the time goes in v9:
time: 182 us; the launch traced here: 181 us
  waiting for transfers between devices  60.4 us (33%)
  local copies, waits for them, and re-layouts  35.6 us (20%)
  other arithmetic  24.5 us (13%)
  starting transfers between devices  24.2 us (13%)
  matrix products  19.6 us (11%)
  between operations  16.5 us (9%)
    reduce_scatter x1, waiting for transfers between devices, on_device(): lax.psum_scatter(partial_out.astype(jnp.bfloat16), ('my', 'mc'), scatter_...  36.8 us
    ppermute x12, waiting for transfers between devices, ring_send(): lax.ppermute(value, axis, [(i, (i + step) % SIDE) for i in range(SIDE)])  23 us
    ppermute x12, starting transfers between devices, ring_send(): lax.ppermute(value, axis, [(i, (i + step) % SIDE) for i in range(SIDE)])  17.5 us
    unnamed x65, local copies, waits for them, and re-layouts  5.7 us
    dot_general x1, matrix products, on_device(): jnp.dot(normalized_input, query_weight, preferred_element_type=jnp.float32)  5.26 us
    all_to_all x1, starting transfers between devices, on_device(): lax.all_to_all(jnp.broadcast_to(chosen_down, (model_count, *chosen_down.s...  4.43 us
    dot_general x1, matrix products, on_device(): jnp.dot(attended, output_weight, preferred_element_type=jnp.float32)  3.89 us
  transfers between devices with their start and end apart: 16, of which 5 were waited for; matrix products, arithmetic and copies ran while one was open for 32% of the time, Pallas kernels for 0%

profile of v9, /device:TPU:0, one launch (start us, length us, event | category | flops | bytes accessed | tf_op | source)
XLA Modules:
  0.0 180.7 jit_solution(10268167382862892183)
XLA Ops:
  6.6 3.2 %collective-permute-start.1 = (bf16[2,256,256]{2,1,0:T(8,128)(2,1)}, bf16[2,256,256]{2,1,0:T(8,128)(2,1)}, u32[]{:S(2)}, u32[]{:S(2)}) collective-permute-start(bf16[2,256,256]{2,1,0:T(8,128)(2,1)} %param.31), channel_id=1, source_target_pairs={{0,64},{32,96},{64,0},{96,32},{1,65},{33,97},{65,1},{97,33},{2,66}... | collective-permute-start | bytes 786440 | tf_op jit(solution)/shard_map/ppermute | solution.py:115
  9.8 0.6 collective-permute-start
  10.4 1.0 pad_maximum_fusion.5
  11.7 1.7 constant_dynamic-update-slice_fusion.1
  13.4 0.7 constant_dynamic-update-slice_fusion
  14.0 4.0 %collective-permute-start.9 = (bf16[3,256,256]{2,1,0:T(8,128)(2,1)}, bf16[3,256,256]{2,1,0:T(8,128)(2,1)}, u32[]{:S(2)}, u32[]{:S(2)}) collective-permute-start(bf16[3,256,256]{2,1,0:T(8,128)(2,1)} %get-tuple-element.35), channel_id=1, source_target_pairs={{0,24},{8,0},{16,8},{24,16},{1,25},{9,1},{17,9},{25,17},{2,26},{10... | collective-permute-start | bytes 1179656 | tf_op jit(solution)/shard_map/ppermute | solution.py:115
  18.1 1.3 collective-permute-start.7
  19.4 0.6 constant_dynamic-slice_fusion.7
  20.6 1.3 dynamic_slice.24
  24.5 0.8 gather_fusion.3
  25.5 0.6 negate_select_fusion.3
  27.1 0.6 pad_clamp_fusion.7
  28.1 1.8 %multiply_cosine_fusion = (f32[512,128]{1,0:T(8,128)}, f32[512,128]{1,0:T(8,128)}) fusion(f32[128]{0:T(128)S(1)} %multiply_power_fusion, f32[512]{0:T(512)S(1)} %add_convert_fusion.1), kind=kLoop, calls=%fused_computation.54 | loop fusion | flops 65536 | bytes 526848 | tf_op jit(solution)/shard_map/cos | solution.py:26
  30.0 1.2 pad_add_fusion
  31.2 0.6 fusion.89
  31.8 0.6 gather_fusion.4
  32.5 5.6 %collective-permute-done.7 = bf16[3,256,256]{2,1,0:T(8,128)(2,1)} collective-permute-done((bf16[3,256,256]{2,1,0:T(8,128)(2,1)}, bf16[3,256,256]{2,1,0:T(8,128)(2,1)}, u32[]{:S(2)}, u32[]{:S(2)}) %collective-permute-start.7) | collective-permute-done | bytes 393248 | tf_op jit(solution)/shard_map/ppermute | solution.py:115
  38.0 2.6 %collective-permute-start.2 = (bf16[2,256,256]{2,1,0:T(8,128)(2,1)}, bf16[2,256,256]{2,1,0:T(8,128)(2,1)}, u32[]{:S(2)}, u32[]{:S(2)}) collective-permute-start(bf16[2,256,256]{2,1,0:T(8,128)(2,1)} %param.31), channel_id=1, source_target_pairs={{0,96},{32,0},{64,32},{96,64},{1,97},{33,1},{65,33},{97,65},{2,98}... | collective-permute-start | bytes 786440 | tf_op jit(solution)/shard_map/ppermute | solution.py:115
  40.7 1.0 constant_dynamic-update-slice_fusion.4
  41.7 1.0 constant_dynamic-update-slice_fusion.3
  42.8 1.0 constant_dynamic-update-slice_fusion.2
  43.8 2.4 %gather_fusion.5 = bf16[80,64,256]{2,1,0:T(8,128)(2,1)} fusion(bf16[48,64,256]{2,1,0:T(8,128)(2,1)S(1)} %bitcast.111, s32[1024]{0:T(1024)S(1)} %pad_clamp_fusion.2), kind=kCustom, calls=%fused_computation.5 | custom fusion | bytes 5243200 | tf_op jit(solution)/shard_map/jit(_take)/gather | solution.py:176
  46.2 3.1 %fusion.95 = (bf16[20,64,256]{2,1,0:T(8,128)(2,1)S(1)}, bf16[20,64,256]{2,1,0:T(8,128)(2,1)}, bf16[20,64,256]{2,1,0:T(8,128)(2,1)}, bf16[20,64,256]{2,1,0:T(8,128)(2,1)}) fusion(bf16[80,64,256]{2,1,0:T(8,128)(2,1)} %gather_fusion.5), kind=kLoop, calls=%fused_computation.217 | loop fusion | bytes 5242880 | tf_op jit(solution)/shard_map/slice | solution.py:178
  49.3 0.6 pad_clamp_fusion
  49.9 0.9 collective-permute-start.10
  50.8 2.3 %collective-permute-start.12 = (bf16[20,64,256]{2,1,0:T(8,128)(2,1)}, bf16[20,64,256]{2,1,0:T(8,128)(2,1)}, u32[]{:S(2)}, u32[]{:S(2)}) collective-permute-start(bf16[20,64,256]{2,1,0:T(8,128)(2,1)} %get-tuple-element.20), channel_id=1, source_target_pairs={{0,96},{32,0},{64,32},{96,64},{1,97},{33,1},{65,33},{97,65},{2,98}... | collective-permute-start | bytes 1966088 | tf_op jit(solution)/shard_map/ppermute | solution.py:115
  53.1 1.2 fusion.90
  54.3 0.7 gather_fusion
  55.1 1.3 pad_maximum_fusion.2
  56.4 2.1 %gather_fusion.1 = bf16[16,256,256]{2,1,0:T(8,128)(2,1)} fusion(bf16[8,256,256]{2,1,0:T(8,128)(2,1)S(1)} %pad_maximum_fusion.2, s32[1024]{0:T(1024)S(1)} %pad_clamp_fusion.6), kind=kCustom, calls=%fused_computation.1 | custom fusion | bytes 4194368 | tf_op jit(solution)/shard_map/jit(_take)/gather | solution.py:131
  58.5 2.7 %fusion.96 = (bf16[4,256,256]{2,1,0:T(8,128)(2,1)S(1)}, bf16[4,256,256]{2,1,0:T(8,128)(2,1)}, bf16[4,256,256]{2,1,0:T(8,128)(2,1)}, bf16[4,256,256]{2,1,0:T(8,128)(2,1)}) fusion(bf16[16,256,256]{2,1,0:T(8,128)(2,1)} %gather_fusion.1), kind=kLoop, calls=%fused_computation.218 | loop fusion | bytes 4194304 | tf_op jit(solution)/shard_map/slice | solution.py:133
  61.2 0.6 collective-permute-start.4
  61.9 1.1 collective-permute-start.3
  62.9 5.9 %collective-permute-done.11 = bf16[20,64,256]{2,1,0:T(8,128)(2,1)} collective-permute-done((bf16[20,64,256]{2,1,0:T(8,128)(2,1)}, bf16[20,64,256]{2,1,0:T(8,128)(2,1)}, u32[]{:S(2)}, u32[]{:S(2)}) %collective-permute-start.11) | collective-permute-done | bytes 655392 | tf_op jit(solution)/shard_map/ppermute | solution.py:115
  68.8 0.8 collective-permute-start.5
  69.6 11.6 %collective-permute-done.10 = bf16[20,64,256]{2,1,0:T(8,128)(2,1)} collective-permute-done((bf16[20,64,256]{2,1,0:T(8,128)(2,1)}, bf16[20,64,256]{2,1,0:T(8,128)(2,1)}, u32[]{:S(2)}, u32[]{:S(2)}) %collective-permute-start.10) | collective-permute-done | bytes 655392 | tf_op jit(solution)/shard_map/ppermute | solution.py:115
  81.2 2.9 %pad_maximum_fusion = bf16[80,64,256]{2,1,0:T(8,128)(2,1)} fusion(bf16[20,64,256]{2,1,0:T(8,128)(2,1)} %collective-permute-done.12, bf16[20,64,256]{2,1,0:T(8,128)(2,1)} %collective-permute-done.11, bf16[20,64,256]{2,1,0:T(8,128)(2,1)} %collective-permute-done.10, bf16[20,64,256]{2,1,0:T(8,128)(2,1)S(1)} %get-tuple-element.17), kind=kLoop, calls=%fused_computation.23 | loop fusion | flops 3932160 | bytes 5242880 | tf_op jit(solution)/shard_map/concatenate | solution.py:177
  84.1 2.4 %gather_fusion.7 = bf16[4,64,256]{2,1,0:T(8,128)(2,1)S(1)} fusion(bf16[80,64,256]{2,1,0:T(8,128)(2,1)} %pad_maximum_fusion, s32[1024]{0:T(1024)} %pad_clamp_fusion), kind=kCustom, calls=%fused_computation.7 | custom fusion | bytes 262160 | tf_op jit(solution)/shard_map/jit(_take)/gather | solution.py:193
  86.9 0.9 broadcast_in_dim.43
  87.7 4.4 %all-to-all-start = ((bf16[8,4,16,448]{3,2,1,0:T(8,128)(2,1)}), bf16[8,4,16,448]{3,2,1,0:T(8,128)(2,1)S(1)}, u32[]{:S(2)}, u32[]{:S(2)}) async-start(bf16[8,4,16,448]{3,2,1,0:T(8,128)(2,1)} %broadcast_in_dim.43), calls=%async_computation | async-start | bytes 1048576 | tf_op jit(solution)/shard_map/all_to_all | solution.py:228
  92.5 3.0 %pad_maximum_fusion.1 = bf16[16,256,256]{2,1,0:T(8,128)(2,1)} fusion(bf16[4,256,256]{2,1,0:T(8,128)(2,1)} %collective-permute-done.5, bf16[4,256,256]{2,1,0:T(8,128)(2,1)} %collective-permute-done.4, bf16[4,256,256]{2,1,0:T(8,128)(2,1)} %collective-permute-done.3, bf16[4,256,256]{2,1,0:T(8,128)(2,1)S(1)} %get-tuple-element.21), kind=kLoop, calls=%fused_computation.24 | loop fusion | flops 3145728 | bytes 4194304 | tf_op jit(solution)/shard_map/concatenate | solution.py:132
  95.5 2.2 %gather_fusion.2 = bf16[4,256,256]{2,1,0:T(8,128)(2,1)S(1)} fusion(bf16[16,256,256]{2,1,0:T(8,128)(2,1)} %pad_maximum_fusion.1, s32[1024]{0:T(1024)S(1)} %pad_clamp_fusion.5), kind=kCustom, calls=%fused_computation.2 | custom fusion | bytes 1048592 | tf_op jit(solution)/shard_map/jit(_take)/gather | solution.py:140
  97.7 1.0 copy.69
  98.8 3.1 %gather_fusion.6 = bf16[16,64,256]{2,1,0:T(8,128)(2,1)} fusion(bf16[80,64,256]{2,1,0:T(8,128)(2,1)} %pad_maximum_fusion, s32[1024]{0:T(1024)S(1)} %pad_clamp_fusion.1), kind=kCustom, calls=%fused_computation.6 | custom fusion | bytes 1048640 | tf_op jit(solution)/shard_map/jit(_take)/gather | solution.py:190
  101.9 0.6 all-to-all-done
  102.8 0.6 dot_general.31
  103.4 3.0 %fusion = f32[512]{0:T(512)S(1)} fusion(bf16[512,3584]{0,1:T(8,128)(2,1)} %all-gather.2.cloned.1.call-done), kind=kLoop, calls=%fused_computation.10 | loop fusion | flops 5504512 | bytes 3672064 | tf_op jit(solution)/shard_map/reduce_sum | solution.py:242
  106.5 1.6 fusion.2
  108.2 1.2 convolution_bitcast_fusion
  109.3 1.2 fusion.36
  110.6 0.4 copy-done.26
  111.0 1.2 convolution_convert_fusion.1
  112.2 0.8 copy.62
  113.0 0.7 pad_maximum_fusion.4
  113.7 2.0 %collective-permute-start.6 = (bf16[256,512]{0,1:T(8,128)(2,1)}, bf16[256,512]{0,1:T(8,128)(2,1)}, u32[]{:S(2)}, u32[]{:S(2)}) collective-permute-start(bf16[256,512]{0,1:T(8,128)(2,1)} %pad_maximum_fusion.4), channel_id=1, source_target_pairs={{0,8},{8,16},{16,24},{24,32},{32,40},{40,48},{48,56},{56,64},{64,7... | collective-permute-start | bytes 786440 | tf_op jit(solution)/shard_map/ppermute | solution.py:17
  115.7 5.3 %fusion.99 = f32[512,512]{0,1:T(8,128)S(1)} fusion(bf16[512,3584]{0,1:T(8,128)(2,1)} %copy-done.3, bf16[3584,512]{1,0:T(8,128)(2,1)} %param.18), kind=kOutput, calls=%fused_computation.221 | convolution fusion | flops 1879048192 | bytes 8388608 | tf_op jit(solution)/shard_map/dot_general | solution.py:261
  121.0 3.0 %fusion.13 = f32[512,512]{0,1:T(8,128)S(1)} fusion(f32[512,512]{0,1:T(8,128)S(1)} %fusion.99, bf16[64,512]{1,0:T(8,128)(2,1)S(1)} %bitcast.118, bf16[512,64]{0,1:T(8,128)(2,1)S(1)} %bitcast.119, bf16[64,3584]{1,0:T(8,128)(2,1)S(1)} %dot_general.31, bf16[512,3584]{0,1:T(8,128)(2,1)} %copy-done.3), kind=kOutput, calls=%fused_computation.28 | convolution fusion | flops 269025280 | bytes 6356992 | tf_op jit(solution)/shard_map/dot_general | solution.py:255
  124.6 0.4 copy-done.6
  125.2 1.0 fusion.98
  126.3 2.6 %fusion.5 = (f32[2,512]{1,0:T(2,128)S(1)}, f32[1792,512,2]{1,0,2:T(8,128)S(1)}) fusion(pred[512,1792]{0,1:T(8,128)(4,1)S(1)} %copy-done.5, bf16[512,2,128]{2,0,1:T(8,128)(2,1)S(1)} %get-tuple-element.26, bf16[512,2,128]{2,0,1:T(8,128)(2,1)S(1)} %get-tuple-element.25, bf16[512,256]{1,0:T(8,128)(2,1)S(1)} %copy-done.9, bf16[256,256]{1,0:T(8,128)(2,1)S(1)} %copy.61, ...), kind=kOutput, calls=%fused_computation.18 | convolution fusion | flops 948829184 | bytes 9703424 | tf_op jit(solution)/shard_map/tkrd,skd->krts/dot_general | solution.py:90
  129.0 1.7 fusion.3
  130.7 2.4 %divide_convert_fusion = bf16[512,1,2,256]{0,3,2,1:T(8,128)(2,1)S(1)} fusion(f32[1792,512,2]{1,0,2:T(8,128)S(1)} %get-tuple-element.44, f32[2,512]{1,0:T(2,128)S(1)} %get-tuple-element.43, pred[512,1792]{0,1:T(8,128)(4,1)S(1)} %copy-done.5, bf16[512,256]{0,1:T(8,128)(2,1)S(1)} %copy-done.11, bf16[256,256]{0,1:T(8,128)(2,1)S(1)} %get-tuple-element.31, ...), kind=kOutput, calls=%fused_computation.34 | convolution fusion | flops 950140928 | bytes 9707520 | tf_op jit(solution)/shard_map/krts,skd->tkrd/dot_general | solution.py:97
  133.2 3.9 %convolution_convert_fusion = bf16[512,3584]{0,1:T(8,128)(2,1)} fusion(bf16[512,512]{0,1:T(8,128)(2,1)S(1)} %bitcast.127, bf16[512,3584]{1,0:T(8,128)(2,1)S(1)} %copy-done.25), kind=kOutput, calls=%fused_computation.17 | convolution fusion | flops 1880883200 | bytes 7864320 | tf_op jit(solution)/shard_map/dot_general | solution.py:290
  137.1 36.8 %reduce-scatter.2.cloned.1.call-done = bf16[512,448]{0,1:T(8,128)(2,1)} async-done(((bf16[512,3584]{0,1:T(8,128)(2,1)}), bf16[512,448]{0,1:T(8,128)(2,1)}) %reduce-scatter.2.cloned.1.call-update) | async-done | bytes 458768 | tf_op jit(solution)/shard_map/reduce_scatter | solution.py:291
  (131 shorter events, 5.0 us)
Async XLA Ops:
  6.5 101.6 %copy-start = (bf16[3584,256]{1,0:T(8,128)(2,1)S(1)}, bf16[3584,256]{1,0:T(8,128)(2,1)}, u32[]{:S(2)}) copy-start(bf16[3584,256]{1,0:T(8,128)(2,1)} %param.19) | copy-start | bytes 5505028
  6.5 12.8 %copy-start.14 = (s32[16,4]{0,1:T(4,128)S(1)}, s32[16,4]{0,1:T(4,128)}, u32[]{:S(2)}) copy-start(s32[16,4]{0,1:T(4,128)} %param.26) | copy-start | bytes 772
  6.5 17.2 %copy-start.13 = (s32[16,4]{0,1:T(4,128)S(1)}, s32[16,4]{0,1:T(4,128)}, u32[]{:S(2)}) copy-start(s32[16,4]{0,1:T(4,128)} %param.29) | copy-start | bytes 772
  6.5 17.7 %copy-start.15 = (s32[16,4]{0,1:T(4,128)S(1)}, s32[16,4]{0,1:T(4,128)}, u32[]{:S(2)}) copy-start(s32[16,4]{0,1:T(4,128)} %param.24) | copy-start | bytes 772
  6.5 17.9 %copy-start.2 = (s32[64]{0:T(128)S(1)}, s32[64]{0:T(128)}, u32[]{:S(2)}) copy-start(s32[64]{0:T(128)} %param.25) | copy-start | bytes 772
  6.5 96.8 %all-gather.2.cloned.1.call-start = ((), (), s32[]{:S(2)}) async-start(), calls=%async_computation.2 | async-start | bytes 4128768 | tf_op jit(solution)/shard_map/all_gather | solution.py:239
  6.6 44.2 %collective-permute-start.1 = (bf16[2,256,256]{2,1,0:T(8,128)(2,1)}, bf16[2,256,256]{2,1,0:T(8,128)(2,1)}, u32[]{:S(2)}, u32[]{:S(2)}) collective-permute-start(bf16[2,256,256]{2,1,0:T(8,128)(2,1)} %param.31), channel_id=1, source_target_pairs={{0,64},{32,96},{64,0},{96,32},{1,65},{33,97},{65,1},{97,33},{2,66}... | collective-permute-start | bytes 786440 | tf_op jit(solution)/shard_map/ppermute | solution.py:115
  9.8 45.3 %collective-permute-start = (bf16[2,256,256]{2,1,0:T(8,128)(2,1)}, bf16[2,256,256]{2,1,0:T(8,128)(2,1)}, u32[]{:S(2)}, u32[]{:S(2)}) collective-permute-start(bf16[2,256,256]{2,1,0:T(8,128)(2,1)} %param.31), channel_id=1, source_target_pairs={{0,32},{32,64},{64,96},{96,0},{1,33},{33,65},{65,97},{97,1},{2,34}... | collective-permute-start | bytes 786440 | tf_op jit(solution)/shard_map/ppermute | solution.py:115
  14.0 28.7 %collective-permute-start.9 = (bf16[3,256,256]{2,1,0:T(8,128)(2,1)}, bf16[3,256,256]{2,1,0:T(8,128)(2,1)}, u32[]{:S(2)}, u32[]{:S(2)}) collective-permute-start(bf16[3,256,256]{2,1,0:T(8,128)(2,1)} %get-tuple-element.35), channel_id=1, source_target_pairs={{0,24},{8,0},{16,8},{24,16},{1,25},{9,1},{17,9},{25,17},{2,26},{10... | collective-permute-start | bytes 1179656 | tf_op jit(solution)/shard_map/ppermute | solution.py:115
  18.1 23.6 %collective-permute-start.8 = (bf16[3,256,256]{2,1,0:T(8,128)(2,1)}, bf16[3,256,256]{2,1,0:T(8,128)(2,1)}, u32[]{:S(2)}, u32[]{:S(2)}) collective-permute-start(bf16[3,256,256]{2,1,0:T(8,128)(2,1)} %get-tuple-element.35), channel_id=1, source_target_pairs={{0,16},{8,24},{16,0},{24,8},{1,17},{9,25},{17,1},{25,9},{2,18},{10... | collective-permute-start | bytes 1179656 | tf_op jit(solution)/shard_map/ppermute | solution.py:115
  18.1 20.0 %collective-permute-start.7 = (bf16[3,256,256]{2,1,0:T(8,128)(2,1)}, bf16[3,256,256]{2,1,0:T(8,128)(2,1)}, u32[]{:S(2)}, u32[]{:S(2)}) collective-permute-start(bf16[3,256,256]{2,1,0:T(8,128)(2,1)} %get-tuple-element.35), channel_id=1, source_target_pairs={{0,8},{8,16},{16,24},{24,0},{1,9},{9,17},{17,25},{25,1},{2,10},{10... | collective-permute-start | bytes 1179656 | tf_op jit(solution)/shard_map/ppermute | solution.py:115
  24.2 2.3 %copy-start.19 = (s32[4,1]{0,1:T(1,128)}, s32[4,1]{0,1:T(1,128)S(1)}, u32[]{:S(2)}) copy-start(s32[4,1]{0,1:T(1,128)S(1)} %reduce-window.4) | copy-start | bytes 52
  24.5 0.9 copy-start.16
  26.5 0.6 copy-start.21
  27.0 16.8 %copy-start.23 = (f32[128]{0:T(128)}, f32[128]{0:T(128)S(1)}, u32[]{:S(2)}) copy-start(f32[128]{0:T(128)S(1)} %multiply_power_fusion) | copy-start | bytes 1540
  38.0 17.1 %collective-permute-start.2 = (bf16[2,256,256]{2,1,0:T(8,128)(2,1)}, bf16[2,256,256]{2,1,0:T(8,128)(2,1)}, u32[]{:S(2)}, u32[]{:S(2)}) collective-permute-start(bf16[2,256,256]{2,1,0:T(8,128)(2,1)} %param.31), channel_id=1, source_target_pairs={{0,96},{32,0},{64,32},{96,64},{1,97},{33,1},{65,33},{97,65},{2,98}... | collective-permute-start | bytes 786440 | tf_op jit(solution)/shard_map/ppermute | solution.py:115
  46.2 3.1 %copy-start.17 = (s32[4]{0:T(128)S(1)}, s32[4]{0:T(128)}, u32[]{:S(2)}) copy-start(s32[4]{0:T(128)} %fusion.89) | copy-start | bytes 52
  49.3 19.5 %collective-permute-start.11 = (bf16[20,64,256]{2,1,0:T(8,128)(2,1)}, bf16[20,64,256]{2,1,0:T(8,128)(2,1)}, u32[]{:S(2)}, u32[]{:S(2)}) collective-permute-start(bf16[20,64,256]{2,1,0:T(8,128)(2,1)} %get-tuple-element.18), channel_id=1, source_target_pairs={{0,64},{32,96},{64,0},{96,32},{1,65},{33,97},{65,1},{97,33},{2,66}... | collective-permute-start | bytes 1966088 | tf_op jit(solution)/shard_map/ppermute | solution.py:115
  49.9 31.3 %collective-permute-start.10 = (bf16[20,64,256]{2,1,0:T(8,128)(2,1)}, bf16[20,64,256]{2,1,0:T(8,128)(2,1)}, u32[]{:S(2)}, u32[]{:S(2)}) collective-permute-start(bf16[20,64,256]{2,1,0:T(8,128)(2,1)} %get-tuple-element.19), channel_id=1, source_target_pairs={{0,32},{32,64},{64,96},{96,0},{1,33},{33,65},{65,97},{97,1},{2,34}... | collective-permute-start | bytes 1966088 | tf_op jit(solution)/shard_map/ppermute | solution.py:115
  50.8 30.4 %collective-permute-start.12 = (bf16[20,64,256]{2,1,0:T(8,128)(2,1)}, bf16[20,64,256]{2,1,0:T(8,128)(2,1)}, u32[]{:S(2)}, u32[]{:S(2)}) collective-permute-start(bf16[20,64,256]{2,1,0:T(8,128)(2,1)} %get-tuple-element.20), channel_id=1, source_target_pairs={{0,96},{32,0},{64,32},{96,64},{1,97},{33,1},{65,33},{97,65},{2,98}... | collective-permute-start | bytes 1966088 | tf_op jit(solution)/shard_map/ppermute | solution.py:115
  58.5 11.1 %copy-start.18 = (s32[4]{0:T(128)S(1)}, s32[4]{0:T(128)}, u32[]{:S(2)}) copy-start(s32[4]{0:T(128)} %fusion.90) | copy-start | bytes 52
  61.2 31.3 %collective-permute-start.4 = (bf16[4,256,256]{2,1,0:T(8,128)(2,1)}, bf16[4,256,256]{2,1,0:T(8,128)(2,1)}, u32[]{:S(2)}, u32[]{:S(2)}) collective-permute-start(bf16[4,256,256]{2,1,0:T(8,128)(2,1)} %get-tuple-element.22), channel_id=1, source_target_pairs={{0,16},{8,24},{16,0},{24,8},{1,17},{9,25},{17,1},{25,9},{2,18},{10... | collective-permute-start | bytes 1572872 | tf_op jit(solution)/shard_map/ppermute | solution.py:115
  61.9 30.6 %collective-permute-start.3 = (bf16[4,256,256]{2,1,0:T(8,128)(2,1)}, bf16[4,256,256]{2,1,0:T(8,128)(2,1)}, u32[]{:S(2)}, u32[]{:S(2)}) collective-permute-start(bf16[4,256,256]{2,1,0:T(8,128)(2,1)} %get-tuple-element.23), channel_id=1, source_target_pairs={{0,8},{8,16},{16,24},{24,0},{1,9},{9,17},{17,25},{25,1},{2,10},{10... | collective-permute-start | bytes 1572872 | tf_op jit(solution)/shard_map/ppermute | solution.py:115
  68.8 23.7 %collective-permute-start.5 = (bf16[4,256,256]{2,1,0:T(8,128)(2,1)}, bf16[4,256,256]{2,1,0:T(8,128)(2,1)}, u32[]{:S(2)}, u32[]{:S(2)}) collective-permute-start(bf16[4,256,256]{2,1,0:T(8,128)(2,1)} %get-tuple-element.24), channel_id=1, source_target_pairs={{0,24},{8,0},{16,8},{24,16},{1,25},{9,1},{17,9},{25,17},{2,26},{10... | collective-permute-start | bytes 1572872 | tf_op jit(solution)/shard_map/ppermute | solution.py:115
  84.1 8.3 %copy-start.20 = (s32[4,1]{0,1:T(1,128)S(1)}, s32[4,1]{0,1:T(1,128)}, u32[]{:S(2)}) copy-start(s32[4,1]{0,1:T(1,128)} %copy-done.19) | copy-start | bytes 52
  84.1 8.3 %copy-start.22 = (s32[4]{0:T(128)S(1)}, s32[4]{0:T(128)}, u32[]{:S(2)}) copy-start(s32[4]{0:T(128)} %copy-done.21) | copy-start | bytes 52
  87.7 14.8 %all-to-all-start = ((bf16[8,4,16,448]{3,2,1,0:T(8,128)(2,1)}), bf16[8,4,16,448]{3,2,1,0:T(8,128)(2,1)S(1)}, u32[]{:S(2)}, u32[]{:S(2)}) async-start(bf16[8,4,16,448]{3,2,1,0:T(8,128)(2,1)} %broadcast_in_dim.43), calls=%async_computation | async-start | bytes 1048576 | tf_op jit(solution)/shard_map/all_to_all | solution.py:228
  92.2 81.7 %reduce-scatter.2.cloned.1.call-start = ((), (), s32[]{:S(2)}) async-start(), calls=%async_computation.3 | async-start | bytes 4128768 | tf_op jit(solution)/shard_map/reduce_scatter | solution.py:291
  102.5 3.9 %copy-start.12 = (f32[3584]{0:T(1024)S(1)}, f32[3584]{0:T(1024)}, u32[]{:S(2)}) copy-start(f32[3584]{0:T(1024)} %param.17) | copy-start | bytes 43012
  103.4 3.1 %copy-start.4 = (bf16[512,3584]{0,1:T(8,128)(2,1)S(1)}, bf16[512,3584]{0,1:T(8,128)(2,1)}, u32[]{:S(2)}) copy-start(bf16[512,3584]{0,1:T(8,128)(2,1)} %all-gather.2.cloned.1.call-done) | copy-start | bytes 11010052
  108.1 2.4 %copy-start.3 = (bf16[512,3584]{0,1:T(8,128)(2,1)}, bf16[512,3584]{0,1:T(8,128)(2,1)S(1)}, u32[]{:S(2)}) copy-start(bf16[512,3584]{0,1:T(8,128)(2,1)S(1)} %fusion.2) | copy-start | bytes 11010052
  108.1 1.2 copy-start.24
  108.1 2.8 %copy-start.26 = (bf16[3584,256]{1,0:T(8,128)(2,1)S(1)}, bf16[3584,256]{1,0:T(8,128)(2,1)}, u32[]{:S(2)}) copy-start(bf16[3584,256]{1,0:T(8,128)(2,1)} %param.20) | copy-start | bytes 5505028
  112.1 1.6 copy-start.10
  113.7 11.5 %collective-permute-start.6 = (bf16[256,512]{0,1:T(8,128)(2,1)}, bf16[256,512]{0,1:T(8,128)(2,1)}, u32[]{:S(2)}, u32[]{:S(2)}) collective-permute-start(bf16[256,512]{0,1:T(8,128)(2,1)} %pad_maximum_fusion.4), channel_id=1, source_target_pairs={{0,8},{8,16},{16,24},{24,32},{32,40},{40,48},{48,56},{56,64},{64,7... | collective-permute-start | bytes 786440 | tf_op jit(solution)/shard_map/ppermute | solution.py:17
  124.0 1.0 copy-start.6
  124.1 1.0 copy-start.7
  124.1 2.2 %copy-start.5 = (pred[512,1792]{0,1:T(8,128)(4,1)S(1)}, pred[512,1792]{0,1:T(8,128)(4,1)}, u32[]{:S(2)}) copy-start(pred[512,1792]{0,1:T(8,128)(4,1)} %pad_add_fusion) | copy-start | bytes 2752516
  124.2 2.2 %copy-start.9 = (bf16[512,256]{1,0:T(8,128)(2,1)S(1)}, bf16[512,256]{1,0:T(8,128)(2,1)}, u32[]{:S(2)}) copy-start(bf16[512,256]{1,0:T(8,128)(2,1)} %copy.62) | copy-start | bytes 786436
  129.0 1.7 copy-start.8
  129.0 1.7 copy-start.11
  130.7 2.5 %copy-start.25 = (bf16[512,3584]{1,0:T(8,128)(2,1)S(1)}, bf16[512,3584]{1,0:T(8,128)(2,1)}, u32[]{:S(2)}) copy-start(bf16[512,3584]{1,0:T(8,128)(2,1)} %param.21) | copy-start | bytes 11010052
  133.2 40.7 %copy-start.1 = (bf16[3584,256]{1,0:T(8,128)(2,1)S(1)}, bf16[3584,256]{1,0:T(8,128)(2,1)}, u32[]{:S(2)}) copy-start(bf16[3584,256]{1,0:T(8,128)(2,1)} %param.19) | copy-start | bytes 5505028
Sparse Core Ops, SparseCore 0:
  19.5 30.1 all-gather.1
  137.2 36.5 reduce-scatter.1

commit v10 on v9

--- a/solution.py
+++ b/solution.py
@@ -120,13 +120,16 @@
     own_a, own_b = coords[first], coords[second]
     per_owner = local.shape[0]
     slots = wanted.shape[1]
-    held = jnp.concatenate([local] + [ring_send(local, first, step) for step in range(1, SIDE)])
+    spread_out = jnp.broadcast_to(local[None], (SIDE, *local.shape))
+    held = lax.all_to_all(spread_out, first, 0, 0, tiled=True).reshape(
+        SIDE * per_owner, *local.shape[1:]
+    )
     me = group_of(first, own_a, own_b)
     askers = group_of(first, own_a, (own_b + jnp.arange(SIDE)) % SIDE)
     owner = wanted // per_owner
     owner_a = (owner // SIDE, owner % SIDE)[first == "gz"]
     owner_b = (owner // SIDE, owner % SIDE)[second == "gz"]
-    table = ((own_a - owner_a) % SIDE) * per_owner + wanted % per_owner
+    table = owner_a * per_owner + wanted % per_owner
     source = jnp.take(table, askers, axis=0, mode="clip")
     outgoing = jnp.take(held, source.reshape(-1), axis=0, mode="clip")
     received = jnp.concatenate(

time: 182 us -> 181 us (level)
  local copies, waits for them, and re-layouts: 35.6 us -> 39.3 us
  other arithmetic: 24.5 us -> 21.5 us
  waiting for transfers between devices: 60.4 us -> 58.2 us
    ppermute x12 -> x9, waiting for transfers between devices: 23 us -> 18.7 us  [ring_send(): lax.ppermute(value, axis, [(i, (i + step) % SIDE) for i in range(SIDE)])]
    all_to_all x0 -> x1, starting transfers between devices: none -> 4.29 us  [route(): lax.all_to_all(spread_out, first, 0, 0, tiled=True)]
    ppermute x12 -> x9, starting transfers between devices: 17.5 us -> 14.3 us  [ring_send(): lax.ppermute(value, axis, [(i, (i + step) % SIDE) for i in range(SIDE)])]
    unnamed x65 -> x67, local copies, waits for them, and re-layouts: 5.7 us -> 7.74 us
    reduce_scatter x1, waiting for transfers between devices: 36.8 us -> 38.7 us  [on_device(): lax.psum_scatter(partial_out.astype(jnp.bfloat16), ('my', 'mc'), scatter_...]
  transfers between devices with their start and end apart: 16 -> 14, of which waited for: 5 -> 6; matrix products, arithmetic and copies ran while one was open for 32% -> 30% of each run, Pallas kernels for 0% -> 0%
where the time goes in v10:
time: 181 us; the launch traced here: 180 us
  waiting for transfers between devices  58.2 us (32%)
  local copies, waits for them, and re-layouts  39.3 us (22%)
  starting transfers between devices  25.3 us (14%)
  other arithmetic  21.5 us (12%)
  matrix products  19.6 us (11%)
  between operations  16.6 us (9%)
    reduce_scatter x1, waiting for transfers between devices, on_device(): lax.psum_scatter(partial_out.astype(jnp.bfloat16), ('my', 'mc'), scatter_...  38.7 us
    ppermute x9, waiting for transfers between devices, ring_send(): lax.ppermute(value, axis, [(i, (i + step) % SIDE) for i in range(SIDE)])  18.7 us
    ppermute x9, starting transfers between devices, ring_send(): lax.ppermute(value, axis, [(i, (i + step) % SIDE) for i in range(SIDE)])  14.3 us
    unnamed x67, local copies, waits for them, and re-layouts  7.74 us
    dot_general x1, matrix products, on_device(): jnp.dot(normalized_input, query_weight, preferred_element_type=jnp.float32)  5.26 us
    all_to_all x1, starting transfers between devices, on_device(): lax.all_to_all(jnp.broadcast_to(chosen_down, (model_count, *chosen_down.s...  4.45 us
    all_to_all x1, starting transfers between devices, route(): lax.all_to_all(spread_out, first, 0, 0, tiled=True)  4.29 us
    dot_general x1, matrix products, on_device(): jnp.dot(attended, output_weight, preferred_element_type=jnp.float32)  3.89 us
  transfers between devices with their start and end apart: 14, of which 6 were waited for; matrix products, arithmetic and copies ran while one was open for 30% of the time, Pallas kernels for 0%

profile of v10, /device:TPU:0, one launch (start us, length us, event | category | flops | bytes accessed | tf_op | source)
XLA Modules:
  0.0 180.4 jit_solution(11351374739193248134)
XLA Ops:
  6.5 1.1 pad_maximum_fusion.4
  8.0 1.8 constant_dynamic-update-slice_fusion.1
  9.8 0.7 constant_dynamic-update-slice_fusion
  10.5 4.1 %collective-permute-start.6 = (bf16[3,256,256]{2,1,0:T(8,128)(2,1)}, bf16[3,256,256]{2,1,0:T(8,128)(2,1)S(1)}, u32[]{:S(2)}, u32[]{:S(2)}) collective-permute-start(bf16[3,256,256]{2,1,0:T(8,128)(2,1)} %get-tuple-element.35), channel_id=1, source_target_pairs={{0,24},{8,0},{16,8},{24,16},{1,25},{9,1},{17,9},{25,17},{2,26},{10... | collective-permute-start | bytes 1179656 | tf_op jit(solution)/shard_map/ppermute | solution.py:115
  14.7 1.3 collective-permute-start.4
  16.0 1.1 broadcast_in_dim.40
  17.1 4.3 %all-to-all-start = ((bf16[4,2,256,256]{3,2,1,0:T(8,128)(2,1)}), bf16[4,2,256,256]{3,2,1,0:T(8,128)(2,1)S(1)}, u32[]{:S(2)}, u32[]{:S(2)}) async-start(bf16[4,2,256,256]{3,2,1,0:T(8,128)(2,1)} %broadcast_in_dim.40), calls=%async_computation | async-start | bytes 2097152 | tf_op jit(solution)/shard_map/all_to_all | solution.py:124
  21.6 0.6 constant_dynamic-slice_fusion.7
  22.2 0.6 dynamic_slice.24
  25.9 0.8 gather_fusion.3
  27.5 0.5 copy-done.21
  28.0 0.3 bitcast_and_fusion
  28.8 1.2 pad_add_fusion
  30.1 0.6 pad_clamp_fusion
  30.7 0.6 gather_fusion
  31.3 0.6 pad_clamp_fusion.6
  31.9 0.6 gather_fusion.4
  32.6 2.6 %collective-permute-done.4 = bf16[3,256,256]{2,1,0:T(8,128)(2,1)} collective-permute-done((bf16[3,256,256]{2,1,0:T(8,128)(2,1)}, bf16[3,256,256]{2,1,0:T(8,128)(2,1)}, u32[]{:S(2)}, u32[]{:S(2)}) %collective-permute-start.4) | collective-permute-done | bytes 393248 | tf_op jit(solution)/shard_map/ppermute | solution.py:115
  35.2 1.8 constant_dynamic-update-slice_fusion.4
  37.0 1.8 %constant_dynamic-update-slice_fusion.3 = bf16[12,256,256]{2,1,0:T(8,128)(2,1)} fusion(bf16[12,256,256]{2,1,0:T(8,128)(2,1)} %constant_dynamic-update-slice_fusion.4, bf16[3,256,256]{2,1,0:T(8,128)(2,1)} %collective-permute-done.5), kind=kLoop, calls=%fused_computation.77 | loop fusion | bytes 786432
  38.8 0.8 constant_dynamic-update-slice_fusion.2
  39.6 3.9 %gather_fusion.5 = bf16[80,64,256]{2,1,0:T(8,128)(2,1)} fusion(bf16[48,64,256]{2,1,0:T(8,128)(2,1)} %bitcast.16, s32[1024]{0:T(1024)S(1)} %pad_clamp_fusion.2), kind=kCustom, calls=%fused_computation.5 | custom fusion | bytes 5243200 | tf_op jit(solution)/shard_map/jit(_take)/gather | solution.py:179
  43.5 3.1 %fusion.92 = (bf16[20,64,256]{2,1,0:T(8,128)(2,1)S(1)}, bf16[20,64,256]{2,1,0:T(8,128)(2,1)}, bf16[20,64,256]{2,1,0:T(8,128)(2,1)}, bf16[20,64,256]{2,1,0:T(8,128)(2,1)}) fusion(bf16[80,64,256]{2,1,0:T(8,128)(2,1)} %gather_fusion.5), kind=kLoop, calls=%fused_computation.211 | loop fusion | bytes 5242880 | tf_op jit(solution)/shard_map/slice | solution.py:181
  46.5 3.0 %collective-permute-start.8 = (bf16[20,64,256]{2,1,0:T(8,128)(2,1)}, bf16[20,64,256]{2,1,0:T(8,128)(2,1)}, u32[]{:S(2)}, u32[]{:S(2)}) collective-permute-start(bf16[20,64,256]{2,1,0:T(8,128)(2,1)} %get-tuple-element.18), channel_id=1, source_target_pairs={{0,64},{32,96},{64,0},{96,32},{1,65},{33,97},{65,1},{97,33},{2,66}... | collective-permute-start | bytes 1966088 | tf_op jit(solution)/shard_map/ppermute | solution.py:115
  49.6 0.7 collective-permute-start.7
  50.2 2.6 %collective-permute-start.9 = (bf16[20,64,256]{2,1,0:T(8,128)(2,1)}, bf16[20,64,256]{2,1,0:T(8,128)(2,1)}, u32[]{:S(2)}, u32[]{:S(2)}) collective-permute-start(bf16[20,64,256]{2,1,0:T(8,128)(2,1)} %get-tuple-element.20), channel_id=1, source_target_pairs={{0,96},{32,0},{64,32},{96,64},{1,97},{33,1},{65,33},{97,65},{2,98}... | collective-permute-start | bytes 1966088 | tf_op jit(solution)/shard_map/ppermute | solution.py:115
  52.9 0.6 fusion.87
  53.5 1.8 multiply_cosine_fusion
  55.3 2.1 %gather_fusion.1 = bf16[16,256,256]{2,1,0:T(8,128)(2,1)} fusion(bf16[8,256,256]{2,1,0:T(8,128)(2,1)S(1)} %bitcast.112, s32[1024]{0:T(1024)} %pad_clamp_fusion.6), kind=kCustom, calls=%fused_computation.1 | custom fusion | bytes 4194368 | tf_op jit(solution)/shard_map/jit(_take)/gather | solution.py:134
  57.4 2.7 %fusion.93 = (bf16[4,256,256]{2,1,0:T(8,128)(2,1)S(1)}, bf16[4,256,256]{2,1,0:T(8,128)(2,1)}, bf16[4,256,256]{2,1,0:T(8,128)(2,1)}, bf16[4,256,256]{2,1,0:T(8,128)(2,1)}) fusion(bf16[16,256,256]{2,1,0:T(8,128)(2,1)} %gather_fusion.1), kind=kLoop, calls=%fused_computation.212 | loop fusion | bytes 4194304 | tf_op jit(solution)/shard_map/slice | solution.py:136
  60.1 0.6 collective-permute-start.1
  60.7 1.1 collective-permute-start
  61.9 4.2 %collective-permute-done.8 = bf16[20,64,256]{2,1,0:T(8,128)(2,1)} collective-permute-done((bf16[20,64,256]{2,1,0:T(8,128)(2,1)}, bf16[20,64,256]{2,1,0:T(8,128)(2,1)}, u32[]{:S(2)}, u32[]{:S(2)}) %collective-permute-start.8) | collective-permute-done | bytes 655392 | tf_op jit(solution)/shard_map/ppermute | solution.py:115
  66.0 0.9 collective-permute-start.2
  67.0 11.8 %collective-permute-done.7 = bf16[20,64,256]{2,1,0:T(8,128)(2,1)} collective-permute-done((bf16[20,64,256]{2,1,0:T(8,128)(2,1)}, bf16[20,64,256]{2,1,0:T(8,128)(2,1)}, u32[]{:S(2)}, u32[]{:S(2)}) %collective-permute-start.7) | collective-permute-done | bytes 655392 | tf_op jit(solution)/shard_map/ppermute | solution.py:115
  78.8 2.9 %pad_maximum_fusion = bf16[80,64,256]{2,1,0:T(8,128)(2,1)} fusion(bf16[20,64,256]{2,1,0:T(8,128)(2,1)} %collective-permute-done.9, bf16[20,64,256]{2,1,0:T(8,128)(2,1)} %collective-permute-done.8, bf16[20,64,256]{2,1,0:T(8,128)(2,1)} %collective-permute-done.7, bf16[20,64,256]{2,1,0:T(8,128)(2,1)S(1)} %get-tuple-element.17), kind=kLoop, calls=%fused_computation.23 | loop fusion | flops 3932160 | bytes 5242880 | tf_op jit(solution)/shard_map/concatenate | solution.py:180
  81.7 2.4 %gather_fusion.7 = bf16[4,64,256]{2,1,0:T(8,128)(2,1)S(1)} fusion(bf16[80,64,256]{2,1,0:T(8,128)(2,1)} %pad_maximum_fusion, s32[1024]{0:T(1024)} %pad_clamp_fusion), kind=kCustom, calls=%fused_computation.7 | custom fusion | bytes 262160 | tf_op jit(solution)/shard_map/jit(_take)/gather | solution.py:196
  84.5 0.9 broadcast_in_dim.46
  85.4 4.4 %all-to-all-start.1 = ((bf16[8,4,16,448]{3,2,1,0:T(8,128)(2,1)}), bf16[8,4,16,448]{3,2,1,0:T(8,128)(2,1)S(1)}, u32[]{:S(2)}, u32[]{:S(2)}) async-start(bf16[8,4,16,448]{3,2,1,0:T(8,128)(2,1)} %broadcast_in_dim.46), calls=%async_computation.1 | async-start | bytes 1048576 | tf_op jit(solution)/shard_map/all_to_all | solution.py:231
  90.2 3.1 %gather_fusion.6 = bf16[16,64,256]{2,1,0:T(8,128)(2,1)} fusion(bf16[80,64,256]{2,1,0:T(8,128)(2,1)} %pad_maximum_fusion, s32[1024]{0:T(1024)S(1)} %pad_clamp_fusion.1), kind=kCustom, calls=%fused_computation.6 | custom fusion | bytes 1048640 | tf_op jit(solution)/shard_map/jit(_take)/gather | solution.py:193
  93.4 2.9 %pad_maximum_fusion.1 = bf16[16,256,256]{2,1,0:T(8,128)(2,1)} fusion(bf16[4,256,256]{2,1,0:T(8,128)(2,1)} %collective-permute-done.2, bf16[4,256,256]{2,1,0:T(8,128)(2,1)} %collective-permute-done.1, bf16[4,256,256]{2,1,0:T(8,128)(2,1)} %collective-permute-done, bf16[4,256,256]{2,1,0:T(8,128)(2,1)S(1)} %get-tuple-element.21), kind=kLoop, calls=%fused_computation.24 | loop fusion | flops 3145728 | bytes 4194304 | tf_op jit(solution)/shard_map/concatenate | solution.py:135
  96.3 2.2 %gather_fusion.2 = bf16[4,256,256]{2,1,0:T(8,128)(2,1)S(1)} fusion(bf16[16,256,256]{2,1,0:T(8,128)(2,1)} %pad_maximum_fusion.1, s32[1024]{0:T(1024)S(1)} %pad_clamp_fusion.5), kind=kCustom, calls=%fused_computation.2 | custom fusion | bytes 1048592 | tf_op jit(solution)/shard_map/jit(_take)/gather | solution.py:143
  98.5 1.0 copy.68
  99.5 0.7 all-to-all-done.1
  100.2 0.3 copy.62
  100.5 0.6 dot_general.31
  101.1 3.0 %fusion = f32[512]{0:T(512)S(1)} fusion(bf16[512,3584]{0,1:T(8,128)(2,1)} %all-gather.2.cloned.1.call-done), kind=kLoop, calls=%fused_computation.10 | loop fusion | flops 5504512 | bytes 3672064 | tf_op jit(solution)/shard_map/reduce_sum | solution.py:245
  104.2 1.6 fusion.2
  105.8 1.2 convolution_bitcast_fusion
  107.0 1.2 fusion.36
  108.2 0.4 copy-done.26
  108.6 1.2 convolution_convert_fusion.1
  109.8 0.9 copy.61
  110.7 0.7 pad_maximum_fusion.3
  111.4 2.0 %collective-permute-start.3 = (bf16[256,512]{0,1:T(8,128)(2,1)}, bf16[256,512]{0,1:T(8,128)(2,1)}, u32[]{:S(2)}, u32[]{:S(2)}) collective-permute-start(bf16[256,512]{0,1:T(8,128)(2,1)} %pad_maximum_fusion.3), channel_id=1, source_target_pairs={{0,8},{8,16},{16,24},{24,32},{32,40},{40,48},{48,56},{56,64},{64,7... | collective-permute-start | bytes 786440 | tf_op jit(solution)/shard_map/ppermute | solution.py:17
  113.4 5.3 %fusion.96 = f32[512,512]{0,1:T(8,128)S(1)} fusion(bf16[512,3584]{0,1:T(8,128)(2,1)} %copy-done.3, bf16[3584,512]{1,0:T(8,128)(2,1)} %param.18), kind=kOutput, calls=%fused_computation.215 | convolution fusion | flops 1879048192 | bytes 8388608 | tf_op jit(solution)/shard_map/dot_general | solution.py:264
  118.7 3.0 %fusion.13 = f32[512,512]{0,1:T(8,128)S(1)} fusion(f32[512,512]{0,1:T(8,128)S(1)} %fusion.96, bf16[64,512]{1,0:T(8,128)(2,1)S(1)} %bitcast.119, bf16[512,64]{0,1:T(8,128)(2,1)S(1)} %bitcast.120, bf16[64,3584]{1,0:T(8,128)(2,1)S(1)} %dot_general.31, bf16[512,3584]{0,1:T(8,128)(2,1)} %copy-done.3), kind=kOutput, calls=%fused_computation.28 | convolution fusion | flops 269025280 | bytes 6356992 | tf_op jit(solution)/shard_map/dot_general | solution.py:258
  122.3 0.4 copy-done.6
  123.0 1.0 fusion.95
  124.1 2.6 %fusion.5 = (f32[2,512]{1,0:T(2,128)S(1)}, f32[1792,512,2]{1,0,2:T(8,128)S(1)}) fusion(pred[512,1792]{0,1:T(8,128)(4,1)S(1)} %copy-done.5, bf16[512,2,128]{2,0,1:T(8,128)(2,1)S(1)} %get-tuple-element.26, bf16[512,2,128]{2,0,1:T(8,128)(2,1)S(1)} %get-tuple-element.25, bf16[512,256]{1,0:T(8,128)(2,1)S(1)} %copy-done.10, bf16[256,256]{1,0:T(8,128)(2,1)S(1)} %copy.60, ...), kind=kOutput, calls=%fused_computation.18 | convolution fusion | flops 948829184 | bytes 9703424 | tf_op jit(solution)/shard_map/tkrd,skd->krts/dot_general | solution.py:90
  126.7 1.7 fusion.3
  128.5 2.4 %divide_convert_fusion = bf16[512,1,2,256]{0,3,2,1:T(8,128)(2,1)S(1)} fusion(f32[1792,512,2]{1,0,2:T(8,128)S(1)} %get-tuple-element.44, f32[2,512]{1,0:T(2,128)S(1)} %get-tuple-element.43, pred[512,1792]{0,1:T(8,128)(4,1)S(1)} %copy-done.5, bf16[512,256]{0,1:T(8,128)(2,1)S(1)} %copy-done.12, bf16[256,256]{0,1:T(8,128)(2,1)S(1)} %get-tuple-element.31, ...), kind=kOutput, calls=%fused_computation.33 | convolution fusion | flops 950140928 | bytes 9707520 | tf_op jit(solution)/shard_map/krts,skd->tkrd/dot_general | solution.py:97
  130.9 3.9 %convolution_convert_fusion = bf16[512,3584]{0,1:T(8,128)(2,1)} fusion(bf16[512,512]{0,1:T(8,128)(2,1)S(1)} %bitcast.128, bf16[512,3584]{1,0:T(8,128)(2,1)S(1)} %copy-done.25), kind=kOutput, calls=%fused_computation.17 | convolution fusion | flops 1880883200 | bytes 7864320 | tf_op jit(solution)/shard_map/dot_general | solution.py:293
  134.8 38.7 %reduce-scatter.2.cloned.1.call-done = bf16[512,448]{0,1:T(8,128)(2,1)} async-done(((bf16[512,3584]{0,1:T(8,128)(2,1)}), bf16[512,448]{0,1:T(8,128)(2,1)}) %reduce-scatter.2.cloned.1.call-update) | async-done | bytes 458768 | tf_op jit(solution)/shard_map/reduce_scatter | solution.py:294
  (129 shorter events, 4.4 us)
Async XLA Ops:
  6.5 99.2 %copy-start = (bf16[3584,256]{1,0:T(8,128)(2,1)S(1)}, bf16[3584,256]{1,0:T(8,128)(2,1)}, u32[]{:S(2)}) copy-start(bf16[3584,256]{1,0:T(8,128)(2,1)} %param.19) | copy-start | bytes 5505028
  6.5 9.4 %copy-start.9 = (bf16[2,256,256]{2,1,0:T(8,128)(2,1)S(1)}, bf16[2,256,256]{2,1,0:T(8,128)(2,1)}, u32[]{:S(2)}) copy-start(bf16[2,256,256]{2,1,0:T(8,128)(2,1)} %param.31) | copy-start | bytes 786436
  6.5 94.5 %all-gather.2.cloned.1.call-start = ((), (), s32[]{:S(2)}) async-start(), calls=%async_computation.3 | async-start | bytes 4128768 | tf_op jit(solution)/shard_map/all_gather | solution.py:242
  7.9 13.5 %copy-start.14 = (s32[16,4]{0,1:T(4,128)S(1)}, s32[16,4]{0,1:T(4,128)}, u32[]{:S(2)}) copy-start(s32[16,4]{0,1:T(4,128)} %param.29) | copy-start | bytes 772
  7.9 13.4 %copy-start.15 = (s32[16,4]{0,1:T(4,128)S(1)}, s32[16,4]{0,1:T(4,128)}, u32[]{:S(2)}) copy-start(s32[16,4]{0,1:T(4,128)} %param.26) | copy-start | bytes 772
  7.9 14.2 %copy-start.27 = (s32[16]{0:T(128)S(1)}, s32[16]{0:T(128)}, u32[]{:S(2)}) copy-start(s32[16]{0:T(128)} %param.27) | copy-start | bytes 196
  8.0 17.7 %copy-start.16 = (s32[16,4]{0,1:T(4,128)S(1)}, s32[16,4]{0,1:T(4,128)}, u32[]{:S(2)}) copy-start(s32[16,4]{0,1:T(4,128)} %param.24) | copy-start | bytes 772
  8.0 17.9 %copy-start.2 = (s32[64]{0:T(128)S(1)}, s32[64]{0:T(128)}, u32[]{:S(2)}) copy-start(s32[64]{0:T(128)} %param.25) | copy-start | bytes 772
  10.5 28.3 %collective-permute-start.6 = (bf16[3,256,256]{2,1,0:T(8,128)(2,1)}, bf16[3,256,256]{2,1,0:T(8,128)(2,1)S(1)}, u32[]{:S(2)}, u32[]{:S(2)}) collective-permute-start(bf16[3,256,256]{2,1,0:T(8,128)(2,1)} %get-tuple-element.35), channel_id=1, source_target_pairs={{0,24},{8,0},{16,8},{24,16},{1,25},{9,1},{17,9},{25,17},{2,26},{10... | collective-permute-start | bytes 1179656 | tf_op jit(solution)/shard_map/ppermute | solution.py:115
  14.7 22.3 %collective-permute-start.5 = (bf16[3,256,256]{2,1,0:T(8,128)(2,1)}, bf16[3,256,256]{2,1,0:T(8,128)(2,1)}, u32[]{:S(2)}, u32[]{:S(2)}) collective-permute-start(bf16[3,256,256]{2,1,0:T(8,128)(2,1)} %get-tuple-element.35), channel_id=1, source_target_pairs={{0,16},{8,24},{16,0},{24,8},{1,17},{9,25},{17,1},{25,9},{2,18},{10... | collective-permute-start | bytes 1179656 | tf_op jit(solution)/shard_map/ppermute | solution.py:115
  14.7 20.5 %collective-permute-start.4 = (bf16[3,256,256]{2,1,0:T(8,128)(2,1)}, bf16[3,256,256]{2,1,0:T(8,128)(2,1)}, u32[]{:S(2)}, u32[]{:S(2)}) collective-permute-start(bf16[3,256,256]{2,1,0:T(8,128)(2,1)} %get-tuple-element.35), channel_id=1, source_target_pairs={{0,8},{8,16},{16,24},{24,0},{1,9},{9,17},{17,25},{25,1},{2,10},{10... | collective-permute-start | bytes 1179656 | tf_op jit(solution)/shard_map/ppermute | solution.py:115
  17.1 38.2 %all-to-all-start = ((bf16[4,2,256,256]{3,2,1,0:T(8,128)(2,1)}), bf16[4,2,256,256]{3,2,1,0:T(8,128)(2,1)S(1)}, u32[]{:S(2)}, u32[]{:S(2)}) async-start(bf16[4,2,256,256]{3,2,1,0:T(8,128)(2,1)} %broadcast_in_dim.40), calls=%async_computation | async-start | bytes 2097152 | tf_op jit(solution)/shard_map/all_to_all | solution.py:124
  25.7 1.7 copy-start.19
  25.9 0.9 copy-start.17
  27.4 0.6 copy-start.21
  46.5 19.5 %collective-permute-start.8 = (bf16[20,64,256]{2,1,0:T(8,128)(2,1)}, bf16[20,64,256]{2,1,0:T(8,128)(2,1)}, u32[]{:S(2)}, u32[]{:S(2)}) collective-permute-start(bf16[20,64,256]{2,1,0:T(8,128)(2,1)} %get-tuple-element.18), channel_id=1, source_target_pairs={{0,64},{32,96},{64,0},{96,32},{1,65},{33,97},{65,1},{97,33},{2,66}... | collective-permute-start | bytes 1966088 | tf_op jit(solution)/shard_map/ppermute | solution.py:115
  49.6 3.9 %copy-start.23 = (f32[128]{0:T(128)}, f32[128]{0:T(128)S(1)}, u32[]{:S(2)}) copy-start(f32[128]{0:T(128)S(1)} %multiply_power_fusion) | copy-start | bytes 1540
  49.6 29.1 %collective-permute-start.7 = (bf16[20,64,256]{2,1,0:T(8,128)(2,1)}, bf16[20,64,256]{2,1,0:T(8,128)(2,1)}, u32[]{:S(2)}, u32[]{:S(2)}) collective-permute-start(bf16[20,64,256]{2,1,0:T(8,128)(2,1)} %get-tuple-element.19), channel_id=1, source_target_pairs={{0,32},{32,64},{64,96},{96,0},{1,33},{33,65},{65,97},{97,1},{2,34}... | collective-permute-start | bytes 1966088 | tf_op jit(solution)/shard_map/ppermute | solution.py:115
  50.2 28.6 %collective-permute-start.9 = (bf16[20,64,256]{2,1,0:T(8,128)(2,1)}, bf16[20,64,256]{2,1,0:T(8,128)(2,1)}, u32[]{:S(2)}, u32[]{:S(2)}) collective-permute-start(bf16[20,64,256]{2,1,0:T(8,128)(2,1)} %get-tuple-element.20), channel_id=1, source_target_pairs={{0,96},{32,0},{64,32},{96,64},{1,97},{33,1},{65,33},{97,65},{2,98}... | collective-permute-start | bytes 1966088 | tf_op jit(solution)/shard_map/ppermute | solution.py:115
  57.4 9.6 %copy-start.18 = (s32[4]{0:T(128)S(1)}, s32[4]{0:T(128)}, u32[]{:S(2)}) copy-start(s32[4]{0:T(128)} %fusion.87) | copy-start | bytes 52
  60.1 33.2 %collective-permute-start.1 = (bf16[4,256,256]{2,1,0:T(8,128)(2,1)}, bf16[4,256,256]{2,1,0:T(8,128)(2,1)}, u32[]{:S(2)}, u32[]{:S(2)}) collective-permute-start(bf16[4,256,256]{2,1,0:T(8,128)(2,1)} %get-tuple-element.22), channel_id=1, source_target_pairs={{0,16},{8,24},{16,0},{24,8},{1,17},{9,25},{17,1},{25,9},{2,18},{10... | collective-permute-start | bytes 1572872 | tf_op jit(solution)/shard_map/ppermute | solution.py:115
  60.7 32.6 %collective-permute-start = (bf16[4,256,256]{2,1,0:T(8,128)(2,1)}, bf16[4,256,256]{2,1,0:T(8,128)(2,1)}, u32[]{:S(2)}, u32[]{:S(2)}) collective-permute-start(bf16[4,256,256]{2,1,0:T(8,128)(2,1)} %get-tuple-element.23), channel_id=1, source_target_pairs={{0,8},{8,16},{16,24},{24,0},{1,9},{9,17},{17,25},{25,1},{2,10},{10... | collective-permute-start | bytes 1572872 | tf_op jit(solution)/shard_map/ppermute | solution.py:115
  66.0 27.3 %collective-permute-start.2 = (bf16[4,256,256]{2,1,0:T(8,128)(2,1)}, bf16[4,256,256]{2,1,0:T(8,128)(2,1)}, u32[]{:S(2)}, u32[]{:S(2)}) collective-permute-start(bf16[4,256,256]{2,1,0:T(8,128)(2,1)} %get-tuple-element.24), channel_id=1, source_target_pairs={{0,24},{8,0},{16,8},{24,16},{1,25},{9,1},{17,9},{25,17},{2,26},{10... | collective-permute-start | bytes 1572872 | tf_op jit(solution)/shard_map/ppermute | solution.py:115
  81.7 8.3 %copy-start.20 = (s32[4,1]{0,1:T(1,128)S(1)}, s32[4,1]{0,1:T(1,128)}, u32[]{:S(2)}) copy-start(s32[4,1]{0,1:T(1,128)} %copy-done.19) | copy-start | bytes 52
  81.7 8.4 %copy-start.22 = (s32[4]{0:T(128)S(1)}, s32[4]{0:T(128)}, u32[]{:S(2)}) copy-start(s32[4]{0:T(128)} %copy-done.21) | copy-start | bytes 52
  85.4 14.8 %all-to-all-start.1 = ((bf16[8,4,16,448]{3,2,1,0:T(8,128)(2,1)}), bf16[8,4,16,448]{3,2,1,0:T(8,128)(2,1)S(1)}, u32[]{:S(2)}, u32[]{:S(2)}) async-start(bf16[8,4,16,448]{3,2,1,0:T(8,128)(2,1)} %broadcast_in_dim.46), calls=%async_computation.1 | async-start | bytes 1048576 | tf_op jit(solution)/shard_map/all_to_all | solution.py:231
  89.8 83.7 %reduce-scatter.2.cloned.1.call-start = ((), (), s32[]{:S(2)}) async-start(), calls=%async_computation.4 | async-start | bytes 4128768 | tf_op jit(solution)/shard_map/reduce_scatter | solution.py:294
  100.2 3.9 %copy-start.13 = (f32[3584]{0:T(1024)S(1)}, f32[3584]{0:T(1024)}, u32[]{:S(2)}) copy-start(f32[3584]{0:T(1024)} %param.17) | copy-start | bytes 43012
  101.0 3.1 %copy-start.4 = (bf16[512,3584]{0,1:T(8,128)(2,1)S(1)}, bf16[512,3584]{0,1:T(8,128)(2,1)}, u32[]{:S(2)}) copy-start(bf16[512,3584]{0,1:T(8,128)(2,1)} %all-gather.2.cloned.1.call-done) | copy-start | bytes 11010052
  105.8 2.4 %copy-start.3 = (bf16[512,3584]{0,1:T(8,128)(2,1)}, bf16[512,3584]{0,1:T(8,128)(2,1)S(1)}, u32[]{:S(2)}) copy-start(bf16[512,3584]{0,1:T(8,128)(2,1)S(1)} %fusion.2) | copy-start | bytes 11010052
  105.8 1.2 copy-start.24
  105.8 2.8 %copy-start.26 = (bf16[3584,256]{1,0:T(8,128)(2,1)S(1)}, bf16[3584,256]{1,0:T(8,128)(2,1)}, u32[]{:S(2)}) copy-start(bf16[3584,256]{1,0:T(8,128)(2,1)} %param.20) | copy-start | bytes 5505028
  109.8 1.7 copy-start.11
  111.4 11.5 %collective-permute-start.3 = (bf16[256,512]{0,1:T(8,128)(2,1)}, bf16[256,512]{0,1:T(8,128)(2,1)}, u32[]{:S(2)}, u32[]{:S(2)}) collective-permute-start(bf16[256,512]{0,1:T(8,128)(2,1)} %pad_maximum_fusion.3), channel_id=1, source_target_pairs={{0,8},{8,16},{16,24},{24,32},{32,40},{40,48},{48,56},{56,64},{64,7... | collective-permute-start | bytes 786440 | tf_op jit(solution)/shard_map/ppermute | solution.py:17
  121.8 1.0 copy-start.6
  121.8 1.0 copy-start.7
  121.9 2.2 %copy-start.5 = (pred[512,1792]{0,1:T(8,128)(4,1)S(1)}, pred[512,1792]{0,1:T(8,128)(4,1)}, u32[]{:S(2)}) copy-start(pred[512,1792]{0,1:T(8,128)(4,1)} %pad_add_fusion) | copy-start | bytes 2752516
  121.9 2.2 %copy-start.10 = (bf16[512,256]{1,0:T(8,128)(2,1)S(1)}, bf16[512,256]{1,0:T(8,128)(2,1)}, u32[]{:S(2)}) copy-start(bf16[512,256]{1,0:T(8,128)(2,1)} %copy.61) | copy-start | bytes 786436
  126.7 1.7 copy-start.8
  126.7 1.7 copy-start.12
  128.4 2.5 %copy-start.25 = (bf16[512,3584]{1,0:T(8,128)(2,1)S(1)}, bf16[512,3584]{1,0:T(8,128)(2,1)}, u32[]{:S(2)}) copy-start(bf16[512,3584]{1,0:T(8,128)(2,1)} %param.21) | copy-start | bytes 11010052
  130.9 42.6 %copy-start.1 = (bf16[3584,256]{1,0:T(8,128)(2,1)S(1)}, bf16[3584,256]{1,0:T(8,128)(2,1)}, u32[]{:S(2)}) copy-start(bf16[3584,256]{1,0:T(8,128)(2,1)} %param.19) | copy-start | bytes 5505028
Sparse Core Ops, SparseCore 0:
  16.1 30.5 all-gather.1
  135.0 38.5 reduce-scatter.1

commit v11 on v10

--- a/solution.py
+++ b/solution.py
@@ -177,13 +177,14 @@
     source = jnp.take(table, askers, axis=0, mode="clip")
     width = source.shape[1]
     outgoing = jnp.take(held, source.reshape(-1), axis=0, mode="clip")
-    received = jnp.concatenate(
-        [outgoing[:width]]
-        + [
-            ring_send(outgoing[step * width:(step + 1) * width], second, step)
-            for step in range(1, SIDE)
-        ]
-    )
+    near, far, back = (outgoing[step * width:(step + 1) * width] for step in range(1, SIDE))
+    half = width // 2
+    ahead = ring_send(jnp.concatenate([near, far[:half]]), second, 1)
+    behind = ring_send(jnp.concatenate([back, far[half:]]), second, SIDE - 1)
+    relayed = jnp.concatenate(
+        [ring_send(ahead[width:], second, 1), ring_send(behind[width:], second, SIDE - 1)]
+    )
+    received = jnp.concatenate([outgoing[:width], ahead[:width], relayed, behind[:width]])
     slots = block_wanted.shape[1]
     slot = jnp.arange(slots)
     block_pick = (

time: 181 us -> 198 us (1.094)
  local copies, waits for them, and re-layouts: 39.3 us -> 49.9 us
  starting transfers between devices: 25.3 us -> 29.2 us
  other arithmetic: 21.5 us -> 24.4 us
    concatenate x0 -> x2, local copies, waits for them, and re-layouts: none -> 4.29 us  [the longest x1 2.3 us: route_with_adapters(): ahead = ring_send(jnp.concatenate([near, far[:half]]), second, 1)]
    unnamed x67 -> x74, local copies, waits for them, and re-layouts: 7.74 us -> 11.5 us
    ppermute x1, waiting for transfers between devices: 0.01 us -> 3.56 us  [shifted(): lax.ppermute(value, axis, [(source, source + steps) for source in range(f...]
    ppermute x9 -> x10, waiting for transfers between devices: 18.7 us -> 15.2 us  [ring_send(): lax.ppermute(value, axis, [(i, (i + step) % SIDE) for i in range(SIDE)])]
    dot_general x1, matrix products: 5.26 us -> 2.1 us  [on_device(): jnp.dot(normalized_input, query_weight, preferred_element_type=jnp.float32)]
    dot_general x1, matrix products: 1.16 us -> 3.82 us  [on_device(): jnp.dot(normalized_input, value_weight, preferred_element_type=jnp.float32)]
    ppermute x9 -> x10, starting transfers between devices: 14.3 us -> 17 us  [ring_send(): lax.ppermute(value, axis, [(i, (i + step) % SIDE) for i in range(SIDE)])]
    slice x1 -> x5, local copies, waits for them, and re-layouts: 3.05 us -> 4.28 us  [the longest x1 2.29 us: route_with_adapters(): outgoing[step * width:(step + 1) * width]]
  transfers between devices with their start and end apart: 14 -> 15, of which waited for: 6 -> 6; matrix products, arithmetic and copies ran while one was open for 30% -> 30% of each run, Pallas kernels for 0% -> 0%
where the time goes in v11:
time: 198 us; the launch traced here: 197 us
  waiting for transfers between devices  58.4 us (29%)
  local copies, waits for them, and re-layouts  49.9 us (25%)
  starting transfers between devices  29.2 us (15%)
  other arithmetic  24.4 us (12%)
  matrix products  19 us (10%)
  between operations  16.4 us (8%)
    reduce_scatter x1, waiting for transfers between devices, on_device(): lax.psum_scatter(partial_out.astype(jnp.bfloat16), ('my', 'mc'), scatter_...  39.6 us
    ppermute x10, starting transfers between devices, ring_send(): lax.ppermute(value, axis, [(i, (i + step) % SIDE) for i in range(SIDE)])  17 us
    ppermute x10, waiting for transfers between devices, ring_send(): lax.ppermute(value, axis, [(i, (i + step) % SIDE) for i in range(SIDE)])  15.2 us
    unnamed x74, local copies, waits for them, and re-layouts  11.5 us
    all_to_all x1, starting transfers between devices, on_device(): lax.all_to_all(jnp.broadcast_to(chosen_down, (model_count, *chosen_down.s...  4.43 us
    all_to_all x1, starting transfers between devices, route(): lax.all_to_all(spread_out, first, 0, 0, tiled=True)  4.29 us
  transfers between devices with their start and end apart: 15, of which 6 were waited for; matrix products, arithmetic and copies ran while one was open for 30% of the time, Pallas kernels for 0%

profile of v11, /device:TPU:0, one launch (start us, length us, event | category | flops | bytes accessed | tf_op | source)
XLA Modules:
  0.0 197.4 jit_solution(1745460012047921047)
XLA Ops:
  6.5 1.9 constant_dynamic-update-slice_fusion.1
  8.5 1.0 pad_maximum_fusion.4
  9.8 0.7 constant_dynamic-update-slice_fusion
  10.5 2.0 %collective-permute-start.4 = (bf16[3,256,256]{2,1,0:T(8,128)(2,1)}, bf16[3,256,256]{2,1,0:T(8,128)(2,1)}, u32[]{:S(2)}, u32[]{:S(2)}) collective-permute-start(bf16[3,256,256]{2,1,0:T(8,128)(2,1)} %get-tuple-element.33), channel_id=1, source_target_pairs={{0,8},{8,16},{16,24},{24,0},{1,9},{9,17},{17,25},{25,1},{2,10},{10... | collective-permute-start | bytes 1179656 | tf_op jit(solution)/shard_map/ppermute | solution.py:115
  12.5 3.6 %collective-permute-start.5 = (bf16[3,256,256]{2,1,0:T(8,128)(2,1)}, bf16[3,256,256]{2,1,0:T(8,128)(2,1)}, u32[]{:S(2)}, u32[]{:S(2)}) collective-permute-start(bf16[3,256,256]{2,1,0:T(8,128)(2,1)} %get-tuple-element.33), channel_id=1, source_target_pairs={{0,16},{8,24},{16,0},{24,8},{1,17},{9,25},{17,1},{25,9},{2,18},{10... | collective-permute-start | bytes 1179656 | tf_op jit(solution)/shard_map/ppermute | solution.py:115
  16.1 1.0 collective-permute-start.6
  17.1 1.1 broadcast_in_dim.40
  18.3 4.3 %all-to-all-start = ((bf16[4,2,256,256]{3,2,1,0:T(8,128)(2,1)}), bf16[4,2,256,256]{3,2,1,0:T(8,128)(2,1)S(1)}, u32[]{:S(2)}, u32[]{:S(2)}) async-start(bf16[4,2,256,256]{3,2,1,0:T(8,128)(2,1)} %broadcast_in_dim.40), calls=%async_computation | async-start | bytes 2097152 | tf_op jit(solution)/shard_map/all_to_all | solution.py:124
  22.8 0.8 gather_fusion.3
  31.6 0.9 fusion.15
  35.8 1.2 pad_clamp_fusion.5
  37.0 1.8 constant_dynamic-update-slice_fusion.4
  38.8 1.8 constant_dynamic-update-slice_fusion.3
  40.6 1.8 constant_dynamic-update-slice_fusion.2
  42.4 3.9 %gather_fusion.5 = bf16[80,64,256]{2,1,0:T(8,128)(2,1)} fusion(bf16[48,64,256]{2,1,0:T(8,128)(2,1)} %bitcast.113, s32[1024]{0:T(1024)} %pad_clamp_fusion.2), kind=kCustom, calls=%fused_computation.5 | custom fusion | bytes 5243200 | tf_op jit(solution)/shard_map/jit(_take)/gather | solution.py:179
  46.3 2.3 %concatenate.59 = bf16[30,64,256]{2,1,0:T(8,128)(2,1)} slice(bf16[80,64,256]{2,1,0:T(8,128)(2,1)} %gather_fusion.5), slice={[20:50], [0:64], [0:256]} | slice | bytes 1966080 | tf_op jit(solution)/shard_map/concatenate | solution.py:182
  48.7 2.0 %collective-permute-start.7 = (bf16[30,64,256]{2,1,0:T(8,128)(2,1)}, bf16[30,64,256]{2,1,0:T(8,128)(2,1)}, u32[]{:S(2)}, u32[]{:S(2)}) collective-permute-start(bf16[30,64,256]{2,1,0:T(8,128)(2,1)} %concatenate.59), channel_id=1, source_target_pairs={{0,32},{32,64},{64,96},{96,0},{1,33},{33,65},{65,97},{97,1},{2,34}... | collective-permute-start | bytes 2949128 | tf_op jit(solution)/shard_map/ppermute | solution.py:115
  50.7 2.3 %fusion.92 = (bf16[20,64,256]{2,1,0:T(8,128)(2,1)S(1)}, bf16[80,64,256]{2,1,0:T(8,128)(2,1)}) fusion(bf16[80,64,256]{2,1,0:T(8,128)(2,1)} %gather_fusion.5), kind=kLoop, calls=%fused_computation.216 | loop fusion | bytes 2621440 | tf_op jit(solution)/shard_map/slice | solution.py:180
  53.0 1.1 pad_maximum_fusion.1
  54.0 1.3 collective-permute-start.9
  55.3 1.8 multiply_cosine_fusion
  57.2 1.2 pad_add_fusion
  58.4 2.1 %gather_fusion.1 = bf16[16,256,256]{2,1,0:T(8,128)(2,1)} fusion(bf16[8,256,256]{2,1,0:T(8,128)(2,1)S(1)} %bitcast.112, s32[1024]{0:T(1024)} %pad_clamp_fusion.6), kind=kCustom, calls=%fused_computation.1 | custom fusion | bytes 4194368 | tf_op jit(solution)/shard_map/jit(_take)/gather | solution.py:134
  60.5 12.0 %collective-permute-done.7 = bf16[30,64,256]{2,1,0:T(8,128)(2,1)} collective-permute-done((bf16[30,64,256]{2,1,0:T(8,128)(2,1)}, bf16[30,64,256]{2,1,0:T(8,128)(2,1)}, u32[]{:S(2)}, u32[]{:S(2)}) %collective-permute-start.7) | collective-permute-done | bytes 983072 | tf_op jit(solution)/shard_map/ppermute | solution.py:115
  72.6 1.0 slice.126
  74.2 2.7 %fusion.93 = (bf16[4,256,256]{2,1,0:T(8,128)(2,1)S(1)}, bf16[4,256,256]{2,1,0:T(8,128)(2,1)}, bf16[4,256,256]{2,1,0:T(8,128)(2,1)}, bf16[4,256,256]{2,1,0:T(8,128)(2,1)S(1)}) fusion(bf16[16,256,256]{2,1,0:T(8,128)(2,1)} %gather_fusion.1), kind=kLoop, calls=%fused_computation.217 | loop fusion | bytes 4194304 | tf_op jit(solution)/shard_map/slice | solution.py:136
  76.9 1.0 collective-permute-start
  77.9 0.8 collective-permute-start.1
  78.7 1.9 collective-permute-start.2
  80.6 1.0 slice.129
  81.6 2.8 %collective-permute-start.10 = (bf16[10,64,256]{2,1,0:T(8,128)(2,1)S(1)}, bf16[10,64,256]{2,1,0:T(8,128)(2,1)S(1)}, u32[]{:S(2)}, u32[]{:S(2)}) collective-permute-start(bf16[10,64,256]{2,1,0:T(8,128)(2,1)S(1)} %slice.129), channel_id=1, source_target_pairs={{0,96},{32,0},{64,32},{96,64},{1,97},{33,1},{65,33},{97,65},{2,98}... | collective-permute-start | bytes 983048 | tf_op jit(solution)/shard_map/ppermute | solution.py:115
  84.4 2.0 %slice_dynamic-update-slice_fusion.1 = bf16[80,64,256]{2,1,0:T(8,128)(2,1)} fusion(bf16[80,64,256]{2,1,0:T(8,128)(2,1)} %get-tuple-element.18, bf16[30,64,256]{2,1,0:T(8,128)(2,1)} %collective-permute-done.7), kind=kLoop, calls=%fused_computation.48 | loop fusion | bytes 1310720
  86.4 0.8 constant_dynamic-update-slice_fusion.8
  87.1 1.8 collective-permute-done.10
  89.0 0.8 constant_dynamic-update-slice_fusion.7
  89.7 2.0 %slice_dynamic-update-slice_fusion = bf16[80,64,256]{2,1,0:T(8,128)(2,1)} fusion(bf16[80,64,256]{2,1,0:T(8,128)(2,1)} %constant_dynamic-update-slice_fusion.7, bf16[30,64,256]{2,1,0:T(8,128)(2,1)} %collective-permute-done.9), kind=kLoop, calls=%fused_computation.47 | loop fusion | bytes 1310720 | tf_op jit(solution)/shard_map/concatenate | solution.py:187
  91.7 2.4 %gather_fusion.7 = bf16[4,64,256]{2,1,0:T(8,128)(2,1)S(1)} fusion(bf16[80,64,256]{2,1,0:T(8,128)(2,1)} %slice_dynamic-update-slice_fusion, s32[1024]{0:T(1024)} %pad_clamp_fusion), kind=kCustom, calls=%fused_computation.7 | custom fusion | bytes 262160 | tf_op jit(solution)/shard_map/jit(_take)/gather | solution.py:197
  94.5 0.9 broadcast_in_dim.46
  95.3 4.4 %all-to-all-start.1 = ((bf16[8,4,16,448]{3,2,1,0:T(8,128)(2,1)}), bf16[8,4,16,448]{3,2,1,0:T(8,128)(2,1)S(1)}, u32[]{:S(2)}, u32[]{:S(2)}) async-start(bf16[8,4,16,448]{3,2,1,0:T(8,128)(2,1)} %broadcast_in_dim.46), calls=%async_computation.1 | async-start | bytes 1048576 | tf_op jit(solution)/shard_map/all_to_all | solution.py:232
  100.1 0.7 collective-permute-done
  100.8 0.6 collective-permute-done.2
  101.4 2.9 %pad_maximum_fusion = bf16[16,256,256]{2,1,0:T(8,128)(2,1)} fusion(bf16[4,256,256]{2,1,0:T(8,128)(2,1)} %collective-permute-done.2, bf16[4,256,256]{2,1,0:T(8,128)(2,1)} %collective-permute-done.1, bf16[4,256,256]{2,1,0:T(8,128)(2,1)} %collective-permute-done, bf16[4,256,256]{2,1,0:T(8,128)(2,1)S(1)} %get-tuple-element.19), kind=kLoop, calls=%fused_computation.23 | loop fusion | flops 3145728 | bytes 4194304 | tf_op jit(solution)/shard_map/concatenate | solution.py:135
  104.3 2.3 %gather_fusion.2 = bf16[4,256,256]{2,1,0:T(8,128)(2,1)S(1)} fusion(bf16[16,256,256]{2,1,0:T(8,128)(2,1)} %pad_maximum_fusion, s32[1024]{0:T(1024)} %pad_clamp_fusion.5), kind=kCustom, calls=%fused_computation.2 | custom fusion | bytes 1048592 | tf_op jit(solution)/shard_map/jit(_take)/gather | solution.py:143
  106.6 1.0 copy.68
  107.8 3.3 %gather_fusion.6 = bf16[16,64,256]{2,1,0:T(8,128)(2,1)} fusion(bf16[80,64,256]{2,1,0:T(8,128)(2,1)} %slice_dynamic-update-slice_fusion, s32[1024]{0:T(1024)} %pad_clamp_fusion.1), kind=kCustom, calls=%fused_computation.6 | custom fusion | bytes 1048640 | tf_op jit(solution)/shard_map/jit(_take)/gather | solution.py:194
  112.0 3.0 %fusion = f32[512]{0:T(512)S(1)} fusion(bf16[512,3584]{0,1:T(8,128)(2,1)} %all-gather.2.cloned.1.call-done), kind=kLoop, calls=%fused_computation.10 | loop fusion | flops 5504512 | bytes 3672064 | tf_op jit(solution)/shard_map/reduce_sum | solution.py:246
  115.1 1.6 fusion.2
  116.7 1.2 convolution_bitcast_fusion
  117.9 1.2 fusion.36
  119.1 0.9 copy-done.27
  120.1 2.1 %fusion.96 = f32[512,512]{0,1:T(8,128)S(1)} fusion(bf16[512,3584]{0,1:T(8,128)(2,1)S(1)} %fusion.2, bf16[3584,512]{1,0:T(8,128)(2,1)S(1)} %copy-done.27), kind=kOutput, calls=%fused_computation.220 | convolution fusion | flops 1879048192 | bytes 8388608 | tf_op jit(solution)/shard_map/dot_general | solution.py:265
  122.2 3.0 %fusion.13 = f32[512,512]{0,1:T(8,128)S(1)} fusion(f32[512,512]{0,1:T(8,128)S(1)} %fusion.96, bf16[64,512]{1,0:T(8,128)(2,1)S(1)} %bitcast.120, bf16[512,64]{0,1:T(8,128)(2,1)S(1)} %bitcast.121, bf16[64,3584]{1,0:T(8,128)(2,1)S(1)} %dot_general.31, bf16[512,3584]{0,1:T(8,128)(2,1)} %copy-done.3), kind=kOutput, calls=%fused_computation.27 | convolution fusion | flops 269025280 | bytes 6356992 | tf_op jit(solution)/shard_map/dot_general | solution.py:259
  125.8 3.8 %convolution_convert_fusion.1 = bf16[512,256]{0,1:T(8,128)(2,1)S(1)} fusion(bf16[512,3584]{0,1:T(8,128)(2,1)} %copy-done.3, bf16[3584,256]{1,0:T(8,128)(2,1)} %param.20), kind=kOutput, calls=%fused_computation.29 | convolution fusion | flops 939655168 | bytes 5767168 | tf_op jit(solution)/shard_map/dot_general | solution.py:274
  129.6 0.7 pad_maximum_fusion.3
  130.4 3.3 %collective-permute-start.3 = (bf16[256,512]{0,1:T(8,128)(2,1)}, bf16[256,512]{0,1:T(8,128)(2,1)}, u32[]{:S(2)}, u32[]{:S(2)}) collective-permute-start(bf16[256,512]{0,1:T(8,128)(2,1)} %pad_maximum_fusion.3), channel_id=1, source_target_pairs={{0,8},{8,16},{16,24},{24,32},{32,40},{40,48},{48,56},{56,64},{64,7... | collective-permute-start | bytes 786440 | tf_op jit(solution)/shard_map/ppermute | solution.py:17
  133.7 0.8 copy.61
  134.5 1.0 subtract_convert_fusion
  135.5 3.6 %collective-permute-done.3 = bf16[256,512]{0,1:T(8,128)(2,1)} collective-permute-done((bf16[256,512]{0,1:T(8,128)(2,1)}, bf16[256,512]{0,1:T(8,128)(2,1)}, u32[]{:S(2)}, u32[]{:S(2)}) %collective-permute-start.3) | collective-permute-done | bytes 262176 | tf_op jit(solution)/shard_map/ppermute | solution.py:17
  139.0 1.0 fusion.95
  140.2 2.6 %fusion.5 = (f32[2,512]{1,0:T(2,128)S(1)}, f32[1792,512,2]{1,0,2:T(8,128)S(1)}) fusion(pred[512,1792]{0,1:T(8,128)(4,1)S(1)} %copy-done.5, bf16[512,2,128]{2,0,1:T(8,128)(2,1)} %get-tuple-element.24, bf16[512,2,128]{2,0,1:T(8,128)(2,1)} %get-tuple-element.23, bf16[512,256]{1,0:T(8,128)(2,1)S(1)} %copy-done.12, bf16[256,256]{1,0:T(8,128)(2,1)S(1)} %copy.60, ...), kind=kOutput, calls=%fused_computation.18 | convolution fusion | flops 948829184 | bytes 9703424 | tf_op jit(solution)/shard_map/tkrd,skd->krts/dot_general | solution.py:90
  142.8 1.7 fusion.3
  144.5 2.4 %divide_convert_fusion = bf16[512,1,2,256]{0,3,2,1:T(8,128)(2,1)S(1)} fusion(f32[1792,512,2]{1,0,2:T(8,128)S(1)} %get-tuple-element.42, f32[2,512]{1,0:T(2,128)S(1)} %get-tuple-element.41, pred[512,1792]{0,1:T(8,128)(4,1)S(1)} %copy-done.5, bf16[512,256]{0,1:T(8,128)(2,1)S(1)} %copy-done.14, bf16[256,256]{0,1:T(8,128)(2,1)S(1)} %get-tuple-element.29, ...), kind=kOutput, calls=%fused_computation.32 | convolution fusion | flops 950140928 | bytes 9707520 | tf_op jit(solution)/shard_map/krts,skd->tkrd/dot_general | solution.py:97
  147.0 3.9 %convolution_convert_fusion = bf16[512,3584]{0,1:T(8,128)(2,1)} fusion(bf16[512,512]{0,1:T(8,128)(2,1)S(1)} %bitcast.129, bf16[512,3584]{1,0:T(8,128)(2,1)S(1)} %copy-done.28), kind=kOutput, calls=%fused_computation.17 | convolution fusion | flops 1880883200 | bytes 7864320 | tf_op jit(solution)/shard_map/dot_general | solution.py:294
  150.9 39.6 %reduce-scatter.2.cloned.1.call-done = bf16[512,448]{0,1:T(8,128)(2,1)} async-done(((bf16[512,3584]{0,1:T(8,128)(2,1)}), bf16[512,448]{0,1:T(8,128)(2,1)}) %reduce-scatter.2.cloned.1.call-update) | async-done | bytes 458768 | tf_op jit(solution)/shard_map/reduce_scatter | solution.py:295
  (144 shorter events, 12.4 us)
Async XLA Ops:
  6.5 110.1 %copy-start = (bf16[3584,256]{1,0:T(8,128)(2,1)S(1)}, bf16[3584,256]{1,0:T(8,128)(2,1)}, u32[]{:S(2)}) copy-start(bf16[3584,256]{1,0:T(8,128)(2,1)} %param.19) | copy-start | bytes 5505028
  6.5 10.6 %copy-start.11 = (bf16[2,256,256]{2,1,0:T(8,128)(2,1)S(1)}, bf16[2,256,256]{2,1,0:T(8,128)(2,1)}, u32[]{:S(2)}) copy-start(bf16[2,256,256]{2,1,0:T(8,128)(2,1)} %param.31) | copy-start | bytes 786436
  6.5 105.4 %all-gather.2.cloned.1.call-start = ((), (), s32[]{:S(2)}) async-start(), calls=%async_computation.3 | async-start | bytes 4128768 | tf_op jit(solution)/shard_map/all_gather | solution.py:243
  8.5 14.1 %copy-start.17 = (s32[16,4]{0,1:T(4,128)S(1)}, s32[16,4]{0,1:T(4,128)}, u32[]{:S(2)}) copy-start(s32[16,4]{0,1:T(4,128)} %param.24) | copy-start | bytes 772
  8.5 14.3 %copy-start.2 = (s32[64]{0:T(128)S(1)}, s32[64]{0:T(128)}, u32[]{:S(2)}) copy-start(s32[64]{0:T(128)} %param.25) | copy-start | bytes 772
  10.5 26.5 %collective-permute-start.4 = (bf16[3,256,256]{2,1,0:T(8,128)(2,1)}, bf16[3,256,256]{2,1,0:T(8,128)(2,1)}, u32[]{:S(2)}, u32[]{:S(2)}) collective-permute-start(bf16[3,256,256]{2,1,0:T(8,128)(2,1)} %get-tuple-element.33), channel_id=1, source_target_pairs={{0,8},{8,16},{16,24},{24,0},{1,9},{9,17},{17,25},{25,1},{2,10},{10... | collective-permute-start | bytes 1179656 | tf_op jit(solution)/shard_map/ppermute | solution.py:115
  12.5 26.3 %collective-permute-start.5 = (bf16[3,256,256]{2,1,0:T(8,128)(2,1)}, bf16[3,256,256]{2,1,0:T(8,128)(2,1)}, u32[]{:S(2)}, u32[]{:S(2)}) collective-permute-start(bf16[3,256,256]{2,1,0:T(8,128)(2,1)} %get-tuple-element.33), channel_id=1, source_target_pairs={{0,16},{8,24},{16,0},{24,8},{1,17},{9,25},{17,1},{25,9},{2,18},{10... | collective-permute-start | bytes 1179656 | tf_op jit(solution)/shard_map/ppermute | solution.py:115
  16.1 24.5 %collective-permute-start.6 = (bf16[3,256,256]{2,1,0:T(8,128)(2,1)}, bf16[3,256,256]{2,1,0:T(8,128)(2,1)}, u32[]{:S(2)}, u32[]{:S(2)}) collective-permute-start(bf16[3,256,256]{2,1,0:T(8,128)(2,1)} %get-tuple-element.33), channel_id=1, source_target_pairs={{0,24},{8,0},{16,8},{24,16},{1,25},{9,1},{17,9},{25,17},{2,26},{10... | collective-permute-start | bytes 1179656 | tf_op jit(solution)/shard_map/ppermute | solution.py:115
  18.3 40.1 %all-to-all-start = ((bf16[4,2,256,256]{3,2,1,0:T(8,128)(2,1)}), bf16[4,2,256,256]{3,2,1,0:T(8,128)(2,1)S(1)}, u32[]{:S(2)}, u32[]{:S(2)}) async-start(bf16[4,2,256,256]{3,2,1,0:T(8,128)(2,1)} %broadcast_in_dim.40), calls=%async_computation | async-start | bytes 2097152 | tf_op jit(solution)/shard_map/all_to_all | solution.py:124
  22.8 0.9 copy-start.18
  22.8 2.1 %copy-start.19 = (s32[16,4]{0,1:T(4,128)S(1)}, s32[16,4]{0,1:T(4,128)}, u32[]{:S(2)}) copy-start(s32[16,4]{0,1:T(4,128)} %param.29) | copy-start | bytes 772
  22.8 2.1 %copy-start.20 = (s32[16,4]{0,1:T(4,128)S(1)}, s32[16,4]{0,1:T(4,128)}, u32[]{:S(2)}) copy-start(s32[16,4]{0,1:T(4,128)} %param.26) | copy-start | bytes 772
  22.8 2.5 %copy-start.29 = (s32[16]{0:T(128)S(1)}, s32[16]{0:T(128)}, u32[]{:S(2)}) copy-start(s32[16]{0:T(128)} %param.27) | copy-start | bytes 196
  25.3 10.1 %copy-start.21 = (s32[4,1]{0,1:T(1,128)}, s32[4,1]{0,1:T(1,128)S(1)}, u32[]{:S(2)}) copy-start(s32[4,1]{0,1:T(1,128)S(1)} %reduce-window.4) | copy-start | bytes 52
  30.4 0.6 copy-start.23
  46.3 6.6 %slice-start = ((bf16[80,64,256]{2,1,0:T(8,128)(2,1)}), bf16[10,64,256]{2,1,0:T(8,128)(2,1)S(1)}, s32[]{:S(2)}) async-start(bf16[80,64,256]{2,1,0:T(8,128)(2,1)} %gather_fusion.5), calls=%async_computation.5 | async-start | bytes 655360 | tf_op jit(solution)/shard_map/slice | solution.py:183
  48.6 6.6 %copy-start.16 = (pred[512]{0:T(512)(128)(4,1)S(1)}, pred[512]{0:T(512)(128)(4,1)}, u32[]{:S(2)}) copy-start(pred[512]{0:T(512)(128)(4,1)} %get-tuple-element.11) | copy-start | bytes 1540
  48.7 6.6 %copy-start.25 = (f32[128]{0:T(128)S(1)}, f32[128]{0:T(128)}, u32[]{:S(2)}) copy-start(f32[128]{0:T(128)} %multiply_power_fusion) | copy-start | bytes 1540
  48.7 8.5 %copy-start.6 = (pred[512,512]{0,1:T(8,128)(4,1)S(1)}, pred[512,512]{0,1:T(8,128)(4,1)}, u32[]{:S(2)}) copy-start(pred[512,512]{0,1:T(8,128)(4,1)} %fusion.15) | copy-start | bytes 786436
  48.7 23.9 %collective-permute-start.7 = (bf16[30,64,256]{2,1,0:T(8,128)(2,1)}, bf16[30,64,256]{2,1,0:T(8,128)(2,1)}, u32[]{:S(2)}, u32[]{:S(2)}) collective-permute-start(bf16[30,64,256]{2,1,0:T(8,128)(2,1)} %concatenate.59), channel_id=1, source_target_pairs={{0,32},{32,64},{64,96},{96,0},{1,33},{33,65},{65,97},{97,1},{2,34}... | collective-permute-start | bytes 2949128 | tf_op jit(solution)/shard_map/ppermute | solution.py:115
  54.0 26.6 %collective-permute-start.9 = (bf16[30,64,256]{2,1,0:T(8,128)(2,1)}, bf16[30,64,256]{2,1,0:T(8,128)(2,1)}, u32[]{:S(2)}, u32[]{:S(2)}) collective-permute-start(bf16[30,64,256]{2,1,0:T(8,128)(2,1)} %pad_maximum_fusion.1), channel_id=1, source_target_pairs={{0,96},{32,0},{64,32},{96,64},{1,97},{33,1},{65,33},{97,65},{2,98}... | collective-permute-start | bytes 2949128 | tf_op jit(solution)/shard_map/ppermute | solution.py:115
  73.6 12.8 %collective-permute-start.8 = (bf16[10,64,256]{2,1,0:T(8,128)(2,1)S(1)}, bf16[10,64,256]{2,1,0:T(8,128)(2,1)S(1)}, u32[]{:S(2)}, u32[]{:S(2)}) collective-permute-start(bf16[10,64,256]{2,1,0:T(8,128)(2,1)S(1)} %slice.126), channel_id=1, source_target_pairs={{0,32},{32,64},{64,96},{96,0},{1,33},{33,65},{65,97},{97,1},{2,34}... | collective-permute-start | bytes 983048 | tf_op jit(solution)/shard_map/ppermute | solution.py:115
  76.9 23.9 %collective-permute-start = (bf16[4,256,256]{2,1,0:T(8,128)(2,1)}, bf16[4,256,256]{2,1,0:T(8,128)(2,1)}, u32[]{:S(2)}, u32[]{:S(2)}) collective-permute-start(bf16[4,256,256]{2,1,0:T(8,128)(2,1)} %get-tuple-element.21), channel_id=1, source_target_pairs={{0,8},{8,16},{16,24},{24,0},{1,9},{9,17},{17,25},{25,1},{2,10},{10... | collective-permute-start | bytes 1572872 | tf_op jit(solution)/shard_map/ppermute | solution.py:115
  77.9 22.8 %collective-permute-start.1 = (bf16[4,256,256]{2,1,0:T(8,128)(2,1)}, bf16[4,256,256]{2,1,0:T(8,128)(2,1)}, u32[]{:S(2)}, u32[]{:S(2)}) collective-permute-start(bf16[4,256,256]{2,1,0:T(8,128)(2,1)} %get-tuple-element.20), channel_id=1, source_target_pairs={{0,16},{8,24},{16,0},{24,8},{1,17},{9,25},{17,1},{25,9},{2,18},{10... | collective-permute-start | bytes 1572872 | tf_op jit(solution)/shard_map/ppermute | solution.py:115
  78.7 22.7 %collective-permute-start.2 = (bf16[4,256,256]{2,1,0:T(8,128)(2,1)S(1)}, bf16[4,256,256]{2,1,0:T(8,128)(2,1)}, u32[]{:S(2)}, u32[]{:S(2)}) collective-permute-start(bf16[4,256,256]{2,1,0:T(8,128)(2,1)S(1)} %get-tuple-element.22), channel_id=1, source_target_pairs={{0,24},{8,0},{16,8},{24,16},{1,25},{9,1},{17,9},{25,17},{2,26},{10... | collective-permute-start | bytes 1572872 | tf_op jit(solution)/shard_map/ppermute | solution.py:115
  81.6 7.4 %collective-permute-start.10 = (bf16[10,64,256]{2,1,0:T(8,128)(2,1)S(1)}, bf16[10,64,256]{2,1,0:T(8,128)(2,1)S(1)}, u32[]{:S(2)}, u32[]{:S(2)}) collective-permute-start(bf16[10,64,256]{2,1,0:T(8,128)(2,1)S(1)} %slice.129), channel_id=1, source_target_pairs={{0,96},{32,0},{64,32},{96,64},{1,97},{33,1},{65,33},{97,65},{2,98}... | collective-permute-start | bytes 983048 | tf_op jit(solution)/shard_map/ppermute | solution.py:115
  86.4 13.6 %copy-start.22 = (s32[4,1]{0,1:T(1,128)S(1)}, s32[4,1]{0,1:T(1,128)}, u32[]{:S(2)}) copy-start(s32[4,1]{0,1:T(1,128)} %copy-done.21) | copy-start | bytes 52
  86.4 13.6 %copy-start.24 = (s32[4]{0:T(128)S(1)}, s32[4]{0:T(128)}, u32[]{:S(2)}) copy-start(s32[4]{0:T(128)} %copy-done.23) | copy-start | bytes 52
  95.3 15.7 %all-to-all-start.1 = ((bf16[8,4,16,448]{3,2,1,0:T(8,128)(2,1)}), bf16[8,4,16,448]{3,2,1,0:T(8,128)(2,1)S(1)}, u32[]{:S(2)}, u32[]{:S(2)}) async-start(bf16[8,4,16,448]{3,2,1,0:T(8,128)(2,1)} %broadcast_in_dim.46), calls=%async_computation.1 | async-start | bytes 1048576 | tf_op jit(solution)/shard_map/all_to_all | solution.py:232
  99.8 90.8 %reduce-scatter.2.cloned.1.call-start = ((), (), s32[]{:S(2)}) async-start(), calls=%async_computation.4 | async-start | bytes 4128768 | tf_op jit(solution)/shard_map/reduce_scatter | solution.py:295
  111.1 3.9 %copy-start.15 = (f32[3584]{0:T(1024)S(1)}, f32[3584]{0:T(1024)}, u32[]{:S(2)}) copy-start(f32[3584]{0:T(1024)} %param.17) | copy-start | bytes 43012
  112.0 3.1 %copy-start.4 = (bf16[512,3584]{0,1:T(8,128)(2,1)S(1)}, bf16[512,3584]{0,1:T(8,128)(2,1)}, u32[]{:S(2)}) copy-start(bf16[512,3584]{0,1:T(8,128)(2,1)} %all-gather.2.cloned.1.call-done) | copy-start | bytes 11010052
  116.7 2.4 %copy-start.3 = (bf16[512,3584]{0,1:T(8,128)(2,1)}, bf16[512,3584]{0,1:T(8,128)(2,1)S(1)}, u32[]{:S(2)}) copy-start(bf16[512,3584]{0,1:T(8,128)(2,1)S(1)} %fusion.2) | copy-start | bytes 11010052
  116.7 1.2 copy-start.26
  116.7 3.4 %copy-start.27 = (bf16[3584,512]{1,0:T(8,128)(2,1)S(1)}, bf16[3584,512]{1,0:T(8,128)(2,1)}, u32[]{:S(2)}) copy-start(bf16[3584,512]{1,0:T(8,128)(2,1)} %param.18) | copy-start | bytes 11010052
  125.7 8.8 %copy-start.7 = (f32[512,128]{1,0:T(8,128)S(1)}, f32[512,128]{1,0:T(8,128)}, u32[]{:S(2)}) copy-start(f32[512,128]{1,0:T(8,128)} %get-tuple-element.39) | copy-start | bytes 786436
  125.7 8.8 %copy-start.8 = (f32[512,128]{1,0:T(8,128)S(1)}, f32[512,128]{1,0:T(8,128)}, u32[]{:S(2)}) copy-start(f32[512,128]{1,0:T(8,128)} %get-tuple-element.40) | copy-start | bytes 786436
  129.6 0.8 copy-start.13
  129.6 10.5 %copy-start.5 = (pred[512,1792]{0,1:T(8,128)(4,1)S(1)}, pred[512,1792]{0,1:T(8,128)(4,1)}, u32[]{:S(2)}) copy-start(pred[512,1792]{0,1:T(8,128)(4,1)} %pad_add_fusion) | copy-start | bytes 2752516
  129.6 10.5 %copy-start.10 = (bf16[16,64,256]{2,1,0:T(8,128)(2,1)S(1)}, bf16[16,64,256]{2,1,0:T(8,128)(2,1)}, u32[]{:S(2)}) copy-start(bf16[16,64,256]{2,1,0:T(8,128)(2,1)} %gather_fusion.6) | copy-start | bytes 1572868
  130.4 8.7 %collective-permute-start.3 = (bf16[256,512]{0,1:T(8,128)(2,1)}, bf16[256,512]{0,1:T(8,128)(2,1)}, u32[]{:S(2)}, u32[]{:S(2)}) collective-permute-start(bf16[256,512]{0,1:T(8,128)(2,1)} %pad_maximum_fusion.3), channel_id=1, source_target_pairs={{0,8},{8,16},{16,24},{24,32},{32,40},{40,48},{48,56},{56,64},{64,7... | collective-permute-start | bytes 786440 | tf_op jit(solution)/shard_map/ppermute | solution.py:17
  134.5 5.6 %copy-start.12 = (bf16[512,256]{1,0:T(8,128)(2,1)S(1)}, bf16[512,256]{1,0:T(8,128)(2,1)}, u32[]{:S(2)}) copy-start(bf16[512,256]{1,0:T(8,128)(2,1)} %copy.61) | copy-start | bytes 786436
  142.8 1.7 copy-start.9
  142.8 1.7 copy-start.14
  144.5 2.4 %copy-start.28 = (bf16[512,3584]{1,0:T(8,128)(2,1)S(1)}, bf16[512,3584]{1,0:T(8,128)(2,1)}, u32[]{:S(2)}) copy-start(bf16[512,3584]{1,0:T(8,128)(2,1)} %param.21) | copy-start | bytes 11010052
  147.0 43.6 %copy-start.1 = (bf16[3584,256]{1,0:T(8,128)(2,1)S(1)}, bf16[3584,256]{1,0:T(8,128)(2,1)}, u32[]{:S(2)}) copy-start(bf16[3584,256]{1,0:T(8,128)(2,1)} %param.19) | copy-start | bytes 5505028
Sparse Core Ops, SparseCore 0:
  17.3 29.3 all-gather.1
  151.0 39.4 reduce-scatter.1

commit v12 on v10

--- a/solution.py
+++ b/solution.py
@@ -177,23 +177,29 @@
     source = jnp.take(table, askers, axis=0, mode="clip")
     width = source.shape[1]
     outgoing = jnp.take(held, source.reshape(-1), axis=0, mode="clip")
-    received = jnp.concatenate(
-        [outgoing[:width]]
-        + [
-            ring_send(outgoing[step * width:(step + 1) * width], second, step)
-            for step in range(1, SIDE)
-        ]
-    )
+    lead = slots_items = block_wanted.shape[1] * pieces
+    adapter_parts = [outgoing[lead:width]] + [
+        ring_send(outgoing[step * width + lead:(step + 1) * width], second, step)
+        for step in range(1, SIDE)
+    ]
+    block_parts = [outgoing[:lead]] + [
+        ring_send(outgoing[step * width:step * width + lead], second, step)
+        for step in range(1, SIDE)
+    ]
+    adapter_received = jnp.concatenate(adapter_parts)
+    received = jnp.concatenate(block_parts)
     slots = block_wanted.shape[1]
     slot = jnp.arange(slots)
     block_pick = (
-        (((own_b - block_b[me]) % SIDE) * width + slot * pieces)[:, None] + quarter
+        (((own_b - block_b[me]) % SIDE) * slots_items + slot * pieces)[:, None] + quarter
     ).reshape(-1)
-    adapter_pick = ((own_b - adapter_b[me]) % SIDE) * width + slots * pieces + slot
+    adapter_pick = ((own_b - adapter_b[me]) % SIDE) * slots + slot
     chosen_blocks = jnp.take(received, block_pick, axis=0, mode="clip").reshape(
         slots, rows, lanes
     )
-    chosen_adapters = jnp.take(received, adapter_pick, axis=0, mode="clip").reshape(slots, -1)
+    chosen_adapters = jnp.take(adapter_received, adapter_pick, axis=0, mode="clip").reshape(
+        slots, -1
+    )
     chosen_adapters = chosen_adapters[:, : flat.shape[1]].reshape(slots, *adapters.shape[1:])
     return chosen_blocks, chosen_adapters
 

time: 181 us -> 185 us (1.022)
  starting transfers between devices: 25.3 us -> 36 us
  waiting for transfers between devices: 58.2 us -> 49.4 us
    ppermute x9 -> x12, waiting for transfers between devices: 18.7 us -> 7.37 us  [ring_send(): lax.ppermute(value, axis, [(i, (i + step) % SIDE) for i in range(SIDE)])]
    ppermute x9 -> x12, starting transfers between devices: 14.3 us -> 24.9 us  [ring_send(): lax.ppermute(value, axis, [(i, (i + step) % SIDE) for i in range(SIDE)])]
    all_to_all x1, waiting for transfers between devices: 0.7 us -> 3.82 us  [on_device(): lax.all_to_all(jnp.broadcast_to(chosen_down, (model_count, *chosen_down.s...]
    slice x1 -> x2, local copies, waits for them, and re-layouts: 3.05 us -> 4.59 us  [the longest x1 2.75 us: route_with_adapters(): outgoing[:lead]]
    concatenate x1 -> x2, other arithmetic: 2.85 us -> 4.04 us  [the longest x1 2.94 us: route_with_adapters(): received = jnp.concatenate(block_parts)]
  transfers between devices with their start and end apart: 14 -> 17, of which waited for: 6 -> 5; matrix products, arithmetic and copies ran while one was open for 30% -> 30% of each run, Pallas kernels for 0% -> 0%
where the time goes in v12:
time: 185 us; the launch traced here: 184 us
  waiting for transfers between devices  49.4 us (27%)
  local copies, waits for them, and re-layouts  39.4 us (21%)
  starting transfers between devices  36 us (19%)
  other arithmetic  23.3 us (13%)
  matrix products  19.6 us (11%)
  between operations  16.6 us (9%)
    reduce_scatter x1, waiting for transfers between devices, on_device(): lax.psum_scatter(partial_out.astype(jnp.bfloat16), ('my', 'mc'), scatter_...  38.2 us
    ppermute x12, starting transfers between devices, ring_send(): lax.ppermute(value, axis, [(i, (i + step) % SIDE) for i in range(SIDE)])  24.9 us
    unnamed x67, local copies, waits for them, and re-layouts  7.71 us
    ppermute x12, waiting for transfers between devices, ring_send(): lax.ppermute(value, axis, [(i, (i + step) % SIDE) for i in range(SIDE)])  7.37 us
    dot_general x1, matrix products, on_device(): jnp.dot(normalized_input, query_weight, preferred_element_type=jnp.float32)  5.26 us
    all_to_all x1, starting transfers between devices, on_device(): lax.all_to_all(jnp.broadcast_to(chosen_down, (model_count, *chosen_down.s...  4.43 us
    all_to_all x1, starting transfers between devices, route(): lax.all_to_all(spread_out, first, 0, 0, tiled=True)  4.29 us
    dot_general x1, matrix products, on_device(): jnp.dot(attended, output_weight, preferred_element_type=jnp.float32)  3.91 us
  transfers between devices with their start and end apart: 17, of which 5 were waited for; matrix products, arithmetic and copies ran while one was open for 30% of the time, Pallas kernels for 0%

profile of v12, /device:TPU:0, one launch (start us, length us, event | category | flops | bytes accessed | tf_op | source)
XLA Modules:
  0.0 184.4 jit_solution(7105777456081900446)
XLA Ops:
  6.5 1.1 pad_maximum_fusion.5
  8.0 1.8 constant_dynamic-update-slice_fusion.1
  9.8 0.7 constant_dynamic-update-slice_fusion
  10.5 4.1 %collective-permute-start.6 = (bf16[3,256,256]{2,1,0:T(8,128)(2,1)}, bf16[3,256,256]{2,1,0:T(8,128)(2,1)S(1)}, u32[]{:S(2)}, u32[]{:S(2)}) collective-permute-start(bf16[3,256,256]{2,1,0:T(8,128)(2,1)} %get-tuple-element.39), channel_id=1, source_target_pairs={{0,24},{8,0},{16,8},{24,16},{1,25},{9,1},{17,9},{25,17},{2,26},{10... | collective-permute-start | bytes 1179656 | tf_op jit(solution)/shard_map/ppermute | solution.py:115
  14.7 1.3 collective-permute-start.4
  16.0 1.1 broadcast_in_dim.40
  17.1 4.3 %all-to-all-start = ((bf16[4,2,256,256]{3,2,1,0:T(8,128)(2,1)}), bf16[4,2,256,256]{3,2,1,0:T(8,128)(2,1)S(1)}, u32[]{:S(2)}, u32[]{:S(2)}) async-start(bf16[4,2,256,256]{3,2,1,0:T(8,128)(2,1)} %broadcast_in_dim.40), calls=%async_computation | async-start | bytes 2097152 | tf_op jit(solution)/shard_map/all_to_all | solution.py:124
  21.8 0.6 constant_dynamic-slice_fusion.7
  22.4 0.6 dynamic_slice.24
  26.0 0.8 gather_fusion.3
  28.4 0.6 pad_clamp_fusion.7
  29.0 0.6 pad_clamp_fusion.1
  30.0 1.8 multiply_cosine_fusion
  31.9 1.2 pad_add_fusion
  33.1 0.6 pad_clamp_fusion
  33.7 0.6 gather_fusion.4
  34.4 0.8 collective-permute-done.4
  35.2 1.8 constant_dynamic-update-slice_fusion.4
  37.0 1.8 constant_dynamic-update-slice_fusion.3
  38.8 0.8 constant_dynamic-update-slice_fusion.2
  39.6 3.9 %gather_fusion.5 = bf16[80,64,256]{2,1,0:T(8,128)(2,1)} fusion(bf16[48,64,256]{2,1,0:T(8,128)(2,1)} %bitcast.16, s32[1024]{0:T(1024)S(1)} %pad_clamp_fusion.2), kind=kCustom, calls=%fused_computation.5 | custom fusion | bytes 5243200 | tf_op jit(solution)/shard_map/jit(_take)/gather | solution.py:179
  43.5 2.7 %fusion.92 = (bf16[16,64,256]{2,1,0:T(8,128)(2,1)S(1)}, bf16[16,64,256]{2,1,0:T(8,128)(2,1)}, bf16[16,64,256]{2,1,0:T(8,128)(2,1)}, bf16[16,64,256]{2,1,0:T(8,128)(2,1)}) fusion(bf16[80,64,256]{2,1,0:T(8,128)(2,1)} %gather_fusion.5), kind=kLoop, calls=%fused_computation.212 | loop fusion | bytes 4194304 | tf_op jit(solution)/shard_map/slice | solution.py:185
  46.2 2.7 %collective-permute-start.9 = (bf16[16,64,256]{2,1,0:T(8,128)(2,1)}, bf16[16,64,256]{2,1,0:T(8,128)(2,1)}, u32[]{:S(2)}, u32[]{:S(2)}) collective-permute-start(bf16[16,64,256]{2,1,0:T(8,128)(2,1)} %get-tuple-element.22), channel_id=1, source_target_pairs={{0,96},{32,0},{64,32},{96,64},{1,97},{33,1},{65,33},{97,65},{2,98}... | collective-permute-start | bytes 1572872 | tf_op jit(solution)/shard_map/ppermute | solution.py:115
  49.0 1.8 %fusion.91 = (bf16[4,64,256]{2,1,0:T(8,128)(2,1)S(1)}, bf16[4,64,256]{2,1,0:T(8,128)(2,1)}, bf16[4,64,256]{2,1,0:T(8,128)(2,1)}, bf16[4,64,256]{2,1,0:T(8,128)(2,1)}) fusion(bf16[80,64,256]{2,1,0:T(8,128)(2,1)} %gather_fusion.5), kind=kLoop, calls=%fused_computation.211 | loop fusion | bytes 1048576 | tf_op jit(solution)/shard_map/slice | solution.py:181
  50.8 0.8 collective-permute-start.11
  51.6 0.6 pad_clamp_fusion.5
  52.2 0.7 gather_fusion
  53.0 0.9 collective-permute-start.10
  53.9 2.4 %collective-permute-start.12 = (bf16[4,64,256]{2,1,0:T(8,128)(2,1)}, bf16[4,64,256]{2,1,0:T(8,128)(2,1)}, u32[]{:S(2)}, u32[]{:S(2)}) collective-permute-start(bf16[4,64,256]{2,1,0:T(8,128)(2,1)} %get-tuple-element.20), channel_id=1, source_target_pairs={{0,96},{32,0},{64,32},{96,64},{1,97},{33,1},{65,33},{97,65},{2,98}... | collective-permute-start | bytes 393224 | tf_op jit(solution)/shard_map/ppermute | solution.py:115
  56.3 1.5 collective-permute-start.8
  57.8 2.0 %gather_fusion.1 = bf16[16,256,256]{2,1,0:T(8,128)(2,1)} fusion(bf16[8,256,256]{2,1,0:T(8,128)(2,1)S(1)} %bitcast.112, s32[1024]{0:T(1024)S(1)} %pad_clamp_fusion.6), kind=kCustom, calls=%fused_computation.1 | custom fusion | bytes 4194368 | tf_op jit(solution)/shard_map/jit(_take)/gather | solution.py:134
  59.8 6.8 %collective-permute-start.7 = (bf16[16,64,256]{2,1,0:T(8,128)(2,1)}, bf16[16,64,256]{2,1,0:T(8,128)(2,1)}, u32[]{:S(2)}, u32[]{:S(2)}) collective-permute-start(bf16[16,64,256]{2,1,0:T(8,128)(2,1)} %get-tuple-element.24), channel_id=1, source_target_pairs={{0,32},{32,64},{64,96},{96,0},{1,33},{33,65},{65,97},{97,1},{2,34}... | collective-permute-start | bytes 1572872 | tf_op jit(solution)/shard_map/ppermute | solution.py:115
  66.6 2.9 %fusion.93 = (bf16[4,256,256]{2,1,0:T(8,128)(2,1)}, bf16[4,256,256]{2,1,0:T(8,128)(2,1)}, bf16[4,256,256]{2,1,0:T(8,128)(2,1)}, bf16[4,256,256]{2,1,0:T(8,128)(2,1)}) fusion(bf16[16,256,256]{2,1,0:T(8,128)(2,1)} %gather_fusion.1), kind=kLoop, calls=%fused_computation.213 | loop fusion | bytes 4194304 | tf_op jit(solution)/shard_map/slice | solution.py:136
  69.5 1.0 collective-permute-done.10
  70.6 1.1 collective-permute-start.1
  71.7 5.5 %collective-permute-done.12 = bf16[4,64,256]{2,1,0:T(8,128)(2,1)} collective-permute-done((bf16[4,64,256]{2,1,0:T(8,128)(2,1)}, bf16[4,64,256]{2,1,0:T(8,128)(2,1)}, u32[]{:S(2)}, u32[]{:S(2)}) %collective-permute-start.12) | collective-permute-done | bytes 131104 | tf_op jit(solution)/shard_map/ppermute | solution.py:115
  77.2 0.6 collective-permute-start
  77.8 2.6 %collective-permute-start.2 = (bf16[4,256,256]{2,1,0:T(8,128)(2,1)}, bf16[4,256,256]{2,1,0:T(8,128)(2,1)}, u32[]{:S(2)}, u32[]{:S(2)}) collective-permute-start(bf16[4,256,256]{2,1,0:T(8,128)(2,1)} %get-tuple-element.28), channel_id=1, source_target_pairs={{0,24},{8,0},{16,8},{24,16},{1,25},{9,1},{17,9},{25,17},{2,26},{10... | collective-permute-start | bytes 1572872 | tf_op jit(solution)/shard_map/ppermute | solution.py:115
  80.4 1.1 pad_maximum_fusion.2
  81.5 0.7 gather_fusion.7
  82.5 0.8 broadcast_in_dim.46
  83.4 4.4 %all-to-all-start.1 = ((bf16[8,4,16,448]{3,2,1,0:T(8,128)(2,1)}), bf16[8,4,16,448]{3,2,1,0:T(8,128)(2,1)S(1)}, u32[]{:S(2)}, u32[]{:S(2)}) async-start(bf16[8,4,16,448]{3,2,1,0:T(8,128)(2,1)} %broadcast_in_dim.46), calls=%async_computation.1 | async-start | bytes 1048576 | tf_op jit(solution)/shard_map/all_to_all | solution.py:237
  88.2 2.9 %pad_maximum_fusion.1 = bf16[64,64,256]{2,1,0:T(8,128)(2,1)} fusion(bf16[16,64,256]{2,1,0:T(8,128)(2,1)} %collective-permute-done.9, bf16[16,64,256]{2,1,0:T(8,128)(2,1)} %collective-permute-done.8, bf16[16,64,256]{2,1,0:T(8,128)(2,1)} %collective-permute-done.7, bf16[16,64,256]{2,1,0:T(8,128)(2,1)S(1)} %get-tuple-element.21), kind=kLoop, calls=%fused_computation.24 | loop fusion | flops 3145728 | bytes 4194304 | tf_op jit(solution)/shard_map/concatenate | solution.py:190
  91.2 3.1 %gather_fusion.6 = bf16[16,64,256]{2,1,0:T(8,128)(2,1)} fusion(bf16[64,64,256]{2,1,0:T(8,128)(2,1)} %pad_maximum_fusion.1, s32[1024]{0:T(1024)} %pad_clamp_fusion.1), kind=kCustom, calls=%fused_computation.6 | custom fusion | bytes 1048640 | tf_op jit(solution)/shard_map/jit(_take)/gather | solution.py:197
  94.3 3.8 %all-to-all-done.1 = bf16[8,4,16,448]{3,2,1,0:T(8,128)(2,1)S(1)} async-done(((bf16[8,4,16,448]{3,2,1,0:T(8,128)(2,1)}), bf16[8,4,16,448]{3,2,1,0:T(8,128)(2,1)S(1)}, u32[]{:S(2)}, u32[]{:S(2)}) %all-to-all-start.1) | async-done | bytes 458784 | tf_op jit(solution)/shard_map/all_to_all | solution.py:237
  98.4 1.3 dot_general.31
  99.8 2.9 %pad_maximum_fusion = bf16[16,256,256]{2,1,0:T(8,128)(2,1)} fusion(bf16[4,256,256]{2,1,0:T(8,128)(2,1)} %collective-permute-done.2, bf16[4,256,256]{2,1,0:T(8,128)(2,1)} %collective-permute-done.1, bf16[4,256,256]{2,1,0:T(8,128)(2,1)} %collective-permute-done, bf16[4,256,256]{2,1,0:T(8,128)(2,1)S(1)} %copy-done.6), kind=kLoop, calls=%fused_computation.23 | loop fusion | flops 3145728 | bytes 4194304 | tf_op jit(solution)/shard_map/concatenate | solution.py:135
  102.7 2.3 %gather_fusion.2 = bf16[4,256,256]{2,1,0:T(8,128)(2,1)S(1)} fusion(bf16[16,256,256]{2,1,0:T(8,128)(2,1)} %pad_maximum_fusion, s32[1024]{0:T(1024)} %pad_clamp_fusion.5), kind=kCustom, calls=%fused_computation.2 | custom fusion | bytes 1048592 | tf_op jit(solution)/shard_map/jit(_take)/gather | solution.py:143
  105.0 1.0 copy.68
  106.0 3.0 %fusion = f32[512]{0:T(512)S(1)} fusion(bf16[512,3584]{0,1:T(8,128)(2,1)} %all-gather.2.cloned.1.call-done), kind=kLoop, calls=%fused_computation.10 | loop fusion | flops 5504512 | bytes 3672064 | tf_op jit(solution)/shard_map/reduce_sum | solution.py:251
  109.2 1.6 fusion.2
  110.8 1.2 convolution_bitcast_fusion
  112.0 1.2 fusion.36
  113.6 1.2 convolution_convert_fusion.1
  114.9 0.8 pad_maximum_fusion.4
  115.7 2.2 %collective-permute-start.3 = (bf16[256,512]{0,1:T(8,128)(2,1)}, bf16[256,512]{0,1:T(8,128)(2,1)}, u32[]{:S(2)}, u32[]{:S(2)}) collective-permute-start(bf16[256,512]{0,1:T(8,128)(2,1)} %pad_maximum_fusion.4), channel_id=1, source_target_pairs={{0,8},{8,16},{16,24},{24,32},{32,40},{40,48},{48,56},{56,64},{64,7... | collective-permute-start | bytes 786440 | tf_op jit(solution)/shard_map/ppermute | solution.py:17
  117.9 5.3 %fusion.96 = f32[512,512]{0,1:T(8,128)S(1)} fusion(bf16[512,3584]{0,1:T(8,128)(2,1)} %copy-done.3, bf16[3584,512]{1,0:T(8,128)(2,1)} %param.18), kind=kOutput, calls=%fused_computation.216 | convolution fusion | flops 1879048192 | bytes 8388608 | tf_op jit(solution)/shard_map/dot_general | solution.py:270
  123.2 3.1 %fusion.13 = f32[512,512]{0,1:T(8,128)S(1)} fusion(f32[512,512]{0,1:T(8,128)S(1)} %fusion.96, bf16[64,512]{1,0:T(8,128)(2,1)S(1)} %bitcast.119, bf16[512,64]{0,1:T(8,128)(2,1)S(1)} %bitcast.120, bf16[64,3584]{1,0:T(8,128)(2,1)S(1)} %copy-done.7, bf16[512,3584]{0,1:T(8,128)(2,1)} %copy-done.3), kind=kOutput, calls=%fused_computation.28 | convolution fusion | flops 269025280 | bytes 6356992 | tf_op jit(solution)/shard_map/dot_general | solution.py:264
  127.5 1.0 fusion.95
  128.6 2.6 %fusion.5 = (f32[2,512]{1,0:T(2,128)S(1)}, f32[1792,512,2]{1,0,2:T(8,128)S(1)}) fusion(pred[512,1792]{0,1:T(8,128)(4,1)S(1)} %copy-done.5, bf16[512,2,128]{2,0,1:T(8,128)(2,1)S(1)} %get-tuple-element.30, bf16[512,2,128]{2,0,1:T(8,128)(2,1)S(1)} %get-tuple-element.29, bf16[512,256]{1,0:T(8,128)(2,1)S(1)} %copy.61, bf16[256,256]{1,0:T(8,128)(2,1)S(1)} %copy.60, ...), kind=kOutput, calls=%fused_computation.18 | convolution fusion | flops 948829184 | bytes 9703424 | tf_op jit(solution)/shard_map/tkrd,skd->krts/dot_general | solution.py:90
  131.2 1.7 fusion.3
  132.9 2.4 %divide_convert_fusion = bf16[512,1,2,256]{0,3,2,1:T(8,128)(2,1)S(1)} fusion(f32[1792,512,2]{1,0,2:T(8,128)S(1)} %get-tuple-element.48, f32[2,512]{1,0:T(2,128)S(1)} %get-tuple-element.47, pred[512,1792]{0,1:T(8,128)(4,1)S(1)} %copy-done.5, bf16[512,256]{0,1:T(8,128)(2,1)S(1)} %copy-done.13, bf16[256,256]{0,1:T(8,128)(2,1)S(1)} %get-tuple-element.35, ...), kind=kOutput, calls=%fused_computation.33 | convolution fusion | flops 950140928 | bytes 9707520 | tf_op jit(solution)/shard_map/krts,skd->tkrd/dot_general | solution.py:97
  135.4 3.9 %convolution_convert_fusion = bf16[512,3584]{0,1:T(8,128)(2,1)} fusion(bf16[512,512]{0,1:T(8,128)(2,1)S(1)} %bitcast.128, bf16[512,3584]{1,0:T(8,128)(2,1)S(1)} %copy-done.25), kind=kOutput, calls=%fused_computation.17 | convolution fusion | flops 1880883200 | bytes 7864320 | tf_op jit(solution)/shard_map/dot_general | solution.py:299
  139.3 38.2 %reduce-scatter.2.cloned.1.call-done = bf16[512,448]{0,1:T(8,128)(2,1)} async-done(((bf16[512,3584]{0,1:T(8,128)(2,1)}), bf16[512,448]{0,1:T(8,128)(2,1)}) %reduce-scatter.2.cloned.1.call-update) | async-done | bytes 458768 | tf_op jit(solution)/shard_map/reduce_scatter | solution.py:300
  (137 shorter events, 6.3 us)
Async XLA Ops:
  6.5 104.2 %copy-start = (bf16[3584,256]{1,0:T(8,128)(2,1)S(1)}, bf16[3584,256]{1,0:T(8,128)(2,1)}, u32[]{:S(2)}) copy-start(bf16[3584,256]{1,0:T(8,128)(2,1)} %param.19) | copy-start | bytes 5505028
  6.5 9.4 %copy-start.11 = (bf16[2,256,256]{2,1,0:T(8,128)(2,1)S(1)}, bf16[2,256,256]{2,1,0:T(8,128)(2,1)}, u32[]{:S(2)}) copy-start(bf16[2,256,256]{2,1,0:T(8,128)(2,1)} %param.31) | copy-start | bytes 786436
  6.5 99.5 %all-gather.2.cloned.1.call-start = ((), (), s32[]{:S(2)}) async-start(), calls=%async_computation.3 | async-start | bytes 4128768 | tf_op jit(solution)/shard_map/all_gather | solution.py:248
  7.9 13.5 %copy-start.15 = (s32[16,4]{0,1:T(4,128)S(1)}, s32[16,4]{0,1:T(4,128)}, u32[]{:S(2)}) copy-start(s32[16,4]{0,1:T(4,128)} %param.24) | copy-start | bytes 772
  8.0 13.6 %copy-start.16 = (s32[16,4]{0,1:T(4,128)S(1)}, s32[16,4]{0,1:T(4,128)}, u32[]{:S(2)}) copy-start(s32[16,4]{0,1:T(4,128)} %param.29) | copy-start | bytes 772
  8.0 13.6 %copy-start.17 = (s32[16,4]{0,1:T(4,128)S(1)}, s32[16,4]{0,1:T(4,128)}, u32[]{:S(2)}) copy-start(s32[16,4]{0,1:T(4,128)} %param.26) | copy-start | bytes 772
  8.0 14.4 %copy-start.27 = (s32[16]{0:T(128)S(1)}, s32[16]{0:T(128)}, u32[]{:S(2)}) copy-start(s32[16]{0:T(128)} %param.27) | copy-start | bytes 196
  8.0 18.0 %copy-start.2 = (s32[64]{0:T(128)S(1)}, s32[64]{0:T(128)}, u32[]{:S(2)}) copy-start(s32[64]{0:T(128)} %param.25) | copy-start | bytes 772
  10.5 28.2 %collective-permute-start.6 = (bf16[3,256,256]{2,1,0:T(8,128)(2,1)}, bf16[3,256,256]{2,1,0:T(8,128)(2,1)S(1)}, u32[]{:S(2)}, u32[]{:S(2)}) collective-permute-start(bf16[3,256,256]{2,1,0:T(8,128)(2,1)} %get-tuple-element.39), channel_id=1, source_target_pairs={{0,24},{8,0},{16,8},{24,16},{1,25},{9,1},{17,9},{25,17},{2,26},{10... | collective-permute-start | bytes 1179656 | tf_op jit(solution)/shard_map/ppermute | solution.py:115
  14.7 22.3 %collective-permute-start.5 = (bf16[3,256,256]{2,1,0:T(8,128)(2,1)}, bf16[3,256,256]{2,1,0:T(8,128)(2,1)}, u32[]{:S(2)}, u32[]{:S(2)}) collective-permute-start(bf16[3,256,256]{2,1,0:T(8,128)(2,1)} %get-tuple-element.39), channel_id=1, source_target_pairs={{0,16},{8,24},{16,0},{24,8},{1,17},{9,25},{17,1},{25,9},{2,18},{10... | collective-permute-start | bytes 1179656 | tf_op jit(solution)/shard_map/ppermute | solution.py:115
  14.7 20.5 %collective-permute-start.4 = (bf16[3,256,256]{2,1,0:T(8,128)(2,1)}, bf16[3,256,256]{2,1,0:T(8,128)(2,1)}, u32[]{:S(2)}, u32[]{:S(2)}) collective-permute-start(bf16[3,256,256]{2,1,0:T(8,128)(2,1)} %get-tuple-element.39), channel_id=1, source_target_pairs={{0,8},{8,16},{16,24},{24,0},{1,9},{9,17},{17,25},{25,1},{2,10},{10... | collective-permute-start | bytes 1179656 | tf_op jit(solution)/shard_map/ppermute | solution.py:115
  17.1 40.7 %all-to-all-start = ((bf16[4,2,256,256]{3,2,1,0:T(8,128)(2,1)}), bf16[4,2,256,256]{3,2,1,0:T(8,128)(2,1)S(1)}, u32[]{:S(2)}, u32[]{:S(2)}) async-start(bf16[4,2,256,256]{3,2,1,0:T(8,128)(2,1)} %broadcast_in_dim.40), calls=%async_computation | async-start | bytes 2097152 | tf_op jit(solution)/shard_map/all_to_all | solution.py:124
  26.0 1.5 copy-start.19
  26.0 0.9 copy-start.18
  27.5 0.6 copy-start.21
  28.4 11.2 %copy-start.23 = (f32[128]{0:T(128)}, f32[128]{0:T(128)S(1)}, u32[]{:S(2)}) copy-start(f32[128]{0:T(128)S(1)} %multiply_power_fusion) | copy-start | bytes 1540
  46.2 31.6 %collective-permute-start.9 = (bf16[16,64,256]{2,1,0:T(8,128)(2,1)}, bf16[16,64,256]{2,1,0:T(8,128)(2,1)}, u32[]{:S(2)}, u32[]{:S(2)}) collective-permute-start(bf16[16,64,256]{2,1,0:T(8,128)(2,1)} %get-tuple-element.22), channel_id=1, source_target_pairs={{0,96},{32,0},{64,32},{96,64},{1,97},{33,1},{65,33},{97,65},{2,98}... | collective-permute-start | bytes 1572872 | tf_op jit(solution)/shard_map/ppermute | solution.py:115
  50.8 9.0 %collective-permute-start.11 = (bf16[4,64,256]{2,1,0:T(8,128)(2,1)}, bf16[4,64,256]{2,1,0:T(8,128)(2,1)}, u32[]{:S(2)}, u32[]{:S(2)}) collective-permute-start(bf16[4,64,256]{2,1,0:T(8,128)(2,1)} %get-tuple-element.18), channel_id=1, source_target_pairs={{0,64},{32,96},{64,0},{96,32},{1,65},{33,97},{65,1},{97,33},{2,66}... | collective-permute-start | bytes 393224 | tf_op jit(solution)/shard_map/ppermute | solution.py:115
  53.0 17.6 %collective-permute-start.10 = (bf16[4,64,256]{2,1,0:T(8,128)(2,1)}, bf16[4,64,256]{2,1,0:T(8,128)(2,1)}, u32[]{:S(2)}, u32[]{:S(2)}) collective-permute-start(bf16[4,64,256]{2,1,0:T(8,128)(2,1)} %get-tuple-element.19), channel_id=1, source_target_pairs={{0,32},{32,64},{64,96},{96,0},{1,33},{33,65},{65,97},{97,1},{2,34}... | collective-permute-start | bytes 393224 | tf_op jit(solution)/shard_map/ppermute | solution.py:115
  53.9 23.2 %collective-permute-start.12 = (bf16[4,64,256]{2,1,0:T(8,128)(2,1)}, bf16[4,64,256]{2,1,0:T(8,128)(2,1)}, u32[]{:S(2)}, u32[]{:S(2)}) collective-permute-start(bf16[4,64,256]{2,1,0:T(8,128)(2,1)} %get-tuple-element.20), channel_id=1, source_target_pairs={{0,96},{32,0},{64,32},{96,64},{1,97},{33,1},{65,33},{97,65},{2,98}... | collective-permute-start | bytes 393224 | tf_op jit(solution)/shard_map/ppermute | solution.py:115
  56.3 31.9 %collective-permute-start.8 = (bf16[16,64,256]{2,1,0:T(8,128)(2,1)}, bf16[16,64,256]{2,1,0:T(8,128)(2,1)}, u32[]{:S(2)}, u32[]{:S(2)}) collective-permute-start(bf16[16,64,256]{2,1,0:T(8,128)(2,1)} %get-tuple-element.23), channel_id=1, source_target_pairs={{0,64},{32,96},{64,0},{96,32},{1,65},{33,97},{65,1},{97,33},{2,66}... | collective-permute-start | bytes 1572872 | tf_op jit(solution)/shard_map/ppermute | solution.py:115
  59.8 28.4 %collective-permute-start.7 = (bf16[16,64,256]{2,1,0:T(8,128)(2,1)}, bf16[16,64,256]{2,1,0:T(8,128)(2,1)}, u32[]{:S(2)}, u32[]{:S(2)}) collective-permute-start(bf16[16,64,256]{2,1,0:T(8,128)(2,1)} %get-tuple-element.24), channel_id=1, source_target_pairs={{0,32},{32,64},{64,96},{96,0},{1,33},{33,65},{65,97},{97,1},{2,34}... | collective-permute-start | bytes 1572872 | tf_op jit(solution)/shard_map/ppermute | solution.py:115
  69.5 18.5 %copy-start.20 = (s32[4,1]{0,1:T(1,128)S(1)}, s32[4,1]{0,1:T(1,128)}, u32[]{:S(2)}) copy-start(s32[4,1]{0,1:T(1,128)} %copy-done.19) | copy-start | bytes 52
  69.5 18.5 %copy-start.22 = (s32[4]{0:T(128)S(1)}, s32[4]{0:T(128)}, u32[]{:S(2)}) copy-start(s32[4]{0:T(128)} %copy-done.21) | copy-start | bytes 52
  70.6 29.2 %collective-permute-start.1 = (bf16[4,256,256]{2,1,0:T(8,128)(2,1)}, bf16[4,256,256]{2,1,0:T(8,128)(2,1)}, u32[]{:S(2)}, u32[]{:S(2)}) collective-permute-start(bf16[4,256,256]{2,1,0:T(8,128)(2,1)} %get-tuple-element.26), channel_id=1, source_target_pairs={{0,16},{8,24},{16,0},{24,8},{1,17},{9,25},{17,1},{25,9},{2,18},{10... | collective-permute-start | bytes 1572872 | tf_op jit(solution)/shard_map/ppermute | solution.py:115
  77.2 22.6 %collective-permute-start = (bf16[4,256,256]{2,1,0:T(8,128)(2,1)}, bf16[4,256,256]{2,1,0:T(8,128)(2,1)}, u32[]{:S(2)}, u32[]{:S(2)}) collective-permute-start(bf16[4,256,256]{2,1,0:T(8,128)(2,1)} %get-tuple-element.27), channel_id=1, source_target_pairs={{0,8},{8,16},{16,24},{24,0},{1,9},{9,17},{17,25},{25,1},{2,10},{10... | collective-permute-start | bytes 1572872 | tf_op jit(solution)/shard_map/ppermute | solution.py:115
  77.8 22.0 %collective-permute-start.2 = (bf16[4,256,256]{2,1,0:T(8,128)(2,1)}, bf16[4,256,256]{2,1,0:T(8,128)(2,1)}, u32[]{:S(2)}, u32[]{:S(2)}) collective-permute-start(bf16[4,256,256]{2,1,0:T(8,128)(2,1)} %get-tuple-element.28), channel_id=1, source_target_pairs={{0,24},{8,0},{16,8},{24,16},{1,25},{9,1},{17,9},{25,17},{2,26},{10... | collective-permute-start | bytes 1572872 | tf_op jit(solution)/shard_map/ppermute | solution.py:115
  83.4 14.8 %all-to-all-start.1 = ((bf16[8,4,16,448]{3,2,1,0:T(8,128)(2,1)}), bf16[8,4,16,448]{3,2,1,0:T(8,128)(2,1)S(1)}, u32[]{:S(2)}, u32[]{:S(2)}) async-start(bf16[8,4,16,448]{3,2,1,0:T(8,128)(2,1)} %broadcast_in_dim.46), calls=%async_computation.1 | async-start | bytes 1048576 | tf_op jit(solution)/shard_map/all_to_all | solution.py:237
  87.8 89.7 %reduce-scatter.2.cloned.1.call-start = ((), (), s32[]{:S(2)}) async-start(), calls=%async_computation.4 | async-start | bytes 4128768 | tf_op jit(solution)/shard_map/reduce_scatter | solution.py:300
  91.2 8.6 %copy-start.6 = (bf16[4,256,256]{2,1,0:T(8,128)(2,1)S(1)}, bf16[4,256,256]{2,1,0:T(8,128)(2,1)}, u32[]{:S(2)}) copy-start(bf16[4,256,256]{2,1,0:T(8,128)(2,1)} %get-tuple-element.25) | copy-start | bytes 1572868
  105.0 4.1 %copy-start.14 = (f32[3584]{0:T(1024)S(1)}, f32[3584]{0:T(1024)}, u32[]{:S(2)}) copy-start(f32[3584]{0:T(1024)} %param.17) | copy-start | bytes 43012
  106.0 3.1 %copy-start.4 = (bf16[512,3584]{0,1:T(8,128)(2,1)S(1)}, bf16[512,3584]{0,1:T(8,128)(2,1)}, u32[]{:S(2)}) copy-start(bf16[512,3584]{0,1:T(8,128)(2,1)} %all-gather.2.cloned.1.call-done) | copy-start | bytes 11010052
  110.8 2.4 %copy-start.3 = (bf16[512,3584]{0,1:T(8,128)(2,1)}, bf16[512,3584]{0,1:T(8,128)(2,1)S(1)}, u32[]{:S(2)}) copy-start(bf16[512,3584]{0,1:T(8,128)(2,1)S(1)} %fusion.2) | copy-start | bytes 11010052
  110.8 1.2 copy-start.24
  110.8 2.8 %copy-start.26 = (bf16[3584,256]{1,0:T(8,128)(2,1)S(1)}, bf16[3584,256]{1,0:T(8,128)(2,1)}, u32[]{:S(2)}) copy-start(bf16[3584,256]{1,0:T(8,128)(2,1)} %param.20) | copy-start | bytes 5505028
  114.8 8.4 %copy-start.12 = (bf16[512,256]{0,1:T(8,128)(2,1)}, bf16[512,256]{0,1:T(8,128)(2,1)S(1)}, u32[]{:S(2)}) copy-start(bf16[512,256]{0,1:T(8,128)(2,1)S(1)} %convolution_convert_fusion.1) | copy-start | bytes 786436
  115.7 7.5 %copy-start.7 = (bf16[64,3584]{1,0:T(8,128)(2,1)S(1)}, bf16[64,3584]{1,0:T(8,128)(2,1)}, u32[]{:S(2)}) copy-start(bf16[64,3584]{1,0:T(8,128)(2,1)} %dot_general.31) | copy-start | bytes 1376260
  115.7 11.7 %collective-permute-start.3 = (bf16[256,512]{0,1:T(8,128)(2,1)}, bf16[256,512]{0,1:T(8,128)(2,1)}, u32[]{:S(2)}, u32[]{:S(2)}) collective-permute-start(bf16[256,512]{0,1:T(8,128)(2,1)} %pad_maximum_fusion.4), channel_id=1, source_target_pairs={{0,8},{8,16},{16,24},{24,32},{32,40},{40,48},{48,56},{56,64},{64,7... | collective-permute-start | bytes 786440 | tf_op jit(solution)/shard_map/ppermute | solution.py:17
  126.3 1.0 copy-start.8
  126.3 1.0 copy-start.9
  126.4 2.2 %copy-start.5 = (pred[512,1792]{0,1:T(8,128)(4,1)S(1)}, pred[512,1792]{0,1:T(8,128)(4,1)}, u32[]{:S(2)}) copy-start(pred[512,1792]{0,1:T(8,128)(4,1)} %pad_add_fusion) | copy-start | bytes 2752516
  131.2 1.7 copy-start.10
  131.2 1.7 copy-start.13
  132.9 2.5 %copy-start.25 = (bf16[512,3584]{1,0:T(8,128)(2,1)S(1)}, bf16[512,3584]{1,0:T(8,128)(2,1)}, u32[]{:S(2)}) copy-start(bf16[512,3584]{1,0:T(8,128)(2,1)} %param.21) | copy-start | bytes 11010052
  135.4 42.1 %copy-start.1 = (bf16[3584,256]{1,0:T(8,128)(2,1)S(1)}, bf16[3584,256]{1,0:T(8,128)(2,1)}, u32[]{:S(2)}) copy-start(bf16[3584,256]{1,0:T(8,128)(2,1)} %param.19) | copy-start | bytes 5505028
Sparse Core Ops, SparseCore 0:
  16.1 30.5 all-gather.1
  139.4 38.0 reduce-scatter.1

commit v13 on v10

--- a/solution.py
+++ b/solution.py
@@ -241,9 +241,13 @@
 
     whole = lax.all_gather(stream, ("my", "mc"), axis=1, tiled=True)
     wide = whole.astype(jnp.float32)
-    normalized_input = (
-        wide * lax.rsqrt(jnp.mean(wide * wide, axis=1, keepdims=True) + 1e-06) * prenorm_gain
-    ).astype(jnp.bfloat16)
+    lanes = 128
+    partial_squares = jnp.sum(
+        (wide * wide).reshape(count, wide.shape[1] // lanes, lanes), axis=2
+    )
+    partial_squares = lax.optimization_barrier(partial_squares)
+    mean_square = jnp.sum(partial_squares, axis=1, keepdims=True) / wide.shape[1]
+    normalized_input = (wide * lax.rsqrt(mean_square + 1e-06) * prenorm_gain).astype(jnp.bfloat16)
     before = jnp.maximum(group_at - 1, 0)
     lengths = request_token_length[group_at]
     cached = cached_length[group_at]

time: 181 us -> 192 us (1.061)
  other arithmetic: 21.5 us -> 30 us
  starting transfers between devices: 25.3 us -> 28 us
    mul x0 -> x1, other arithmetic: none -> 6.02 us  [on_device(): wide * wide]
    ppermute x1, waiting for transfers between devices: 0.01 us -> 4.45 us  [shifted(): lax.ppermute(value, axis, [(source, source + steps) for source in range(f...]
    dot_general x1, matrix products: 5.26 us -> 2.09 us  [on_device(): jnp.dot(normalized_input, query_weight, preferred_element_type=jnp.float32)]
    dot_general x1, matrix products: 1.16 us -> 3.81 us  [on_device(): jnp.dot(normalized_input, value_weight, preferred_element_type=jnp.float32)]
    reduce_sum x1 -> x2, other arithmetic: 3.03 us -> 4.11 us  [the longest x1 4.09 us: on_device(): jnp.sum((wide * wide).reshape(count, wide.shape[1] // lanes, lanes), axis=2)]
    unnamed x67 -> x65, local copies, waits for them, and re-layouts: 7.74 us -> 7.67 us
  transfers between devices with their start and end apart: 14 -> 14, of which waited for: 6 -> 5; matrix products, arithmetic and copies ran while one was open for 30% -> 24% of each run, Pallas kernels for 0% -> 0%
where the time goes in v13:
time: 192 us; the launch traced here: 191 us
  waiting for transfers between devices  60.1 us (31%)
  local copies, waits for them, and re-layouts  37.5 us (20%)
  other arithmetic  30 us (16%)
  starting transfers between devices  28 us (15%)
  matrix products  19 us (10%)
  between operations  16.5 us (9%)
    reduce_scatter x1, waiting for transfers between devices, on_device(): lax.psum_scatter(partial_out.astype(jnp.bfloat16), ('my', 'mc'), scatter_...  37.4 us
    ppermute x9, waiting for transfers between devices, ring_send(): lax.ppermute(value, axis, [(i, (i + step) % SIDE) for i in range(SIDE)])  17.7 us
    ppermute x9, starting transfers between devices, ring_send(): lax.ppermute(value, axis, [(i, (i + step) % SIDE) for i in range(SIDE)])  15.7 us
    unnamed x65, local copies, waits for them, and re-layouts  7.67 us
    mul x1, other arithmetic, on_device(): wide * wide  6.02 us
    all_to_all x1, starting transfers between devices, on_device(): lax.all_to_all(jnp.broadcast_to(chosen_down, (model_count, *chosen_down.s...  4.46 us
    ppermute x1, waiting for transfers between devices, shifted(): lax.ppermute(value, axis, [(source, source + steps) for source in range(f...  4.45 us
    all_to_all x1, starting transfers between devices, route(): lax.all_to_all(spread_out, first, 0, 0, tiled=True)  4.29 us
  transfers between devices with their start and end apart: 14, of which 5 were waited for; matrix products, arithmetic and copies ran while one was open for 24% of the time, Pallas kernels for 0%

profile of v13, /device:TPU:0, one launch (start us, length us, event | category | flops | bytes accessed | tf_op | source)
XLA Modules:
  0.0 191.0 jit_solution(10433249287694393702)
XLA Ops:
  6.5 1.9 %constant_dynamic-update-slice_fusion.1 = (bf16[3,256,256]{2,1,0:T(8,128)(2,1)}, bf16[12,256,256]{2,1,0:T(8,128)(2,1)}) fusion(bf16[2,256,256]{2,1,0:T(8,128)(2,1)} %param.30), kind=kLoop, calls=%fused_computation.74 | loop fusion | bytes 786432
  8.5 1.0 pad_maximum_fusion.4
  9.8 0.7 constant_dynamic-update-slice_fusion
  10.6 2.0 %collective-permute-start.4 = (bf16[3,256,256]{2,1,0:T(8,128)(2,1)}, bf16[3,256,256]{2,1,0:T(8,128)(2,1)}, u32[]{:S(2)}, u32[]{:S(2)}) collective-permute-start(bf16[3,256,256]{2,1,0:T(8,128)(2,1)} %get-tuple-element.35), channel_id=1, source_target_pairs={{0,8},{8,16},{16,24},{24,0},{1,9},{9,17},{17,25},{25,1},{2,10},{10... | collective-permute-start | bytes 1179656 | tf_op jit(solution)/shard_map/ppermute | solution.py:115
  12.6 3.6 %collective-permute-start.5 = (bf16[3,256,256]{2,1,0:T(8,128)(2,1)}, bf16[3,256,256]{2,1,0:T(8,128)(2,1)}, u32[]{:S(2)}, u32[]{:S(2)}) collective-permute-start(bf16[3,256,256]{2,1,0:T(8,128)(2,1)} %get-tuple-element.35), channel_id=1, source_target_pairs={{0,16},{8,24},{16,0},{24,8},{1,17},{9,25},{17,1},{25,9},{2,18},{10... | collective-permute-start | bytes 1179656 | tf_op jit(solution)/shard_map/ppermute | solution.py:115
  16.1 1.0 collective-permute-start.6
  17.2 1.1 broadcast_in_dim.40
  18.3 4.3 %all-to-all-start = ((bf16[4,2,256,256]{3,2,1,0:T(8,128)(2,1)}), bf16[4,2,256,256]{3,2,1,0:T(8,128)(2,1)S(1)}, u32[]{:S(2)}, u32[]{:S(2)}) async-start(bf16[4,2,256,256]{3,2,1,0:T(8,128)(2,1)} %broadcast_in_dim.40), calls=%async_computation | async-start | bytes 2097152 | tf_op jit(solution)/shard_map/all_to_all | solution.py:124
  23.1 0.6 dynamic_slice.24
  23.6 0.6 constant_dynamic-slice_fusion.7
  26.9 0.8 gather_fusion.3
  28.3 0.6 gather_fusion.4
  29.3 0.4 copy-done.20
  29.7 0.3 bitcast_and_fusion
  30.2 0.2 fusion.14
  30.4 1.2 pad_add_fusion
  31.7 0.6 pad_clamp_fusion
  32.3 0.6 pad_clamp_fusion.1
  32.9 0.6 gather_fusion
  33.5 1.8 constant_dynamic-update-slice_fusion.4
  35.3 1.8 constant_dynamic-update-slice_fusion.3
  37.1 0.8 constant_dynamic-update-slice_fusion.2
  37.8 3.8 %gather_fusion.5 = bf16[80,64,256]{2,1,0:T(8,128)(2,1)} fusion(bf16[48,64,256]{2,1,0:T(8,128)(2,1)} %bitcast.115, s32[1024]{0:T(1024)S(1)} %pad_clamp_fusion.2), kind=kCustom, calls=%fused_computation.5 | custom fusion | bytes 5243200 | tf_op jit(solution)/shard_map/jit(_take)/gather | solution.py:179
  41.7 3.0 %fusion.91 = (bf16[20,64,256]{2,1,0:T(8,128)(2,1)S(1)}, bf16[20,64,256]{2,1,0:T(8,128)(2,1)}, bf16[20,64,256]{2,1,0:T(8,128)(2,1)}, bf16[20,64,256]{2,1,0:T(8,128)(2,1)}) fusion(bf16[80,64,256]{2,1,0:T(8,128)(2,1)} %gather_fusion.5), kind=kLoop, calls=%fused_computation.210 | loop fusion | bytes 5242880 | tf_op jit(solution)/shard_map/slice | solution.py:181
  44.7 3.3 %collective-permute-start.9 = (bf16[20,64,256]{2,1,0:T(8,128)(2,1)}, bf16[20,64,256]{2,1,0:T(8,128)(2,1)}, u32[]{:S(2)}, u32[]{:S(2)}) collective-permute-start(bf16[20,64,256]{2,1,0:T(8,128)(2,1)} %get-tuple-element.20), channel_id=1, source_target_pairs={{0,96},{32,0},{64,32},{96,64},{1,97},{33,1},{65,33},{97,65},{2,98}... | collective-permute-start | bytes 1966088 | tf_op jit(solution)/shard_map/ppermute | solution.py:115
  48.0 0.9 collective-permute-start.8
  48.9 0.9 collective-permute-start.7
  49.8 0.6 fusion.86
  50.3 1.8 multiply_cosine_fusion
  52.1 2.0 %gather_fusion.1 = bf16[16,256,256]{2,1,0:T(8,128)(2,1)} fusion(bf16[8,256,256]{2,1,0:T(8,128)(2,1)S(1)} %bitcast.114, s32[1024]{0:T(1024)S(1)} %pad_clamp_fusion.6), kind=kCustom, calls=%fused_computation.1 | custom fusion | bytes 4194368 | tf_op jit(solution)/shard_map/jit(_take)/gather | solution.py:134
  54.2 2.7 %fusion.92 = (bf16[4,256,256]{2,1,0:T(8,128)(2,1)S(1)}, bf16[4,256,256]{2,1,0:T(8,128)(2,1)}, bf16[4,256,256]{2,1,0:T(8,128)(2,1)}, bf16[4,256,256]{2,1,0:T(8,128)(2,1)}) fusion(bf16[16,256,256]{2,1,0:T(8,128)(2,1)} %gather_fusion.1), kind=kLoop, calls=%fused_computation.211 | loop fusion | bytes 4194304 | tf_op jit(solution)/shard_map/slice | solution.py:136
  56.9 3.0 %collective-permute-start.1 = (bf16[4,256,256]{2,1,0:T(8,128)(2,1)}, bf16[4,256,256]{2,1,0:T(8,128)(2,1)}, u32[]{:S(2)}, u32[]{:S(2)}) collective-permute-start(bf16[4,256,256]{2,1,0:T(8,128)(2,1)} %get-tuple-element.22), channel_id=1, source_target_pairs={{0,16},{8,24},{16,0},{24,8},{1,17},{9,25},{17,1},{25,9},{2,18},{10... | collective-permute-start | bytes 1572872 | tf_op jit(solution)/shard_map/ppermute | solution.py:115
  59.9 15.0 %collective-permute-done.9 = bf16[20,64,256]{2,1,0:T(8,128)(2,1)} collective-permute-done((bf16[20,64,256]{2,1,0:T(8,128)(2,1)}, bf16[20,64,256]{2,1,0:T(8,128)(2,1)}, u32[]{:S(2)}, u32[]{:S(2)}) %collective-permute-start.9) | collective-permute-done | bytes 655392 | tf_op jit(solution)/shard_map/ppermute | solution.py:115
  74.9 1.0 collective-permute-start
  76.0 2.7 %collective-permute-done.7 = bf16[20,64,256]{2,1,0:T(8,128)(2,1)} collective-permute-done((bf16[20,64,256]{2,1,0:T(8,128)(2,1)}, bf16[20,64,256]{2,1,0:T(8,128)(2,1)}, u32[]{:S(2)}, u32[]{:S(2)}) %collective-permute-start.7) | collective-permute-done | bytes 655392 | tf_op jit(solution)/shard_map/ppermute | solution.py:115
  78.7 2.8 %pad_maximum_fusion = bf16[80,64,256]{2,1,0:T(8,128)(2,1)} fusion(bf16[20,64,256]{2,1,0:T(8,128)(2,1)} %collective-permute-done.9, bf16[20,64,256]{2,1,0:T(8,128)(2,1)} %collective-permute-done.8, bf16[20,64,256]{2,1,0:T(8,128)(2,1)} %collective-permute-done.7, bf16[20,64,256]{2,1,0:T(8,128)(2,1)S(1)} %get-tuple-element.17), kind=kLoop, calls=%fused_computation.22 | loop fusion | flops 3932160 | bytes 5242880 | tf_op jit(solution)/shard_map/concatenate | solution.py:180
  81.6 2.4 %gather_fusion.7 = bf16[4,64,256]{2,1,0:T(8,128)(2,1)S(1)} fusion(bf16[80,64,256]{2,1,0:T(8,128)(2,1)} %pad_maximum_fusion, s32[1024]{0:T(1024)} %pad_clamp_fusion), kind=kCustom, calls=%fused_computation.7 | custom fusion | bytes 262160 | tf_op jit(solution)/shard_map/jit(_take)/gather | solution.py:196
  84.4 0.8 broadcast_in_dim.46
  85.2 4.5 %all-to-all-start.1 = ((bf16[8,4,16,448]{3,2,1,0:T(8,128)(2,1)}), bf16[8,4,16,448]{3,2,1,0:T(8,128)(2,1)S(1)}, u32[]{:S(2)}, u32[]{:S(2)}) async-start(bf16[8,4,16,448]{3,2,1,0:T(8,128)(2,1)} %broadcast_in_dim.46), calls=%async_computation.1 | async-start | bytes 1048576 | tf_op jit(solution)/shard_map/all_to_all | solution.py:231
  89.7 0.2 reduce-scatter.2.cloned.1.call-start
  90.1 3.3 %gather_fusion.6 = bf16[16,64,256]{2,1,0:T(8,128)(2,1)} fusion(bf16[80,64,256]{2,1,0:T(8,128)(2,1)} %pad_maximum_fusion, s32[1024]{0:T(1024)} %pad_clamp_fusion.1), kind=kCustom, calls=%fused_computation.6 | custom fusion | bytes 1048640 | tf_op jit(solution)/shard_map/jit(_take)/gather | solution.py:193
  93.3 3.0 %pad_maximum_fusion.1 = bf16[16,256,256]{2,1,0:T(8,128)(2,1)} fusion(bf16[4,256,256]{2,1,0:T(8,128)(2,1)} %collective-permute-done.2, bf16[4,256,256]{2,1,0:T(8,128)(2,1)} %collective-permute-done.1, bf16[4,256,256]{2,1,0:T(8,128)(2,1)} %collective-permute-done, bf16[4,256,256]{2,1,0:T(8,128)(2,1)S(1)} %get-tuple-element.21), kind=kLoop, calls=%fused_computation.23 | loop fusion | flops 3145728 | bytes 4194304 | tf_op jit(solution)/shard_map/concatenate | solution.py:135
  96.3 2.2 %gather_fusion.2 = bf16[4,256,256]{2,1,0:T(8,128)(2,1)S(1)} fusion(bf16[16,256,256]{2,1,0:T(8,128)(2,1)} %pad_maximum_fusion.1, s32[1024]{0:T(1024)S(1)} %pad_clamp_fusion.5), kind=kCustom, calls=%fused_computation.2 | custom fusion | bytes 1048592 | tf_op jit(solution)/shard_map/jit(_take)/gather | solution.py:143
  98.5 1.1 copy.68
  99.6 0.4 all-to-all-done.1
  100.0 0.3 copy.62
  100.3 0.6 dot_general.31
  100.9 6.0 %convert_multiply_fusion.1 = f32[512,3584]{0,1:T(8,128)} fusion(bf16[512,3584]{0,1:T(8,128)(2,1)} %all-gather.2.cloned.1.call-done), kind=kLoop, calls=%fused_computation.9 | loop fusion | flops 3670016 | bytes 11010048 | tf_op jit(solution)/shard_map/mul | solution.py:246
  106.9 4.1 %reduce_sum.56 = f32[512,28]{0,1:T(8,128)S(1)} reduce(f32[512,28,128]{0,2,1:T(8,128)} %bitcast.113, f32[]{:T(128)} %constant.165.clone.1), dimensions={2}, to_apply=%region_0.1 | reduce | flops 1820672 | bytes 7397380 | tf_op jit(solution)/shard_map/reduce_sum | solution.py:245
  111.1 3.1 %fusion.1 = bf16[512,3584]{0,1:T(8,128)(2,1)S(1)} fusion(bf16[512,3584]{0,1:T(8,128)(2,1)} %all-gather.2.cloned.1.call-done, f32[3584]{0:T(1024)S(1)} %copy-done.12, f32[512]{0:T(512)S(1)} %add_rsqrt_fusion), kind=kLoop, calls=%fused_computation.11 | loop fusion | flops 7340032 | bytes 7356416 | tf_op jit(solution)/shard_map/convert_element_type | solution.py:250
  114.2 1.2 convolution_bitcast_fusion
  115.4 1.2 fusion.35
  116.6 0.9 copy-done.24
  117.6 2.1 %fusion.95 = f32[512,512]{0,1:T(8,128)S(1)} fusion(bf16[512,3584]{0,1:T(8,128)(2,1)S(1)} %fusion.1, bf16[3584,512]{1,0:T(8,128)(2,1)S(1)} %copy-done.24), kind=kOutput, calls=%fused_computation.214 | convolution fusion | flops 1879048192 | bytes 8388608 | tf_op jit(solution)/shard_map/dot_general | solution.py:268
  119.7 3.0 %fusion.12 = f32[512,512]{0,1:T(8,128)S(1)} fusion(f32[512,512]{0,1:T(8,128)S(1)} %fusion.95, bf16[64,512]{1,0:T(8,128)(2,1)S(1)} %bitcast.122, bf16[512,64]{0,1:T(8,128)(2,1)S(1)} %bitcast.123, bf16[64,3584]{1,0:T(8,128)(2,1)S(1)} %dot_general.31, bf16[512,3584]{0,1:T(8,128)(2,1)} %copy-done.3), kind=kOutput, calls=%fused_computation.27 | convolution fusion | flops 269025280 | bytes 6356992 | tf_op jit(solution)/shard_map/dot_general | solution.py:262
  123.4 3.8 %convolution_convert_fusion.1 = bf16[512,256]{0,1:T(8,128)(2,1)S(1)} fusion(bf16[512,3584]{0,1:T(8,128)(2,1)} %copy-done.3, bf16[3584,256]{1,0:T(8,128)(2,1)} %param.20), kind=kOutput, calls=%fused_computation.29 | convolution fusion | flops 939655168 | bytes 5767168 | tf_op jit(solution)/shard_map/dot_general | solution.py:277
  127.3 3.3 %collective-permute-start.3 = (bf16[256,512]{0,1:T(8,128)(2,1)S(1)}, bf16[256,512]{0,1:T(8,128)(2,1)S(1)}, u32[]{:S(2)}, u32[]{:S(2)}) collective-permute-start(bf16[256,512]{0,1:T(8,128)(2,1)S(1)} %pad_maximum_fusion.3), channel_id=1, source_target_pairs={{0,8},{8,16},{16,24},{24,32},{32,40},{40,48},{48,56},{56,64},{64,7... | collective-permute-start | bytes 786440 | tf_op jit(solution)/shard_map/ppermute | solution.py:17
  130.6 0.8 subtract_convert_fusion
  131.4 4.4 %collective-permute-done.3 = bf16[256,512]{0,1:T(8,128)(2,1)S(1)} collective-permute-done((bf16[256,512]{0,1:T(8,128)(2,1)S(1)}, bf16[256,512]{0,1:T(8,128)(2,1)S(1)}, u32[]{:S(2)}, u32[]{:S(2)}) %collective-permute-start.3) | collective-permute-done | bytes 262176 | tf_op jit(solution)/shard_map/ppermute | solution.py:17
  136.0 2.5 %fusion.4 = (f32[2,512]{1,0:T(2,128)S(1)}, f32[1792,512,2]{1,0,2:T(8,128)S(1)}) fusion(pred[512,1792]{0,1:T(8,128)(4,1)S(1)} %copy-done.4, bf16[512,2,128]{2,0,1:T(8,128)(2,1)} %get-tuple-element.26, bf16[512,2,128]{2,0,1:T(8,128)(2,1)S(1)} %get-tuple-element.25, bf16[512,256]{1,0:T(8,128)(2,1)S(1)} %copy.61, bf16[256,256]{1,0:T(8,128)(2,1)S(1)} %copy.60, ...), kind=kOutput, calls=%fused_computation.17 | convolution fusion | flops 948829184 | bytes 9703424 | tf_op jit(solution)/shard_map/tkrd,skd->krts/dot_general | solution.py:90
  138.6 1.7 fusion.2
  140.3 2.4 %divide_convert_fusion = bf16[512,1,2,256]{0,3,2,1:T(8,128)(2,1)S(1)} fusion(f32[1792,512,2]{1,0,2:T(8,128)S(1)} %get-tuple-element.44, f32[2,512]{1,0:T(2,128)S(1)} %get-tuple-element.43, pred[512,1792]{0,1:T(8,128)(4,1)S(1)} %copy-done.4, bf16[512,256]{0,1:T(8,128)(2,1)S(1)} %copy-done.11, bf16[256,256]{0,1:T(8,128)(2,1)S(1)} %get-tuple-element.31, ...), kind=kOutput, calls=%fused_computation.32 | convolution fusion | flops 950140928 | bytes 9707520 | tf_op jit(solution)/shard_map/krts,skd->tkrd/dot_general | solution.py:97
  142.8 3.9 %convolution_convert_fusion = bf16[512,3584]{0,1:T(8,128)(2,1)} fusion(bf16[512,512]{0,1:T(8,128)(2,1)S(1)} %bitcast.131, bf16[512,3584]{1,0:T(8,128)(2,1)S(1)} %copy-done.25), kind=kOutput, calls=%fused_computation.16 | convolution fusion | flops 1880883200 | bytes 7864320 | tf_op jit(solution)/shard_map/dot_general | solution.py:297
  146.7 37.4 %reduce-scatter.2.cloned.1.call-done = bf16[512,448]{0,1:T(8,128)(2,1)} async-done(((bf16[512,3584]{0,1:T(8,128)(2,1)}), bf16[512,448]{0,1:T(8,128)(2,1)}) %reduce-scatter.2.cloned.1.call-update) | async-done | bytes 458768 | tf_op jit(solution)/shard_map/reduce_scatter | solution.py:298
  (129 shorter events, 3.8 us)
Async XLA Ops:
  6.5 107.6 %copy-start = (bf16[3584,256]{1,0:T(8,128)(2,1)S(1)}, bf16[3584,256]{1,0:T(8,128)(2,1)}, u32[]{:S(2)}) copy-start(bf16[3584,256]{1,0:T(8,128)(2,1)} %param.19) | copy-start | bytes 5505028
  6.5 10.6 %copy-start.9 = (bf16[2,256,256]{2,1,0:T(8,128)(2,1)S(1)}, bf16[2,256,256]{2,1,0:T(8,128)(2,1)}, u32[]{:S(2)}) copy-start(bf16[2,256,256]{2,1,0:T(8,128)(2,1)} %param.31) | copy-start | bytes 786436
  6.5 94.4 %all-gather.2.cloned.1.call-start = ((), (), s32[]{:S(2)}) async-start(), calls=%async_computation.3 | async-start | bytes 4128768 | tf_op jit(solution)/shard_map/all_gather | solution.py:242
  8.5 14.1 %copy-start.13 = (s32[16,4]{0,1:T(4,128)S(1)}, s32[16,4]{0,1:T(4,128)}, u32[]{:S(2)}) copy-start(s32[16,4]{0,1:T(4,128)} %param.29) | copy-start | bytes 772
  8.5 14.1 %copy-start.14 = (s32[16,4]{0,1:T(4,128)S(1)}, s32[16,4]{0,1:T(4,128)}, u32[]{:S(2)}) copy-start(s32[16,4]{0,1:T(4,128)} %param.26) | copy-start | bytes 772
  8.5 14.6 %copy-start.26 = (s32[16]{0:T(128)S(1)}, s32[16]{0:T(128)}, u32[]{:S(2)}) copy-start(s32[16]{0:T(128)} %param.27) | copy-start | bytes 196
  8.5 18.2 %copy-start.15 = (s32[16,4]{0,1:T(4,128)S(1)}, s32[16,4]{0,1:T(4,128)}, u32[]{:S(2)}) copy-start(s32[16,4]{0,1:T(4,128)} %param.24) | copy-start | bytes 772
  9.5 17.3 %copy-start.2 = (s32[64]{0:T(128)S(1)}, s32[64]{0:T(128)}, u32[]{:S(2)}) copy-start(s32[64]{0:T(128)} %param.25) | copy-start | bytes 772
  10.6 23.0 %collective-permute-start.4 = (bf16[3,256,256]{2,1,0:T(8,128)(2,1)}, bf16[3,256,256]{2,1,0:T(8,128)(2,1)}, u32[]{:S(2)}, u32[]{:S(2)}) collective-permute-start(bf16[3,256,256]{2,1,0:T(8,128)(2,1)} %get-tuple-element.35), channel_id=1, source_target_pairs={{0,8},{8,16},{16,24},{24,0},{1,9},{9,17},{17,25},{25,1},{2,10},{10... | collective-permute-start | bytes 1179656 | tf_op jit(solution)/shard_map/ppermute | solution.py:115
  12.6 22.7 %collective-permute-start.5 = (bf16[3,256,256]{2,1,0:T(8,128)(2,1)}, bf16[3,256,256]{2,1,0:T(8,128)(2,1)}, u32[]{:S(2)}, u32[]{:S(2)}) collective-permute-start(bf16[3,256,256]{2,1,0:T(8,128)(2,1)} %get-tuple-element.35), channel_id=1, source_target_pairs={{0,16},{8,24},{16,0},{24,8},{1,17},{9,25},{17,1},{25,9},{2,18},{10... | collective-permute-start | bytes 1179656 | tf_op jit(solution)/shard_map/ppermute | solution.py:115
  16.1 20.9 %collective-permute-start.6 = (bf16[3,256,256]{2,1,0:T(8,128)(2,1)}, bf16[3,256,256]{2,1,0:T(8,128)(2,1)S(1)}, u32[]{:S(2)}, u32[]{:S(2)}) collective-permute-start(bf16[3,256,256]{2,1,0:T(8,128)(2,1)} %get-tuple-element.35), channel_id=1, source_target_pairs={{0,24},{8,0},{16,8},{24,16},{1,25},{9,1},{17,9},{25,17},{2,26},{10... | collective-permute-start | bytes 1179656 | tf_op jit(solution)/shard_map/ppermute | solution.py:115
  18.3 33.9 %all-to-all-start = ((bf16[4,2,256,256]{3,2,1,0:T(8,128)(2,1)}), bf16[4,2,256,256]{3,2,1,0:T(8,128)(2,1)S(1)}, u32[]{:S(2)}, u32[]{:S(2)}) async-start(bf16[4,2,256,256]{3,2,1,0:T(8,128)(2,1)} %broadcast_in_dim.40), calls=%async_computation | async-start | bytes 2097152 | tf_op jit(solution)/shard_map/all_to_all | solution.py:124
  23.1 6.1 %copy-start.18 = (s32[4,1]{0,1:T(1,128)}, s32[4,1]{0,1:T(1,128)S(1)}, u32[]{:S(2)}) copy-start(s32[4,1]{0,1:T(1,128)S(1)} %reduce-window.4) | copy-start | bytes 52
  26.8 0.9 copy-start.16
  29.2 0.5 copy-start.20
  44.7 30.2 %collective-permute-start.9 = (bf16[20,64,256]{2,1,0:T(8,128)(2,1)}, bf16[20,64,256]{2,1,0:T(8,128)(2,1)}, u32[]{:S(2)}, u32[]{:S(2)}) collective-permute-start(bf16[20,64,256]{2,1,0:T(8,128)(2,1)} %get-tuple-element.20), channel_id=1, source_target_pairs={{0,96},{32,0},{64,32},{96,64},{1,97},{33,1},{65,33},{97,65},{2,98}... | collective-permute-start | bytes 1966088 | tf_op jit(solution)/shard_map/ppermute | solution.py:115
  48.0 2.3 %copy-start.22 = (f32[128]{0:T(128)}, f32[128]{0:T(128)S(1)}, u32[]{:S(2)}) copy-start(f32[128]{0:T(128)S(1)} %multiply_power_fusion) | copy-start | bytes 1540
  48.0 28.0 %collective-permute-start.8 = (bf16[20,64,256]{2,1,0:T(8,128)(2,1)}, bf16[20,64,256]{2,1,0:T(8,128)(2,1)}, u32[]{:S(2)}, u32[]{:S(2)}) collective-permute-start(bf16[20,64,256]{2,1,0:T(8,128)(2,1)} %get-tuple-element.18), channel_id=1, source_target_pairs={{0,64},{32,96},{64,0},{96,32},{1,65},{33,97},{65,1},{97,33},{2,66}... | collective-permute-start | bytes 1966088 | tf_op jit(solution)/shard_map/ppermute | solution.py:115
  48.9 29.8 %collective-permute-start.7 = (bf16[20,64,256]{2,1,0:T(8,128)(2,1)}, bf16[20,64,256]{2,1,0:T(8,128)(2,1)}, u32[]{:S(2)}, u32[]{:S(2)}) collective-permute-start(bf16[20,64,256]{2,1,0:T(8,128)(2,1)} %get-tuple-element.19), channel_id=1, source_target_pairs={{0,32},{32,64},{64,96},{96,0},{1,33},{33,65},{65,97},{97,1},{2,34}... | collective-permute-start | bytes 1966088 | tf_op jit(solution)/shard_map/ppermute | solution.py:115
  54.2 21.8 %copy-start.17 = (s32[4]{0:T(128)S(1)}, s32[4]{0:T(128)}, u32[]{:S(2)}) copy-start(s32[4]{0:T(128)} %fusion.86) | copy-start | bytes 52
  56.9 36.5 %collective-permute-start.2 = (bf16[4,256,256]{2,1,0:T(8,128)(2,1)}, bf16[4,256,256]{2,1,0:T(8,128)(2,1)}, u32[]{:S(2)}, u32[]{:S(2)}) collective-permute-start(bf16[4,256,256]{2,1,0:T(8,128)(2,1)} %get-tuple-element.24), channel_id=1, source_target_pairs={{0,24},{8,0},{16,8},{24,16},{1,25},{9,1},{17,9},{25,17},{2,26},{10... | collective-permute-start | bytes 1572872 | tf_op jit(solution)/shard_map/ppermute | solution.py:115
  56.9 36.4 %collective-permute-start.1 = (bf16[4,256,256]{2,1,0:T(8,128)(2,1)}, bf16[4,256,256]{2,1,0:T(8,128)(2,1)}, u32[]{:S(2)}, u32[]{:S(2)}) collective-permute-start(bf16[4,256,256]{2,1,0:T(8,128)(2,1)} %get-tuple-element.22), channel_id=1, source_target_pairs={{0,16},{8,24},{16,0},{24,8},{1,17},{9,25},{17,1},{25,9},{2,18},{10... | collective-permute-start | bytes 1572872 | tf_op jit(solution)/shard_map/ppermute | solution.py:115
  74.9 18.4 %collective-permute-start = (bf16[4,256,256]{2,1,0:T(8,128)(2,1)}, bf16[4,256,256]{2,1,0:T(8,128)(2,1)}, u32[]{:S(2)}, u32[]{:S(2)}) collective-permute-start(bf16[4,256,256]{2,1,0:T(8,128)(2,1)} %get-tuple-element.23), channel_id=1, source_target_pairs={{0,8},{8,16},{16,24},{24,0},{1,9},{9,17},{17,25},{25,1},{2,10},{10... | collective-permute-start | bytes 1572872 | tf_op jit(solution)/shard_map/ppermute | solution.py:115
  81.6 8.3 %copy-start.19 = (s32[4,1]{0,1:T(1,128)S(1)}, s32[4,1]{0,1:T(1,128)}, u32[]{:S(2)}) copy-start(s32[4,1]{0,1:T(1,128)} %copy-done.18) | copy-start | bytes 52
  81.6 8.3 %copy-start.21 = (s32[4]{0:T(128)S(1)}, s32[4]{0:T(128)}, u32[]{:S(2)}) copy-start(s32[4]{0:T(128)} %copy-done.20) | copy-start | bytes 52
  85.2 14.8 %all-to-all-start.1 = ((bf16[8,4,16,448]{3,2,1,0:T(8,128)(2,1)}), bf16[8,4,16,448]{3,2,1,0:T(8,128)(2,1)S(1)}, u32[]{:S(2)}, u32[]{:S(2)}) async-start(bf16[8,4,16,448]{3,2,1,0:T(8,128)(2,1)} %broadcast_in_dim.46), calls=%async_computation.1 | async-start | bytes 1048576 | tf_op jit(solution)/shard_map/all_to_all | solution.py:231
  89.7 94.5 %reduce-scatter.2.cloned.1.call-start = ((), (), s32[]{:S(2)}) async-start(), calls=%async_computation.4 | async-start | bytes 4128768 | tf_op jit(solution)/shard_map/reduce_scatter | solution.py:298
  106.9 4.1 %copy-start.12 = (f32[3584]{0:T(1024)S(1)}, f32[3584]{0:T(1024)}, u32[]{:S(2)}) copy-start(f32[3584]{0:T(1024)} %param.17) | copy-start | bytes 43012
  114.2 2.4 %copy-start.3 = (bf16[512,3584]{0,1:T(8,128)(2,1)}, bf16[512,3584]{0,1:T(8,128)(2,1)S(1)}, u32[]{:S(2)}) copy-start(bf16[512,3584]{0,1:T(8,128)(2,1)S(1)} %fusion.1) | copy-start | bytes 11010052
  114.2 1.2 copy-start.23
  114.2 3.4 %copy-start.24 = (bf16[3584,512]{1,0:T(8,128)(2,1)S(1)}, bf16[3584,512]{1,0:T(8,128)(2,1)}, u32[]{:S(2)}) copy-start(bf16[3584,512]{1,0:T(8,128)(2,1)} %param.18) | copy-start | bytes 11010052
  123.4 7.2 %copy-start.5 = (f32[512,128]{1,0:T(8,128)S(1)}, f32[512,128]{1,0:T(8,128)}, u32[]{:S(2)}) copy-start(f32[512,128]{1,0:T(8,128)} %get-tuple-element.41) | copy-start | bytes 786436
  123.4 7.2 %copy-start.6 = (f32[512,128]{1,0:T(8,128)S(1)}, f32[512,128]{1,0:T(8,128)}, u32[]{:S(2)}) copy-start(f32[512,128]{1,0:T(8,128)} %get-tuple-element.42) | copy-start | bytes 786436
  127.2 8.7 %copy-start.10 = (bf16[512,256]{0,1:T(8,128)(2,1)}, bf16[512,256]{0,1:T(8,128)(2,1)S(1)}, u32[]{:S(2)}) copy-start(bf16[512,256]{0,1:T(8,128)(2,1)S(1)} %convolution_convert_fusion.1) | copy-start | bytes 786436
  127.2 8.8 %copy-start.4 = (pred[512,1792]{0,1:T(8,128)(4,1)S(1)}, pred[512,1792]{0,1:T(8,128)(4,1)}, u32[]{:S(2)}) copy-start(pred[512,1792]{0,1:T(8,128)(4,1)} %pad_add_fusion) | copy-start | bytes 2752516
  127.2 8.8 %copy-start.8 = (bf16[16,64,256]{2,1,0:T(8,128)(2,1)S(1)}, bf16[16,64,256]{2,1,0:T(8,128)(2,1)}, u32[]{:S(2)}) copy-start(bf16[16,64,256]{2,1,0:T(8,128)(2,1)} %gather_fusion.6) | copy-start | bytes 1572868
  127.3 8.6 %collective-permute-start.3 = (bf16[256,512]{0,1:T(8,128)(2,1)S(1)}, bf16[256,512]{0,1:T(8,128)(2,1)S(1)}, u32[]{:S(2)}, u32[]{:S(2)}) collective-permute-start(bf16[256,512]{0,1:T(8,128)(2,1)S(1)} %pad_maximum_fusion.3), channel_id=1, source_target_pairs={{0,8},{8,16},{16,24},{24,32},{32,40},{40,48},{48,56},{56,64},{64,7... | collective-permute-start | bytes 786440 | tf_op jit(solution)/shard_map/ppermute | solution.py:17
  138.6 1.7 copy-start.7
  138.6 1.7 copy-start.11
  140.3 2.4 %copy-start.25 = (bf16[512,3584]{1,0:T(8,128)(2,1)S(1)}, bf16[512,3584]{1,0:T(8,128)(2,1)}, u32[]{:S(2)}) copy-start(bf16[512,3584]{1,0:T(8,128)(2,1)} %param.21) | copy-start | bytes 11010052
  142.8 41.3 %copy-start.1 = (bf16[3584,256]{1,0:T(8,128)(2,1)S(1)}, bf16[3584,256]{1,0:T(8,128)(2,1)}, u32[]{:S(2)}) copy-start(bf16[3584,256]{1,0:T(8,128)(2,1)} %param.19) | copy-start | bytes 5505028
Sparse Core Ops, SparseCore 0:
  17.3 29.3 all-gather.1
  146.8 37.2 reduce-scatter.1

commit v14 on v10

--- a/solution.py
+++ b/solution.py
@@ -130,8 +130,8 @@
     owner_a = (owner // SIDE, owner % SIDE)[first == "gz"]
     owner_b = (owner // SIDE, owner % SIDE)[second == "gz"]
     table = owner_a * per_owner + wanted % per_owner
-    source = jnp.take(table, askers, axis=0, mode="clip")
-    outgoing = jnp.take(held, source.reshape(-1), axis=0, mode="clip")
+    source = table.at[askers].get(mode="promise_in_bounds")
+    outgoing = held.at[source.reshape(-1)].get(mode="promise_in_bounds")
     received = jnp.concatenate(
         [outgoing[:slots]]
         + [
@@ -140,7 +140,7 @@
         ]
     )
     pick = ((own_b - owner_b[me]) % SIDE) * slots + jnp.arange(slots)
-    return jnp.take(received, pick, axis=0, mode="clip")
+    return received.at[pick].get(mode="promise_in_bounds")
 
 
 def route_with_adapters(blocks, adapters, block_wanted, adapter_wanted, first, second):
@@ -174,9 +174,9 @@
     table = jnp.concatenate(
         [block_table.reshape(block_table.shape[0], -1), adapter_table], axis=1
     )
-    source = jnp.take(table, askers, axis=0, mode="clip")
+    source = table.at[askers].get(mode="promise_in_bounds")
     width = source.shape[1]
-    outgoing = jnp.take(held, source.reshape(-1), axis=0, mode="clip")
+    outgoing = held.at[source.reshape(-1)].get(mode="promise_in_bounds")
     received = jnp.concatenate(
         [outgoing[:width]]
         + [
@@ -190,10 +190,10 @@
         (((own_b - block_b[me]) % SIDE) * width + slot * pieces)[:, None] + quarter
     ).reshape(-1)
     adapter_pick = ((own_b - adapter_b[me]) % SIDE) * width + slots * pieces + slot
-    chosen_blocks = jnp.take(received, block_pick, axis=0, mode="clip").reshape(
+    chosen_blocks = received.at[block_pick].get(mode="promise_in_bounds").reshape(
         slots, rows, lanes
     )
-    chosen_adapters = jnp.take(received, adapter_pick, axis=0, mode="clip").reshape(slots, -1)
+    chosen_adapters = received.at[adapter_pick].get(mode="promise_in_bounds").reshape(slots, -1)
     chosen_adapters = chosen_adapters[:, : flat.shape[1]].reshape(slots, *adapters.shape[1:])
     return chosen_blocks, chosen_adapters
 

time: 181 us -> 181 us (level)
  no operation moved by 1% of the time
where the time goes in v14:
time: 181 us; the launch traced here: 180 us
  waiting for transfers between devices  58 us (32%)
  local copies, waits for them, and re-layouts  39.3 us (22%)
  starting transfers between devices  25.3 us (14%)
  other arithmetic  21.5 us (12%)
  matrix products  19.6 us (11%)
  between operations  16.6 us (9%)
    reduce_scatter x1, waiting for transfers between devices, on_device(): lax.psum_scatter(partial_out.astype(jnp.bfloat16), ('my', 'mc'), scatter_...  38.7 us
    ppermute x9, waiting for transfers between devices, ring_send(): lax.ppermute(value, axis, [(i, (i + step) % SIDE) for i in range(SIDE)])  18.6 us
    ppermute x9, starting transfers between devices, ring_send(): lax.ppermute(value, axis, [(i, (i + step) % SIDE) for i in range(SIDE)])  14.3 us
    unnamed x67, local copies, waits for them, and re-layouts  7.74 us
    dot_general x1, matrix products, on_device(): jnp.dot(normalized_input, query_weight, preferred_element_type=jnp.float32)  5.26 us
    all_to_all x1, starting transfers between devices, on_device(): lax.all_to_all(jnp.broadcast_to(chosen_down, (model_count, *chosen_down.s...  4.47 us
    all_to_all x1, starting transfers between devices, route(): lax.all_to_all(spread_out, first, 0, 0, tiled=True)  4.29 us
    dot_general x1, matrix products, on_device(): jnp.dot(attended, output_weight, preferred_element_type=jnp.float32)  3.89 us
  transfers between devices with their start and end apart: 14, of which 6 were waited for; matrix products, arithmetic and copies ran while one was open for 30% of the time, Pallas kernels for 0%

profile of v14, /device:TPU:0, one launch (start us, length us, event | category | flops | bytes accessed | tf_op | source)
XLA Modules:
  0.0 180.3 jit_solution(2216085877900478046)
XLA Ops:
  6.5 1.1 pad_maximum_fusion.4
  8.0 1.8 constant_dynamic-update-slice_fusion.1
  9.8 0.7 constant_dynamic-update-slice_fusion
  10.5 4.1 %collective-permute-start.6 = (bf16[3,256,256]{2,1,0:T(8,128)(2,1)}, bf16[3,256,256]{2,1,0:T(8,128)(2,1)S(1)}, u32[]{:S(2)}, u32[]{:S(2)}) collective-permute-start(bf16[3,256,256]{2,1,0:T(8,128)(2,1)} %get-tuple-element.35), channel_id=1, source_target_pairs={{0,24},{8,0},{16,8},{24,16},{1,25},{9,1},{17,9},{25,17},{2,26},{10... | collective-permute-start | bytes 1179656 | tf_op jit(solution)/shard_map/ppermute | solution.py:115
  14.6 1.3 collective-permute-start.4
  15.9 1.1 broadcast_in_dim.20
  17.0 4.3 %all-to-all-start = ((bf16[4,2,256,256]{3,2,1,0:T(8,128)(2,1)}), bf16[4,2,256,256]{3,2,1,0:T(8,128)(2,1)S(1)}, u32[]{:S(2)}, u32[]{:S(2)}) async-start(bf16[4,2,256,256]{3,2,1,0:T(8,128)(2,1)} %broadcast_in_dim.20), calls=%async_computation | async-start | bytes 2097152 | tf_op jit(solution)/shard_map/all_to_all | solution.py:124
  21.6 0.8 gather_fusion.3
  22.7 0.6 constant_dynamic-slice_fusion.7
  23.3 0.6 dynamic_slice.24
  27.0 0.6 gather_fusion
  28.1 0.6 gather_fusion.4
  28.9 0.5 copy-done.21
  29.4 0.3 bitcast_and_fusion
  30.1 1.2 pad_add_fusion
  31.4 0.6 pad_clamp_fusion
  32.0 0.6 pad_clamp_fusion.6
  32.6 2.6 %collective-permute-done.4 = bf16[3,256,256]{2,1,0:T(8,128)(2,1)} collective-permute-done((bf16[3,256,256]{2,1,0:T(8,128)(2,1)}, bf16[3,256,256]{2,1,0:T(8,128)(2,1)}, u32[]{:S(2)}, u32[]{:S(2)}) %collective-permute-start.4) | collective-permute-done | bytes 393248 | tf_op jit(solution)/shard_map/ppermute | solution.py:115
  35.1 1.8 constant_dynamic-update-slice_fusion.4
  36.9 1.8 %constant_dynamic-update-slice_fusion.3 = bf16[12,256,256]{2,1,0:T(8,128)(2,1)} fusion(bf16[12,256,256]{2,1,0:T(8,128)(2,1)} %constant_dynamic-update-slice_fusion.4, bf16[3,256,256]{2,1,0:T(8,128)(2,1)} %collective-permute-done.5), kind=kLoop, calls=%fused_computation.77 | loop fusion | bytes 786432
  38.8 0.8 constant_dynamic-update-slice_fusion.2
  39.6 3.9 %gather_fusion.5 = bf16[80,64,256]{2,1,0:T(8,128)(2,1)} fusion(bf16[48,64,256]{2,1,0:T(8,128)(2,1)} %bitcast.17, s32[1024]{0:T(1024)S(1)} %pad_clamp_fusion.2), kind=kCustom, calls=%fused_computation.5 | custom fusion | bytes 5243200 | tf_op jit(solution)/shard_map/gather | solution.py:179
  43.4 3.1 %fusion.95 = (bf16[20,64,256]{2,1,0:T(8,128)(2,1)S(1)}, bf16[20,64,256]{2,1,0:T(8,128)(2,1)}, bf16[20,64,256]{2,1,0:T(8,128)(2,1)}, bf16[20,64,256]{2,1,0:T(8,128)(2,1)}) fusion(bf16[80,64,256]{2,1,0:T(8,128)(2,1)} %gather_fusion.5), kind=kLoop, calls=%fused_computation.221 | loop fusion | bytes 5242880 | tf_op jit(solution)/shard_map/slice | solution.py:181
  46.5 3.0 %collective-permute-start.8 = (bf16[20,64,256]{2,1,0:T(8,128)(2,1)}, bf16[20,64,256]{2,1,0:T(8,128)(2,1)}, u32[]{:S(2)}, u32[]{:S(2)}) collective-permute-start(bf16[20,64,256]{2,1,0:T(8,128)(2,1)} %get-tuple-element.18), channel_id=1, source_target_pairs={{0,64},{32,96},{64,0},{96,32},{1,65},{33,97},{65,1},{97,33},{2,66}... | collective-permute-start | bytes 1966088 | tf_op jit(solution)/shard_map/ppermute | solution.py:115
  49.5 0.7 collective-permute-start.7
  50.2 2.6 %collective-permute-start.9 = (bf16[20,64,256]{2,1,0:T(8,128)(2,1)}, bf16[20,64,256]{2,1,0:T(8,128)(2,1)}, u32[]{:S(2)}, u32[]{:S(2)}) collective-permute-start(bf16[20,64,256]{2,1,0:T(8,128)(2,1)} %get-tuple-element.20), channel_id=1, source_target_pairs={{0,96},{32,0},{64,32},{96,64},{1,97},{33,1},{65,33},{97,65},{2,98}... | collective-permute-start | bytes 1966088 | tf_op jit(solution)/shard_map/ppermute | solution.py:115
  52.8 0.6 fusion.85
  53.4 1.8 multiply_cosine_fusion
  55.2 2.1 %gather_fusion.1 = bf16[16,256,256]{2,1,0:T(8,128)(2,1)} fusion(bf16[8,256,256]{2,1,0:T(8,128)(2,1)S(1)} %bitcast.118, s32[1024]{0:T(1024)} %pad_clamp_fusion.6), kind=kCustom, calls=%fused_computation.1 | custom fusion | bytes 4194368 | tf_op jit(solution)/shard_map/gather | solution.py:134
  57.3 2.7 %fusion.96 = (bf16[4,256,256]{2,1,0:T(8,128)(2,1)S(1)}, bf16[4,256,256]{2,1,0:T(8,128)(2,1)}, bf16[4,256,256]{2,1,0:T(8,128)(2,1)}, bf16[4,256,256]{2,1,0:T(8,128)(2,1)}) fusion(bf16[16,256,256]{2,1,0:T(8,128)(2,1)} %gather_fusion.1), kind=kLoop, calls=%fused_computation.222 | loop fusion | bytes 4194304 | tf_op jit(solution)/shard_map/slice | solution.py:136
  60.1 0.6 collective-permute-start.1
  60.7 1.1 collective-permute-start
  61.8 4.2 %collective-permute-done.8 = bf16[20,64,256]{2,1,0:T(8,128)(2,1)} collective-permute-done((bf16[20,64,256]{2,1,0:T(8,128)(2,1)}, bf16[20,64,256]{2,1,0:T(8,128)(2,1)}, u32[]{:S(2)}, u32[]{:S(2)}) %collective-permute-start.8) | collective-permute-done | bytes 655392 | tf_op jit(solution)/shard_map/ppermute | solution.py:115
  66.0 0.9 collective-permute-start.2
  66.9 11.8 %collective-permute-done.7 = bf16[20,64,256]{2,1,0:T(8,128)(2,1)} collective-permute-done((bf16[20,64,256]{2,1,0:T(8,128)(2,1)}, bf16[20,64,256]{2,1,0:T(8,128)(2,1)}, u32[]{:S(2)}, u32[]{:S(2)}) %collective-permute-start.7) | collective-permute-done | bytes 655392 | tf_op jit(solution)/shard_map/ppermute | solution.py:115
  78.8 2.9 %pad_maximum_fusion = bf16[80,64,256]{2,1,0:T(8,128)(2,1)} fusion(bf16[20,64,256]{2,1,0:T(8,128)(2,1)} %collective-permute-done.9, bf16[20,64,256]{2,1,0:T(8,128)(2,1)} %collective-permute-done.8, bf16[20,64,256]{2,1,0:T(8,128)(2,1)} %collective-permute-done.7, bf16[20,64,256]{2,1,0:T(8,128)(2,1)S(1)} %get-tuple-element.17), kind=kLoop, calls=%fused_computation.23 | loop fusion | flops 3932160 | bytes 5242880 | tf_op jit(solution)/shard_map/concatenate | solution.py:180
  81.6 2.4 %gather_fusion.7 = bf16[4,64,256]{2,1,0:T(8,128)(2,1)S(1)} fusion(bf16[80,64,256]{2,1,0:T(8,128)(2,1)} %pad_maximum_fusion, s32[1024]{0:T(1024)} %pad_clamp_fusion), kind=kCustom, calls=%fused_computation.7 | custom fusion | bytes 262160 | tf_op jit(solution)/shard_map/gather | solution.py:196
  84.4 0.9 broadcast_in_dim.24
  85.3 4.5 %all-to-all-start.1 = ((bf16[8,4,16,448]{3,2,1,0:T(8,128)(2,1)}), bf16[8,4,16,448]{3,2,1,0:T(8,128)(2,1)S(1)}, u32[]{:S(2)}, u32[]{:S(2)}) async-start(bf16[8,4,16,448]{3,2,1,0:T(8,128)(2,1)} %broadcast_in_dim.24), calls=%async_computation.1 | async-start | bytes 1048576 | tf_op jit(solution)/shard_map/all_to_all | solution.py:231
  90.2 3.1 %gather_fusion.6 = bf16[16,64,256]{2,1,0:T(8,128)(2,1)} fusion(bf16[80,64,256]{2,1,0:T(8,128)(2,1)} %pad_maximum_fusion, s32[1024]{0:T(1024)S(1)} %pad_clamp_fusion.1), kind=kCustom, calls=%fused_computation.6 | custom fusion | bytes 1048640 | tf_op jit(solution)/shard_map/gather | solution.py:193
  93.3 2.9 %pad_maximum_fusion.1 = bf16[16,256,256]{2,1,0:T(8,128)(2,1)} fusion(bf16[4,256,256]{2,1,0:T(8,128)(2,1)} %collective-permute-done.2, bf16[4,256,256]{2,1,0:T(8,128)(2,1)} %collective-permute-done.1, bf16[4,256,256]{2,1,0:T(8,128)(2,1)} %collective-permute-done, bf16[4,256,256]{2,1,0:T(8,128)(2,1)S(1)} %get-tuple-element.21), kind=kLoop, calls=%fused_computation.24 | loop fusion | flops 3145728 | bytes 4194304 | tf_op jit(solution)/shard_map/concatenate | solution.py:135
  96.2 2.2 %gather_fusion.2 = bf16[4,256,256]{2,1,0:T(8,128)(2,1)S(1)} fusion(bf16[16,256,256]{2,1,0:T(8,128)(2,1)} %pad_maximum_fusion.1, s32[1024]{0:T(1024)S(1)} %pad_clamp_fusion.5), kind=kCustom, calls=%fused_computation.2 | custom fusion | bytes 1048592 | tf_op jit(solution)/shard_map/gather | solution.py:143
  98.4 1.0 copy.68
  99.4 0.7 all-to-all-done.1
  100.1 0.3 copy.62
  100.4 0.6 dot_general.31
  101.0 3.0 %fusion = f32[512]{0:T(512)S(1)} fusion(bf16[512,3584]{0,1:T(8,128)(2,1)} %all-gather.2.cloned.1.call-done), kind=kLoop, calls=%fused_computation.10 | loop fusion | flops 5504512 | bytes 3672064 | tf_op jit(solution)/shard_map/reduce_sum | solution.py:245
  104.1 1.6 fusion.2
  105.8 1.2 convolution_bitcast_fusion
  106.9 1.2 fusion.36
  108.2 0.4 copy-done.26
  108.6 1.2 convolution_convert_fusion.1
  109.8 0.9 copy.61
  110.7 0.7 pad_maximum_fusion.3
  111.4 2.0 %collective-permute-start.3 = (bf16[256,512]{0,1:T(8,128)(2,1)}, bf16[256,512]{0,1:T(8,128)(2,1)}, u32[]{:S(2)}, u32[]{:S(2)}) collective-permute-start(bf16[256,512]{0,1:T(8,128)(2,1)} %pad_maximum_fusion.3), channel_id=1, source_target_pairs={{0,8},{8,16},{16,24},{24,32},{32,40},{40,48},{48,56},{56,64},{64,7... | collective-permute-start | bytes 786440 | tf_op jit(solution)/shard_map/ppermute | solution.py:17
  113.4 5.3 %fusion.99 = f32[512,512]{0,1:T(8,128)S(1)} fusion(bf16[512,3584]{0,1:T(8,128)(2,1)} %copy-done.3, bf16[3584,512]{1,0:T(8,128)(2,1)} %param.18), kind=kOutput, calls=%fused_computation.225 | convolution fusion | flops 1879048192 | bytes 8388608 | tf_op jit(solution)/shard_map/dot_general | solution.py:264
  118.7 3.0 %fusion.13 = f32[512,512]{0,1:T(8,128)S(1)} fusion(f32[512,512]{0,1:T(8,128)S(1)} %fusion.99, bf16[64,512]{1,0:T(8,128)(2,1)S(1)} %bitcast.125, bf16[512,64]{0,1:T(8,128)(2,1)S(1)} %bitcast.126, bf16[64,3584]{1,0:T(8,128)(2,1)S(1)} %dot_general.31, bf16[512,3584]{0,1:T(8,128)(2,1)} %copy-done.3), kind=kOutput, calls=%fused_computation.28 | convolution fusion | flops 269025280 | bytes 6356992 | tf_op jit(solution)/shard_map/dot_general | solution.py:258
  122.3 0.4 copy-done.6
  122.9 1.0 fusion.98
  124.0 2.6 %fusion.5 = (f32[2,512]{1,0:T(2,128)S(1)}, f32[1792,512,2]{1,0,2:T(8,128)S(1)}) fusion(pred[512,1792]{0,1:T(8,128)(4,1)S(1)} %copy-done.5, bf16[512,2,128]{2,0,1:T(8,128)(2,1)S(1)} %get-tuple-element.26, bf16[512,2,128]{2,0,1:T(8,128)(2,1)S(1)} %get-tuple-element.25, bf16[512,256]{1,0:T(8,128)(2,1)S(1)} %copy-done.10, bf16[256,256]{1,0:T(8,128)(2,1)S(1)} %copy.60, ...), kind=kOutput, calls=%fused_computation.18 | convolution fusion | flops 948829184 | bytes 9703424 | tf_op jit(solution)/shard_map/tkrd,skd->krts/dot_general | solution.py:90
  126.7 1.7 fusion.3
  128.4 2.4 %divide_convert_fusion = bf16[512,1,2,256]{0,3,2,1:T(8,128)(2,1)S(1)} fusion(f32[1792,512,2]{1,0,2:T(8,128)S(1)} %get-tuple-element.44, f32[2,512]{1,0:T(2,128)S(1)} %get-tuple-element.43, pred[512,1792]{0,1:T(8,128)(4,1)S(1)} %copy-done.5, bf16[512,256]{0,1:T(8,128)(2,1)S(1)} %copy-done.12, bf16[256,256]{0,1:T(8,128)(2,1)S(1)} %get-tuple-element.31, ...), kind=kOutput, calls=%fused_computation.33 | convolution fusion | flops 950140928 | bytes 9707520 | tf_op jit(solution)/shard_map/krts,skd->tkrd/dot_general | solution.py:97
  130.9 3.9 %convolution_convert_fusion = bf16[512,3584]{0,1:T(8,128)(2,1)} fusion(bf16[512,512]{0,1:T(8,128)(2,1)S(1)} %bitcast.134, bf16[512,3584]{1,0:T(8,128)(2,1)S(1)} %copy-done.25), kind=kOutput, calls=%fused_computation.17 | convolution fusion | flops 1880883200 | bytes 7864320 | tf_op jit(solution)/shard_map/dot_general | solution.py:293
  134.8 38.7 %reduce-scatter.2.cloned.1.call-done = bf16[512,448]{0,1:T(8,128)(2,1)} async-done(((bf16[512,3584]{0,1:T(8,128)(2,1)}), bf16[512,448]{0,1:T(8,128)(2,1)}) %reduce-scatter.2.cloned.1.call-update) | async-done | bytes 458768 | tf_op jit(solution)/shard_map/reduce_scatter | solution.py:294
  (132 shorter events, 4.4 us)
Async XLA Ops:
  6.5 99.2 %copy-start = (bf16[3584,256]{1,0:T(8,128)(2,1)S(1)}, bf16[3584,256]{1,0:T(8,128)(2,1)}, u32[]{:S(2)}) copy-start(bf16[3584,256]{1,0:T(8,128)(2,1)} %param.19) | copy-start | bytes 5505028
  6.5 9.4 %copy-start.9 = (bf16[2,256,256]{2,1,0:T(8,128)(2,1)S(1)}, bf16[2,256,256]{2,1,0:T(8,128)(2,1)}, u32[]{:S(2)}) copy-start(bf16[2,256,256]{2,1,0:T(8,128)(2,1)} %param.31) | copy-start | bytes 786436
  6.5 94.5 %all-gather.2.cloned.1.call-start = ((), (), s32[]{:S(2)}) async-start(), calls=%async_computation.3 | async-start | bytes 4128768 | tf_op jit(solution)/shard_map/all_gather | solution.py:242
  7.9 13.4 %copy-start.14 = (s32[16,4]{0,1:T(4,128)S(1)}, s32[16,4]{0,1:T(4,128)}, u32[]{:S(2)}) copy-start(s32[16,4]{0,1:T(4,128)} %param.24) | copy-start | bytes 772
  8.0 13.5 %copy-start.2 = (s32[64]{0:T(128)S(1)}, s32[64]{0:T(128)}, u32[]{:S(2)}) copy-start(s32[64]{0:T(128)} %param.25) | copy-start | bytes 772
  10.5 28.3 %collective-permute-start.6 = (bf16[3,256,256]{2,1,0:T(8,128)(2,1)}, bf16[3,256,256]{2,1,0:T(8,128)(2,1)S(1)}, u32[]{:S(2)}, u32[]{:S(2)}) collective-permute-start(bf16[3,256,256]{2,1,0:T(8,128)(2,1)} %get-tuple-element.35), channel_id=1, source_target_pairs={{0,24},{8,0},{16,8},{24,16},{1,25},{9,1},{17,9},{25,17},{2,26},{10... | collective-permute-start | bytes 1179656 | tf_op jit(solution)/shard_map/ppermute | solution.py:115
  14.6 22.3 %collective-permute-start.5 = (bf16[3,256,256]{2,1,0:T(8,128)(2,1)}, bf16[3,256,256]{2,1,0:T(8,128)(2,1)}, u32[]{:S(2)}, u32[]{:S(2)}) collective-permute-start(bf16[3,256,256]{2,1,0:T(8,128)(2,1)} %get-tuple-element.35), channel_id=1, source_target_pairs={{0,16},{8,24},{16,0},{24,8},{1,17},{9,25},{17,1},{25,9},{2,18},{10... | collective-permute-start | bytes 1179656 | tf_op jit(solution)/shard_map/ppermute | solution.py:115
  14.6 20.5 %collective-permute-start.4 = (bf16[3,256,256]{2,1,0:T(8,128)(2,1)}, bf16[3,256,256]{2,1,0:T(8,128)(2,1)}, u32[]{:S(2)}, u32[]{:S(2)}) collective-permute-start(bf16[3,256,256]{2,1,0:T(8,128)(2,1)} %get-tuple-element.35), channel_id=1, source_target_pairs={{0,8},{8,16},{16,24},{24,0},{1,9},{9,17},{17,25},{25,1},{2,10},{10... | collective-permute-start | bytes 1179656 | tf_op jit(solution)/shard_map/ppermute | solution.py:115
  17.0 38.2 %all-to-all-start = ((bf16[4,2,256,256]{3,2,1,0:T(8,128)(2,1)}), bf16[4,2,256,256]{3,2,1,0:T(8,128)(2,1)S(1)}, u32[]{:S(2)}, u32[]{:S(2)}) async-start(bf16[4,2,256,256]{3,2,1,0:T(8,128)(2,1)} %broadcast_in_dim.20), calls=%async_computation | async-start | bytes 2097152 | tf_op jit(solution)/shard_map/all_to_all | solution.py:124
  21.5 0.9 copy-start.15
  21.5 0.9 copy-start.16
  21.5 1.8 copy-start.27
  21.6 5.3 %copy-start.17 = (s32[16,4]{0,1:T(4,128)S(1)}, s32[16,4]{0,1:T(4,128)}, u32[]{:S(2)}) copy-start(s32[16,4]{0,1:T(4,128)} %param.28) | copy-start | bytes 772
  26.8 12.7 %copy-start.19 = (s32[4,1]{0,1:T(1,128)}, s32[4,1]{0,1:T(1,128)S(1)}, u32[]{:S(2)}) copy-start(s32[4,1]{0,1:T(1,128)S(1)} %reduce-window.4) | copy-start | bytes 52
  28.8 0.6 copy-start.21
  46.5 19.5 %collective-permute-start.8 = (bf16[20,64,256]{2,1,0:T(8,128)(2,1)}, bf16[20,64,256]{2,1,0:T(8,128)(2,1)}, u32[]{:S(2)}, u32[]{:S(2)}) collective-permute-start(bf16[20,64,256]{2,1,0:T(8,128)(2,1)} %get-tuple-element.18), channel_id=1, source_target_pairs={{0,64},{32,96},{64,0},{96,32},{1,65},{33,97},{65,1},{97,33},{2,66}... | collective-permute-start | bytes 1966088 | tf_op jit(solution)/shard_map/ppermute | solution.py:115
  49.5 3.9 %copy-start.23 = (f32[128]{0:T(128)}, f32[128]{0:T(128)S(1)}, u32[]{:S(2)}) copy-start(f32[128]{0:T(128)S(1)} %multiply_power_fusion) | copy-start | bytes 1540
  49.5 29.1 %collective-permute-start.7 = (bf16[20,64,256]{2,1,0:T(8,128)(2,1)}, bf16[20,64,256]{2,1,0:T(8,128)(2,1)}, u32[]{:S(2)}, u32[]{:S(2)}) collective-permute-start(bf16[20,64,256]{2,1,0:T(8,128)(2,1)} %get-tuple-element.19), channel_id=1, source_target_pairs={{0,32},{32,64},{64,96},{96,0},{1,33},{33,65},{65,97},{97,1},{2,34}... | collective-permute-start | bytes 1966088 | tf_op jit(solution)/shard_map/ppermute | solution.py:115
  50.2 28.6 %collective-permute-start.9 = (bf16[20,64,256]{2,1,0:T(8,128)(2,1)}, bf16[20,64,256]{2,1,0:T(8,128)(2,1)}, u32[]{:S(2)}, u32[]{:S(2)}) collective-permute-start(bf16[20,64,256]{2,1,0:T(8,128)(2,1)} %get-tuple-element.20), channel_id=1, source_target_pairs={{0,96},{32,0},{64,32},{96,64},{1,97},{33,1},{65,33},{97,65},{2,98}... | collective-permute-start | bytes 1966088 | tf_op jit(solution)/shard_map/ppermute | solution.py:115
  57.3 9.6 %copy-start.18 = (s32[4]{0:T(128)S(1)}, s32[4]{0:T(128)}, u32[]{:S(2)}) copy-start(s32[4]{0:T(128)} %fusion.85) | copy-start | bytes 52
  60.1 33.2 %collective-permute-start.1 = (bf16[4,256,256]{2,1,0:T(8,128)(2,1)}, bf16[4,256,256]{2,1,0:T(8,128)(2,1)}, u32[]{:S(2)}, u32[]{:S(2)}) collective-permute-start(bf16[4,256,256]{2,1,0:T(8,128)(2,1)} %get-tuple-element.22), channel_id=1, source_target_pairs={{0,16},{8,24},{16,0},{24,8},{1,17},{9,25},{17,1},{25,9},{2,18},{10... | collective-permute-start | bytes 1572872 | tf_op jit(solution)/shard_map/ppermute | solution.py:115
  60.7 32.6 %collective-permute-start = (bf16[4,256,256]{2,1,0:T(8,128)(2,1)}, bf16[4,256,256]{2,1,0:T(8,128)(2,1)}, u32[]{:S(2)}, u32[]{:S(2)}) collective-permute-start(bf16[4,256,256]{2,1,0:T(8,128)(2,1)} %get-tuple-element.23), channel_id=1, source_target_pairs={{0,8},{8,16},{16,24},{24,0},{1,9},{9,17},{17,25},{25,1},{2,10},{10... | collective-permute-start | bytes 1572872 | tf_op jit(solution)/shard_map/ppermute | solution.py:115
  66.0 27.3 %collective-permute-start.2 = (bf16[4,256,256]{2,1,0:T(8,128)(2,1)}, bf16[4,256,256]{2,1,0:T(8,128)(2,1)}, u32[]{:S(2)}, u32[]{:S(2)}) collective-permute-start(bf16[4,256,256]{2,1,0:T(8,128)(2,1)} %get-tuple-element.24), channel_id=1, source_target_pairs={{0,24},{8,0},{16,8},{24,16},{1,25},{9,1},{17,9},{25,17},{2,26},{10... | collective-permute-start | bytes 1572872 | tf_op jit(solution)/shard_map/ppermute | solution.py:115
  81.6 8.4 %copy-start.20 = (s32[4,1]{0,1:T(1,128)S(1)}, s32[4,1]{0,1:T(1,128)}, u32[]{:S(2)}) copy-start(s32[4,1]{0,1:T(1,128)} %copy-done.19) | copy-start | bytes 52
  81.6 8.4 %copy-start.22 = (s32[4]{0:T(128)S(1)}, s32[4]{0:T(128)}, u32[]{:S(2)}) copy-start(s32[4]{0:T(128)} %copy-done.21) | copy-start | bytes 52
  85.3 14.8 %all-to-all-start.1 = ((bf16[8,4,16,448]{3,2,1,0:T(8,128)(2,1)}), bf16[8,4,16,448]{3,2,1,0:T(8,128)(2,1)S(1)}, u32[]{:S(2)}, u32[]{:S(2)}) async-start(bf16[8,4,16,448]{3,2,1,0:T(8,128)(2,1)} %broadcast_in_dim.24), calls=%async_computation.1 | async-start | bytes 1048576 | tf_op jit(solution)/shard_map/all_to_all | solution.py:231
  89.8 83.7 %reduce-scatter.2.cloned.1.call-start = ((), (), s32[]{:S(2)}) async-start(), calls=%async_computation.4 | async-start | bytes 4128768 | tf_op jit(solution)/shard_map/reduce_scatter | solution.py:294
  100.1 3.9 %copy-start.13 = (f32[3584]{0:T(1024)S(1)}, f32[3584]{0:T(1024)}, u32[]{:S(2)}) copy-start(f32[3584]{0:T(1024)} %param.17) | copy-start | bytes 43012
  101.0 3.1 %copy-start.4 = (bf16[512,3584]{0,1:T(8,128)(2,1)S(1)}, bf16[512,3584]{0,1:T(8,128)(2,1)}, u32[]{:S(2)}) copy-start(bf16[512,3584]{0,1:T(8,128)(2,1)} %all-gather.2.cloned.1.call-done) | copy-start | bytes 11010052
  105.7 2.4 %copy-start.3 = (bf16[512,3584]{0,1:T(8,128)(2,1)}, bf16[512,3584]{0,1:T(8,128)(2,1)S(1)}, u32[]{:S(2)}) copy-start(bf16[512,3584]{0,1:T(8,128)(2,1)S(1)} %fusion.2) | copy-start | bytes 11010052
  105.7 1.2 copy-start.24
  105.7 2.8 %copy-start.26 = (bf16[3584,256]{1,0:T(8,128)(2,1)S(1)}, bf16[3584,256]{1,0:T(8,128)(2,1)}, u32[]{:S(2)}) copy-start(bf16[3584,256]{1,0:T(8,128)(2,1)} %param.20) | copy-start | bytes 5505028
  109.7 1.7 copy-start.11
  111.4 11.5 %collective-permute-start.3 = (bf16[256,512]{0,1:T(8,128)(2,1)}, bf16[256,512]{0,1:T(8,128)(2,1)}, u32[]{:S(2)}, u32[]{:S(2)}) collective-permute-start(bf16[256,512]{0,1:T(8,128)(2,1)} %pad_maximum_fusion.3), channel_id=1, source_target_pairs={{0,8},{8,16},{16,24},{24,32},{32,40},{40,48},{48,56},{56,64},{64,7... | collective-permute-start | bytes 786440 | tf_op jit(solution)/shard_map/ppermute | solution.py:17
  121.7 1.0 copy-start.6
  121.7 1.0 copy-start.7
  121.8 2.2 %copy-start.5 = (pred[512,1792]{0,1:T(8,128)(4,1)S(1)}, pred[512,1792]{0,1:T(8,128)(4,1)}, u32[]{:S(2)}) copy-start(pred[512,1792]{0,1:T(8,128)(4,1)} %pad_add_fusion) | copy-start | bytes 2752516
  121.8 2.2 %copy-start.10 = (bf16[512,256]{1,0:T(8,128)(2,1)S(1)}, bf16[512,256]{1,0:T(8,128)(2,1)}, u32[]{:S(2)}) copy-start(bf16[512,256]{1,0:T(8,128)(2,1)} %copy.61) | copy-start | bytes 786436
  126.7 1.7 copy-start.8
  126.7 1.7 copy-start.12
  128.4 2.5 %copy-start.25 = (bf16[512,3584]{1,0:T(8,128)(2,1)S(1)}, bf16[512,3584]{1,0:T(8,128)(2,1)}, u32[]{:S(2)}) copy-start(bf16[512,3584]{1,0:T(8,128)(2,1)} %param.21) | copy-start | bytes 11010052
  130.9 42.6 %copy-start.1 = (bf16[3584,256]{1,0:T(8,128)(2,1)S(1)}, bf16[3584,256]{1,0:T(8,128)(2,1)}, u32[]{:S(2)}) copy-start(bf16[3584,256]{1,0:T(8,128)(2,1)} %param.19) | copy-start | bytes 5505028
Sparse Core Ops, SparseCore 0:
  16.0 30.6 all-gather.1
  134.9 38.5 reduce-scatter.1
